TPU v7x, 32 devices: a whole 2x2x4 slice. The times are simulated.
32 devices in a mesh: px: 4 (over y, x), py: 8 (over z, core).
Axes of the slice: x: 2, y: 2, z: 4, core: 2. Of those that a mesh axis runs over, the one named last changes fastest.
Arguments:
- residual: float32 [10, 2048, 2048], P(None, 'py', 'px'), may hold values from -6 to 6
- lambda_x: float32 [2048], P('px'), may hold values from 0.1 to 4
- lambda_y: float32 [2048], P('py'), may hold values from 0.1 to 4
- coupling: float32 [9], replicated, may hold values from 0.2 to 2
- layer_shift: float32 [10], replicated, may hold values from 0.05 to 1
- left_x: bfloat16 [2048, 2048], P(None, 'px'), may hold values from -0.125 to 0.125
- left_y: bfloat16 [2048, 2048], P('py'), may hold values from -0.125 to 0.125
- right_y: bfloat16 [2048, 2048], P('py'), may hold values from -0.125 to 0.125
- right_x: bfloat16 [2048, 2048], P(None, 'px'), may hold values from -0.125 to 0.125
- regime_code: int32 [10, 2048, 2048], P(None, 'py', 'px'), may hold values from 0 to 3
- upwind_flag: int32 [2, 10, 2048, 2048], P(None, None, 'py', 'px'), may hold values from 0 to 1
- mobility_table: float32 [4], replicated, may hold values from 0.3 to 3
Outputs:
- correction: float32 [10, 2048, 2048], P(None, 'py', 'px')
- balance: float32 [10, 2048, 2048], P(None, 'py', 'px')
Inputs may be any that keep to these rules, and one draw needn't show every extreme that they name: `regime_code`: a regime number of each cell.
All inputs are finite; a program needn't handle non-finite values.
Results may differ from a plain program's by a relative error of at most 0.0057.
Values may be sent and summed in bfloat16 or wider, within the bound.
No kernel may reach another device: no remote copies, remote signals or barrier semaphores. Data moves between devices by JAX's collectives and lax.ppermute only.
A program may use at most 192 MiB of HBM per device.

v0:
```python
import jax
import jax.numpy as jnp
from jax import lax
from jax.sharding import PartitionSpec as P


def with_halo(block, sides, width):
    for axis, dim in sides:
        count = lax.axis_size(axis)
        forward = [(i, i + 1) for i in range(count - 1)]
        backward = [(target, source) for source, target in forward]
        low = lax.ppermute(
            lax.slice_in_dim(block, block.shape[dim] - width, None, axis=dim), axis, forward
        )
        high = lax.ppermute(lax.slice_in_dim(block, 0, width, axis=dim), axis, backward)
        block = jnp.concatenate([low, block, high], axis=dim)
    return block


def thomas_solve(rhs, lambda_x, lambda_y, coupling, layer_shift):
    layers = rhs.shape[0]
    mode_sum = lambda_y[:, None] + lambda_x[None, :]
    ratios = []
    partial_values = []
    for layer_index in range(layers):
        diagonal = mode_sum + layer_shift[layer_index]
        if layer_index > 0:
            diagonal = diagonal + coupling[layer_index - 1]
        if layer_index < layers - 1:
            diagonal = diagonal + coupling[layer_index]
        if layer_index == 0:
            pivots = diagonal
            solved = rhs[0] / pivots
        else:
            pivots = diagonal + coupling[layer_index - 1] * ratios[-1]
            solved = (rhs[layer_index] + coupling[layer_index - 1] * partial_values[-1]) / pivots
        partial_values.append(solved)
        if layer_index < layers - 1:
            ratios.append(-coupling[layer_index] / pivots)
    results = [partial_values[layers - 1]]
    for layer_index in range(layers - 2, -1, -1):
        results.append(partial_values[layer_index] - ratios[layer_index] * results[-1])
    return jnp.stack(results[::-1])


def shards(
    residual,
    lambda_x,
    lambda_y,
    coupling,
    layer_shift,
    left_x,
    left_y,
    right_y,
    right_x,
    regime_code,
    upwind_flag,
    mobility_table,
):
    rounded = residual.astype(jnp.bfloat16)

    def forward(block):
        weights = left_x
        spectral_x = jnp.einsum(
            "zyx,xi->zyi",
            lax.all_gather(block, "px", axis=2, tiled=True),
            weights,
            preferred_element_type=jnp.float32,
        ).astype(jnp.bfloat16)
        weights = left_y
        return jnp.einsum(
            "jy,zyi->zji",
            weights,
            lax.all_gather(spectral_x, "py", axis=1, tiled=True),
            preferred_element_type=jnp.float32,
        )

    mobility = jnp.zeros(regime_code.shape, jnp.float32)
    for regime in range(mobility_table.shape[0]):
        mobility = jnp.where(regime_code == regime, mobility_table[regime], mobility)
    spectral = forward(rounded)
    solved = thomas_solve(spectral, lambda_x, lambda_y, coupling, layer_shift).astype(jnp.bfloat16)
    weights = right_y
    back_y = jnp.einsum(
        "yj,zji->zyi",
        weights,
        lax.all_gather(solved, "py", axis=1, tiled=True),
        preferred_element_type=jnp.float32,
    ).astype(jnp.bfloat16)
    weights = right_x
    correction = jnp.einsum(
        "zyi,ix->zyx",
        lax.all_gather(back_y, "px", axis=2, tiled=True),
        weights,
        preferred_element_type=jnp.float32,
    )
    width_x = correction.shape[2]
    width_y = correction.shape[1]
    stacked = jnp.stack(
        [
            correction,
            mobility,
            upwind_flag[0].astype(jnp.float32),
            upwind_flag[1].astype(jnp.float32),
        ]
    )
    extended = with_halo(stacked, (("px", 3), ("py", 2)), 1)
    press_x = extended[0][:, 1:-1, :]
    mobil_x = extended[1][:, 1:-1, :]
    flags_x = extended[2][:, 1:-1, :]
    upwind_x = jnp.where(flags_x[:, :, :-1] > 0.5, mobil_x[:, :, :-1], mobil_x[:, :, 1:])
    flux_x = upwind_x * (press_x[:, :, :-1] - press_x[:, :, 1:])
    faces_x = lax.axis_index("px") * width_x + jnp.arange(width_x + 1, dtype=jnp.int32)
    valid_x = (faces_x >= 1) & (faces_x <= width_x * lax.axis_size("px") - 1)
    flux_x = jnp.where(valid_x[None, None, :], flux_x, 0.0)
    net_x = flux_x[:, :, 1:] - flux_x[:, :, :-1]
    press_y = extended[0][:, :, 1:-1]
    mobil_y = extended[1][:, :, 1:-1]
    flags_y = extended[3][:, :, 1:-1]
    upwind_y = jnp.where(flags_y[:, :-1, :] > 0.5, mobil_y[:, :-1, :], mobil_y[:, 1:, :])
    flux_y = upwind_y * (press_y[:, :-1, :] - press_y[:, 1:, :])
    faces_y = lax.axis_index("py") * width_y + jnp.arange(width_y + 1, dtype=jnp.int32)
    valid_y = (faces_y >= 1) & (faces_y <= width_y * lax.axis_size("py") - 1)
    flux_y = jnp.where(valid_y[None, :, None], flux_y, 0.0)
    net_y = flux_y[:, 1:, :] - flux_y[:, :-1, :]
    balance = net_x + net_y
    return (correction, balance)


def solution(mesh):
    return jax.shard_map(
        shards,
        mesh=mesh,
        in_specs=(
            P(None, "py", "px"),
            P("px"),
            P("py"),
            P(),
            P(),
            P(None, "px"),
            P("py", None),
            P("py", None),
            P(None, "px"),
            P(None, "py", "px"),
            P(None, None, "py", "px"),
            P(),
        ),
        out_specs=(P(None, "py", "px"), P(None, "py", "px")),
        check_vma=False,
    )
```

profile of v0, /device:TPU:1, one launch (start us, length us, event | category | flops | bytes accessed | tf_op | source)
XLA Modules:
  0.0 841.0 jit_solution(6633718282841774213)
XLA Ops:
  7.2 4.5 convert_element_type.21
  11.8 107.1 %all-gather.5.cloned.1.call-done = bf16[10,256,2048]{2,1,0:T(8,128)(2,1)} async-done(((bf16[10,256,512]{2,1,0:T(8,128)(2,1)}), bf16[10,256,2048]{2,1,0:T(8,128)(2,1)}) %all-gather.5.cloned.1.call-update) | async-done | bytes 10485776 | tf_op jit(solution)/shard_map/all_gather | solution.py:66
  118.9 9.4 %fusion.9 = bf16[10,256,512]{1,2,0:T(8,128)(2,1)} fusion(bf16[10,256,2048]{2,1,0:T(8,128)(2,1)} %all-gather.5.cloned.1.call-done, bf16[2048,512]{1,0:T(8,128)(2,1)S(1)} %copy-done), kind=kOutput, calls=%fused_computation.41 | convolution fusion | flops 5370019840 | bytes 15204352 | tf_op jit(solution)/shard_map/zyx,xi->zyi/dot_general | solution.py:64
  135.5 179.9 %all-gather.7.cloned.1.call-done = bf16[10,2048,512]{1,2,0:T(8,128)(2,1)} async-done(((bf16[10,256,512]{1,2,0:T(8,128)(2,1)}), bf16[10,2048,512]{1,2,0:T(8,128)(2,1)}) %all-gather.7.cloned.1.call-update) | async-done | bytes 20971536 | tf_op jit(solution)/shard_map/all_gather | solution.py:74
  315.4 10.3 %convolution_bitcast_fusion = f32[10,256,512]{1,2,0:T(8,128)S(1)} fusion(bf16[10,2048,512]{1,2,0:T(8,128)(2,1)} %all-gather.7.cloned.1.call-done, bf16[256,2048]{1,0:T(8,128)(2,1)S(1)} %copy-done.16), kind=kOutput, calls=%fused_computation.36 | convolution fusion | flops 5368709120 | bytes 27262976 | tf_op jit(solution)/shard_map/jy,zyi->zji/dot_general | solution.py:71
  325.7 14.8 %fusion.59 = (bf16[10,256,512]{1,2,0:T(8,128)(2,1)}, bf16[1,256,512]{1,2,0:T(8,128)(2,1)S(1)}, f32[1,256,512]{1,2,0:T(8,128)S(1)}, f32[1,256,512]{1,2,0:T(8,128)...) fusion(f32[]{:T(128)S(6)} %neg.27, f32[]{:T(128)} %bitcast.4, ...), kind=kLoop, calls=%fused_computation.107 | loop fusion | flops 13631487 | bytes 8916080
  341.3 4.8 convert_dynamic-update-slice_fusion.7
  346.8 7.5 convert_dynamic-update-slice_fusion.5
  355.0 10.2 %convert_dynamic-update-slice_fusion.3 = bf16[10,256,512]{1,2,0:T(8,128)(2,1)} fusion(bf16[10,256,512]{1,2,0:T(8,128)(2,1)} %convert_dynamic-update-slice_fusion.4, f32[1,256,512]{1,2,0:T(8,128)S(1)} %get-tuple-element.7, f32[1,256,512]{1,2,0:T(8,128)S(1)} %get-tuple-element.6, f32[]{:T(128)} %bitcast.3, f32[]{:T(128)S(6)} %neg.27, f32[]{:T(128)} %bitcast.4, ...), kind=kLoop, calls=%fused_computation.111 | loop fusion | flops 5636096 | bytes 1320988
  365.9 13.9 %convert_dynamic-update-slice_fusion.1 = bf16[10,256,512]{1,2,0:T(8,128)(2,1)} fusion(bf16[10,256,512]{1,2,0:T(8,128)(2,1)} %convert_dynamic-update-slice_fusion.2, f32[]{:T(128)} %bitcast.3, f32[]{:T(128)S(6)} %neg.27, f32[]{:T(128)} %bitcast.4, f32[]{:T(128)} %bitcast.5, f32[]{:T(128)S(6)} %neg.28, f32[]{:T(128)} %bitcast.6, f32[]{:T(128)} %bitcast.7, ...), kind=kLoop, calls=%fused_computation.109 | loop fusion | flops 8912896 | bytes 2372132
  379.8 13.9 %convert_dynamic-update-slice_fusion = bf16[10,256,512]{1,2,0:T(8,128)(2,1)} fusion(bf16[10,256,512]{1,2,0:T(8,128)(2,1)} %convert_dynamic-update-slice_fusion.1, f32[]{:T(128)} %bitcast.3, f32[]{:T(128)S(6)} %neg.27, f32[]{:T(128)} %bitcast.4, f32[]{:T(128)} %bitcast.5, f32[]{:T(128)S(6)} %neg.28, f32[]{:T(128)} %bitcast.6, f32[]{:T(128)} %bitcast.7, ...), kind=kLoop, calls=%fused_computation.108 | loop fusion | flops 8650752 | bytes 2372132 | tf_op jit(solution)/shard_map/stack | solution.py:43
  394.2 184.4 %all-gather.9.cloned.1.call-done = bf16[10,2048,512]{1,2,0:T(8,128)(2,1)} async-done(((bf16[10,256,512]{1,2,0:T(8,128)(2,1)}), bf16[10,2048,512]{1,2,0:T(8,128)(2,1)}) %all-gather.9.cloned.1.call-update) | async-done | bytes 20971536 | tf_op jit(solution)/shard_map/all_gather | solution.py:87
  578.6 22.0 %convert_bitcast_fusion = bf16[10,256,512]{2,1,0:T(8,128)(2,1)} fusion(bf16[10,2048,512]{1,2,0:T(8,128)(2,1)} %all-gather.9.cloned.1.call-done, bf16[256,2048]{1,0:T(8,128)(2,1)S(1)} %copy-done.17), kind=kOutput, calls=%fused_computation.25 | convolution fusion | flops 5370019840 | bytes 24641536 | tf_op jit(solution)/shard_map/yj,zji->zyi/dot_general | solution.py:84
  601.3 9.3 %select_bitcast_fusion = f32[1,10,256,512]{3,2,1,0:T(8,128)} fusion(s32[10,256,512]{2,1,0:T(8,128)} %param.21, f32[]{:T(128)} %bitcast.29, f32[]{:T(128)} %bitcast.28, f32[]{:T(128)} %bitcast.27, f32[]{:T(128)} %bitcast.26), kind=kLoop, calls=%fused_computation.24 | loop fusion | flops 10485760 | bytes 10485776 | tf_op jit(solution)/shard_map/stack | solution.py:99
  610.6 10.4 %slice_convert_fusion.1 = (f32[1,10,256,512]{3,2,1,0:T(8,128)}, f32[1,10,256,512]{3,2,1,0:T(8,128)}) fusion(s32[2,10,256,512]{3,2,1,0:T(8,128)} %param.22), kind=kLoop, calls=%fused_computation.23 | loop fusion | flops 2621440 | bytes 20971520 | tf_op jit(solution)/shard_map/convert_element_type | solution.py:103
  621.0 82.5 %all-gather.11.cloned.1.call-done = bf16[10,256,2048]{2,1,0:T(8,128)(2,1)} async-done(((bf16[10,256,512]{2,1,0:T(8,128)(2,1)}), bf16[10,256,2048]{2,1,0:T(8,128)(2,1)}) %all-gather.11.cloned.1.call-update) | async-done | bytes 10485776 | tf_op jit(solution)/shard_map/all_gather | solution.py:93
  703.5 8.5 %fusion.5 = f32[10,256,512]{2,1,0:T(8,128)S(1)} fusion(bf16[10,256,2048]{2,1,0:T(8,128)(2,1)} %all-gather.11.cloned.1.call-done, bf16[2048,512]{1,0:T(8,128)(2,1)S(1)} %copy-done.15), kind=kOutput, calls=%fused_computation.37 | convolution fusion | flops 5368709120 | bytes 17825792 | tf_op jit(solution)/shard_map/zyi,ix->zyx/dot_general | solution.py:91
  712.1 5.9 pad_maximum_fusion.4
  718.0 3.3 copy.14
  721.3 3.1 collective-permute-start
  724.4 3.3 copy.15
  729.0 3.2 copy.16
  732.4 3.1 copy.17
  735.5 2.3 pad_maximum_fusion.10
  737.8 5.4 collective-permute-start.2
  743.2 2.1 collective-permute-start.3
  745.3 3.9 collective-permute-done.3
  749.2 27.6 %pad_maximum_fusion = f32[4,10,258,514]{3,2,1,0:T(8,128)} fusion(f32[4,10,1,514]{3,2,1,0:T(1,128)S(1)} %collective-permute-done.3, f32[4,10,256,1]{3,2,1,0:T(8,128)S(1)} %copy-done.8, f32[1,10,256,512]{3,2,1,0:T(8,128)} %get-tuple-element.19, f32[1,10,256,512]{3,2,1,0:T(8,128)S(1)} %bitcast.57, f32[1,10,256,512]{3,2,1,0:T(8,128)} %select_bitcast_fusion, ...), kind=kLoop, calls=%fused_computation | loop fusion | flops 37131360 | bytes 42435840 | tf_op jit(solution)/shard_map/concatenate | solution.py:16
  776.8 18.6 %slice_bitcast_fusion.3 = (f32[10,258,514]{2,1,0:T(8,128)}, f32[10,258,514]{2,1,0:T(8,128)}, f32[10,258,514]{2,1,0:T(8,128)}, f32[10,258,514]{2,1,0:T(8,128)}) fusion(f32[4,10,258,514]{3,2,1,0:T(8,128)} %pad_maximum_fusion), kind=kLoop, calls=%fused_computation.4 | loop fusion | bytes 42435840 | tf_op jit(solution)/shard_map/squeeze | solution.py:110
  795.4 14.9 %fusion.1 = f32[10,256,513]{2,1,0:T(8,128)} fusion(f32[10,258,514]{2,1,0:T(8,128)} %get-tuple-element.14, f32[10,258,514]{2,1,0:T(8,128)} %get-tuple-element.15, f32[10,258,514]{2,1,0:T(8,128)} %get-tuple-element.12, pred[513]{0:T(1024)(128)(4,1)S(1)} %fusion.62), kind=kLoop, calls=%fused_computation.7 | loop fusion | flops 6566400 | bytes 31519232 | tf_op jit(solution)/shard_map/jit(_where)/select_n | solution.py:115
  812.3 10.7 %fusion.3 = f32[10,257,512]{2,1,0:T(8,128)} fusion(f32[10,258,514]{2,1,0:T(8,128)S(1)} %copy-done.2, f32[10,258,514]{2,1,0:T(8,128)S(1)} %copy-done.3, f32[10,258,514]{2,1,0:T(8,128)} %get-tuple-element.13, pred[257]{0:T(512)(128)(4,1)S(1)} %fusion.65), kind=kLoop, calls=%fused_computation.12 | loop fusion | flops 6579200 | bytes 31580416 | tf_op jit(solution)/shard_map/jit(_where)/select_n | solution.py:124
  823.0 11.2 %fusion.4 = f32[10,256,512]{2,1,0:T(8,128)} fusion(f32[10,257,512]{2,1,0:T(8,128)} %fusion.3, f32[10,256,513]{2,1,0:T(8,128)} %fusion.1), kind=kLoop, calls=%fused_computation.16 | loop fusion | flops 3932160 | bytes 26214400 | tf_op jit(solution)/shard_map/add | solution.py:126
  (62 shorter events, 9.4 us)
Async XLA Ops:
  7.2 111.7 %copy-start = (bf16[2048,512]{1,0:T(8,128)(2,1)S(1)}, bf16[2048,512]{1,0:T(8,128)(2,1)}, u32[]{:S(2)}) copy-start(bf16[2048,512]{1,0:T(8,128)(2,1)} %param.17) | copy-start | bytes 6291460
  7.2 111.7 %all-gather.5.cloned.1.call-start = ((), (), s32[]{:S(2)}) async-start(), calls=%async_computation | async-start | bytes 13107200 | tf_op jit(solution)/shard_map/all_gather | solution.py:66
  11.7 116.8 %copy-start.12 = (f32[9]{0:T(128)S(1)}, f32[9]{0:T(128)}, u32[]{:S(2)}) copy-start(f32[9]{0:T(128)} %param.15) | copy-start | bytes 112
  11.7 123.0 %copy-start.11 = (f32[10]{0:T(128)S(1)}, f32[10]{0:T(128)}, u32[]{:S(2)}) copy-start(f32[10]{0:T(128)} %param.16) | copy-start | bytes 124
  11.8 303.7 %copy-start.16 = (bf16[256,2048]{1,0:T(8,128)(2,1)S(1)}, bf16[256,2048]{1,0:T(8,128)(2,1)}, u32[]{:S(2)}) copy-start(bf16[256,2048]{1,0:T(8,128)(2,1)} %param.18) | copy-start | bytes 3145732
  11.8 303.7 %all-gather.7.cloned.1.call-start = ((), (), s32[]{:S(2)}) async-start(), calls=%async_computation.1 | async-start | bytes 23592960 | tf_op jit(solution)/shard_map/all_gather | solution.py:74
  128.3 450.2 %all-gather.9.cloned.1.call-start = ((), (), s32[]{:S(2)}) async-start(), calls=%async_computation.2 | async-start | bytes 23592960 | tf_op jit(solution)/shard_map/all_gather | solution.py:87
  135.5 190.3 %copy-start.10 = (f32[512]{0:T(512)S(1)}, f32[512]{0:T(512)}, u32[]{:S(2)}) copy-start(f32[512]{0:T(512)} %param.13) | copy-start | bytes 6148
  135.5 190.3 %copy-start.13 = (f32[256]{0:T(256)S(1)}, f32[256]{0:T(256)}, u32[]{:S(2)}) copy-start(f32[256]{0:T(256)} %param.14) | copy-start | bytes 3076
  354.2 224.4 %copy-start.17 = (bf16[256,2048]{1,0:T(8,128)(2,1)S(1)}, bf16[256,2048]{1,0:T(8,128)(2,1)}, u32[]{:S(2)}) copy-start(bf16[256,2048]{1,0:T(8,128)(2,1)} %param.19) | copy-start | bytes 3145732
  393.8 206.9 %copy-start.14 = (f32[4]{0:T(128)S(1)}, f32[4]{0:T(128)}, u32[]{:S(2)}) copy-start(f32[4]{0:T(128)} %param.23) | copy-start | bytes 52
  393.8 309.7 %all-gather.11.cloned.1.call-start = ((), (), s32[]{:S(2)}) async-start(), calls=%async_computation.3 | async-start | bytes 13107200 | tf_op jit(solution)/shard_map/all_gather | solution.py:93
  610.6 92.9 %copy-start.15 = (bf16[2048,512]{1,0:T(8,128)(2,1)S(1)}, bf16[2048,512]{1,0:T(8,128)(2,1)}, u32[]{:S(2)}) copy-start(bf16[2048,512]{1,0:T(8,128)(2,1)} %param.20) | copy-start | bytes 6291460
  703.5 8.5 %copy-start.4 = (f32[1,10,256,512]{3,2,1,0:T(8,128)S(1)}, f32[1,10,256,512]{3,2,1,0:T(8,128)}, u32[]{:S(2)}) copy-start(f32[1,10,256,512]{3,2,1,0:T(8,128)} %get-tuple-element.18) | copy-start | bytes 15728644
  703.5 8.5 %copy-start.5 = (f32[1,10,256,512]{3,2,1,0:T(8,128)S(1)}, f32[1,10,256,512]{3,2,1,0:T(8,128)}, u32[]{:S(2)}) copy-start(f32[1,10,256,512]{3,2,1,0:T(8,128)} %get-tuple-element.19) | copy-start | bytes 15728644
  703.5 8.6 %copy-start.6 = (f32[1,10,256,512]{3,2,1,0:T(8,128)S(1)}, f32[1,10,256,512]{3,2,1,0:T(8,128)}, u32[]{:S(2)}) copy-start(f32[1,10,256,512]{3,2,1,0:T(8,128)} %select_bitcast_fusion) | copy-start | bytes 15728644
  712.0 6.0 copy-start.9
  721.3 7.7 collective-permute-start
  727.7 4.7 collective-permute-start.1
  732.4 16.8 %slice-start = ((s8[5242880]{0:T(1024)(128)(4,1)}), s8[1048576]{0:T(1024)(128)(4,1)S(1)}, s32[]{:S(2)}) async-start(s8[5242880]{0:T(1024)(128)(4,1)} %bitcast.56), calls=%async_computation.4 | async-start | bytes 2097152
  735.5 13.7 %slice-start.1 = ((s8[5242880]{0:T(1024)(128)(4,1)}), s8[4194304]{0:T(1024)(128)(4,1)S(1)}, s32[]{:S(2)}) async-start(s8[5242880]{0:T(1024)(128)(4,1)} %bitcast.56), calls=%async_computation.5 | async-start | bytes 8388608
  735.5 13.7 %copy-start.7 = (f32[4,10,256,1]{3,2,1,0:T(8,128)S(1)}, f32[4,10,256,1]{3,2,1,0:T(8,128)}, u32[]{:S(2)}) copy-start(f32[4,10,256,1]{3,2,1,0:T(8,128)} %copy.16) | copy-start | bytes 122884
  735.5 13.7 %copy-start.8 = (f32[4,10,256,1]{3,2,1,0:T(8,128)S(1)}, f32[4,10,256,1]{3,2,1,0:T(8,128)}, u32[]{:S(2)}) copy-start(f32[4,10,256,1]{3,2,1,0:T(8,128)} %copy.17) | copy-start | bytes 122884
  737.8 7.5 collective-permute-start.2
  743.2 6.0 collective-permute-start.3
  795.4 14.9 %copy-start.2 = (f32[10,258,514]{2,1,0:T(8,128)S(1)}, f32[10,258,514]{2,1,0:T(8,128)}, u32[]{:S(2)}) copy-start(f32[10,258,514]{2,1,0:T(8,128)} %get-tuple-element.14) | copy-start | bytes 15913444
  795.4 16.9 %copy-start.3 = (f32[10,258,514]{2,1,0:T(8,128)S(1)}, f32[10,258,514]{2,1,0:T(8,128)}, u32[]{:S(2)}) copy-start(f32[10,258,514]{2,1,0:T(8,128)} %get-tuple-element.15) | copy-start | bytes 15913444
  823.0 11.2 %copy-start.1 = (bf16[2048,512]{1,0:T(8,128)(2,1)S(1)}, bf16[2048,512]{1,0:T(8,128)(2,1)}, u32[]{:S(2)}) copy-start(bf16[2048,512]{1,0:T(8,128)(2,1)} %param.17) | copy-start | bytes 6291460
Sparse Core Ops, SparseCore 0:
  11.9 106.9 all-gather.4
  128.5 186.9 all-gather.6
  393.9 184.6 all-gather.8
  600.8 102.6 all-gather.10
where the time goes:
time: 845 us; the launch traced here: 841 us
  waiting for transfers between devices  558 us (66%)
  other arithmetic  164 us (19%)
  matrix products  50.2 us (6%)
  local copies, waits for them, and re-layouts  36.2 us (4%)
  between operations  19.7 us (2%)
  starting transfers between devices  12.6 us (1%)
    all_gather x1, waiting for transfers between devices, shards(): lax.all_gather(solved, 'py', axis=1, tiled=True)  184 us
    all_gather x1, waiting for transfers between devices, forward(): lax.all_gather(spectral_x, 'py', axis=1, tiled=True)  180 us
    all_gather x1, waiting for transfers between devices, forward(): lax.all_gather(block, 'px', axis=2, tiled=True)  107 us
    all_gather x1, waiting for transfers between devices, shards(): lax.all_gather(back_y, 'px', axis=2, tiled=True)  82.5 us
    unnamed x9, other arithmetic  53.4 us
    concatenate x1, other arithmetic, with_halo(): block = jnp.concatenate([low, block, high], axis=dim)  27.6 us
    dot_general x1, matrix products, shards(): jnp.einsum('yj,zji->zyi', weights, lax.all_gather(solved, 'py', axis=1, t...  22 us
    squeeze x1, local copies, waits for them, and re-layouts, shards(): flags_x = extended[2][:, 1:-1, :]  18.6 us
  transfers between devices with their start and end apart: 8, of which 6 were waited for; matrix products, arithmetic and copies ran while one was open for 3% of the time, Pallas kernels for 0%

commit v1 on v0

--- a/solution.py
+++ b/solution.py
@@ -57,41 +57,41 @@
     upwind_flag,
     mobility_table,
 ):
+    count_y = lax.axis_size("py")
     rounded = residual.astype(jnp.bfloat16)
-
-    def forward(block):
-        weights = left_x
-        spectral_x = jnp.einsum(
-            "zyx,xi->zyi",
-            lax.all_gather(block, "px", axis=2, tiled=True),
-            weights,
-            preferred_element_type=jnp.float32,
-        ).astype(jnp.bfloat16)
-        weights = left_y
-        return jnp.einsum(
-            "jy,zyi->zji",
-            weights,
-            lax.all_gather(spectral_x, "py", axis=1, tiled=True),
-            preferred_element_type=jnp.float32,
-        )
+    spectral_x = jnp.einsum(
+        "zyx,xi->zyi",
+        lax.all_gather(rounded, "px", axis=2, tiled=True),
+        left_x,
+        preferred_element_type=jnp.float32,
+    ).astype(jnp.bfloat16)
+    pencil = lax.all_to_all(spectral_x, "py", 2, 1, tiled=True)
+    modes = pencil.shape[2]
+    spectral = jnp.einsum(
+        "jy,zyi->zji",
+        lax.all_gather(left_y, "py", axis=0, tiled=True),
+        pencil,
+        preferred_element_type=jnp.float32,
+    )
+    own_x = lax.dynamic_slice_in_dim(lambda_x, lax.axis_index("py") * modes, modes)
+    all_y = lax.all_gather(lambda_y, "py", axis=0, tiled=True)
+    solved = thomas_solve(spectral, own_x, all_y, coupling, layer_shift).astype(jnp.bfloat16)
+    back_pencil = jnp.einsum(
+        "yj,zji->zyi",
+        lax.all_gather(right_y, "py", axis=0, tiled=True),
+        solved,
+        preferred_element_type=jnp.float32,
+    ).astype(jnp.bfloat16)
+    back_y = lax.all_to_all(back_pencil, "py", 1, 2, tiled=True)
+    del count_y
 
     mobility = jnp.zeros(regime_code.shape, jnp.float32)
     for regime in range(mobility_table.shape[0]):
         mobility = jnp.where(regime_code == regime, mobility_table[regime], mobility)
-    spectral = forward(rounded)
-    solved = thomas_solve(spectral, lambda_x, lambda_y, coupling, layer_shift).astype(jnp.bfloat16)
-    weights = right_y
-    back_y = jnp.einsum(
-        "yj,zji->zyi",
-        weights,
-        lax.all_gather(solved, "py", axis=1, tiled=True),
-        preferred_element_type=jnp.float32,
-    ).astype(jnp.bfloat16)
-    weights = right_x
     correction = jnp.einsum(
         "zyi,ix->zyx",
         lax.all_gather(back_y, "px", axis=2, tiled=True),
-        weights,
+        right_x,
         preferred_element_type=jnp.float32,
     )
     width_x = correction.shape[2]

time: 845 us -> 755 us (0.89)
  waiting for transfers between devices: 558 us -> 222 us
  blocking collectives: 0 us -> 188 us
  local copies, waits for them, and re-layouts: 36.2 us -> 97.5 us
  matrix products: 50.2 us -> 39 us
    all_gather x3, waiting for transfers between devices: 471 us -> 106 us  [the longest x1 106 us: shards(): lax.all_gather(rounded, 'px', axis=2, tiled=True)]
    all_gather x0 -> x1, blocking collectives: none -> 122 us  [shards(): all_y = lax.all_gather(lambda_y, 'py', axis=0, tiled=True)]
    all_to_all x0 -> x1, blocking collectives: none -> 66.5 us  [shards(): back_y = lax.all_to_all(back_pencil, 'py', 1, 2, tiled=True)]
    all_to_all x0 -> x1, waiting for transfers between devices: none -> 27.1 us  [shards(): pencil = lax.all_to_all(spectral_x, 'py', 2, 1, tiled=True)]
    all_to_all x0 -> x4, local copies, waits for them, and re-layouts: none -> 24.2 us  [the longest x2 13.4 us: shards(): back_y = lax.all_to_all(back_pencil, 'py', 1, 2, tiled=True)]
    convert_element_type x0 -> x2, local copies, waits for them, and re-layouts: none -> 18.4 us  [the longest x1 10.7 us: shards(): back_pencil = jnp.einsum('yj,zji->zyi', lax.all_gather(right_y, 'py', axi...]
    unnamed x41 -> x37, local copies, waits for them, and re-layouts: 2.82 us -> 20.7 us
    dot_general x3, matrix products: 41.8 us -> 30.5 us  [the longest x1 10.8 us: shards(): jnp.einsum('zyx,xi->zyi', lax.all_gather(rounded, 'px', axis=2, tiled=Tru...]
  transfers between devices with their start and end apart: 8 -> 9, of which waited for: 6 -> 5; matrix products, arithmetic and copies ran while one was open for 3% -> 17% of each run, Pallas kernels for 0% -> 0%
where the time goes in v1:
time: 755 us; the launch traced here: 748 us
  waiting for transfers between devices  222 us (29%)
  blocking collectives  188 us (25%)
  other arithmetic  165 us (22%)
  local copies, waits for them, and re-layouts  97.5 us (13%)
  matrix products  39 us (5%)
  between operations  19.7 us (3%)
  starting transfers between devices  17.1 us (2%)
    all_gather x1, blocking collectives, shards(): all_y = lax.all_gather(lambda_y, 'py', axis=0, tiled=True)  122 us
    all_gather x1, waiting for transfers between devices, shards(): lax.all_gather(rounded, 'px', axis=2, tiled=True)  106 us
    all_gather x1, waiting for transfers between devices, shards(): lax.all_gather(back_y, 'px', axis=2, tiled=True)  83.4 us
    all_to_all x1, blocking collectives, shards(): back_y = lax.all_to_all(back_pencil, 'py', 1, 2, tiled=True)  66.5 us
    unnamed x9, other arithmetic  54 us
    concatenate x1, other arithmetic, with_halo(): block = jnp.concatenate([low, block, high], axis=dim)  27.8 us
    all_to_all x1, waiting for transfers between devices, shards(): pencil = lax.all_to_all(spectral_x, 'py', 2, 1, tiled=True)  27.1 us
    unnamed x37, local copies, waits for them, and re-layouts  20.7 us
  transfers between devices with their start and end apart: 9, of which 5 were waited for; matrix products, arithmetic and copies ran while one was open for 17% of the time, Pallas kernels for 0%

profile of v1, /device:TPU:1, one launch (start us, length us, event | category | flops | bytes accessed | tf_op | source)
XLA Modules:
  0.0 748.1 jit_solution(3291203513705140137)
XLA Ops:
  13.2 105.7 %all-gather.6.cloned.1.call-done = bf16[10,256,2048]{2,1,0:T(8,128)(2,1)} async-done(((bf16[10,256,512]{2,1,0:T(8,128)(2,1)}), bf16[10,256,2048]{2,1,0:T(8,128)(2,1)}) %all-gather.6.cloned.1.call-update) | async-done | bytes 10485776 | tf_op jit(solution)/shard_map/all_gather | solution.py:64
  118.9 10.8 %fusion.22 = bf16[10,256,512]{2,1,0:T(8,128)(2,1)} fusion(bf16[10,256,2048]{2,1,0:T(8,128)(2,1)} %all-gather.6.cloned.1.call-done, bf16[2048,512]{1,0:T(8,128)(2,1)S(1)} %copy-done), kind=kOutput, calls=%fused_computation.46 | convolution fusion | flops 5370019840 | bytes 15204352 | tf_op jit(solution)/shard_map/zyx,xi->zyi/dot_general | solution.py:62
  129.7 7.7 %copy.29 = bf16[10,256,512]{1,0,2:T(8,128)(2,1)} copy(bf16[10,256,512]{2,1,0:T(8,128)(2,1)} %fusion.22) | data formatting | bytes 5242880 | tf_op jit(solution)/shard_map/convert_element_type | solution.py:67
  137.5 5.4 all-to-all-start
  149.9 121.6 %all-gather = f32[8,1,256]{2,1,0:T(1,128)S(1)} all-gather(f32[1,1,256]{2,1,0:T(1,128)S(1)} %bitcast.92), channel_id=1, replica_groups=mesh['px'=4,'py'=8] {'py'}, dimensions={0}, use_global_device_ids=true | all-gather | bytes 9216 | tf_op jit(solution)/shard_map/all_gather | solution.py:77
  272.1 27.1 %all-to-all-done = bf16[10,256,512]{1,0,2:T(8,128)(2,1)} async-done(((bf16[10,256,512]{1,0,2:T(8,128)(2,1)}), bf16[10,256,512]{1,0,2:T(8,128)(2,1)}, u32[]{:S(2)}, u32[]{:S(2)}) %all-to-all-start) | async-done | bytes 2621472 | tf_op jit(solution)/shard_map/all_to_all | solution.py:68
  299.2 5.3 copy.31
  304.5 5.4 all_to_all.29
  309.9 9.0 %fusion.9 = f32[10,2048,64]{1,2,0:T(8,128)S(1)} fusion(bf16[10,2048,64]{1,2,0:T(8,128)(2,1)} %all_to_all.29, bf16[2048,2048]{1,0:T(8,128)(2,1)} %all-gather.8.cloned.1.call-done), kind=kOutput, calls=%fused_computation.29 | convolution fusion | flops 5368709120 | bytes 16252928 | tf_op jit(solution)/shard_map/jy,zyi->zji/dot_general | solution.py:70
  319.0 14.9 %fusion.70 = (bf16[10,2048,64]{1,2,0:T(8,128)(2,1)}, bf16[1,2048,64]{1,2,0:T(8,128)(2,1)S(1)}, f32[1,2048,64]{1,2,0:T(8,128)S(1)}, f32[1,2048,64]{1,2,0:T(8,128)...) fusion(f32[]{:T(128)S(6)} %neg.27, f32[]{:T(128)} %bitcast.9, ...), kind=kLoop, calls=%fused_computation.110 | loop fusion | flops 13631487 | bytes 8921456
  334.6 4.8 convert_dynamic-update-slice_fusion.7
  340.2 7.6 %convert_dynamic-update-slice_fusion.5 = bf16[10,2048,64]{1,2,0:T(8,128)(2,1)} fusion(bf16[10,2048,64]{1,2,0:T(8,128)(2,1)} %convert_dynamic-update-slice_fusion.6, f32[1,2048,64]{1,2,0:T(8,128)S(1)} %get-tuple-element.8, f32[1,2048,64]{1,2,0:T(8,128)S(1)} %get-tuple-element.5, f32[]{:T(128)} %bitcast.8, f32[]{:T(128)S(6)} %neg.27, f32[]{:T(128)} %bitcast.9, ...), kind=kLoop, calls=%fused_computation.116 | loop fusion | flops 4063232 | bytes 1324308
  348.5 10.4 %convert_dynamic-update-slice_fusion.3 = bf16[10,2048,64]{1,2,0:T(8,128)(2,1)} fusion(bf16[10,2048,64]{1,2,0:T(8,128)(2,1)} %convert_dynamic-update-slice_fusion.4, f32[1,2048,64]{1,2,0:T(8,128)S(1)} %get-tuple-element.7, f32[1,2048,64]{1,2,0:T(8,128)S(1)} %get-tuple-element.6, f32[]{:T(128)} %bitcast.8, f32[]{:T(128)S(6)} %neg.27, f32[]{:T(128)} %bitcast.9, ...), kind=kLoop, calls=%fused_computation.114 | loop fusion | flops 5636096 | bytes 1326364
  359.7 14.0 %convert_dynamic-update-slice_fusion.1 = bf16[10,2048,64]{1,2,0:T(8,128)(2,1)} fusion(bf16[10,2048,64]{1,2,0:T(8,128)(2,1)} %convert_dynamic-update-slice_fusion.2, f32[]{:T(128)} %bitcast.8, f32[]{:T(128)S(6)} %neg.27, f32[]{:T(128)} %bitcast.9, f32[]{:T(128)} %bitcast.10, f32[]{:T(128)S(6)} %neg.28, f32[]{:T(128)} %bitcast.11, f32[]{:T(128)} %bitcast.12, ...), kind=kLoop, calls=%fused_computation.112 | loop fusion | flops 8912896 | bytes 2377508
  373.7 14.0 %convert_dynamic-update-slice_fusion = bf16[10,2048,64]{1,2,0:T(8,128)(2,1)} fusion(bf16[10,2048,64]{1,2,0:T(8,128)(2,1)} %convert_dynamic-update-slice_fusion.1, f32[]{:T(128)} %bitcast.8, f32[]{:T(128)S(6)} %neg.27, f32[]{:T(128)} %bitcast.9, f32[]{:T(128)} %bitcast.10, f32[]{:T(128)S(6)} %neg.28, f32[]{:T(128)} %bitcast.11, f32[]{:T(128)} %bitcast.12, ...), kind=kLoop, calls=%fused_computation.111 | loop fusion | flops 8650752 | bytes 2377508 | tf_op jit(solution)/shard_map/stack | solution.py:43
  387.7 10.7 %fusion.15 = bf16[10,2048,64]{1,2,0:T(8,128)(2,1)} fusion(bf16[10,2048,64]{1,2,0:T(8,128)(2,1)} %convert_dynamic-update-slice_fusion, bf16[2048,2048]{1,0:T(8,128)(2,1)} %all-gather.10.cloned.1.call-done), kind=kOutput, calls=%fused_computation.31 | convolution fusion | flops 5370019840 | bytes 13631488 | tf_op jit(solution)/shard_map/yj,zji->zyi/dot_general | solution.py:79
  398.3 10.7 %copy.32 = bf16[10,2048,64]{2,0,1:T(8,128)(2,1)} copy(bf16[10,2048,64]{1,2,0:T(8,128)(2,1)} %fusion.15) | data formatting | bytes 5242880 | tf_op jit(solution)/shard_map/convert_element_type | solution.py:84
  409.0 9.0 %reshape.799 = bf16[8,2,81920]{2,1,0:T(2,128)(2,1)} reshape(bf16[2048,10,64]{2,1,0:T(8,128)(2,1)} %bitcast.83) | data formatting | bytes 5242880
  418.0 66.5 %all_to_all.36 = bf16[8,2,81920]{2,1,0:T(2,128)(2,1)} all-to-all(bf16[8,2,81920]{2,1,0:T(2,128)(2,1)} %reshape.799), channel_id=1, replica_groups=mesh['px'=4,'py'=8] {'py'}, dimensions={0} | all-to-all | bytes 5242880 | tf_op jit(solution)/shard_map/all_to_all | solution.py:85
  484.5 8.9 %reshape.800 = bf16[2048,10,64]{2,1,0:T(8,128)(2,1)} reshape(bf16[8,2,81920]{2,1,0:T(2,128)(2,1)} %all_to_all.36) | data formatting | bytes 5242880
  493.4 9.1 %copy.34 = bf16[10,256,8,64]{1,3,2,0:T(8,128)(2,1)} copy(bf16[10,256,8,64]{3,0,1,2:T(8,128)(2,1)} %bitcast.84) | data formatting | bytes 5242880 | tf_op jit(solution)/shard_map/all_to_all | solution.py:85
  507.6 9.1 %select_bitcast_fusion = f32[1,10,256,512]{3,2,1,0:T(8,128)} fusion(s32[10,256,512]{2,1,0:T(8,128)} %param.21, f32[]{:T(128)} %bitcast.38, f32[]{:T(128)} %bitcast.37, f32[]{:T(128)} %bitcast.36, f32[]{:T(128)} %bitcast.35), kind=kLoop, calls=%fused_computation.28 | loop fusion | flops 10485760 | bytes 10485776 | tf_op jit(solution)/shard_map/stack | solution.py:99
  516.6 10.4 %slice_convert_fusion.1 = (f32[1,10,256,512]{3,2,1,0:T(8,128)}, f32[1,10,256,512]{3,2,1,0:T(8,128)}) fusion(s32[2,10,256,512]{3,2,1,0:T(8,128)} %param.22), kind=kLoop, calls=%fused_computation.27 | loop fusion | flops 2621440 | bytes 20971520 | tf_op jit(solution)/shard_map/convert_element_type | solution.py:103
  527.0 83.4 %all-gather.12.cloned.1.call-done = bf16[10,256,2048]{2,1,0:T(8,128)(2,1)} async-done(((bf16[10,256,512]{2,1,0:T(8,128)(2,1)}), bf16[10,256,2048]{2,1,0:T(8,128)(2,1)}) %all-gather.12.cloned.1.call-update) | async-done | bytes 10485776 | tf_op jit(solution)/shard_map/all_gather | solution.py:93
  610.5 8.5 %fusion.18 = f32[10,256,512]{2,1,0:T(8,128)S(1)} fusion(bf16[10,256,2048]{2,1,0:T(8,128)(2,1)} %all-gather.12.cloned.1.call-done, bf16[2048,512]{1,0:T(8,128)(2,1)S(1)} %copy-done.14), kind=kOutput, calls=%fused_computation.42 | convolution fusion | flops 5368709120 | bytes 17825792 | tf_op jit(solution)/shard_map/zyi,ix->zyx/dot_general | solution.py:91
  619.1 5.9 pad_maximum_fusion.4
  644.8 5.4 collective-permute-start.2
  656.2 27.8 %pad_maximum_fusion = f32[4,10,258,514]{3,2,1,0:T(8,128)} fusion(f32[4,10,1,514]{3,2,1,0:T(1,128)S(1)} %collective-permute-done.3, f32[4,10,256,1]{3,2,1,0:T(8,128)S(1)} %copy-done.8, f32[1,10,256,512]{3,2,1,0:T(8,128)} %get-tuple-element.19, f32[1,10,256,512]{3,2,1,0:T(8,128)S(1)} %bitcast.79, f32[1,10,256,512]{3,2,1,0:T(8,128)} %select_bitcast_fusion, ...), kind=kLoop, calls=%fused_computation | loop fusion | flops 37131360 | bytes 42435840 | tf_op jit(solution)/shard_map/concatenate | solution.py:16
  684.0 18.6 %slice_bitcast_fusion.3 = (f32[10,258,514]{2,1,0:T(8,128)}, f32[10,258,514]{2,1,0:T(8,128)}, f32[10,258,514]{2,1,0:T(8,128)}, f32[10,258,514]{2,1,0:T(8,128)}) fusion(f32[4,10,258,514]{3,2,1,0:T(8,128)} %pad_maximum_fusion), kind=kLoop, calls=%fused_computation.8 | loop fusion | bytes 42435840 | tf_op jit(solution)/shard_map/squeeze | solution.py:110
  702.6 14.9 %fusion.5 = f32[10,256,513]{2,1,0:T(8,128)} fusion(f32[10,258,514]{2,1,0:T(8,128)} %get-tuple-element.14, f32[10,258,514]{2,1,0:T(8,128)} %get-tuple-element.15, f32[10,258,514]{2,1,0:T(8,128)} %get-tuple-element.12, pred[513]{0:T(1024)(128)(4,1)S(1)} %fusion.73), kind=kLoop, calls=%fused_computation.11 | loop fusion | flops 6566400 | bytes 31519232 | tf_op jit(solution)/shard_map/jit(_where)/select_n | solution.py:115
  719.4 10.7 %fusion.7 = f32[10,257,512]{2,1,0:T(8,128)} fusion(f32[10,258,514]{2,1,0:T(8,128)S(1)} %copy-done.2, f32[10,258,514]{2,1,0:T(8,128)S(1)} %copy-done.3, f32[10,258,514]{2,1,0:T(8,128)} %get-tuple-element.13, pred[257]{0:T(512)(128)(4,1)S(1)} %fusion.76), kind=kLoop, calls=%fused_computation.16 | loop fusion | flops 6579200 | bytes 31580416 | tf_op jit(solution)/shard_map/jit(_where)/select_n | solution.py:124
  730.2 11.2 %fusion.8 = f32[10,256,512]{2,1,0:T(8,128)} fusion(f32[10,257,512]{2,1,0:T(8,128)} %fusion.7, f32[10,256,513]{2,1,0:T(8,128)} %fusion.5), kind=kLoop, calls=%fused_computation.20 | loop fusion | flops 3932160 | bytes 26214400 | tf_op jit(solution)/shard_map/add | solution.py:126
  (69 shorter events, 43.9 us)
Async XLA Ops:
  7.2 111.7 %copy-start = (bf16[2048,512]{1,0:T(8,128)(2,1)S(1)}, bf16[2048,512]{1,0:T(8,128)(2,1)}, u32[]{:S(2)}) copy-start(bf16[2048,512]{1,0:T(8,128)(2,1)} %param.17) | copy-start | bytes 6291460
  7.2 111.7 %all-gather.6.cloned.1.call-start = ((), (), s32[]{:S(2)}) async-start(), calls=%async_computation.2 | async-start | bytes 13107200 | tf_op jit(solution)/shard_map/all_gather | solution.py:64
  11.7 298.2 %all-gather.8.cloned.1.call-start = ((), (), s32[]{:S(2)}) async-start(), calls=%async_computation.3 | async-start | bytes 9437184 | tf_op jit(solution)/shard_map/all_gather | solution.py:72
  12.5 375.2 %all-gather.10.cloned.1.call-start = ((), (), s32[]{:S(2)}) async-start(), calls=%async_computation.4 | async-start | bytes 9437184 | tf_op jit(solution)/shard_map/all_gather | solution.py:81
  137.5 5.4 copy-start.11
  137.5 12.4 %copy-start.13 = (f32[256]{0:T(256)S(1)}, f32[256]{0:T(256)}, u32[]{:S(2)}) copy-start(f32[256]{0:T(256)} %param.14) | copy-start | bytes 3076
  137.5 134.0 %copy-start.10 = (f32[10]{0:T(128)S(1)}, f32[10]{0:T(128)}, u32[]{:S(2)}) copy-start(f32[10]{0:T(128)} %param.16) | copy-start | bytes 124
  137.5 161.7 %all-to-all-start = ((bf16[10,256,512]{1,0,2:T(8,128)(2,1)}), bf16[10,256,512]{1,0,2:T(8,128)(2,1)}, u32[]{:S(2)}, u32[]{:S(2)}) async-start(bf16[10,256,512]{1,0,2:T(8,128)(2,1)} %copy.29), calls=%async_computation | async-start | bytes 8388608 | tf_op jit(solution)/shard_map/all_to_all | solution.py:68
  142.8 467.6 %all-gather.12.cloned.1.call-start = ((), (), s32[]{:S(2)}) async-start(), calls=%async_computation.5 | async-start | bytes 13107200 | tf_op jit(solution)/shard_map/all_gather | solution.py:93
  502.5 4.4 copy-start.12
  516.6 93.8 %copy-start.14 = (bf16[2048,512]{1,0:T(8,128)(2,1)S(1)}, bf16[2048,512]{1,0:T(8,128)(2,1)}, u32[]{:S(2)}) copy-start(bf16[2048,512]{1,0:T(8,128)(2,1)} %param.20) | copy-start | bytes 6291460
  610.5 8.5 %copy-start.4 = (f32[1,10,256,512]{3,2,1,0:T(8,128)S(1)}, f32[1,10,256,512]{3,2,1,0:T(8,128)}, u32[]{:S(2)}) copy-start(f32[1,10,256,512]{3,2,1,0:T(8,128)} %get-tuple-element.18) | copy-start | bytes 15728644
  610.5 8.5 %copy-start.5 = (f32[1,10,256,512]{3,2,1,0:T(8,128)S(1)}, f32[1,10,256,512]{3,2,1,0:T(8,128)}, u32[]{:S(2)}) copy-start(f32[1,10,256,512]{3,2,1,0:T(8,128)} %get-tuple-element.19) | copy-start | bytes 15728644
  610.5 8.6 %copy-start.6 = (f32[1,10,256,512]{3,2,1,0:T(8,128)S(1)}, f32[1,10,256,512]{3,2,1,0:T(8,128)}, u32[]{:S(2)}) copy-start(f32[1,10,256,512]{3,2,1,0:T(8,128)} %select_bitcast_fusion) | copy-start | bytes 15728644
  619.0 6.0 copy-start.9
  628.3 7.7 %collective-permute-start = (f32[4,10,256,1]{2,0,3,1:T(4,128)S(1)}, f32[4,10,256,1]{2,0,3,1:T(4,128)S(1)}, u32[]{:S(2)}, u32[]{:S(2)}) collective-permute-start(f32[4,10,256,1]{2,0,3,1:T(4,128)S(1)} %copy.36), channel_id=1, source_target_pairs={{0,8},{8,16},{16,24},{1,9},{9,17},{17,25},{2,10},{10,18},{18,26},{... | collective-permute-start | bytes 122888 | tf_op jit(solution)/shard_map/ppermute | solution.py:12
  634.7 4.7 collective-permute-start.1
  639.4 16.8 %slice-start = ((s8[5242880]{0:T(1024)(128)(4,1)}), s8[1048576]{0:T(1024)(128)(4,1)S(1)}, s32[]{:S(2)}) async-start(s8[5242880]{0:T(1024)(128)(4,1)} %bitcast.78), calls=%async_computation.6 | async-start | bytes 2097152
  642.5 13.7 %slice-start.1 = ((s8[5242880]{0:T(1024)(128)(4,1)}), s8[4194304]{0:T(1024)(128)(4,1)S(1)}, s32[]{:S(2)}) async-start(s8[5242880]{0:T(1024)(128)(4,1)} %bitcast.78), calls=%async_computation.7 | async-start | bytes 8388608
  642.5 13.7 %copy-start.7 = (f32[4,10,256,1]{3,2,1,0:T(8,128)S(1)}, f32[4,10,256,1]{3,2,1,0:T(8,128)}, u32[]{:S(2)}) copy-start(f32[4,10,256,1]{3,2,1,0:T(8,128)} %copy.38) | copy-start | bytes 122884
  642.5 13.7 %copy-start.8 = (f32[4,10,256,1]{3,2,1,0:T(8,128)S(1)}, f32[4,10,256,1]{3,2,1,0:T(8,128)}, u32[]{:S(2)}) copy-start(f32[4,10,256,1]{3,2,1,0:T(8,128)} %copy.39) | copy-start | bytes 122884
  644.8 7.3 collective-permute-start.2
  650.2 6.0 collective-permute-start.3
  702.6 14.9 %copy-start.2 = (f32[10,258,514]{2,1,0:T(8,128)S(1)}, f32[10,258,514]{2,1,0:T(8,128)}, u32[]{:S(2)}) copy-start(f32[10,258,514]{2,1,0:T(8,128)} %get-tuple-element.14) | copy-start | bytes 15913444
  702.6 16.9 %copy-start.3 = (f32[10,258,514]{2,1,0:T(8,128)S(1)}, f32[10,258,514]{2,1,0:T(8,128)}, u32[]{:S(2)}) copy-start(f32[10,258,514]{2,1,0:T(8,128)} %get-tuple-element.15) | copy-start | bytes 15913444
  730.2 11.2 %copy-start.1 = (bf16[2048,512]{1,0:T(8,128)(2,1)S(1)}, bf16[2048,512]{1,0:T(8,128)(2,1)}, u32[]{:S(2)}) copy-start(bf16[2048,512]{1,0:T(8,128)(2,1)} %param.17) | copy-start | bytes 6291460
Sparse Core Ops, SparseCore 0:
  11.8 106.9 all-gather.5
  120.5 154.9 all-gather.7
  277.1 83.3 all-gather.9
  507.0 103.3 all-gather.11

commit v2 on v1

v2 whole, which is shorter than its diff:
```python
import jax
import jax.numpy as jnp
from jax import lax
from jax.experimental import pallas as pl
from jax.experimental.pallas import tpu as pltpu
from jax.sharding import PartitionSpec as P


def exchange(block, axis):
    count = lax.axis_size(axis)
    parts = [block]
    for k in range(1, count):
        parts.append(lax.ppermute(block, axis, [(s, s ^ k) for s in range(count)]))
    return parts


def in_exchange_order(matrix, axis):
    count = lax.axis_size(axis)
    own = lax.axis_index(axis)
    blocks = matrix.reshape(count, matrix.shape[0] // count, matrix.shape[1])
    return jnp.concatenate(
        [lax.dynamic_index_in_dim(blocks, own ^ k, 0, keepdims=False) for k in range(count)]
    )


def thomas_kernel(coupling_ref, shift_ref, ly_ref, lx_ref, rhs_ref, out_ref):
    layers = rhs_ref.shape[0]
    mode_sum = ly_ref[...] + lx_ref[...]
    ratios = []
    partial_values = []
    for layer_index in range(layers):
        diagonal = mode_sum + shift_ref[layer_index]
        if layer_index > 0:
            diagonal = diagonal + coupling_ref[layer_index - 1]
        if layer_index < layers - 1:
            diagonal = diagonal + coupling_ref[layer_index]
        if layer_index == 0:
            pivots = diagonal
            solved = rhs_ref[0] / pivots
        else:
            pivots = diagonal + coupling_ref[layer_index - 1] * ratios[-1]
            solved = (rhs_ref[layer_index] + coupling_ref[layer_index - 1] * partial_values[-1]) / pivots
        partial_values.append(solved)
        if layer_index < layers - 1:
            ratios.append(-coupling_ref[layer_index] / pivots)
    result = partial_values[layers - 1]
    out_ref[layers - 1] = result.astype(out_ref.dtype)
    for layer_index in range(layers - 2, -1, -1):
        result = partial_values[layer_index] - ratios[layer_index] * result
        out_ref[layer_index] = result.astype(out_ref.dtype)


def thomas_solve(rhs, lambda_x, lambda_y, coupling, layer_shift):
    layers, rows, modes = rhs.shape
    tile = min(rows, 256)
    smem = pl.BlockSpec(memory_space=pltpu.SMEM)
    return pl.pallas_call(
        thomas_kernel,
        grid=(rows // tile,),
        in_specs=[
            smem,
            smem,
            pl.BlockSpec((tile, 1), lambda j: (j, 0)),
            pl.BlockSpec((1, modes), lambda j: (0, 0)),
            pl.BlockSpec((layers, tile, modes), lambda j: (0, j, 0)),
        ],
        out_specs=pl.BlockSpec((layers, tile, modes), lambda j: (0, j, 0)),
        out_shape=jax.ShapeDtypeStruct(rhs.shape, jnp.bfloat16),
    )(coupling, layer_shift, lambda_y.reshape(rows, 1), lambda_x.reshape(1, modes), rhs)


def shards(
    residual,
    lambda_x,
    lambda_y,
    coupling,
    layer_shift,
    left_x,
    left_y,
    right_y,
    right_x,
    regime_code,
    upwind_flag,
    mobility_table,
):
    count_x = lax.axis_size("px")
    count_y = lax.axis_size("py")
    at_x = lax.axis_index("px")
    at_y = lax.axis_index("py")
    layers, height, width = residual.shape
    modes = left_x.shape[1] // count_y

    rounded = residual.astype(jnp.bfloat16)
    spectral_x = jnp.einsum(
        "zyx,xci->czyi",
        jnp.concatenate(exchange(rounded, "px"), axis=2),
        in_exchange_order(left_x, "px").reshape(-1, count_y, modes),
        preferred_element_type=jnp.float32,
    ).astype(jnp.bfloat16)
    pencil = lax.all_to_all(spectral_x, "py", 0, 0, tiled=True)
    spectral = jnp.einsum(
        "jsy,szyi->zji",
        lax.all_gather(left_y, "py", axis=0, tiled=True).reshape(-1, count_y, height),
        pencil,
        preferred_element_type=jnp.float32,
    )
    own_x = lax.dynamic_slice_in_dim(lambda_x, at_y * modes, modes)
    spread_y = jnp.zeros((count_y, lambda_y.shape[0]), lambda_y.dtype)
    spread_y = lax.dynamic_update_index_in_dim(spread_y, lambda_y, at_y, 0)
    all_y = lax.psum(spread_y, "py").reshape(-1)
    solved = thomas_solve(spectral, own_x, all_y, coupling, layer_shift)
    back_pencil = jnp.einsum(
        "syj,zji->szyi",
        lax.all_gather(right_y, "py", axis=0, tiled=True).reshape(count_y, height, -1),
        solved,
        preferred_element_type=jnp.float32,
    ).astype(jnp.bfloat16)
    back_y = lax.all_to_all(back_pencil, "py", 0, 0, tiled=True)
    back_y = jnp.moveaxis(back_y, 0, 2).reshape(layers, height, -1)
    correction = jnp.einsum(
        "zyi,ix->zyx",
        jnp.concatenate(exchange(back_y, "px"), axis=2),
        in_exchange_order(right_x, "px"),
        preferred_element_type=jnp.float32,
    )

    mobility = jnp.zeros(regime_code.shape, jnp.float32)
    for regime in range(mobility_table.shape[0]):
        mobility = jnp.where(regime_code == regime, mobility_table[regime], mobility)
    flag_x = upwind_flag[0]
    flag_y = upwind_flag[1]

    def net(axis, dim, flag, at, count):
        forward = [(i, i + 1) for i in range(count - 1)]
        backward = [(i + 1, i) for i in range(count - 1)]
        first = lambda a: lax.slice_in_dim(a, 0, 1, axis=dim)
        last = lambda a: lax.slice_in_dim(a, a.shape[dim] - 1, None, axis=dim)
        rest = lambda a: lax.slice_in_dim(a, 1, None, axis=dim)
        head = lambda a: lax.slice_in_dim(a, 0, a.shape[dim] - 1, axis=dim)
        high = lax.ppermute(jnp.stack([first(correction), first(mobility)]), axis, backward)
        low = lax.ppermute(
            jnp.stack([last(correction), last(mobility), last(flag).astype(jnp.float32)]), axis, forward
        )
        press_next = jnp.concatenate([rest(correction), high[0]], axis=dim)
        mobil_next = jnp.concatenate([rest(mobility), high[1]], axis=dim)
        flux_high = jnp.where(flag == 1, mobility, mobil_next) * (correction - press_next)
        place = lax.broadcasted_iota(jnp.int32, correction.shape, dim)
        edge = (at == count - 1) & (place == correction.shape[dim] - 1)
        flux_high = jnp.where(edge, 0.0, flux_high)
        flux_edge = jnp.where(low[2] > 0.5, low[1], first(mobility)) * (low[0] - first(correction))
        flux_edge = jnp.where(at == 0, 0.0, flux_edge)
        flux_low = jnp.concatenate([flux_edge, head(flux_high)], axis=dim)
        return flux_high - flux_low

    balance = net("px", 2, flag_x, at_x, count_x) + net("py", 1, flag_y, at_y, count_y)
    return (correction, balance)


def solution(mesh):
    return jax.shard_map(
        shards,
        mesh=mesh,
        in_specs=(
            P(None, "py", "px"),
            P("px"),
            P("py"),
            P(),
            P(),
            P(None, "px"),
            P("py", None),
            P("py", None),
            P(None, "px"),
            P(None, "py", "px"),
            P(None, None, "py", "px"),
            P(),
        ),
        out_specs=(P(None, "py", "px"), P(None, "py", "px")),
        check_vma=False,
    )
```

time: 755 us -> 567 us (0.75)
  other arithmetic: 165 us -> 35.9 us
  local copies, waits for them, and re-layouts: 97.5 us -> 50.4 us
  waiting for transfers between devices: 222 us -> 186 us
  Pallas kernels: 0 us -> 10.8 us
  matrix products: 39 us -> 48.6 us
  starting transfers between devices: 17.1 us -> 25.7 us
    all_gather x2 -> x0, waiting for transfers between devices: 189 us -> none  [the longest x1 106 us: shards(): lax.all_gather(rounded, 'px', axis=2, tiled=True)]
    ppermute x4 -> x10, waiting for transfers between devices: 4.28 us -> 185 us  [the longest x6 185 us: exchange(): parts.append(lax.ppermute(block, axis, [(s, s ^ k) for s in range(count)]))]
    psum x0 -> x1, blocking collectives: none -> 128 us  [shards(): all_y = lax.psum(spread_y, 'py').reshape(-1)]
    all_gather x1 -> x0, blocking collectives: 122 us -> none  [shards(): all_y = lax.all_gather(lambda_y, 'py', axis=0, tiled=True)]
    unnamed x9 -> x0, other arithmetic: 54 us -> none
    concatenate x1 -> x0, other arithmetic: 27.8 us -> none  [with_halo(): block = jnp.concatenate([low, block, high], axis=dim)]
    all_to_all x1, waiting for transfers between devices: 27.1 us -> 0.01 us  [shards(): pencil = lax.all_to_all(spectral_x, 'py', 0, 0, tiled=True)]
    all_to_all x4 -> x1, local copies, waits for them, and re-layouts: 24.2 us -> 0.18 us  [shards(): back_y = lax.all_to_all(back_pencil, 'py', 0, 0, tiled=True)]
  transfers between devices with their start and end apart: 9 -> 13, of which waited for: 5 -> 6; matrix products, arithmetic and copies ran while one was open for 17% -> 13% of each run, Pallas kernels for 0% -> 2%
where the time goes in v2:
time: 567 us; the launch traced here: 565 us
  blocking collectives  194 us (34%)
  waiting for transfers between devices  186 us (33%)
  local copies, waits for them, and re-layouts  50.4 us (9%)
  matrix products  48.6 us (9%)
  other arithmetic  35.9 us (6%)
  starting transfers between devices  25.7 us (5%)
  between operations  14.4 us (3%)
  Pallas kernels  10.8 us (2%)
    ppermute x6, waiting for transfers between devices, exchange(): parts.append(lax.ppermute(block, axis, [(s, s ^ k) for s in range(count)]))  185 us
    psum x1, blocking collectives, shards(): all_y = lax.psum(spread_y, 'py').reshape(-1)  128 us
    all_to_all x1, blocking collectives, shards(): back_y = lax.all_to_all(back_pencil, 'py', 0, 0, tiled=True)  65.6 us
    select_n x1, other arithmetic, net(): flux_high = jnp.where(edge, 0.0, flux_high)  16.2 us
    dot_general x1, matrix products, shards(): jnp.einsum('jsy,szyi->zji', lax.all_gather(left_y, 'py', axis=0, tiled=Tr...  15.6 us
    dot_general x1, matrix products, shards(): jnp.einsum('syj,zji->szyi', lax.all_gather(right_y, 'py', axis=0, tiled=T...  15 us
    slice x4, local copies, waits for them, and re-layouts, net(): rest = lambda a: lax.slice_in_dim(a, 1, None, axis=dim)  14.1 us
  transfers between devices with their start and end apart: 13, of which 6 were waited for; matrix products, arithmetic and copies ran while one was open for 13% of the time, Pallas kernels for 2%

profile of v2, /device:TPU:1, one launch (start us, length us, event | category | flops | bytes accessed | tf_op | source)
XLA Modules:
  0.0 565.4 jit_solution(2377846564692051894)
XLA Ops:
  7.2 2.3 copy.262
  10.3 2.8 convert_element_type.21
  13.2 2.1 collective-permute-start
  16.5 2.7 constant_dynamic-slice_fusion.3
  19.2 2.1 copy.258
  21.4 2.1 copy.259
  26.6 45.4 %collective-permute-done = bf16[10,256,512]{2,1,0:T(8,128)(2,1)} collective-permute-done((bf16[10,256,512]{2,1,0:T(8,128)(2,1)S(1)}, bf16[10,256,512]{2,1,0:T(8,128)(2,1)}, u32[]{:S(2)}, u32[]{:S(2)}) %collective-permute-start) | collective-permute-done | bytes 2621472 | tf_op jit(solution)/shard_map/ppermute | solution.py:13
  72.8 56.3 %collective-permute-done.2 = bf16[10,256,512]{2,1,0:T(8,128)(2,1)} collective-permute-done((bf16[10,256,512]{2,1,0:T(8,128)(2,1)S(1)}, bf16[10,256,512]{2,1,0:T(8,128)(2,1)}, u32[]{:S(2)}, u32[]{:S(2)}) %collective-permute-start.2) | collective-permute-done | bytes 2621472 | tf_op jit(solution)/shard_map/ppermute | solution.py:13
  129.1 9.7 %convert_bitcast_fusion.1 = bf16[8,10,256,64]{2,3,1,0:T(8,128)(2,1)} fusion(bf16[10,256,512]{2,1,0:T(8,128)(2,1)} %collective-permute-done.2, bf16[10,256,512]{2,1,0:T(8,128)(2,1)} %collective-permute-done.1, bf16[10,256,512]{2,1,0:T(8,128)(2,1)} %collective-permute-done, bf16[10,256,512]{2,1,0:T(8,128)(2,1)S(1)} %convert_element_type.21, ...), kind=kOutput, calls=%fused_computation.34 | convolution fusion | flops 5420351488 | bytes 15204352 | tf_op jit(solution)/shard_map/zyx,xci->czyi/dot_general | solution.py:94
  138.8 6.7 %all-to-all-start = ((bf16[8,10,256,64]{2,3,1,0:T(8,128)(2,1)}), bf16[8,10,256,64]{2,3,1,0:T(8,128)(2,1)}, u32[]{:S(2)}, u32[]{:S(2)}) async-start(bf16[8,10,256,64]{2,3,1,0:T(8,128)(2,1)} %convert_bitcast_fusion.1), calls=%async_computation | async-start | bytes 5242880 | tf_op jit(solution)/shard_map/all_to_all | solution.py:100
  145.9 128.0 %psum.7.ly_ref = f32[2048,1]{1,0:T(8,128)} all-reduce(f32[2048,1]{1,0:T(8,128)S(1)} %bitcast.117), channel_id=1, replica_groups=mesh['px'=4,'py'=8] {'py'}, use_global_device_ids=true, to_apply=%region_0.1 | all-reduce | flops 2048 | bytes 16384 | tf_op jit(solution)/shard_map/psum | solution.py:110
  274.6 15.6 %convolution_bitcast_fusion.rhs_ref = f32[10,2048,64]{2,1,0:T(8,128)} fusion(bf16[8,10,256,64]{2,3,1,0:T(8,128)(2,1)} %all-to-all-done, bf16[2048,8,256,1]{0,2,3,1:T(8,128)(2,1)} %bitcast.128), kind=kOutput, calls=%fused_computation.32 | convolution fusion | flops 5368709120 | bytes 16252928 | tf_op jit(solution)/shard_map/jsy,szyi->zji/dot_general | solution.py:101
  290.2 10.8 %shard_map.131 = bf16[10,2048,64]{2,1,0:T(8,128)(2,1)} custom-call(f32[9]{0:T(128)} %coupling_ref.1, f32[10]{0:T(128)} %shift_ref.1, f32[2048,1]{1,0:T(8,128)} %psum.7.ly_ref, f32[1,64]{1,0:T(1,128)} %dynamic-slice_bitcast_fusion.4.lx_ref, f32[10,2048,64]{2,1,0:T(8,128)} %convolution_bitcast_fusion.rhs_ref), custom_call_target="tpu_custom_call" | custom-call | tf_op jit(solution)/shard_map/pallas_call | solution.py:57
  301.1 15.0 %convert_bitcast_fusion = bf16[8,10,256,64]{2,3,0,1:T(8,128)(2,1)S(1)} fusion(bf16[8,256,2048,1]{2,1,0,3:T(8,128)(2,1)} %bitcast.127, bf16[10,2048,64]{2,1,0:T(8,128)(2,1)} %shard_map.131), kind=kOutput, calls=%fused_computation.33 | convolution fusion | flops 5370019840 | bytes 13631488 | tf_op jit(solution)/shard_map/syj,zji->szyi/dot_general | solution.py:112
  316.4 65.6 %all_to_all.10 = bf16[8,10,256,64]{2,3,1,0:T(8,128)(2,1)S(1)} all-to-all(bf16[8,10,256,64]{2,3,1,0:T(8,128)(2,1)S(1)} %copy.266), channel_id=1, replica_groups=mesh['px'=4,'py'=8] {'py'}, dimensions={0} | all-to-all | bytes 5242880 | tf_op jit(solution)/shard_map/all_to_all | solution.py:118
  382.1 2.8 copy.271
  388.2 6.4 %select_select_fusion = f32[10,256,512]{2,1,0:T(8,128)S(1)} fusion(s32[10,256,512]{2,1,0:T(8,128)} %param.21, f32[]{:T(128)} %bitcast.32, f32[]{:T(128)} %bitcast.31, f32[]{:T(128)} %bitcast.30, f32[]{:T(128)} %bitcast.29), kind=kLoop, calls=%fused_computation.30 | loop fusion | flops 10485760 | bytes 10485776 | tf_op jit(solution)/shard_map/jit(_where)/select_n | solution.py:129
  394.6 3.9 slice.132
  398.5 3.0 slice.145
  401.5 2.8 slice_reduce_fusion
  404.4 8.3 %slice_bitcast_fusion = (s32[10,256,512]{2,1,0:T(8,128)}, s32[10,256,512]{2,1,0:T(8,128)S(1)}) fusion(s32[2,10,256,512]{3,2,1,0:T(8,128)} %param.22), kind=kLoop, calls=%fused_computation.29 | loop fusion | bytes 20971520 | tf_op jit(solution)/shard_map/squeeze | solution.py:131
  417.1 25.4 %collective-permute-done.3 = bf16[10,256,512]{2,1,0:T(8,128)(2,1)} collective-permute-done((bf16[10,256,512]{2,1,0:T(8,128)(2,1)}, bf16[10,256,512]{2,1,0:T(8,128)(2,1)}, u32[]{:S(2)}, u32[]{:S(2)}) %collective-permute-start.3) | collective-permute-done | bytes 2621472 | tf_op jit(solution)/shard_map/ppermute | solution.py:13
  443.6 56.3 %collective-permute-done.5 = bf16[10,256,512]{2,1,0:T(8,128)(2,1)} collective-permute-done((bf16[10,256,512]{2,1,0:T(8,128)(2,1)}, bf16[10,256,512]{2,1,0:T(8,128)(2,1)}, u32[]{:S(2)}, u32[]{:S(2)}) %collective-permute-start.5) | collective-permute-done | bytes 2621472 | tf_op jit(solution)/shard_map/ppermute | solution.py:13
  499.9 8.3 %fusion.7 = f32[10,256,512]{2,1,0:T(8,128)S(1)} fusion(bf16[10,256,512]{2,1,0:T(8,128)(2,1)} %collective-permute-done.5, bf16[10,256,512]{2,1,0:T(8,128)(2,1)} %collective-permute-done.4, bf16[10,256,512]{2,1,0:T(8,128)(2,1)} %collective-permute-done.3, bf16[10,256,512]{2,1,0:T(8,128)(2,1)S(1)} %copy-done.5, bf16[512,512]{1,0:T(8,128)(2,1)S(1)} %get-tuple-element.14, ...), kind=kOutput, calls=%fused_computation.8 | convolution fusion | flops 5419040768 | bytes 17825792 | tf_op jit(solution)/shard_map/zyi,ix->zyx/dot_general | solution.py:120
  509.3 3.8 slice.136
  513.1 3.4 slice.149
  516.5 3.1 collective-permute-start.7
  521.0 3.3 collective-permute-start.9
  529.7 5.2 collective-permute-start.8
  535.0 2.8 multiply_select_fusion
  537.8 16.2 %fusion.19 = (f32[10,256,512]{2,1,0:T(8,128)S(1)}, f32[10,256,512]{2,1,0:T(8,128)S(1)}) fusion(f32[10,1,512]{2,1,0:T(1,128)S(1)} %get-tuple-element.22, f32[10,255,512]{2,1,0:T(8,128)} %slice.145, f32[10,256,512]{2,1,0:T(8,128)S(1)} %copy-done.3, f32[10,1,512]{2,1,0:T(1,128)S(1)} %get-tuple-element.21, f32[10,255,512]{2,1,0:T(8,128)} %slice.149, ...), kind=kLoop, calls=%fused_computation.24 | loop fusion | flops 28835840 | bytes 52429584 | tf_op jit(solution)/shard_map/jit(_where)/select_n | solution.py:149
  554.1 4.5 fusion.17
  (73 shorter events, 24.1 us)
Async XLA Ops:
  7.2 266.8 %copy-start = (f32[512]{0:T(512)S(1)}, f32[512]{0:T(512)}, u32[]{:S(2)}) copy-start(f32[512]{0:T(512)} %param.13) | copy-start | bytes 6148
  7.2 267.4 %all-gather.3.cloned.1.call-start = ((), (), s32[]{:S(2)}) async-start(), calls=%async_computation.2 | async-start | bytes 9437184 | tf_op jit(solution)/shard_map/all_gather | solution.py:103
  9.6 291.5 %all-gather.5.cloned.1.call-start = ((), (), s32[]{:S(2)}) async-start(), calls=%async_computation.3 | async-start | bytes 9437184 | tf_op jit(solution)/shard_map/all_gather | solution.py:114
  13.2 58.8 %collective-permute-start = (bf16[10,256,512]{2,1,0:T(8,128)(2,1)S(1)}, bf16[10,256,512]{2,1,0:T(8,128)(2,1)}, u32[]{:S(2)}, u32[]{:S(2)}) collective-permute-start(bf16[10,256,512]{2,1,0:T(8,128)(2,1)S(1)} %convert_element_type.21), channel_id=1, source_target_pairs={{0,8},{8,0},{16,24},{24,16},{1,9},{9,1},{17,25},{25,17},{2,10},{10... | collective-permute-start | bytes 7864328 | tf_op jit(solution)/shard_map/ppermute | solution.py:13
  15.3 57.5 %collective-permute-start.1 = (bf16[10,256,512]{2,1,0:T(8,128)(2,1)S(1)}, bf16[10,256,512]{2,1,0:T(8,128)(2,1)}, u32[]{:S(2)}, u32[]{:S(2)}) collective-permute-start(bf16[10,256,512]{2,1,0:T(8,128)(2,1)S(1)} %convert_element_type.21), channel_id=1, source_target_pairs={{0,16},{8,24},{16,0},{24,8},{1,17},{9,25},{17,1},{25,9},{2,18},{10... | collective-permute-start | bytes 7864328 | tf_op jit(solution)/shard_map/ppermute | solution.py:13
  16.5 112.6 %collective-permute-start.2 = (bf16[10,256,512]{2,1,0:T(8,128)(2,1)S(1)}, bf16[10,256,512]{2,1,0:T(8,128)(2,1)}, u32[]{:S(2)}, u32[]{:S(2)}) collective-permute-start(bf16[10,256,512]{2,1,0:T(8,128)(2,1)S(1)} %convert_element_type.21), channel_id=1, source_target_pairs={{0,24},{8,16},{16,8},{24,0},{1,25},{9,17},{17,9},{25,1},{2,26},{10... | collective-permute-start | bytes 7864328 | tf_op jit(solution)/shard_map/ppermute | solution.py:13
  138.8 6.7 %copy-start.7 = (f32[256]{0:T(256)S(1)}, f32[256]{0:T(256)}, u32[]{:S(2)}) copy-start(f32[256]{0:T(256)} %param.14) | copy-start | bytes 3076
  138.8 135.8 %all-to-all-start = ((bf16[8,10,256,64]{2,3,1,0:T(8,128)(2,1)}), bf16[8,10,256,64]{2,3,1,0:T(8,128)(2,1)}, u32[]{:S(2)}, u32[]{:S(2)}) async-start(bf16[8,10,256,64]{2,3,1,0:T(8,128)(2,1)} %convert_bitcast_fusion.1), calls=%async_computation | async-start | bytes 5242880 | tf_op jit(solution)/shard_map/all_to_all | solution.py:100
  381.9 5.6 copy-start.6
  384.9 57.6 %collective-permute-start.3 = (bf16[10,256,512]{2,1,0:T(8,128)(2,1)}, bf16[10,256,512]{2,1,0:T(8,128)(2,1)}, u32[]{:S(2)}, u32[]{:S(2)}) collective-permute-start(bf16[10,256,512]{2,1,0:T(8,128)(2,1)} %copy.271), channel_id=1, source_target_pairs={{0,8},{8,0},{16,24},{24,16},{1,9},{9,1},{17,25},{25,17},{2,10},{10... | collective-permute-start | bytes 7864328 | tf_op jit(solution)/shard_map/ppermute | solution.py:13
  386.2 57.4 %collective-permute-start.4 = (bf16[10,256,512]{2,1,0:T(8,128)(2,1)}, bf16[10,256,512]{2,1,0:T(8,128)(2,1)}, u32[]{:S(2)}, u32[]{:S(2)}) collective-permute-start(bf16[10,256,512]{2,1,0:T(8,128)(2,1)} %copy.271), channel_id=1, source_target_pairs={{0,16},{8,24},{16,0},{24,8},{1,17},{9,25},{17,1},{25,9},{2,18},{10... | collective-permute-start | bytes 7864328 | tf_op jit(solution)/shard_map/ppermute | solution.py:13
  387.5 112.4 %collective-permute-start.5 = (bf16[10,256,512]{2,1,0:T(8,128)(2,1)}, bf16[10,256,512]{2,1,0:T(8,128)(2,1)}, u32[]{:S(2)}, u32[]{:S(2)}) collective-permute-start(bf16[10,256,512]{2,1,0:T(8,128)(2,1)} %copy.271), channel_id=1, source_target_pairs={{0,24},{8,16},{16,8},{24,0},{1,25},{9,17},{17,9},{25,1},{2,26},{10... | collective-permute-start | bytes 7864328 | tf_op jit(solution)/shard_map/ppermute | solution.py:13
  394.6 3.9 copy-start.4
  412.7 87.2 %copy-start.5 = (bf16[10,256,512]{2,1,0:T(8,128)(2,1)S(1)}, bf16[10,256,512]{2,1,0:T(8,128)(2,1)}, u32[]{:S(2)}) copy-start(bf16[10,256,512]{2,1,0:T(8,128)(2,1)} %copy.271) | copy-start | bytes 7864324
  508.2 4.9 copy-start.2
  516.5 8.8 %collective-permute-start.7 = (f32[3,10,256,1]{2,0,1,3:T(4,128)S(1)}, f32[3,10,256,1]{2,0,1,3:T(4,128)S(1)}, u32[]{:S(2)}, u32[]{:S(2)}) collective-permute-start(f32[3,10,256,1]{2,0,1,3:T(4,128)S(1)} %pad_maximum_fusion.1), channel_id=1, source_target_pairs={{0,8},{8,16},{16,24},{1,9},{9,17},{17,25},{2,10},{10,18},{18,26},{... | collective-permute-start | bytes 92168 | tf_op jit(solution)/shard_map/ppermute | solution.py:141
  519.7 4.7 collective-permute-start.6
  521.0 7.4 %collective-permute-start.9 = (f32[3,10,1,512]{3,2,1,0:T(1,128)S(1)}, f32[3,10,1,512]{3,2,1,0:T(1,128)S(1)}, u32[]{:S(2)}, u32[]{:S(2)}) collective-permute-start(f32[3,10,1,512]{3,2,1,0:T(1,128)S(1)} %pad_maximum_fusion), channel_id=1, source_target_pairs={{0,1},{1,2},{2,3},{3,4},{4,5},{5,6},{6,7},{8,9},{9,10},{10,11},{11... | collective-permute-start | bytes 184328 | tf_op jit(solution)/shard_map/ppermute | solution.py:141
  528.4 9.4 %copy-start.3 = (f32[10,256,512]{2,1,0:T(8,128)S(1)}, f32[10,256,512]{2,1,0:T(8,128)}, u32[]{:S(2)}) copy-start(f32[10,256,512]{2,1,0:T(8,128)} %copy-done.2) | copy-start | bytes 15728644
  529.7 8.1 %collective-permute-start.8 = (f32[2,10,1,512]{3,2,1,0:T(1,128)S(1)}, f32[2,10,1,512]{3,2,1,0:T(1,128)S(1)}, u32[]{:S(2)}, u32[]{:S(2)}) collective-permute-start(f32[2,10,1,512]{3,2,1,0:T(1,128)S(1)} %pad_maximum_fusion.2), channel_id=1, source_target_pairs={{1,0},{2,1},{3,2},{4,3},{5,4},{6,5},{7,6},{9,8},{10,9},{11,10},{12... | collective-permute-start | bytes 122888 | tf_op jit(solution)/shard_map/ppermute | solution.py:140
  554.1 4.5 copy-start.1
Sparse Core Ops, SparseCore 0:
  9.7 84.9 all-gather.2
  96.3 107.2 all-gather.4

commit v3 on v2

--- a/solution.py
+++ b/solution.py
@@ -98,16 +98,23 @@
         preferred_element_type=jnp.float32,
     ).astype(jnp.bfloat16)
     pencil = lax.all_to_all(spectral_x, "py", 0, 0, tiled=True)
+    high = lambda_y.astype(jnp.bfloat16)
+    rest = lambda_y - high.astype(jnp.float32)
+    middle = rest.astype(jnp.bfloat16)
+    low = (rest - middle.astype(jnp.float32)).astype(jnp.bfloat16)
+    pieces = jnp.zeros((lambda_y.shape[0], 128), jnp.bfloat16)
+    pieces = pieces.at[:, 0].set(high).at[:, 1].set(middle).at[:, 2].set(low)
+    carried = lax.all_gather(jnp.concatenate([left_y, pieces], axis=1), "py", axis=0, tiled=True)
+    columns = left_y.shape[1]
     spectral = jnp.einsum(
         "jsy,szyi->zji",
-        lax.all_gather(left_y, "py", axis=0, tiled=True).reshape(-1, count_y, height),
+        carried[:, :columns].reshape(-1, count_y, height),
         pencil,
         preferred_element_type=jnp.float32,
     )
     own_x = lax.dynamic_slice_in_dim(lambda_x, at_y * modes, modes)
-    spread_y = jnp.zeros((count_y, lambda_y.shape[0]), lambda_y.dtype)
-    spread_y = lax.dynamic_update_index_in_dim(spread_y, lambda_y, at_y, 0)
-    all_y = lax.psum(spread_y, "py").reshape(-1)
+    got = carried[:, columns:columns + 3].astype(jnp.float32)
+    all_y = got[:, 0] + (got[:, 1] + got[:, 2])
     solved = thomas_solve(spectral, own_x, all_y, coupling, layer_shift)
     back_pencil = jnp.einsum(
         "syj,zji->szyi",
@@ -119,8 +126,8 @@
     back_y = jnp.moveaxis(back_y, 0, 2).reshape(layers, height, -1)
     correction = jnp.einsum(
         "zyi,ix->zyx",
-        jnp.concatenate(exchange(back_y, "px"), axis=2),
-        in_exchange_order(right_x, "px"),
+        lax.all_gather(back_y, "px", axis=2, tiled=True),
+        right_x,
         preferred_element_type=jnp.float32,
     )
 

time: 567 us -> 537 us (0.947); the launches traced: 565 us -> 528 us
  blocking collectives: 194 us -> 62.4 us
  waiting for transfers between devices: 186 us -> 245 us
  local copies, waits for them, and re-layouts: 50.4 us -> 69.9 us
  other arithmetic: 35.9 us -> 51 us
    psum x1 -> x0, blocking collectives: 128 us -> none  [shards(): all_y = lax.psum(spread_y, 'py').reshape(-1)]
    ppermute x6 -> x3, waiting for transfers between devices: 185 us -> 105 us  [exchange(): parts.append(lax.ppermute(block, axis, [(s, s ^ k) for s in range(count)]))]
    all_gather x1 -> x2, waiting for transfers between devices: 0.01 us -> 74.5 us  [the longest x1 74.5 us: shards(): lax.all_gather(back_y, 'px', axis=2, tiled=True)]
    all_to_all x1, waiting for transfers between devices: 0.01 us -> 65.1 us  [shards(): pencil = lax.all_to_all(spectral_x, 'py', 0, 0, tiled=True)]
    unnamed x19 -> x13, local copies, waits for them, and re-layouts: 2.72 us -> 11.1 us
    slice x0 -> x1, local copies, waits for them, and re-layouts: none -> 8.29 us  [shards(): carried[:, :columns].reshape(-1, count_y, height)]
  transfers between devices with their start and end apart: 13 -> 11, of which waited for: 6 -> 5; matrix products, arithmetic and copies ran while one was open for 13% -> 19% of each run, Pallas kernels for 2% -> 2%
where the time goes in v3:
time: 537 us; the launch traced here: 528 us
  waiting for transfers between devices  245 us (46%)
  local copies, waits for them, and re-layouts  69.9 us (13%)
  blocking collectives  62.4 us (12%)
  matrix products  52.1 us (10%)
  other arithmetic  51 us (9%)
  starting transfers between devices  22.2 us (4%)
  between operations  14.5 us (3%)
  Pallas kernels  10.8 us (2%)
    ppermute x3, waiting for transfers between devices, exchange(): parts.append(lax.ppermute(block, axis, [(s, s ^ k) for s in range(count)]))  105 us
    all_gather x1, waiting for transfers between devices, shards(): lax.all_gather(back_y, 'px', axis=2, tiled=True)  74.5 us
    all_to_all x1, waiting for transfers between devices, shards(): pencil = lax.all_to_all(spectral_x, 'py', 0, 0, tiled=True)  65.1 us
    all_to_all x1, blocking collectives, shards(): back_y = lax.all_to_all(back_pencil, 'py', 0, 0, tiled=True)  62.4 us
    dot_general x1, matrix products, shards(): jnp.einsum('jsy,szyi->zji', carried[:, :columns].reshape(-1, count_y, hei...  18.7 us
    select_n x1, other arithmetic, net(): flux_high = jnp.where(edge, 0.0, flux_high)  16.2 us
    dot_general x1, matrix products, shards(): jnp.einsum('syj,zji->szyi', lax.all_gather(right_y, 'py', axis=0, tiled=T...  15 us
    slice x4, local copies, waits for them, and re-layouts, net(): rest = lambda a: lax.slice_in_dim(a, 1, None, axis=dim)  13.8 us
  transfers between devices with their start and end apart: 11, of which 5 were waited for; matrix products, arithmetic and copies ran while one was open for 19% of the time, Pallas kernels for 2%

profile of v3, /device:TPU:1, one launch (start us, length us, event | category | flops | bytes accessed | tf_op | source)
XLA Modules:
  0.0 527.8 jit_solution(9797010394736615110)
XLA Ops:
  10.0 2.1 broadcast_select_fusion.1
  13.6 2.3 pad_maximum_fusion
  16.7 4.3 convert_element_type.45
  24.3 2.9 constant_dynamic-slice_fusion.3
  27.2 2.1 copy.243
  32.5 47.4 %collective-permute-done = bf16[10,256,512]{2,1,0:T(8,128)(2,1)} collective-permute-done((bf16[10,256,512]{2,1,0:T(8,128)(2,1)}, bf16[10,256,512]{2,1,0:T(8,128)(2,1)}, u32[]{:S(2)}, u32[]{:S(2)}) %collective-permute-start) | collective-permute-done | bytes 2621472 | tf_op jit(solution)/shard_map/ppermute | solution.py:13
  80.8 56.3 %collective-permute-done.2 = bf16[10,256,512]{2,1,0:T(8,128)(2,1)} collective-permute-done((bf16[10,256,512]{2,1,0:T(8,128)(2,1)}, bf16[10,256,512]{2,1,0:T(8,128)(2,1)}, u32[]{:S(2)}, u32[]{:S(2)}) %collective-permute-start.2) | collective-permute-done | bytes 2621472 | tf_op jit(solution)/shard_map/ppermute | solution.py:13
  137.1 9.8 %convert_bitcast_fusion.1 = bf16[8,10,256,64]{2,3,1,0:T(8,128)(2,1)} fusion(bf16[10,256,512]{2,1,0:T(8,128)(2,1)} %collective-permute-done.2, bf16[10,256,512]{2,1,0:T(8,128)(2,1)} %collective-permute-done.1, bf16[10,256,512]{2,1,0:T(8,128)(2,1)} %collective-permute-done, bf16[10,256,512]{2,1,0:T(8,128)(2,1)} %convert_element_type.45, ...), kind=kOutput, calls=%fused_computation.28 | convolution fusion | flops 5420351488 | bytes 15204352 | tf_op jit(solution)/shard_map/zyx,xci->czyi/dot_general | solution.py:94
  146.9 6.7 %all-to-all-start = ((bf16[8,10,256,64]{2,3,1,0:T(8,128)(2,1)}), bf16[8,10,256,64]{2,3,1,0:T(8,128)(2,1)}, u32[]{:S(2)}, u32[]{:S(2)}) async-start(bf16[8,10,256,64]{2,3,1,0:T(8,128)(2,1)} %convert_bitcast_fusion.1), calls=%async_computation | async-start | bytes 5242880 | tf_op jit(solution)/shard_map/all_to_all | solution.py:100
  154.9 8.3 %slice.204 = bf16[2048,2048]{1,0:T(8,128)(2,1)} slice(bf16[2048,2176]{1,0:T(8,128)(2,1)} %all-gather.4.cloned.1.call-done), slice={[0:2048], [0:2048]} | slice | bytes 16777216 | tf_op jit(solution)/shard_map/slice | solution.py:111
  163.2 10.4 %copy.270 = bf16[256,8,8,256]{3,2,1,0:T(8,128)(2,1)} copy(bf16[256,8,8,256]{3,1,2,0:T(8,128)(2,1)} %bitcast.101) | data formatting | bytes 16777216
  176.3 65.1 %all-to-all-done = bf16[8,10,256,64]{2,3,1,0:T(8,128)(2,1)} async-done(((bf16[8,10,256,64]{2,3,1,0:T(8,128)(2,1)}), bf16[8,10,256,64]{2,3,1,0:T(8,128)(2,1)}, u32[]{:S(2)}, u32[]{:S(2)}) %all-to-all-start) | async-done | bytes 2621472 | tf_op jit(solution)/shard_map/all_to_all | solution.py:100
  241.4 18.7 %fusion.16.rhs_ref = f32[10,2048,64]{2,1,0:T(8,128)} fusion(bf16[8,10,256,64]{2,3,1,0:T(8,128)(2,1)} %all-to-all-done, bf16[2048,8,256,1]{2,1,0,3:T(8,128)(2,1)} %bitcast.103), kind=kOutput, calls=%fused_computation.26 | convolution fusion | flops 5368709120 | bytes 16252928 | tf_op jit(solution)/shard_map/jsy,szyi->zji/dot_general | solution.py:109
  260.1 10.8 %shard_map.131 = bf16[10,2048,64]{2,1,0:T(8,128)(2,1)} custom-call(f32[9]{0:T(128)} %coupling_ref.1, f32[10]{0:T(128)} %shift_ref.1, f32[2048,1]{1,0:T(8,128)} %fusion.30.ly_ref, f32[1,64]{1,0:T(1,128)} %dynamic-slice_bitcast_fusion.lx_ref, f32[10,2048,64]{2,1,0:T(8,128)} %fusion.16.rhs_ref), custom_call_target="tpu_custom_call" | custom-call | tf_op jit(solution)/shard_map/pallas_call | solution.py:57
  271.0 15.0 %convert_bitcast_fusion = bf16[8,10,256,64]{2,3,0,1:T(8,128)(2,1)S(1)} fusion(bf16[8,256,2048,1]{2,1,0,3:T(8,128)(2,1)} %bitcast.109, bf16[10,2048,64]{2,1,0:T(8,128)(2,1)} %shard_map.131), kind=kOutput, calls=%fused_computation.27 | convolution fusion | flops 5370019840 | bytes 13631488 | tf_op jit(solution)/shard_map/syj,zji->szyi/dot_general | solution.py:119
  286.3 62.4 %all_to_all.10 = bf16[8,10,256,64]{2,3,1,0:T(8,128)(2,1)S(1)} all-to-all(bf16[8,10,256,64]{2,3,1,0:T(8,128)(2,1)S(1)} %copy.250), channel_id=1, replica_groups=mesh['px'=4,'py'=8] {'py'}, dimensions={0} | all-to-all | bytes 5242880 | tf_op jit(solution)/shard_map/all_to_all | solution.py:125
  350.5 4.4 copy.252
  355.6 6.3 %select_select_fusion = f32[10,256,512]{2,1,0:T(8,128)S(1)} fusion(s32[10,256,512]{2,1,0:T(8,128)} %param.27, f32[]{:T(128)} %bitcast.24, f32[]{:T(128)} %bitcast.23, f32[]{:T(128)} %bitcast.22, f32[]{:T(128)} %bitcast.21), kind=kLoop, calls=%fused_computation.24 | loop fusion | flops 10485760 | bytes 10485776 | tf_op jit(solution)/shard_map/jit(_where)/select_n | solution.py:136
  361.9 4.0 slice.205
  366.6 3.1 slice.218
  369.6 3.0 slice_reduce_fusion
  372.6 8.3 %slice_bitcast_fusion = (s32[10,256,512]{2,1,0:T(8,128)}, s32[10,256,512]{2,1,0:T(8,128)S(1)}) fusion(s32[2,10,256,512]{3,2,1,0:T(8,128)} %param.28), kind=kLoop, calls=%fused_computation.23 | loop fusion | bytes 20971520 | tf_op jit(solution)/shard_map/squeeze | solution.py:138
  384.7 74.5 %all-gather.8.cloned.1.call-done = bf16[10,256,2048]{2,1,0:T(8,128)(2,1)} async-done(((bf16[10,256,512]{2,1,0:T(8,128)(2,1)}), bf16[10,256,2048]{2,1,0:T(8,128)(2,1)}) %all-gather.8.cloned.1.call-update) | async-done | bytes 10485776 | tf_op jit(solution)/shard_map/all_gather | solution.py:129
  459.2 8.6 %fusion.25 = f32[10,256,512]{2,1,0:T(8,128)S(1)} fusion(bf16[10,256,2048]{2,1,0:T(8,128)(2,1)} %all-gather.8.cloned.1.call-done, bf16[2048,512]{1,0:T(8,128)(2,1)S(1)} %copy-done), kind=kOutput, calls=%fused_computation.36 | convolution fusion | flops 5368709120 | bytes 17825792 | tf_op jit(solution)/shard_map/zyi,ix->zyx/dot_general | solution.py:127
  468.9 3.7 slice.209
  472.6 3.0 slice.222
  476.3 3.7 collective-permute-start.4
  481.4 4.0 collective-permute-start.6
  494.0 3.2 collective-permute-start.5
  497.2 2.8 multiply_select_fusion
  500.1 16.2 %fusion.13 = (f32[10,256,512]{2,1,0:T(8,128)S(1)}, f32[10,256,512]{2,1,0:T(8,128)S(1)}) fusion(f32[10,1,512]{2,1,0:T(1,128)S(1)} %get-tuple-element.54, f32[10,255,512]{2,1,0:T(8,128)} %slice.218, f32[10,256,512]{2,1,0:T(8,128)S(1)} %copy-done.2, f32[10,1,512]{2,1,0:T(1,128)S(1)} %get-tuple-element.53, f32[10,255,512]{2,1,0:T(8,128)} %slice.222, ...), kind=kLoop, calls=%fused_computation.18 | loop fusion | flops 28835840 | bytes 52429584 | tf_op jit(solution)/shard_map/jit(_where)/select_n | solution.py:156
  516.3 4.5 fusion.11
  (75 shorter events, 35.4 us)
Async XLA Ops:
  7.2 452.0 %copy-start = (bf16[2048,512]{1,0:T(8,128)(2,1)S(1)}, bf16[2048,512]{1,0:T(8,128)(2,1)}, u32[]{:S(2)}) copy-start(bf16[2048,512]{1,0:T(8,128)(2,1)} %param.26) | copy-start | bytes 6291460
  7.2 147.7 %all-gather.4.cloned.1.call-start = ((), (), s32[]{:S(2)}) async-start(), calls=%async_computation.2 | async-start | bytes 10027008 | tf_op jit(solution)/shard_map/all_gather | solution.py:107
  15.9 255.1 %all-gather.6.cloned.1.call-start = ((), (), s32[]{:S(2)}) async-start(), calls=%async_computation.3 | async-start | bytes 9437184 | tf_op jit(solution)/shard_map/all_gather | solution.py:121
  21.0 58.9 %collective-permute-start = (bf16[10,256,512]{2,1,0:T(8,128)(2,1)}, bf16[10,256,512]{2,1,0:T(8,128)(2,1)}, u32[]{:S(2)}, u32[]{:S(2)}) collective-permute-start(bf16[10,256,512]{2,1,0:T(8,128)(2,1)} %convert_element_type.45), channel_id=1, source_target_pairs={{0,8},{8,0},{16,24},{24,16},{1,9},{9,1},{17,25},{25,17},{2,10},{10... | collective-permute-start | bytes 7864328 | tf_op jit(solution)/shard_map/ppermute | solution.py:13
  23.1 57.7 %collective-permute-start.1 = (bf16[10,256,512]{2,1,0:T(8,128)(2,1)}, bf16[10,256,512]{2,1,0:T(8,128)(2,1)}, u32[]{:S(2)}, u32[]{:S(2)}) collective-permute-start(bf16[10,256,512]{2,1,0:T(8,128)(2,1)} %convert_element_type.45), channel_id=1, source_target_pairs={{0,16},{8,24},{16,0},{24,8},{1,17},{9,25},{17,1},{25,9},{2,18},{10... | collective-permute-start | bytes 7864328 | tf_op jit(solution)/shard_map/ppermute | solution.py:13
  24.3 112.8 %collective-permute-start.2 = (bf16[10,256,512]{2,1,0:T(8,128)(2,1)}, bf16[10,256,512]{2,1,0:T(8,128)(2,1)}, u32[]{:S(2)}, u32[]{:S(2)}) collective-permute-start(bf16[10,256,512]{2,1,0:T(8,128)(2,1)} %convert_element_type.45), channel_id=1, source_target_pairs={{0,24},{8,16},{16,8},{24,0},{1,25},{9,17},{17,9},{25,1},{2,26},{10... | collective-permute-start | bytes 7864328 | tf_op jit(solution)/shard_map/ppermute | solution.py:13
  146.9 94.5 %all-to-all-start = ((bf16[8,10,256,64]{2,3,1,0:T(8,128)(2,1)}), bf16[8,10,256,64]{2,3,1,0:T(8,128)(2,1)}, u32[]{:S(2)}, u32[]{:S(2)}) async-start(bf16[8,10,256,64]{2,3,1,0:T(8,128)(2,1)} %convert_bitcast_fusion.1), calls=%async_computation | async-start | bytes 5242880 | tf_op jit(solution)/shard_map/all_to_all | solution.py:100
  153.6 305.6 %all-gather.8.cloned.1.call-start = ((), (), s32[]{:S(2)}) async-start(), calls=%async_computation.4 | async-start | bytes 13107200 | tf_op jit(solution)/shard_map/all_gather | solution.py:129
  350.5 4.4 copy-start.5
  361.9 4.6 copy-start.3
  467.8 4.9 copy-start.1
  476.3 11.1 %collective-permute-start.4 = (f32[3,10,256,1]{2,0,1,3:T(4,128)}, f32[3,10,256,1]{2,0,1,3:T(4,128)}, u32[]{:S(2)}, u32[]{:S(2)}) collective-permute-start(f32[3,10,256,1]{2,0,1,3:T(4,128)} %pad_maximum_fusion.2), channel_id=1, source_target_pairs={{0,8},{8,16},{16,24},{1,9},{9,17},{17,25},{2,10},{10,18},{18,26},{... | collective-permute-start | bytes 92168 | tf_op jit(solution)/shard_map/ppermute | solution.py:148
  480.0 5.3 %collective-permute-start.3 = (f32[2,10,256,1]{2,0,1,3:T(2,128)S(1)}, f32[2,10,256,1]{2,0,1,3:T(2,128)S(1)}, u32[]{:S(2)}, u32[]{:S(2)}) collective-permute-start(f32[2,10,256,1]{2,0,1,3:T(2,128)S(1)} %pad_maximum_fusion.4), channel_id=1, source_target_pairs={{8,0},{16,8},{24,16},{9,1},{17,9},{25,17},{10,2},{18,10},{26,18},{... | collective-permute-start | bytes 61448 | tf_op jit(solution)/shard_map/ppermute | solution.py:147
  481.4 10.9 %collective-permute-start.6 = (f32[3,10,1,512]{3,2,1,0:T(1,128)S(1)}, f32[3,10,1,512]{3,2,1,0:T(1,128)S(1)}, u32[]{:S(2)}, u32[]{:S(2)}) collective-permute-start(f32[3,10,1,512]{3,2,1,0:T(1,128)S(1)} %pad_maximum_fusion.1), channel_id=1, source_target_pairs={{0,1},{1,2},{2,3},{3,4},{4,5},{5,6},{6,7},{8,9},{9,10},{10,11},{11... | collective-permute-start | bytes 184328 | tf_op jit(solution)/shard_map/ppermute | solution.py:148
  491.4 8.7 %copy-start.2 = (f32[10,256,512]{2,1,0:T(8,128)S(1)}, f32[10,256,512]{2,1,0:T(8,128)}, u32[]{:S(2)}) copy-start(f32[10,256,512]{2,1,0:T(8,128)} %copy-done.1) | copy-start | bytes 15728644
  491.4 8.7 %copy-start.4 = (f32[10,256,1]{2,1,0:T(8,128)S(1)}, f32[10,256,1]{2,1,0:T(8,128)}, u32[]{:S(2)}) copy-start(f32[10,256,1]{2,1,0:T(8,128)} %copy.254) | copy-start | bytes 30724
  494.0 6.0 %collective-permute-start.5 = (f32[2,10,1,512]{3,2,1,0:T(1,128)S(1)}, f32[2,10,1,512]{3,2,1,0:T(1,128)S(1)}, u32[]{:S(2)}, u32[]{:S(2)}) collective-permute-start(f32[2,10,1,512]{3,2,1,0:T(1,128)S(1)} %pad_maximum_fusion.3), channel_id=1, source_target_pairs={{1,0},{2,1},{3,2},{4,3},{5,4},{6,5},{7,6},{9,8},{10,9},{11,10},{12... | collective-permute-start | bytes 122888 | tf_op jit(solution)/shard_map/ppermute | solution.py:147
Sparse Core Ops, SparseCore 0:
  16.0 88.8 all-gather.3
  106.6 107.9 all-gather.5
  355.0 104.1 all-gather.7

commit v4 on v2

--- a/solution.py
+++ b/solution.py
@@ -12,6 +12,38 @@
     for k in range(1, count):
         parts.append(lax.ppermute(block, axis, [(s, s ^ k) for s in range(count)]))
     return parts
+
+
+def arrange(received, axis):
+    own = lax.axis_index(axis)
+    stacked = jnp.stack(received)
+    return jnp.stack(
+        [lax.dynamic_index_in_dim(stacked, own ^ s, 0, keepdims=False) for s in range(len(received))]
+    )
+
+
+def chip_gather(block, axis):
+    count = lax.axis_size(axis)
+    same_core = [block]
+    for k in range(2, count, 2):
+        same_core.append(lax.ppermute(block, axis, [(s, s ^ k) for s in range(count)]))
+    mine = jnp.stack(same_core)
+    other = lax.ppermute(mine, axis, [(s, s ^ 1) for s in range(count)])
+    received = [None] * count
+    for k in range(0, count, 2):
+        received[k] = mine[k // 2]
+        received[k + 1] = other[k // 2]
+    return arrange(received, axis)
+
+
+def swap_chunks(chunks, axis):
+    count = lax.axis_size(axis)
+    own = lax.axis_index(axis)
+    received = [lax.dynamic_index_in_dim(chunks, own, 0, keepdims=False)]
+    for k in range(1, count):
+        piece = lax.dynamic_index_in_dim(chunks, own ^ k, 0, keepdims=False)
+        received.append(lax.ppermute(piece, axis, [(s, s ^ k) for s in range(count)]))
+    return arrange(received, axis)
 
 
 def in_exchange_order(matrix, axis):
@@ -97,30 +129,28 @@
         in_exchange_order(left_x, "px").reshape(-1, count_y, modes),
         preferred_element_type=jnp.float32,
     ).astype(jnp.bfloat16)
-    pencil = lax.all_to_all(spectral_x, "py", 0, 0, tiled=True)
+    pencil = swap_chunks(spectral_x, "py")
     spectral = jnp.einsum(
-        "jsy,szyi->zji",
-        lax.all_gather(left_y, "py", axis=0, tiled=True).reshape(-1, count_y, height),
+        "sjty,tzyi->zsji",
+        chip_gather(left_y, "py").reshape(count_y, -1, count_y, height),
         pencil,
         preferred_element_type=jnp.float32,
-    )
+    ).reshape(layers, -1, modes)
     own_x = lax.dynamic_slice_in_dim(lambda_x, at_y * modes, modes)
-    spread_y = jnp.zeros((count_y, lambda_y.shape[0]), lambda_y.dtype)
-    spread_y = lax.dynamic_update_index_in_dim(spread_y, lambda_y, at_y, 0)
-    all_y = lax.psum(spread_y, "py").reshape(-1)
+    all_y = chip_gather(lambda_y, "py").reshape(-1)
     solved = thomas_solve(spectral, own_x, all_y, coupling, layer_shift)
     back_pencil = jnp.einsum(
         "syj,zji->szyi",
-        lax.all_gather(right_y, "py", axis=0, tiled=True).reshape(count_y, height, -1),
+        chip_gather(right_y, "py"),
         solved,
         preferred_element_type=jnp.float32,
     ).astype(jnp.bfloat16)
-    back_y = lax.all_to_all(back_pencil, "py", 0, 0, tiled=True)
+    back_y = swap_chunks(back_pencil, "py")
     back_y = jnp.moveaxis(back_y, 0, 2).reshape(layers, height, -1)
     correction = jnp.einsum(
         "zyi,ix->zyx",
-        jnp.concatenate(exchange(back_y, "px"), axis=2),
-        in_exchange_order(right_x, "px"),
+        lax.all_gather(back_y, "px", axis=2, tiled=True),
+        right_x,
         preferred_element_type=jnp.float32,
     )
 

time: 567 us -> 632 us (1.11); the launches traced: 565 us -> 621 us
  blocking collectives: 194 us -> 0 us
  waiting for transfers between devices: 186 us -> 299 us
  starting transfers between devices: 25.7 us -> 108 us
  local copies, waits for them, and re-layouts: 50.4 us -> 100 us
  other arithmetic: 35.9 us -> 46.8 us
  matrix products: 48.6 us -> 40.6 us
    ppermute x0 -> x26, waiting for transfers between devices: none -> 209 us  [the longest x9 125 us: chip_gather(): lax.ppermute(block, axis, [(s, s ^ k) for s in range(count)])]
    ppermute x6 -> x3, waiting for transfers between devices: 185 us -> 0.01 us  [exchange(): parts.append(lax.ppermute(block, axis, [(s, s ^ k) for s in range(count)]))]
    psum x1 -> x0, blocking collectives: 128 us -> none  [shards(): all_y = lax.psum(spread_y, 'py').reshape(-1)]
    ppermute x0 -> x26, starting transfers between devices: none -> 92.7 us  [the longest x14 49.8 us: swap_chunks(): lax.ppermute(piece, axis, [(s, s ^ k) for s in range(count)])]
    all_gather x2 -> x1, waiting for transfers between devices: 0.01 us -> 90.1 us  [shards(): lax.all_gather(back_y, 'px', axis=2, tiled=True)]
    all_to_all x1 -> x0, blocking collectives: 65.6 us -> none  [shards(): back_y = lax.all_to_all(back_pencil, 'py', 0, 0, tiled=True)]
    unnamed x19 -> x85, local copies, waits for them, and re-layouts: 2.72 us -> 44 us
    transpose x0 -> x2, local copies, waits for them, and re-layouts: none -> 10.2 us  [the longest x1 8.43 us: shards(): jnp.einsum('sjty,tzyi->zsji', chip_gather(left_y, 'py').reshape(count_y,...]
  transfers between devices with their start and end apart: 13 -> 34, of which waited for: 6 -> 12; matrix products, arithmetic and copies ran while one was open for 13% -> 16% of each run, Pallas kernels for 2% -> 0%
where the time goes in v4:
time: 632 us; the launch traced here: 621 us
  waiting for transfers between devices  299 us (47%)
  starting transfers between devices  108 us (17%)
  local copies, waits for them, and re-layouts  100 us (16%)
  other arithmetic  46.8 us (7%)
  matrix products  40.6 us (6%)
  between operations  15.3 us (2%)
  Pallas kernels  11 us (2%)
    ppermute x9, waiting for transfers between devices, chip_gather(): lax.ppermute(block, axis, [(s, s ^ k) for s in range(count)])  125 us
    all_gather x1, waiting for transfers between devices, shards(): lax.all_gather(back_y, 'px', axis=2, tiled=True)  90.1 us
    ppermute x14, waiting for transfers between devices, swap_chunks(): lax.ppermute(piece, axis, [(s, s ^ k) for s in range(count)])  83.9 us
    ppermute x14, starting transfers between devices, swap_chunks(): lax.ppermute(piece, axis, [(s, s ^ k) for s in range(count)])  49.8 us
    unnamed x85, local copies, waits for them, and re-layouts  44 us
    ppermute x9, starting transfers between devices, chip_gather(): lax.ppermute(block, axis, [(s, s ^ k) for s in range(count)])  35.4 us
    select_n x1, other arithmetic, net(): flux_high = jnp.where(edge, 0.0, flux_high)  16 us
    dot_general x1, matrix products, shards(): jnp.einsum('syj,zji->szyi', chip_gather(right_y, 'py'), solved, preferred...  15 us
  transfers between devices with their start and end apart: 34, of which 12 were waited for; matrix products, arithmetic and copies ran while one was open for 16% of the time, Pallas kernels for 0%

profile of v4, /device:TPU:1, one launch (start us, length us, event | category | flops | bytes accessed | tf_op | source)
XLA Modules:
  0.0 621.4 jit_solution(17724214851421080811)
XLA Ops:
  7.2 4.5 convert_element_type.17
  18.1 22.0 %collective-permute-done = f32[256]{0:T(256)S(1)} collective-permute-done((f32[256]{0:T(256)S(1)}, f32[256]{0:T(256)S(1)}, u32[]{:S(2)}, u32[]{:S(2)}) %collective-permute-start) | collective-permute-done | bytes 1056 | tf_op jit(solution)/shard_map/ppermute | solution.py:29
  47.7 4.5 collective-permute-start.3
  73.0 50.9 %collective-permute-done.15 = bf16[256,2048]{0,1:T(8,128)(2,1)} collective-permute-done((bf16[256,2048]{0,1:T(8,128)(2,1)S(1)}, bf16[256,2048]{0,1:T(8,128)(2,1)}, u32[]{:S(2)}, u32[]{:S(2)}) %collective-permute-start.15) | collective-permute-done | bytes 1048608 | tf_op jit(solution)/shard_map/ppermute | solution.py:29
  123.9 23.6 %collective-permute-start.19 = (bf16[256,2048]{1,0:T(8,128)(2,1)}, bf16[256,2048]{1,0:T(8,128)(2,1)}, u32[]{:S(2)}, u32[]{:S(2)}) collective-permute-start(bf16[256,2048]{1,0:T(8,128)(2,1)} %param.19), channel_id=1, source_target_pairs={{0,4},{1,5},{2,6},{3,7},{4,0},{5,1},{6,2},{7,3},{8,12},{9,13},{10,... | collective-permute-start | bytes 3145736 | tf_op jit(solution)/shard_map/ppermute | solution.py:29
  147.5 3.6 pad_maximum_fusion
  153.8 10.1 %fusion.33 = bf16[8,64,10,256]{3,1,2,0:T(8,128)(2,1)} fusion(bf16[10,256,512]{2,1,0:T(8,128)(2,1)} %collective-permute-done.6, bf16[10,256,512]{2,1,0:T(8,128)(2,1)} %collective-permute-done.5, bf16[10,256,512]{2,1,0:T(8,128)(2,1)} %collective-permute-done.4, bf16[10,256,512]{2,1,0:T(8,128)(2,1)} %convert_element_type.17, ...), kind=kOutput, calls=%fused_computation.40 | convolution fusion | flops 5420351488 | bytes 15204352 | tf_op jit(solution)/shard_map/zyx,xci->czyi/dot_general | solution.py:126
  165.7 50.2 %collective-permute-done.19 = bf16[256,2048]{1,0:T(8,128)(2,1)} collective-permute-done((bf16[256,2048]{1,0:T(8,128)(2,1)}, bf16[256,2048]{1,0:T(8,128)(2,1)}, u32[]{:S(2)}, u32[]{:S(2)}) %collective-permute-start.19) | collective-permute-done | bytes 1048608 | tf_op jit(solution)/shard_map/ppermute | solution.py:29
  215.9 4.0 pad_maximum_fusion.1
  221.5 22.2 %collective-permute-start.8 = (bf16[10,256,64]{1,2,0:T(8,128)(2,1)S(1)}, bf16[10,256,64]{1,2,0:T(8,128)(2,1)S(1)}, u32[]{:S(2)}, u32[]{:S(2)}) collective-permute-start(bf16[10,256,64]{1,2,0:T(8,128)(2,1)S(1)} %get-tuple-element.25), channel_id=1, source_target_pairs={{0,2},{1,3},{2,0},{3,1},{4,6},{5,7},{6,4},{7,5},{8,10},{9,11},{10,... | collective-permute-start | bytes 983048 | tf_op jit(solution)/shard_map/ppermute | solution.py:45
  246.5 12.3 %collective-permute-done.8 = bf16[10,256,64]{1,2,0:T(8,128)(2,1)S(1)} collective-permute-done((bf16[10,256,64]{1,2,0:T(8,128)(2,1)S(1)}, bf16[10,256,64]{1,2,0:T(8,128)(2,1)S(1)}, u32[]{:S(2)}, u32[]{:S(2)}) %collective-permute-start.8) | collective-permute-done | bytes 327712 | tf_op jit(solution)/shard_map/ppermute | solution.py:45
  258.8 7.3 %collective-permute-done.9 = bf16[10,256,64]{1,2,0:T(8,128)(2,1)S(1)} collective-permute-done((bf16[10,256,64]{1,2,0:T(8,128)(2,1)S(1)}, bf16[10,256,64]{1,2,0:T(8,128)(2,1)S(1)}, u32[]{:S(2)}, u32[]{:S(2)}) %collective-permute-start.9) | collective-permute-done | bytes 327712 | tf_op jit(solution)/shard_map/ppermute | solution.py:45
  269.9 25.5 %collective-permute-done.11 = bf16[10,256,64]{1,2,0:T(8,128)(2,1)S(1)} collective-permute-done((bf16[10,256,64]{1,2,0:T(8,128)(2,1)S(1)}, bf16[10,256,64]{1,2,0:T(8,128)(2,1)S(1)}, u32[]{:S(2)}, u32[]{:S(2)}) %collective-permute-start.11) | collective-permute-done | bytes 327712 | tf_op jit(solution)/shard_map/ppermute | solution.py:45
  300.7 7.3 %fusion.17 = f32[10,8,256,64]{2,3,1,0:T(8,128)} fusion(bf16[8,256,8,256,1]{1,3,2,0,4:T(8,128)(2,1)S(1)} %bitcast.240, bf16[8,10,256,64]{2,3,1,0:T(8,128)(2,1)S(1)} %dynamic-slice_dynamic-update-slice_fusion.24), kind=kOutput, calls=%fused_computation.29 | convolution fusion | flops 5368709120 | bytes 16252928 | tf_op jit(solution)/shard_map/sjty,tzyi->zsji/dot_general | solution.py:133
  308.0 8.4 %copy.318 = f32[10,8,256,64]{3,2,1,0:T(8,128)} copy(f32[10,8,256,64]{2,3,1,0:T(8,128)} %fusion.17) | data formatting | bytes 10485760 | tf_op jit(solution)/shard_map/sjty,tzyi->zsji/transpose | solution.py:133
  342.1 11.0 %shard_map.131 = bf16[10,2048,64]{2,1,0:T(8,128)(2,1)} custom-call(f32[9]{0:T(128)} %coupling_ref.1, f32[10]{0:T(128)} %shift_ref.1, f32[2048,1]{1,0:T(8,128)} %bitcast.233, f32[1,64]{1,0:T(1,128)} %dynamic-slice_bitcast_fusion.14.lx_ref, f32[10,2048,64]{2,1,0:T(8,128)} %bitcast.228), custom_call_target="tpu_custom_call" | custom-call | tf_op jit(solution)/shard_map/pallas_call | solution.py:89
  353.1 15.0 %fusion.28 = bf16[10,64,8,256]{3,1,2,0:T(8,128)(2,1)S(1)} fusion(bf16[8,256,2048]{2,1,0:T(8,128)(2,1)} %copy-done.6, bf16[10,2048,64]{2,1,0:T(8,128)(2,1)} %shard_map.131), kind=kOutput, calls=%fused_computation.39 | convolution fusion | flops 5370019840 | bytes 13631488 | tf_op jit(solution)/shard_map/syj,zji->szyi/dot_general | solution.py:142
  368.7 14.3 %collective-permute-start.23 = (bf16[10,256,64]{1,2,0:T(8,128)(2,1)S(1)}, bf16[10,256,64]{1,2,0:T(8,128)(2,1)S(1)}, u32[]{:S(2)}, u32[]{:S(2)}) collective-permute-start(bf16[10,256,64]{1,2,0:T(8,128)(2,1)S(1)} %get-tuple-element.17), channel_id=1, source_target_pairs={{0,2},{1,3},{2,0},{3,1},{4,6},{5,7},{6,4},{7,5},{8,10},{9,11},{10,... | collective-permute-start | bytes 983048 | tf_op jit(solution)/shard_map/ppermute | solution.py:45
  388.0 16.4 %collective-permute-done.23 = bf16[10,256,64]{1,2,0:T(8,128)(2,1)S(1)} collective-permute-done((bf16[10,256,64]{1,2,0:T(8,128)(2,1)S(1)}, bf16[10,256,64]{1,2,0:T(8,128)(2,1)S(1)}, u32[]{:S(2)}, u32[]{:S(2)}) %collective-permute-start.23) | collective-permute-done | bytes 327712 | tf_op jit(solution)/shard_map/ppermute | solution.py:45
  406.7 4.7 collective-permute-done.24
  411.5 17.8 %collective-permute-done.26 = bf16[10,256,64]{1,2,0:T(8,128)(2,1)S(1)} collective-permute-done((bf16[10,256,64]{1,2,0:T(8,128)(2,1)S(1)}, bf16[10,256,64]{1,2,0:T(8,128)(2,1)S(1)}, u32[]{:S(2)}, u32[]{:S(2)}) %collective-permute-start.26) | collective-permute-done | bytes 327712 | tf_op jit(solution)/shard_map/ppermute | solution.py:45
  431.5 4.6 copy.329
  436.7 6.1 select_select_fusion
  442.9 4.0 slice.192
  452.7 7.2 %slice_bitcast_fusion = (s32[10,256,512]{2,1,0:T(8,128)S(1)}, s32[10,256,512]{2,1,0:T(8,128)S(1)}) fusion(s32[2,10,256,512]{3,2,1,0:T(8,128)} %param.22), kind=kLoop, calls=%fused_computation.22 | loop fusion | bytes 20971520 | tf_op jit(solution)/shard_map/squeeze | solution.py:161
  462.8 90.1 %all-gather.2.cloned.1.call-done = bf16[10,256,2048]{2,1,0:T(8,128)(2,1)} async-done(((bf16[10,256,512]{2,1,0:T(8,128)(2,1)}), bf16[10,256,2048]{2,1,0:T(8,128)(2,1)}) %all-gather.2.cloned.1.call-update) | async-done | bytes 10485776 | tf_op jit(solution)/shard_map/all_gather | solution.py:152
  552.9 8.3 %fusion.26 = f32[10,256,512]{2,1,0:T(8,128)S(1)} fusion(bf16[10,256,2048]{2,1,0:T(8,128)(2,1)} %all-gather.2.cloned.1.call-done, bf16[2048,512]{1,0:T(8,128)(2,1)S(1)} %copy-done), kind=kOutput, calls=%fused_computation.37 | convolution fusion | flops 5368709120 | bytes 17825792 | tf_op jit(solution)/shard_map/zyi,ix->zyx/dot_general | solution.py:150
  562.4 3.8 slice.196
  569.8 3.7 collective-permute-start.30
  575.1 3.9 collective-permute-start.32
  593.6 16.0 %fusion.13 = (f32[10,256,512]{2,1,0:T(8,128)S(1)}, f32[10,256,512]{2,1,0:T(8,128)S(1)}) fusion(f32[10,1,512]{2,1,0:T(1,128)S(1)} %get-tuple-element.32, f32[10,255,512]{2,1,0:T(8,128)} %slice.205, f32[10,256,512]{2,1,0:T(8,128)S(1)} %copy-done.2, f32[10,1,512]{2,1,0:T(1,128)S(1)} %get-tuple-element.31, f32[10,255,512]{2,1,0:T(8,128)} %slice.209, ...), kind=kLoop, calls=%fused_computation.18 | loop fusion | flops 28835840 | bytes 52429584 | tf_op jit(solution)/shard_map/jit(_where)/select_n | solution.py:179
  609.6 4.5 fusion.11
  (189 shorter events, 118.5 us)
Async XLA Ops:
  7.2 545.7 %all-gather.2.cloned.1.call-start = ((), (), s32[]{:S(2)}) async-start(), calls=%async_computation | async-start | bytes 13107200 | tf_op jit(solution)/shard_map/all_gather | solution.py:152
  11.7 139.4 %collective-permute-start.4 = (bf16[10,256,512]{2,1,0:T(8,128)(2,1)}, bf16[10,256,512]{2,1,0:T(8,128)(2,1)}, u32[]{:S(2)}, u32[]{:S(2)}) collective-permute-start(bf16[10,256,512]{2,1,0:T(8,128)(2,1)} %convert_element_type.17), channel_id=1, source_target_pairs={{0,8},{8,0},{16,24},{24,16},{1,9},{9,1},{17,25},{25,17},{2,10},{10... | collective-permute-start | bytes 7864328 | tf_op jit(solution)/shard_map/ppermute | solution.py:13
  13.8 138.6 %collective-permute-start.5 = (bf16[10,256,512]{2,1,0:T(8,128)(2,1)}, bf16[10,256,512]{2,1,0:T(8,128)(2,1)}, u32[]{:S(2)}, u32[]{:S(2)}) collective-permute-start(bf16[10,256,512]{2,1,0:T(8,128)(2,1)} %convert_element_type.17), channel_id=1, source_target_pairs={{0,16},{8,24},{16,0},{24,8},{1,17},{9,25},{17,1},{25,9},{2,18},{10... | collective-permute-start | bytes 7864328 | tf_op jit(solution)/shard_map/ppermute | solution.py:13
  15.0 138.8 %collective-permute-start.6 = (bf16[10,256,512]{2,1,0:T(8,128)(2,1)}, bf16[10,256,512]{2,1,0:T(8,128)(2,1)}, u32[]{:S(2)}, u32[]{:S(2)}) collective-permute-start(bf16[10,256,512]{2,1,0:T(8,128)(2,1)} %convert_element_type.17), channel_id=1, source_target_pairs={{0,24},{8,16},{16,8},{24,0},{1,25},{9,17},{17,9},{25,1},{2,26},{10... | collective-permute-start | bytes 7864328 | tf_op jit(solution)/shard_map/ppermute | solution.py:13
  16.5 37.5 %collective-permute-start.14 = (bf16[256,2048]{0,1:T(8,128)(2,1)S(1)}, bf16[256,2048]{0,1:T(8,128)(2,1)}, u32[]{:S(2)}, u32[]{:S(2)}) collective-permute-start(bf16[256,2048]{0,1:T(8,128)(2,1)S(1)} %copy.312), channel_id=1, source_target_pairs={{0,2},{1,3},{2,0},{3,1},{4,6},{5,7},{6,4},{7,5},{8,10},{9,11},{10,... | collective-permute-start | bytes 3145736 | tf_op jit(solution)/shard_map/ppermute | solution.py:29
  18.0 22.1 %collective-permute-start = (f32[256]{0:T(256)S(1)}, f32[256]{0:T(256)S(1)}, u32[]{:S(2)}, u32[]{:S(2)}) collective-permute-start(f32[256]{0:T(256)S(1)} %copy-done.8), channel_id=1, source_target_pairs={{0,2},{1,3},{2,0},{3,1},{4,6},{5,7},{6,4},{7,5},{8,10},{9,11},{10,... | collective-permute-start | bytes 3080 | tf_op jit(solution)/shard_map/ppermute | solution.py:29
  47.7 5.6 collective-permute-start.3
  53.3 70.7 %collective-permute-start.15 = (bf16[256,2048]{0,1:T(8,128)(2,1)S(1)}, bf16[256,2048]{0,1:T(8,128)(2,1)}, u32[]{:S(2)}, u32[]{:S(2)}) collective-permute-start(bf16[256,2048]{0,1:T(8,128)(2,1)S(1)} %copy.312), channel_id=1, source_target_pairs={{0,4},{1,5},{2,6},{3,7},{4,0},{5,1},{6,2},{7,3},{8,12},{9,13},{10,... | collective-permute-start | bytes 3145736 | tf_op jit(solution)/shard_map/ppermute | solution.py:29
  53.9 70.0 %collective-permute-start.16 = (bf16[256,2048]{0,1:T(8,128)(2,1)S(1)}, bf16[256,2048]{0,1:T(8,128)(2,1)}, u32[]{:S(2)}, u32[]{:S(2)}) collective-permute-start(bf16[256,2048]{0,1:T(8,128)(2,1)S(1)} %copy.312), channel_id=1, source_target_pairs={{0,6},{1,7},{2,4},{3,5},{4,2},{5,3},{6,0},{7,1},{8,14},{9,15},{10,... | collective-permute-start | bytes 3145736 | tf_op jit(solution)/shard_map/ppermute | solution.py:29
  123.9 41.8 %collective-permute-start.18 = (bf16[256,2048]{1,0:T(8,128)(2,1)}, bf16[256,2048]{1,0:T(8,128)(2,1)}, u32[]{:S(2)}, u32[]{:S(2)}) collective-permute-start(bf16[256,2048]{1,0:T(8,128)(2,1)} %param.19), channel_id=1, source_target_pairs={{0,2},{1,3},{2,0},{3,1},{4,6},{5,7},{6,4},{7,5},{8,10},{9,11},{10,... | collective-permute-start | bytes 3145736 | tf_op jit(solution)/shard_map/ppermute | solution.py:29
  123.9 92.0 %collective-permute-start.19 = (bf16[256,2048]{1,0:T(8,128)(2,1)}, bf16[256,2048]{1,0:T(8,128)(2,1)}, u32[]{:S(2)}, u32[]{:S(2)}) collective-permute-start(bf16[256,2048]{1,0:T(8,128)(2,1)} %param.19), channel_id=1, source_target_pairs={{0,4},{1,5},{2,6},{3,7},{4,0},{5,1},{6,2},{7,3},{8,12},{9,13},{10,... | collective-permute-start | bytes 3145736 | tf_op jit(solution)/shard_map/ppermute | solution.py:29
  151.1 64.8 %collective-permute-start.20 = (bf16[256,2048]{1,0:T(8,128)(2,1)}, bf16[256,2048]{1,0:T(8,128)(2,1)}, u32[]{:S(2)}, u32[]{:S(2)}) collective-permute-start(bf16[256,2048]{1,0:T(8,128)(2,1)} %param.19), channel_id=1, source_target_pairs={{0,6},{1,7},{2,4},{3,5},{4,2},{5,3},{6,0},{7,1},{8,14},{9,15},{10,... | collective-permute-start | bytes 3145736 | tf_op jit(solution)/shard_map/ppermute | solution.py:29
  152.4 143.4 %collective-permute-start.17 = (bf16[4,256,2048]{1,2,0:T(8,128)(2,1)}, bf16[4,256,2048]{1,2,0:T(8,128)(2,1)S(1)}, u32[]{:S(2)}, u32[]{:S(2)}) collective-permute-start(bf16[4,256,2048]{1,2,0:T(8,128)(2,1)} %pad_maximum_fusion), channel_id=1, source_target_pairs={{0,1},{1,0},{2,3},{3,2},{4,5},{5,4},{6,7},{7,6},{8,9},{9,8},{10,11... | collective-permute-start | bytes 12582920 | tf_op jit(solution)/shard_map/ppermute | solution.py:31
  165.6 79.1 %collective-permute-start.7 = (bf16[10,256,64]{1,2,0:T(8,128)(2,1)S(1)}, bf16[10,256,64]{1,2,0:T(8,128)(2,1)S(1)}, u32[]{:S(2)}, u32[]{:S(2)}) collective-permute-start(bf16[10,256,64]{1,2,0:T(8,128)(2,1)S(1)} %get-tuple-element.26), channel_id=1, source_target_pairs={{0,1},{1,0},{2,3},{3,2},{4,5},{5,4},{6,7},{7,6},{8,9},{9,8},{10,11... | collective-permute-start | bytes 983048 | tf_op jit(solution)/shard_map/ppermute | solution.py:45
  220.0 96.4 %collective-permute-start.21 = (bf16[4,256,2048]{2,1,0:T(8,128)(2,1)}, bf16[4,256,2048]{2,1,0:T(8,128)(2,1)}, u32[]{:S(2)}, u32[]{:S(2)}) collective-permute-start(bf16[4,256,2048]{2,1,0:T(8,128)(2,1)} %pad_maximum_fusion.1), channel_id=1, source_target_pairs={{0,1},{1,0},{2,3},{3,2},{4,5},{5,4},{6,7},{7,6},{8,9},{9,8},{10,11... | collective-permute-start | bytes 12582920 | tf_op jit(solution)/shard_map/ppermute | solution.py:31
  221.5 37.3 %collective-permute-start.8 = (bf16[10,256,64]{1,2,0:T(8,128)(2,1)S(1)}, bf16[10,256,64]{1,2,0:T(8,128)(2,1)S(1)}, u32[]{:S(2)}, u32[]{:S(2)}) collective-permute-start(bf16[10,256,64]{1,2,0:T(8,128)(2,1)S(1)} %get-tuple-element.25), channel_id=1, source_target_pairs={{0,2},{1,3},{2,0},{3,1},{4,6},{5,7},{6,4},{7,5},{8,10},{9,11},{10,... | collective-permute-start | bytes 983048 | tf_op jit(solution)/shard_map/ppermute | solution.py:45
  243.7 22.4 %collective-permute-start.9 = (bf16[10,256,64]{1,2,0:T(8,128)(2,1)S(1)}, bf16[10,256,64]{1,2,0:T(8,128)(2,1)S(1)}, u32[]{:S(2)}, u32[]{:S(2)}) collective-permute-start(bf16[10,256,64]{1,2,0:T(8,128)(2,1)S(1)} %get-tuple-element.24), channel_id=1, source_target_pairs={{0,3},{1,2},{2,1},{3,0},{4,7},{5,6},{6,5},{7,4},{8,11},{9,10},{10,... | collective-permute-start | bytes 983048 | tf_op jit(solution)/shard_map/ppermute | solution.py:45
  244.7 22.7 %collective-permute-start.10 = (bf16[10,256,64]{1,2,0:T(8,128)(2,1)S(1)}, bf16[10,256,64]{1,2,0:T(8,128)(2,1)S(1)}, u32[]{:S(2)}, u32[]{:S(2)}) collective-permute-start(bf16[10,256,64]{1,2,0:T(8,128)(2,1)S(1)} %get-tuple-element.23), channel_id=1, source_target_pairs={{0,4},{1,5},{2,6},{3,7},{4,0},{5,1},{6,2},{7,3},{8,12},{9,13},{10,... | collective-permute-start | bytes 983048 | tf_op jit(solution)/shard_map/ppermute | solution.py:45
  258.8 36.6 %collective-permute-start.11 = (bf16[10,256,64]{1,2,0:T(8,128)(2,1)S(1)}, bf16[10,256,64]{1,2,0:T(8,128)(2,1)S(1)}, u32[]{:S(2)}, u32[]{:S(2)}) collective-permute-start(bf16[10,256,64]{1,2,0:T(8,128)(2,1)S(1)} %get-tuple-element.22), channel_id=1, source_target_pairs={{0,5},{1,4},{2,7},{3,6},{4,1},{5,0},{6,3},{7,2},{8,13},{9,12},{10,... | collective-permute-start | bytes 983048 | tf_op jit(solution)/shard_map/ppermute | solution.py:45
  266.1 29.3 %collective-permute-start.12 = (bf16[10,256,64]{1,2,0:T(8,128)(2,1)S(1)}, bf16[10,256,64]{1,2,0:T(8,128)(2,1)S(1)}, u32[]{:S(2)}, u32[]{:S(2)}) collective-permute-start(bf16[10,256,64]{1,2,0:T(8,128)(2,1)S(1)} %get-tuple-element.21), channel_id=1, source_target_pairs={{0,6},{1,7},{2,4},{3,5},{4,2},{5,3},{6,0},{7,1},{8,14},{9,15},{10,... | collective-permute-start | bytes 983048 | tf_op jit(solution)/shard_map/ppermute | solution.py:45
  267.4 28.0 %collective-permute-start.13 = (bf16[10,256,64]{1,2,0:T(8,128)(2,1)S(1)}, bf16[10,256,64]{1,2,0:T(8,128)(2,1)S(1)}, u32[]{:S(2)}, u32[]{:S(2)}) collective-permute-start(bf16[10,256,64]{1,2,0:T(8,128)(2,1)S(1)} %get-tuple-element.20), channel_id=1, source_target_pairs={{0,7},{1,6},{2,5},{3,4},{4,3},{5,2},{6,1},{7,0},{8,15},{9,14},{10,... | collective-permute-start | bytes 983048 | tf_op jit(solution)/shard_map/ppermute | solution.py:45
  368.2 17.7 %collective-permute-start.22 = (bf16[10,256,64]{1,2,0:T(8,128)(2,1)S(1)}, bf16[10,256,64]{1,2,0:T(8,128)(2,1)S(1)}, u32[]{:S(2)}, u32[]{:S(2)}) collective-permute-start(bf16[10,256,64]{1,2,0:T(8,128)(2,1)S(1)} %get-tuple-element.18), channel_id=1, source_target_pairs={{0,1},{1,0},{2,3},{3,2},{4,5},{5,4},{6,7},{7,6},{8,9},{9,8},{10,11... | collective-permute-start | bytes 983048 | tf_op jit(solution)/shard_map/ppermute | solution.py:45
  368.7 35.7 %collective-permute-start.23 = (bf16[10,256,64]{1,2,0:T(8,128)(2,1)S(1)}, bf16[10,256,64]{1,2,0:T(8,128)(2,1)S(1)}, u32[]{:S(2)}, u32[]{:S(2)}) collective-permute-start(bf16[10,256,64]{1,2,0:T(8,128)(2,1)S(1)} %get-tuple-element.17), channel_id=1, source_target_pairs={{0,2},{1,3},{2,0},{3,1},{4,6},{5,7},{6,4},{7,5},{8,10},{9,11},{10,... | collective-permute-start | bytes 983048 | tf_op jit(solution)/shard_map/ppermute | solution.py:45
  383.0 28.4 %collective-permute-start.24 = (bf16[10,256,64]{1,2,0:T(8,128)(2,1)S(1)}, bf16[10,256,64]{1,2,0:T(8,128)(2,1)S(1)}, u32[]{:S(2)}, u32[]{:S(2)}) collective-permute-start(bf16[10,256,64]{1,2,0:T(8,128)(2,1)S(1)} %get-tuple-element.16), channel_id=1, source_target_pairs={{0,3},{1,2},{2,1},{3,0},{4,7},{5,6},{6,5},{7,4},{8,11},{9,10},{10,... | collective-permute-start | bytes 983048 | tf_op jit(solution)/shard_map/ppermute | solution.py:45
  383.0 28.4 %collective-permute-start.25 = (bf16[10,256,64]{1,2,0:T(8,128)(2,1)S(1)}, bf16[10,256,64]{1,2,0:T(8,128)(2,1)S(1)}, u32[]{:S(2)}, u32[]{:S(2)}) collective-permute-start(bf16[10,256,64]{1,2,0:T(8,128)(2,1)S(1)} %get-tuple-element.15), channel_id=1, source_target_pairs={{0,4},{1,5},{2,6},{3,7},{4,0},{5,1},{6,2},{7,3},{8,12},{9,13},{10,... | collective-permute-start | bytes 983048 | tf_op jit(solution)/shard_map/ppermute | solution.py:45
  385.5 43.8 %collective-permute-start.26 = (bf16[10,256,64]{1,2,0:T(8,128)(2,1)S(1)}, bf16[10,256,64]{1,2,0:T(8,128)(2,1)S(1)}, u32[]{:S(2)}, u32[]{:S(2)}) collective-permute-start(bf16[10,256,64]{1,2,0:T(8,128)(2,1)S(1)} %get-tuple-element.14), channel_id=1, source_target_pairs={{0,5},{1,4},{2,7},{3,6},{4,1},{5,0},{6,3},{7,2},{8,13},{9,12},{10,... | collective-permute-start | bytes 983048 | tf_op jit(solution)/shard_map/ppermute | solution.py:45
  385.9 43.4 %collective-permute-start.27 = (bf16[10,256,64]{1,2,0:T(8,128)(2,1)S(1)}, bf16[10,256,64]{1,2,0:T(8,128)(2,1)S(1)}, u32[]{:S(2)}, u32[]{:S(2)}) collective-permute-start(bf16[10,256,64]{1,2,0:T(8,128)(2,1)S(1)} %get-tuple-element.19), channel_id=1, source_target_pairs={{0,6},{1,7},{2,4},{3,5},{4,2},{5,3},{6,0},{7,1},{8,14},{9,15},{10,... | collective-permute-start | bytes 983048 | tf_op jit(solution)/shard_map/ppermute | solution.py:45
  404.4 25.0 %collective-permute-start.28 = (bf16[10,256,64]{1,2,0:T(8,128)(2,1)S(1)}, bf16[10,256,64]{1,2,0:T(8,128)(2,1)S(1)}, u32[]{:S(2)}, u32[]{:S(2)}) collective-permute-start(bf16[10,256,64]{1,2,0:T(8,128)(2,1)S(1)} %get-tuple-element.13), channel_id=1, source_target_pairs={{0,7},{1,6},{2,5},{3,4},{4,3},{5,2},{6,1},{7,0},{8,15},{9,14},{10,... | collective-permute-start | bytes 983048 | tf_op jit(solution)/shard_map/ppermute | solution.py:45
  569.8 11.3 %collective-permute-start.30 = (f32[3,10,256,1]{2,0,1,3:T(4,128)}, f32[3,10,256,1]{2,0,1,3:T(4,128)}, u32[]{:S(2)}, u32[]{:S(2)}) collective-permute-start(f32[3,10,256,1]{2,0,1,3:T(4,128)} %pad_maximum_fusion.3), channel_id=1, source_target_pairs={{0,8},{8,16},{16,24},{1,9},{9,17},{17,25},{2,10},{10,18},{18,26},{... | collective-permute-start | bytes 92168 | tf_op jit(solution)/shard_map/ppermute | solution.py:171
  573.5 5.6 collective-permute-start.29
  575.1 11.0 %collective-permute-start.32 = (f32[3,10,1,512]{3,2,1,0:T(1,128)S(1)}, f32[3,10,1,512]{3,2,1,0:T(1,128)S(1)}, u32[]{:S(2)}, u32[]{:S(2)}) collective-permute-start(f32[3,10,1,512]{3,2,1,0:T(1,128)S(1)} %pad_maximum_fusion.2), channel_id=1, source_target_pairs={{0,1},{1,2},{2,3},{3,4},{4,5},{5,6},{6,7},{8,9},{9,10},{10,11},{11... | collective-permute-start | bytes 184328 | tf_op jit(solution)/shard_map/ppermute | solution.py:171
  587.8 5.8 collective-permute-start.31
  (13 other events, 734.4 us)
Sparse Core Ops, SparseCore 0:
  436.2 116.5 all-gather.1

commit v5 on v3

--- a/solution.py
+++ b/solution.py
@@ -98,10 +98,11 @@
         preferred_element_type=jnp.float32,
     ).astype(jnp.bfloat16)
     pencil = lax.all_to_all(spectral_x, "py", 0, 0, tiled=True)
-    high = lambda_y.astype(jnp.bfloat16)
-    rest = lambda_y - high.astype(jnp.float32)
-    middle = rest.astype(jnp.bfloat16)
-    low = (rest - middle.astype(jnp.float32)).astype(jnp.bfloat16)
+    high = lax.reduce_precision(lambda_y, exponent_bits=8, mantissa_bits=7)
+    rest = lambda_y - high
+    middle = lax.reduce_precision(rest, exponent_bits=8, mantissa_bits=7)
+    low = lax.reduce_precision(rest - middle, exponent_bits=8, mantissa_bits=7)
+    high, middle, low = (p.astype(jnp.bfloat16) for p in (high, middle, low))
     pieces = jnp.zeros((lambda_y.shape[0], 128), jnp.bfloat16)
     pieces = pieces.at[:, 0].set(high).at[:, 1].set(middle).at[:, 2].set(low)
     carried = lax.all_gather(jnp.concatenate([left_y, pieces], axis=1), "py", axis=0, tiled=True)

time: 537 us -> 537 us (level)
  no operation moved by 1% of the time
where the time goes in v5:
time: 537 us; the launch traced here: 528 us
  waiting for transfers between devices  245 us (46%)
  local copies, waits for them, and re-layouts  69.9 us (13%)
  blocking collectives  62.4 us (12%)
  matrix products  52.1 us (10%)
  other arithmetic  50.8 us (9%)
  starting transfers between devices  22.2 us (4%)
  between operations  14.5 us (3%)
  Pallas kernels  10.8 us (2%)
    ppermute x3, waiting for transfers between devices, exchange(): parts.append(lax.ppermute(block, axis, [(s, s ^ k) for s in range(count)]))  105 us
    all_gather x1, waiting for transfers between devices, shards(): lax.all_gather(back_y, 'px', axis=2, tiled=True)  74.5 us
    all_to_all x1, waiting for transfers between devices, shards(): pencil = lax.all_to_all(spectral_x, 'py', 0, 0, tiled=True)  65.1 us
    all_to_all x1, blocking collectives, shards(): back_y = lax.all_to_all(back_pencil, 'py', 0, 0, tiled=True)  62.4 us
    dot_general x1, matrix products, shards(): jnp.einsum('jsy,szyi->zji', carried[:, :columns].reshape(-1, count_y, hei...  18.7 us
    select_n x1, other arithmetic, net(): flux_high = jnp.where(edge, 0.0, flux_high)  16.2 us
    dot_general x1, matrix products, shards(): jnp.einsum('syj,zji->szyi', lax.all_gather(right_y, 'py', axis=0, tiled=T...  15 us
    slice x4, local copies, waits for them, and re-layouts, net(): rest = lambda a: lax.slice_in_dim(a, 1, None, axis=dim)  13.8 us
  transfers between devices with their start and end apart: 11, of which 5 were waited for; matrix products, arithmetic and copies ran while one was open for 19% of the time, Pallas kernels for 2%

profile of v5, /device:TPU:1, one launch (start us, length us, event | category | flops | bytes accessed | tf_op | source)
XLA Modules:
  0.0 527.6 jit_solution(3886009522724962547)
XLA Ops:
  13.4 2.3 pad_maximum_fusion
  16.5 4.3 convert_element_type.37
  24.2 2.9 constant_dynamic-slice_fusion.3
  27.0 2.1 copy.243
  29.1 2.0 copy.244
  32.4 47.4 %collective-permute-done = bf16[10,256,512]{2,1,0:T(8,128)(2,1)} collective-permute-done((bf16[10,256,512]{2,1,0:T(8,128)(2,1)}, bf16[10,256,512]{2,1,0:T(8,128)(2,1)}, u32[]{:S(2)}, u32[]{:S(2)}) %collective-permute-start) | collective-permute-done | bytes 2621472 | tf_op jit(solution)/shard_map/ppermute | solution.py:13
  80.6 56.3 %collective-permute-done.2 = bf16[10,256,512]{2,1,0:T(8,128)(2,1)} collective-permute-done((bf16[10,256,512]{2,1,0:T(8,128)(2,1)}, bf16[10,256,512]{2,1,0:T(8,128)(2,1)}, u32[]{:S(2)}, u32[]{:S(2)}) %collective-permute-start.2) | collective-permute-done | bytes 2621472 | tf_op jit(solution)/shard_map/ppermute | solution.py:13
  136.9 9.8 %convert_bitcast_fusion.1 = bf16[8,10,256,64]{2,3,1,0:T(8,128)(2,1)} fusion(bf16[10,256,512]{2,1,0:T(8,128)(2,1)} %collective-permute-done.2, bf16[10,256,512]{2,1,0:T(8,128)(2,1)} %collective-permute-done.1, bf16[10,256,512]{2,1,0:T(8,128)(2,1)} %collective-permute-done, bf16[10,256,512]{2,1,0:T(8,128)(2,1)} %convert_element_type.37, ...), kind=kOutput, calls=%fused_computation.28 | convolution fusion | flops 5420351488 | bytes 15204352 | tf_op jit(solution)/shard_map/zyx,xci->czyi/dot_general | solution.py:94
  146.8 6.7 %all-to-all-start = ((bf16[8,10,256,64]{2,3,1,0:T(8,128)(2,1)}), bf16[8,10,256,64]{2,3,1,0:T(8,128)(2,1)}, u32[]{:S(2)}, u32[]{:S(2)}) async-start(bf16[8,10,256,64]{2,3,1,0:T(8,128)(2,1)} %convert_bitcast_fusion.1), calls=%async_computation | async-start | bytes 5242880 | tf_op jit(solution)/shard_map/all_to_all | solution.py:100
  154.8 8.3 %slice.204 = bf16[2048,2048]{1,0:T(8,128)(2,1)} slice(bf16[2048,2176]{1,0:T(8,128)(2,1)} %all-gather.4.cloned.1.call-done), slice={[0:2048], [0:2048]} | slice | bytes 16777216 | tf_op jit(solution)/shard_map/slice | solution.py:112
  163.1 10.4 %copy.270 = bf16[256,8,8,256]{3,2,1,0:T(8,128)(2,1)} copy(bf16[256,8,8,256]{3,1,2,0:T(8,128)(2,1)} %bitcast.101) | data formatting | bytes 16777216
  176.2 65.1 %all-to-all-done = bf16[8,10,256,64]{2,3,1,0:T(8,128)(2,1)} async-done(((bf16[8,10,256,64]{2,3,1,0:T(8,128)(2,1)}), bf16[8,10,256,64]{2,3,1,0:T(8,128)(2,1)}, u32[]{:S(2)}, u32[]{:S(2)}) %all-to-all-start) | async-done | bytes 2621472 | tf_op jit(solution)/shard_map/all_to_all | solution.py:100
  241.3 18.7 %fusion.16.rhs_ref = f32[10,2048,64]{2,1,0:T(8,128)} fusion(bf16[8,10,256,64]{2,3,1,0:T(8,128)(2,1)} %all-to-all-done, bf16[2048,8,256,1]{2,1,0,3:T(8,128)(2,1)} %bitcast.103), kind=kOutput, calls=%fused_computation.26 | convolution fusion | flops 5368709120 | bytes 16252928 | tf_op jit(solution)/shard_map/jsy,szyi->zji/dot_general | solution.py:110
  260.0 10.8 %shard_map.131 = bf16[10,2048,64]{2,1,0:T(8,128)(2,1)} custom-call(f32[9]{0:T(128)} %coupling_ref.1, f32[10]{0:T(128)} %shift_ref.1, f32[2048,1]{1,0:T(8,128)} %fusion.30.ly_ref, f32[1,64]{1,0:T(1,128)} %dynamic-slice_bitcast_fusion.lx_ref, f32[10,2048,64]{2,1,0:T(8,128)} %fusion.16.rhs_ref), custom_call_target="tpu_custom_call" | custom-call | tf_op jit(solution)/shard_map/pallas_call | solution.py:57
  270.8 15.0 %convert_bitcast_fusion = bf16[8,10,256,64]{2,3,0,1:T(8,128)(2,1)S(1)} fusion(bf16[8,256,2048,1]{2,1,0,3:T(8,128)(2,1)} %bitcast.109, bf16[10,2048,64]{2,1,0:T(8,128)(2,1)} %shard_map.131), kind=kOutput, calls=%fused_computation.27 | convolution fusion | flops 5370019840 | bytes 13631488 | tf_op jit(solution)/shard_map/syj,zji->szyi/dot_general | solution.py:120
  286.1 62.4 %all_to_all.10 = bf16[8,10,256,64]{2,3,1,0:T(8,128)(2,1)S(1)} all-to-all(bf16[8,10,256,64]{2,3,1,0:T(8,128)(2,1)S(1)} %copy.250), channel_id=1, replica_groups=mesh['px'=4,'py'=8] {'py'}, dimensions={0} | all-to-all | bytes 5242880 | tf_op jit(solution)/shard_map/all_to_all | solution.py:126
  350.3 4.4 copy.252
  355.4 6.3 %select_select_fusion = f32[10,256,512]{2,1,0:T(8,128)S(1)} fusion(s32[10,256,512]{2,1,0:T(8,128)} %param.27, f32[]{:T(128)} %bitcast.24, f32[]{:T(128)} %bitcast.23, f32[]{:T(128)} %bitcast.22, f32[]{:T(128)} %bitcast.21), kind=kLoop, calls=%fused_computation.24 | loop fusion | flops 10485760 | bytes 10485776 | tf_op jit(solution)/shard_map/jit(_where)/select_n | solution.py:137
  361.8 4.0 slice.205
  366.4 3.1 slice.218
  369.5 3.0 slice_reduce_fusion
  372.4 8.3 %slice_bitcast_fusion = (s32[10,256,512]{2,1,0:T(8,128)}, s32[10,256,512]{2,1,0:T(8,128)S(1)}) fusion(s32[2,10,256,512]{3,2,1,0:T(8,128)} %param.28), kind=kLoop, calls=%fused_computation.23 | loop fusion | bytes 20971520 | tf_op jit(solution)/shard_map/squeeze | solution.py:139
  384.5 74.5 %all-gather.8.cloned.1.call-done = bf16[10,256,2048]{2,1,0:T(8,128)(2,1)} async-done(((bf16[10,256,512]{2,1,0:T(8,128)(2,1)}), bf16[10,256,2048]{2,1,0:T(8,128)(2,1)}) %all-gather.8.cloned.1.call-update) | async-done | bytes 10485776 | tf_op jit(solution)/shard_map/all_gather | solution.py:130
  459.0 8.6 %fusion.25 = f32[10,256,512]{2,1,0:T(8,128)S(1)} fusion(bf16[10,256,2048]{2,1,0:T(8,128)(2,1)} %all-gather.8.cloned.1.call-done, bf16[2048,512]{1,0:T(8,128)(2,1)S(1)} %copy-done), kind=kOutput, calls=%fused_computation.36 | convolution fusion | flops 5368709120 | bytes 17825792 | tf_op jit(solution)/shard_map/zyi,ix->zyx/dot_general | solution.py:128
  468.8 3.7 slice.209
  472.5 3.0 slice.222
  476.2 3.7 collective-permute-start.4
  481.3 4.0 collective-permute-start.6
  493.8 3.2 collective-permute-start.5
  497.0 2.8 multiply_select_fusion
  499.9 16.2 %fusion.13 = (f32[10,256,512]{2,1,0:T(8,128)S(1)}, f32[10,256,512]{2,1,0:T(8,128)S(1)}) fusion(f32[10,1,512]{2,1,0:T(1,128)S(1)} %get-tuple-element.54, f32[10,255,512]{2,1,0:T(8,128)} %slice.218, f32[10,256,512]{2,1,0:T(8,128)S(1)} %copy-done.2, f32[10,1,512]{2,1,0:T(1,128)S(1)} %get-tuple-element.53, f32[10,255,512]{2,1,0:T(8,128)} %slice.222, ...), kind=kLoop, calls=%fused_computation.18 | loop fusion | flops 28835840 | bytes 52429584 | tf_op jit(solution)/shard_map/jit(_where)/select_n | solution.py:157
  516.1 4.5 fusion.11
  (75 shorter events, 35.3 us)
Async XLA Ops:
  7.2 451.9 %copy-start = (bf16[2048,512]{1,0:T(8,128)(2,1)S(1)}, bf16[2048,512]{1,0:T(8,128)(2,1)}, u32[]{:S(2)}) copy-start(bf16[2048,512]{1,0:T(8,128)(2,1)} %param.26) | copy-start | bytes 6291460
  7.2 147.6 %all-gather.4.cloned.1.call-start = ((), (), s32[]{:S(2)}) async-start(), calls=%async_computation.2 | async-start | bytes 10027008 | tf_op jit(solution)/shard_map/all_gather | solution.py:108
  15.8 255.1 %all-gather.6.cloned.1.call-start = ((), (), s32[]{:S(2)}) async-start(), calls=%async_computation.3 | async-start | bytes 9437184 | tf_op jit(solution)/shard_map/all_gather | solution.py:122
  20.9 58.9 %collective-permute-start = (bf16[10,256,512]{2,1,0:T(8,128)(2,1)}, bf16[10,256,512]{2,1,0:T(8,128)(2,1)}, u32[]{:S(2)}, u32[]{:S(2)}) collective-permute-start(bf16[10,256,512]{2,1,0:T(8,128)(2,1)} %convert_element_type.37), channel_id=1, source_target_pairs={{0,8},{8,0},{16,24},{24,16},{1,9},{9,1},{17,25},{25,17},{2,10},{10... | collective-permute-start | bytes 7864328 | tf_op jit(solution)/shard_map/ppermute | solution.py:13
  22.9 57.7 %collective-permute-start.1 = (bf16[10,256,512]{2,1,0:T(8,128)(2,1)}, bf16[10,256,512]{2,1,0:T(8,128)(2,1)}, u32[]{:S(2)}, u32[]{:S(2)}) collective-permute-start(bf16[10,256,512]{2,1,0:T(8,128)(2,1)} %convert_element_type.37), channel_id=1, source_target_pairs={{0,16},{8,24},{16,0},{24,8},{1,17},{9,25},{17,1},{25,9},{2,18},{10... | collective-permute-start | bytes 7864328 | tf_op jit(solution)/shard_map/ppermute | solution.py:13
  24.2 112.8 %collective-permute-start.2 = (bf16[10,256,512]{2,1,0:T(8,128)(2,1)}, bf16[10,256,512]{2,1,0:T(8,128)(2,1)}, u32[]{:S(2)}, u32[]{:S(2)}) collective-permute-start(bf16[10,256,512]{2,1,0:T(8,128)(2,1)} %convert_element_type.37), channel_id=1, source_target_pairs={{0,24},{8,16},{16,8},{24,0},{1,25},{9,17},{17,9},{25,1},{2,26},{10... | collective-permute-start | bytes 7864328 | tf_op jit(solution)/shard_map/ppermute | solution.py:13
  146.8 94.5 %all-to-all-start = ((bf16[8,10,256,64]{2,3,1,0:T(8,128)(2,1)}), bf16[8,10,256,64]{2,3,1,0:T(8,128)(2,1)}, u32[]{:S(2)}, u32[]{:S(2)}) async-start(bf16[8,10,256,64]{2,3,1,0:T(8,128)(2,1)} %convert_bitcast_fusion.1), calls=%async_computation | async-start | bytes 5242880 | tf_op jit(solution)/shard_map/all_to_all | solution.py:100
  153.5 305.6 %all-gather.8.cloned.1.call-start = ((), (), s32[]{:S(2)}) async-start(), calls=%async_computation.4 | async-start | bytes 13107200 | tf_op jit(solution)/shard_map/all_gather | solution.py:130
  350.3 4.4 copy-start.5
  361.8 4.6 copy-start.3
  467.6 4.9 copy-start.1
  476.2 11.1 %collective-permute-start.4 = (f32[3,10,256,1]{2,0,1,3:T(4,128)}, f32[3,10,256,1]{2,0,1,3:T(4,128)}, u32[]{:S(2)}, u32[]{:S(2)}) collective-permute-start(f32[3,10,256,1]{2,0,1,3:T(4,128)} %pad_maximum_fusion.2), channel_id=1, source_target_pairs={{0,8},{8,16},{16,24},{1,9},{9,17},{17,25},{2,10},{10,18},{18,26},{... | collective-permute-start | bytes 92168 | tf_op jit(solution)/shard_map/ppermute | solution.py:149
  479.9 5.3 %collective-permute-start.3 = (f32[2,10,256,1]{2,0,1,3:T(2,128)S(1)}, f32[2,10,256,1]{2,0,1,3:T(2,128)S(1)}, u32[]{:S(2)}, u32[]{:S(2)}) collective-permute-start(f32[2,10,256,1]{2,0,1,3:T(2,128)S(1)} %pad_maximum_fusion.4), channel_id=1, source_target_pairs={{8,0},{16,8},{24,16},{9,1},{17,9},{25,17},{10,2},{18,10},{26,18},{... | collective-permute-start | bytes 61448 | tf_op jit(solution)/shard_map/ppermute | solution.py:148
  481.3 10.9 %collective-permute-start.6 = (f32[3,10,1,512]{3,2,1,0:T(1,128)S(1)}, f32[3,10,1,512]{3,2,1,0:T(1,128)S(1)}, u32[]{:S(2)}, u32[]{:S(2)}) collective-permute-start(f32[3,10,1,512]{3,2,1,0:T(1,128)S(1)} %pad_maximum_fusion.1), channel_id=1, source_target_pairs={{0,1},{1,2},{2,3},{3,4},{4,5},{5,6},{6,7},{8,9},{9,10},{10,11},{11... | collective-permute-start | bytes 184328 | tf_op jit(solution)/shard_map/ppermute | solution.py:149
  491.2 8.7 %copy-start.2 = (f32[10,256,512]{2,1,0:T(8,128)S(1)}, f32[10,256,512]{2,1,0:T(8,128)}, u32[]{:S(2)}) copy-start(f32[10,256,512]{2,1,0:T(8,128)} %copy-done.1) | copy-start | bytes 15728644
  491.2 8.7 %copy-start.4 = (f32[10,256,1]{2,1,0:T(8,128)S(1)}, f32[10,256,1]{2,1,0:T(8,128)}, u32[]{:S(2)}) copy-start(f32[10,256,1]{2,1,0:T(8,128)} %copy.254) | copy-start | bytes 30724
  493.8 6.0 %collective-permute-start.5 = (f32[2,10,1,512]{3,2,1,0:T(1,128)S(1)}, f32[2,10,1,512]{3,2,1,0:T(1,128)S(1)}, u32[]{:S(2)}, u32[]{:S(2)}) collective-permute-start(f32[2,10,1,512]{3,2,1,0:T(1,128)S(1)} %pad_maximum_fusion.3), channel_id=1, source_target_pairs={{1,0},{2,1},{3,2},{4,3},{5,4},{6,5},{7,6},{9,8},{10,9},{11,10},{12... | collective-permute-start | bytes 122888 | tf_op jit(solution)/shard_map/ppermute | solution.py:148
Sparse Core Ops, SparseCore 0:
  15.9 88.8 all-gather.3
  106.4 107.9 all-gather.5
  354.9 104.1 all-gather.7

commit v6 on v5

--- a/solution.py
+++ b/solution.py
@@ -117,50 +117,60 @@
     got = carried[:, columns:columns + 3].astype(jnp.float32)
     all_y = got[:, 0] + (got[:, 1] + got[:, 2])
     solved = thomas_solve(spectral, own_x, all_y, coupling, layer_shift)
-    back_pencil = jnp.einsum(
-        "syj,zji->szyi",
-        lax.all_gather(right_y, "py", axis=0, tiled=True).reshape(count_y, height, -1),
-        solved,
-        preferred_element_type=jnp.float32,
-    ).astype(jnp.bfloat16)
-    back_y = lax.all_to_all(back_pencil, "py", 0, 0, tiled=True)
-    back_y = jnp.moveaxis(back_y, 0, 2).reshape(layers, height, -1)
-    correction = jnp.einsum(
-        "zyi,ix->zyx",
-        lax.all_gather(back_y, "px", axis=2, tiled=True),
-        right_x,
-        preferred_element_type=jnp.float32,
-    )
+    right_all = lax.all_gather(right_y, "py", axis=0, tiled=True).reshape(count_y, height, -1)
 
     mobility = jnp.zeros(regime_code.shape, jnp.float32)
     for regime in range(mobility_table.shape[0]):
         mobility = jnp.where(regime_code == regime, mobility_table[regime], mobility)
-    flag_x = upwind_flag[0]
-    flag_y = upwind_flag[1]
 
-    def net(axis, dim, flag, at, count):
-        forward = [(i, i + 1) for i in range(count - 1)]
-        backward = [(i + 1, i) for i in range(count - 1)]
-        first = lambda a: lax.slice_in_dim(a, 0, 1, axis=dim)
-        last = lambda a: lax.slice_in_dim(a, a.shape[dim] - 1, None, axis=dim)
-        rest = lambda a: lax.slice_in_dim(a, 1, None, axis=dim)
-        head = lambda a: lax.slice_in_dim(a, 0, a.shape[dim] - 1, axis=dim)
-        high = lax.ppermute(jnp.stack([first(correction), first(mobility)]), axis, backward)
-        low = lax.ppermute(
-            jnp.stack([last(correction), last(mobility), last(flag).astype(jnp.float32)]), axis, forward
+    def back_half(solved, mobility, flag_x, flag_y):
+        back_pencil = jnp.einsum(
+            "syj,zji->szyi",
+            right_all,
+            solved,
+            preferred_element_type=jnp.float32,
+        ).astype(jnp.bfloat16)
+        back_y = lax.all_to_all(back_pencil, "py", 0, 0, tiled=True)
+        back_y = jnp.moveaxis(back_y, 0, 2).reshape(solved.shape[0], height, -1)
+        correction = jnp.einsum(
+            "zyi,ix->zyx",
+            lax.all_gather(back_y, "px", axis=2, tiled=True),
+            right_x,
+            preferred_element_type=jnp.float32,
         )
-        press_next = jnp.concatenate([rest(correction), high[0]], axis=dim)
-        mobil_next = jnp.concatenate([rest(mobility), high[1]], axis=dim)
-        flux_high = jnp.where(flag == 1, mobility, mobil_next) * (correction - press_next)
-        place = lax.broadcasted_iota(jnp.int32, correction.shape, dim)
-        edge = (at == count - 1) & (place == correction.shape[dim] - 1)
-        flux_high = jnp.where(edge, 0.0, flux_high)
-        flux_edge = jnp.where(low[2] > 0.5, low[1], first(mobility)) * (low[0] - first(correction))
-        flux_edge = jnp.where(at == 0, 0.0, flux_edge)
-        flux_low = jnp.concatenate([flux_edge, head(flux_high)], axis=dim)
-        return flux_high - flux_low
 
-    balance = net("px", 2, flag_x, at_x, count_x) + net("py", 1, flag_y, at_y, count_y)
+        def net(axis, dim, flag, at, count):
+            forward = [(i, i + 1) for i in range(count - 1)]
+            backward = [(i + 1, i) for i in range(count - 1)]
+            first = lambda a: lax.slice_in_dim(a, 0, 1, axis=dim)
+            last = lambda a: lax.slice_in_dim(a, a.shape[dim] - 1, None, axis=dim)
+            rest = lambda a: lax.slice_in_dim(a, 1, None, axis=dim)
+            head = lambda a: lax.slice_in_dim(a, 0, a.shape[dim] - 1, axis=dim)
+            high = lax.ppermute(jnp.stack([first(correction), first(mobility)]), axis, backward)
+            low = lax.ppermute(
+                jnp.stack([last(correction), last(mobility), last(flag).astype(jnp.float32)]), axis, forward
+            )
+            press_next = jnp.concatenate([rest(correction), high[0]], axis=dim)
+            mobil_next = jnp.concatenate([rest(mobility), high[1]], axis=dim)
+            flux_high = jnp.where(flag == 1, mobility, mobil_next) * (correction - press_next)
+            place = lax.broadcasted_iota(jnp.int32, correction.shape, dim)
+            edge = (at == count - 1) & (place == correction.shape[dim] - 1)
+            flux_high = jnp.where(edge, 0.0, flux_high)
+            flux_edge = jnp.where(low[2] > 0.5, low[1], first(mobility)) * (low[0] - first(correction))
+            flux_edge = jnp.where(at == 0, 0.0, flux_edge)
+            flux_low = jnp.concatenate([flux_edge, head(flux_high)], axis=dim)
+            return flux_high - flux_low
+
+        balance = net("px", 2, flag_x, at_x, count_x) + net("py", 1, flag_y, at_y, count_y)
+        return correction, balance
+
+    split = layers // 2
+    parts = [
+        back_half(solved[lo:hi], mobility[lo:hi], upwind_flag[0, lo:hi], upwind_flag[1, lo:hi])
+        for lo, hi in ((0, split), (split, layers))
+    ]
+    correction = jnp.concatenate([p[0] for p in parts])
+    balance = jnp.concatenate([p[1] for p in parts])
     return (correction, balance)
 
 

time: 537 us -> 556 us (1.035)
  waiting for transfers between devices: 245 us -> 172 us
  local copies, waits for them, and re-layouts: 69.9 us -> 117 us
  blocking collectives: 62.4 us -> 77.2 us
  other arithmetic: 50.8 us -> 64 us
  starting transfers between devices: 22.2 us -> 31.1 us
  matrix products: 52.1 us -> 58.9 us
    all_gather x1 -> x2, waiting for transfers between devices: 74.5 us -> 1.55 us  [back_half(): lax.all_gather(back_y, 'px', axis=2, tiled=True)]
    unnamed x13 -> x55, local copies, waits for them, and re-layouts: 11.1 us -> 39.8 us
    all_to_all x1 -> x2, blocking collectives: 62.4 us -> 77.2 us  [back_half(): back_y = lax.all_to_all(back_pencil, 'py', 0, 0, tiled=True)]
    slice x1, local copies, waits for them, and re-layouts: 0.01 us -> 8.83 us  [shards(): upwind_flag[1, lo:hi]]
    squeeze x1 -> x0, local copies, waits for them, and re-layouts: 8.29 us -> none  [shards(): flag_y = upwind_flag[1]]
    dot_general x2 -> x4, matrix products: 23.5 us -> 31.3 us  [the longest x2 19.6 us: back_half(): jnp.einsum('syj,zji->szyi', right_all, solved, preferred_element_type=jnp...]
    dot_general x0 -> x2, local copies, waits for them, and re-layouts: none -> 6.59 us  [back_half(): jnp.einsum('zyi,ix->zyx', lax.all_gather(back_y, 'px', axis=2, tiled=True...]
    concatenate x0 -> x2, other arithmetic: none -> 5.9 us  [the longest x1 2.96 us: shards(): balance = jnp.concatenate([p[1] for p in parts])]
  transfers between devices with their start and end apart: 11 -> 16, of which waited for: 5 -> 6; matrix products, arithmetic and copies ran while one was open for 19% -> 29% of each run, Pallas kernels for 2% -> 2%
where the time goes in v6:
time: 556 us; the launch traced here: 546 us
  waiting for transfers between devices  172 us (31%)
  local copies, waits for them, and re-layouts  117 us (21%)
  blocking collectives  77.2 us (14%)
  other arithmetic  64 us (12%)
  matrix products  58.9 us (11%)
  starting transfers between devices  31.1 us (6%)
  between operations  14.8 us (3%)
  Pallas kernels  10.8 us (2%)
    ppermute x3, waiting for transfers between devices, exchange(): parts.append(lax.ppermute(block, axis, [(s, s ^ k) for s in range(count)]))  104 us
    all_to_all x2, blocking collectives, back_half(): back_y = lax.all_to_all(back_pencil, 'py', 0, 0, tiled=True)  77.2 us
    all_to_all x1, waiting for transfers between devices, shards(): pencil = lax.all_to_all(spectral_x, 'py', 0, 0, tiled=True)  64.3 us
    unnamed x55, local copies, waits for them, and re-layouts  39.8 us
    dot_general x2, matrix products, back_half(): jnp.einsum('syj,zji->szyi', right_all, solved, preferred_element_type=jnp...  19.6 us
    slice x6, local copies, waits for them, and re-layouts, net(): rest = lambda a: lax.slice_in_dim(a, 1, None, axis=dim)  19.2 us
    dot_general x1, matrix products, shards(): jnp.einsum('jsy,szyi->zji', carried[:, :columns].reshape(-1, count_y, hei...  18.8 us
    select_n x2, other arithmetic, net(): flux_high = jnp.where(edge, 0.0, flux_high)  15 us
  transfers between devices with their start and end apart: 16, of which 6 were waited for; matrix products, arithmetic and copies ran while one was open for 29% of the time, Pallas kernels for 2%

profile of v6, /device:TPU:1, one launch (start us, length us, event | category | flops | bytes accessed | tf_op | source)
XLA Modules:
  0.0 545.9 jit_solution(1907889773731763104)
XLA Ops:
  16.3 4.3 convert_element_type.49
  32.2 47.4 %collective-permute-done = bf16[10,256,512]{2,1,0:T(8,128)(2,1)} collective-permute-done((bf16[10,256,512]{2,1,0:T(8,128)(2,1)}, bf16[10,256,512]{2,1,0:T(8,128)(2,1)}, u32[]{:S(2)}, u32[]{:S(2)}) %collective-permute-start) | collective-permute-done | bytes 2621472 | tf_op jit(solution)/shard_map/ppermute | solution.py:13
  80.5 56.3 %collective-permute-done.2 = bf16[10,256,512]{2,1,0:T(8,128)(2,1)} collective-permute-done((bf16[10,256,512]{2,1,0:T(8,128)(2,1)}, bf16[10,256,512]{2,1,0:T(8,128)(2,1)}, u32[]{:S(2)}, u32[]{:S(2)}) %collective-permute-start.2) | collective-permute-done | bytes 2621472 | tf_op jit(solution)/shard_map/ppermute | solution.py:13
  136.7 8.8 %convert_bitcast_fusion = bf16[8,10,256,64]{2,3,0,1:T(8,128)(2,1)S(1)} fusion(bf16[10,256,512]{2,1,0:T(8,128)(2,1)} %collective-permute-done.2, bf16[10,256,512]{2,1,0:T(8,128)(2,1)} %collective-permute-done.1, bf16[10,256,512]{2,1,0:T(8,128)(2,1)} %collective-permute-done, bf16[10,256,512]{2,1,0:T(8,128)(2,1)} %convert_element_type.49, ...), kind=kOutput, calls=%fused_computation.40 | convolution fusion | flops 5420351488 | bytes 15204352 | tf_op jit(solution)/shard_map/zyx,xci->czyi/dot_general | solution.py:94
  147.2 6.7 %all-to-all-start = ((bf16[8,10,256,64]{2,3,1,0:T(8,128)(2,1)}), bf16[8,10,256,64]{2,3,1,0:T(8,128)(2,1)}, u32[]{:S(2)}, u32[]{:S(2)}) async-start(bf16[8,10,256,64]{2,3,1,0:T(8,128)(2,1)} %copy.2197), calls=%async_computation | async-start | bytes 5242880 | tf_op jit(solution)/shard_map/all_to_all | solution.py:100
  155.3 8.4 %slice.348 = bf16[2048,2048]{1,0:T(8,128)(2,1)} slice(bf16[2048,2176]{1,0:T(8,128)(2,1)} %all-gather.5.cloned.1.call-done), slice={[0:2048], [0:2048]} | slice | bytes 16777216 | tf_op jit(solution)/shard_map/slice | solution.py:112
  163.7 10.4 %copy.2261 = bf16[256,8,8,256]{3,2,1,0:T(8,128)(2,1)} copy(bf16[256,8,8,256]{3,1,2,0:T(8,128)(2,1)} %bitcast.182) | data formatting | bytes 16777216
  176.8 64.3 %all-to-all-done = bf16[8,10,256,64]{2,3,1,0:T(8,128)(2,1)} async-done(((bf16[8,10,256,64]{2,3,1,0:T(8,128)(2,1)}), bf16[8,10,256,64]{2,3,1,0:T(8,128)(2,1)}, u32[]{:S(2)}, u32[]{:S(2)}) %all-to-all-start) | async-done | bytes 2621472 | tf_op jit(solution)/shard_map/all_to_all | solution.py:100
  241.2 18.8 %fusion.9.rhs_ref = f32[10,2048,64]{2,1,0:T(8,128)} fusion(bf16[8,10,256,64]{2,3,1,0:T(8,128)(2,1)} %all-to-all-done, bf16[2048,8,256,1]{2,1,0,3:T(8,128)(2,1)} %bitcast.191), kind=kOutput, calls=%fused_computation.13 | convolution fusion | flops 5368709120 | bytes 16252928 | tf_op jit(solution)/shard_map/jsy,szyi->zji/dot_general | solution.py:110
  260.0 10.8 %shard_map.131 = bf16[10,2048,64]{2,1,0:T(8,128)(2,1)} custom-call(f32[9]{0:T(128)} %coupling_ref.1, f32[10]{0:T(128)} %shift_ref.1, f32[2048,1]{1,0:T(8,128)} %fusion.40.ly_ref, f32[1,64]{1,0:T(1,128)} %dynamic-slice_bitcast_fusion.lx_ref, f32[10,2048,64]{2,1,0:T(8,128)} %fusion.9.rhs_ref), custom_call_target="tpu_custom_call" | custom-call | tf_op jit(solution)/shard_map/pallas_call | solution.py:57
  270.9 9.8 %fusion.37 = bf16[8,5,256,64]{2,3,0,1:T(8,128)(2,1)S(1)} fusion(bf16[8,256,2048,1]{2,1,0,3:T(8,128)(2,1)} %bitcast.199, bf16[10,2048,64]{2,1,0:T(8,128)(2,1)} %shard_map.131), kind=kOutput, calls=%fused_computation.55 | convolution fusion | flops 2685009920 | bytes 12320768 | tf_op jit(solution)/shard_map/syj,zji->szyi/dot_general | solution.py:127
  280.7 34.0 %all_to_all.15 = bf16[8,5,256,64]{2,3,1,0:T(8,128)(2,1)S(1)} all-to-all(bf16[8,5,256,64]{2,3,1,0:T(8,128)(2,1)S(1)} %copy.2201), channel_id=1, replica_groups=mesh['px'=4,'py'=8] {'py'}, dimensions={0} | all-to-all | bytes 2621440 | tf_op jit(solution)/shard_map/all_to_all | solution.py:133
  316.5 9.8 %fusion.36 = bf16[8,5,256,64]{2,3,0,1:T(8,128)(2,1)S(1)} fusion(bf16[8,256,2048,1]{2,1,0,3:T(8,128)(2,1)} %bitcast.200, bf16[10,2048,64]{2,1,0:T(8,128)(2,1)} %shard_map.131), kind=kOutput, calls=%fused_computation.54 | convolution fusion | flops 2685009920 | bytes 12320768 | tf_op jit(solution)/shard_map/syj,zji->szyi/dot_general | solution.py:127
  326.4 43.2 %all_to_all.16 = bf16[8,5,256,64]{2,3,1,0:T(8,128)(2,1)S(1)} all-to-all(bf16[8,5,256,64]{2,3,1,0:T(8,128)(2,1)S(1)} %copy.2205), channel_id=1, replica_groups=mesh['px'=4,'py'=8] {'py'}, dimensions={0} | all-to-all | bytes 2621440 | tf_op jit(solution)/shard_map/all_to_all | solution.py:133
  371.4 5.9 %copy.2209 = s32[10,256,512]{1,2,0:T(8,128)} copy(s32[10,256,512]{2,1,0:T(8,128)} %param.27) | data formatting | bytes 10485760 | tf_op args[9]
  377.3 8.8 %fusion.51 = (s32[1,5,256,512]{3,2,1,0:T(8,128)}, s32[1,5,256,512]{3,2,1,0:T(8,128)}, s32[1,5,256,512]{3,2,1,0:T(8,128)}, s32[1,5,256,512]{3,2,1,0:T(8,128)}) fusion(s32[2,10,256,512]{3,2,1,0:T(8,128)} %param.28), kind=kLoop, calls=%fused_computation.146 | loop fusion | bytes 20971520 | tf_op jit(solution)/shard_map/slice | solution.py:169
  386.1 3.6 copy.2257
  389.7 3.3 copy.2258
  393.0 3.3 copy.2260
  396.9 6.3 %select_select_fusion = f32[10,256,512]{1,2,0:T(8,128)S(1)} fusion(s32[10,256,512]{1,2,0:T(8,128)} %copy.2209, f32[]{:T(128)} %bitcast.29, f32[]{:T(128)} %bitcast.28, f32[]{:T(128)} %bitcast.27, f32[]{:T(128)} %bitcast.26), kind=kLoop, calls=%fused_computation.12 | loop fusion | flops 10485760 | bytes 10485776 | tf_op jit(solution)/shard_map/jit(_where)/select_n | solution.py:124
  416.7 6.4 %fusion.52 = (f32[5,255,512]{1,2,0:T(8,128)}, f32[5,255,512]{1,2,0:T(8,128)}) fusion(f32[10,256,512]{1,2,0:T(8,128)} %copy-done.1), kind=kLoop, calls=%fused_computation.147 | loop fusion | bytes 10444800 | tf_op jit(solution)/shard_map/slice | solution.py:147
  425.9 6.9 %fusion.32 = f32[5,256,512]{2,1,0:T(8,128)} fusion(bf16[5,256,2048]{2,1,0:T(8,128)(2,1)} %all-gather.9.cloned.1.call-done, bf16[2048,512]{1,0:T(8,128)(2,1)S(1)} %copy-done), kind=kOutput, calls=%fused_computation.50 | convolution fusion | flops 2684354560 | bytes 9961472 | tf_op jit(solution)/shard_map/zyi,ix->zyx/dot_general | solution.py:135
  432.8 3.4 copy.2213
  440.1 4.8 fusion.30
  449.7 3.6 slice.356
  466.9 4.0 collective-permute-start.6
  476.2 4.6 collective-permute-start.8
  486.5 5.6 %multiply_select_fusion.1 = (f32[5,1,512]{1,2,0:T(8,128)}, f32[5,1,512]{1,2,0:T(8,128)}, f32[5,512]{1,0:T(8,128)S(1)}, f32[5,512]{1,0:T(8,128)S(1)}) fusion(f32[5,1,512]{1,2,0:T(8,128)} %copy.2227, f32[5,1,512]{1,2,0:T(8,128)S(1)} %copy.2226, pred[5,512]{1,0:T(8,128)(4,1)S(1)} %compare_reduce_fusion.1, f32[10,256,512]{1,2,0:T(8,128)} %copy-done.1, ...), kind=kLoop, calls=%fused_computation.63 | loop fusion | flops 20480 | bytes 128001 | tf_op jit(solution)/shard_map/jit(_where)/select_n | solution.py:160
  506.9 9.7 %fusion.18 = (f32[5,256,512]{1,2,0:T(8,128)S(1)}, f32[5,256,512]{1,2,0:T(8,128)S(1)}) fusion(f32[5,1,512]{1,2,0:T(8,128)} %copy.2219, f32[5,255,512]{1,2,0:T(8,128)} %get-tuple-element.114, f32[5,256,512]{1,2,0:T(8,128)} %copy.2213, f32[5,1,512]{1,2,0:T(8,128)} %copy.2221, f32[5,255,512]{1,2,0:T(8,128)} %slice.369, f32[10,256,512]{1,2,0:T(8,128)} %copy-done.1, ...), kind=kLoop, calls=%fused_computation.26 | loop fusion | flops 9175040 | bytes 26215168 | tf_op jit(solution)/shard_map/jit(_where)/select_n | solution.py:158
  516.7 3.9 fusion.16
  522.4 5.4 fusion.23
  533.0 5.9 %copy.2244 = f32[10,256,512]{2,1,0:T(8,128)} copy(f32[10,256,512]{1,2,0:T(8,128)} %pad_maximum_fusion.1) | data formatting | bytes 10485760
  (165 shorter events, 102.7 us)
Async XLA Ops:
  7.2 418.8 %copy-start = (bf16[2048,512]{1,0:T(8,128)(2,1)S(1)}, bf16[2048,512]{1,0:T(8,128)(2,1)}, u32[]{:S(2)}) copy-start(bf16[2048,512]{1,0:T(8,128)(2,1)} %param.26) | copy-start | bytes 6291460
  7.2 148.1 %all-gather.5.cloned.1.call-start = ((), (), s32[]{:S(2)}) async-start(), calls=%async_computation.3 | async-start | bytes 10027008 | tf_op jit(solution)/shard_map/all_gather | solution.py:108
  15.6 255.3 %all-gather.7.cloned.1.call-start = ((), (), s32[]{:S(2)}) async-start(), calls=%async_computation.4 | async-start | bytes 9437184 | tf_op jit(solution)/shard_map/all_gather | solution.py:120
  20.7 58.9 %collective-permute-start = (bf16[10,256,512]{2,1,0:T(8,128)(2,1)}, bf16[10,256,512]{2,1,0:T(8,128)(2,1)}, u32[]{:S(2)}, u32[]{:S(2)}) collective-permute-start(bf16[10,256,512]{2,1,0:T(8,128)(2,1)} %convert_element_type.49), channel_id=1, source_target_pairs={{0,8},{8,0},{16,24},{24,16},{1,9},{9,1},{17,25},{25,17},{2,10},{10... | collective-permute-start | bytes 7864328 | tf_op jit(solution)/shard_map/ppermute | solution.py:13
  22.7 57.7 %collective-permute-start.1 = (bf16[10,256,512]{2,1,0:T(8,128)(2,1)}, bf16[10,256,512]{2,1,0:T(8,128)(2,1)}, u32[]{:S(2)}, u32[]{:S(2)}) collective-permute-start(bf16[10,256,512]{2,1,0:T(8,128)(2,1)} %convert_element_type.49), channel_id=1, source_target_pairs={{0,16},{8,24},{16,0},{24,8},{1,17},{9,25},{17,1},{25,9},{2,18},{10... | collective-permute-start | bytes 7864328 | tf_op jit(solution)/shard_map/ppermute | solution.py:13
  24.0 112.8 %collective-permute-start.2 = (bf16[10,256,512]{2,1,0:T(8,128)(2,1)}, bf16[10,256,512]{2,1,0:T(8,128)(2,1)}, u32[]{:S(2)}, u32[]{:S(2)}) collective-permute-start(bf16[10,256,512]{2,1,0:T(8,128)(2,1)} %convert_element_type.49), channel_id=1, source_target_pairs={{0,24},{8,16},{16,8},{24,0},{1,25},{9,17},{17,9},{25,1},{2,26},{10... | collective-permute-start | bytes 7864328 | tf_op jit(solution)/shard_map/ppermute | solution.py:13
  147.2 93.9 %all-to-all-start = ((bf16[8,10,256,64]{2,3,1,0:T(8,128)(2,1)}), bf16[8,10,256,64]{2,3,1,0:T(8,128)(2,1)}, u32[]{:S(2)}, u32[]{:S(2)}) async-start(bf16[8,10,256,64]{2,3,1,0:T(8,128)(2,1)} %copy.2197), calls=%async_computation | async-start | bytes 5242880 | tf_op jit(solution)/shard_map/all_to_all | solution.py:100
  153.9 272.0 %all-gather.9.cloned.1.call-start = ((), (), s32[]{:S(2)}) async-start(), calls=%async_computation.5 | async-start | bytes 6553600 | tf_op jit(solution)/shard_map/all_gather | solution.py:137
  316.5 123.7 %all-gather.11.cloned.1.call-start = ((), (), s32[]{:S(2)}) async-start(), calls=%async_computation.6 | async-start | bytes 6553600 | tf_op jit(solution)/shard_map/all_gather | solution.py:137
  412.1 11.1 %slice-start = ((s8[5242880]{0:T(1024)(128)(4,1)}), s8[4194304]{0:T(1024)(128)(4,1)S(1)}, s32[]{:S(2)}) async-start(s8[5242880]{0:T(1024)(128)(4,1)} %bitcast.178), calls=%async_computation.7 | async-start | bytes 8388608
  416.7 6.4 %slice-start.1 = ((s8[5242880]{0:T(1024)(128)(4,1)}), s8[1048576]{0:T(1024)(128)(4,1)S(1)}, s32[]{:S(2)}) async-start(s8[5242880]{0:T(1024)(128)(4,1)} %bitcast.178), calls=%async_computation.8 | async-start | bytes 2097152
  463.8 9.1 %collective-permute-start.4 = (f32[3,5,256,1]{2,0,1,3:T(4,128)S(1)}, f32[3,5,256,1]{2,0,1,3:T(4,128)S(1)}, u32[]{:S(2)}, u32[]{:S(2)}) collective-permute-start(f32[3,5,256,1]{2,0,1,3:T(4,128)S(1)} %pad_maximum_fusion.5), channel_id=1, source_target_pairs={{0,8},{8,16},{16,24},{1,9},{9,17},{17,25},{2,10},{10,18},{18,26},{... | collective-permute-start | bytes 46088 | tf_op jit(solution)/shard_map/ppermute | solution.py:150
  466.9 14.5 %collective-permute-start.6 = (f32[3,5,1,512]{3,2,1,0:T(1,128)S(1)}, f32[3,5,1,512]{3,2,1,0:T(1,128)S(1)}, u32[]{:S(2)}, u32[]{:S(2)}) collective-permute-start(f32[3,5,1,512]{3,2,1,0:T(1,128)S(1)} %pad_maximum_fusion.3), channel_id=1, source_target_pairs={{0,1},{1,2},{2,3},{3,4},{4,5},{5,6},{6,7},{8,9},{9,10},{10,11},{11... | collective-permute-start | bytes 92168 | tf_op jit(solution)/shard_map/ppermute | solution.py:150
  470.9 12.5 %collective-permute-start.10 = (f32[3,5,1,512]{3,2,1,0:T(1,128)S(1)}, f32[3,5,1,512]{3,2,1,0:T(1,128)S(1)}, u32[]{:S(2)}, u32[]{:S(2)}) collective-permute-start(f32[3,5,1,512]{3,2,1,0:T(1,128)S(1)} %pad_maximum_fusion.4), channel_id=1, source_target_pairs={{0,1},{1,2},{2,3},{3,4},{4,5},{5,6},{6,7},{8,9},{9,10},{10,11},{11... | collective-permute-start | bytes 92168 | tf_op jit(solution)/shard_map/ppermute | solution.py:150
  474.3 6.5 %collective-permute-start.3 = (f32[2,5,256,1]{2,0,1,3:T(2,128)S(1)}, f32[2,5,256,1]{2,0,1,3:T(2,128)S(1)}, u32[]{:S(2)}, u32[]{:S(2)}) collective-permute-start(f32[2,5,256,1]{2,0,1,3:T(2,128)S(1)} %pad_maximum_fusion.9), channel_id=1, source_target_pairs={{8,0},{16,8},{24,16},{9,1},{17,9},{25,17},{10,2},{18,10},{26,18},{... | collective-permute-start | bytes 30728 | tf_op jit(solution)/shard_map/ppermute | solution.py:149
  476.2 18.9 %collective-permute-start.8 = (f32[3,5,256,1]{2,0,1,3:T(4,128)}, f32[3,5,256,1]{2,0,1,3:T(4,128)}, u32[]{:S(2)}, u32[]{:S(2)}) collective-permute-start(f32[3,5,256,1]{2,0,1,3:T(4,128)} %pad_maximum_fusion.7), channel_id=1, source_target_pairs={{0,8},{8,16},{16,24},{1,9},{9,17},{17,25},{2,10},{10,18},{18,26},{... | collective-permute-start | bytes 46088 | tf_op jit(solution)/shard_map/ppermute | solution.py:150
  486.5 9.6 %copy-start.15 = (f32[1,5,256,1]{2,0,1,3:T(1,128)S(1)}, f32[1,5,256,1]{2,0,1,3:T(1,128)}, u32[]{:S(2)}) copy-start(f32[1,5,256,1]{2,0,1,3:T(1,128)} %get-tuple-element.118) | copy-start | bytes 15364
  492.2 8.5 %collective-permute-start.5 = (f32[2,5,1,512]{3,0,1,2:T(2,128)S(1)}, f32[2,5,1,512]{3,0,1,2:T(2,128)S(1)}, u32[]{:S(2)}, u32[]{:S(2)}) collective-permute-start(f32[2,5,1,512]{3,0,1,2:T(2,128)S(1)} %pad_maximum_fusion.6), channel_id=1, source_target_pairs={{1,0},{2,1},{3,2},{4,3},{5,4},{6,5},{7,6},{9,8},{10,9},{11,10},{12... | collective-permute-start | bytes 61448 | tf_op jit(solution)/shard_map/ppermute | solution.py:149
  496.1 4.6 collective-permute-start.7
  497.4 6.4 %collective-permute-start.9 = (f32[2,5,1,512]{3,0,1,2:T(2,128)S(1)}, f32[2,5,1,512]{3,0,1,2:T(2,128)S(1)}, u32[]{:S(2)}, u32[]{:S(2)}) collective-permute-start(f32[2,5,1,512]{3,0,1,2:T(2,128)S(1)} %pad_maximum_fusion.8), channel_id=1, source_target_pairs={{1,0},{2,1},{3,2},{4,3},{5,4},{6,5},{7,6},{9,8},{10,9},{11,10},{12... | collective-permute-start | bytes 61448 | tf_op jit(solution)/shard_map/ppermute | solution.py:149
  500.7 6.2 %copy-start.13 = (f32[5,256,1]{1,2,0:T(1,128)S(1)}, f32[5,256,1]{1,2,0:T(1,128)}, u32[]{:S(2)}) copy-start(f32[5,256,1]{1,2,0:T(1,128)} %get-tuple-element.139) | copy-start | bytes 15364
  500.7 6.2 %copy-start.14 = (f32[5,256,1]{1,2,0:T(1,128)S(1)}, f32[5,256,1]{1,2,0:T(1,128)}, u32[]{:S(2)}) copy-start(f32[5,256,1]{1,2,0:T(1,128)} %get-tuple-element.140) | copy-start | bytes 15364
  500.7 6.2 %copy-start.18 = (pred[512]{0:T(512)(128)(4,1)S(1)}, pred[512]{0:T(512)(128)(4,1)}, u32[]{:S(2)}) copy-start(pred[512]{0:T(512)(128)(4,1)} %fusion.47) | copy-start | bytes 1540
  500.7 6.2 %copy-start.19 = (pred[256]{0:T(512)(128)(4,1)S(1)}, pred[256]{0:T(512)(128)(4,1)}, u32[]{:S(2)}) copy-start(pred[256]{0:T(512)(128)(4,1)} %compare_and_fusion) | copy-start | bytes 772
  503.9 16.8 %slice-start.2 = ((s8[5242880]{0:T(1024)(128)(4,1)}), s8[1048576]{0:T(1024)(128)(4,1)S(1)}, s32[]{:S(2)}) async-start(s8[5242880]{0:T(1024)(128)(4,1)} %bitcast.180), calls=%async_computation.9 | async-start | bytes 2097152
  506.9 9.7 %copy-start.16 = (f32[5,256,1]{1,2,0:T(1,128)S(1)}, f32[5,256,1]{1,2,0:T(1,128)}, u32[]{:S(2)}) copy-start(f32[5,256,1]{1,2,0:T(1,128)} %get-tuple-element.116) | copy-start | bytes 15364
  506.9 13.7 %slice-start.3 = ((s8[5242880]{0:T(1024)(128)(4,1)}), s8[4194304]{0:T(1024)(128)(4,1)S(1)}, s32[]{:S(2)}) async-start(s8[5242880]{0:T(1024)(128)(4,1)} %bitcast.180), calls=%async_computation.10 | async-start | bytes 8388608
  516.7 4.0 copy-start.3
  516.7 4.0 copy-start.5
  516.7 4.4 copy-start.9
  516.7 5.4 copy-start.10
  516.7 5.7 %copy-start.12 = (f32[5,1,512]{1,2,0:T(8,128)S(1)}, f32[5,1,512]{1,2,0:T(8,128)}, u32[]{:S(2)}) copy-start(f32[5,1,512]{1,2,0:T(8,128)} %copy.2235) | copy-start | bytes 30724
  (8 other events, 21.2 us)
Sparse Core Ops, SparseCore 0:
  15.7 88.8 all-gather.4
  106.2 107.5 all-gather.6
  316.6 60.4 all-gather.8
  378.8 61.2 all-gather.10

commit v7 on v5

--- a/solution.py
+++ b/solution.py
@@ -123,11 +123,13 @@
         solved,
         preferred_element_type=jnp.float32,
     ).astype(jnp.bfloat16)
-    back_y = lax.all_to_all(back_pencil, "py", 0, 0, tiled=True)
+    spread = jnp.broadcast_to(back_pencil[None], (count_x,) + back_pencil.shape)
+    spread = spread.reshape((count_x * count_y,) + back_pencil.shape[1:])
+    back_y = lax.all_to_all(spread, ("px", "py"), 0, 0, tiled=True)
     back_y = jnp.moveaxis(back_y, 0, 2).reshape(layers, height, -1)
     correction = jnp.einsum(
         "zyi,ix->zyx",
-        lax.all_gather(back_y, "px", axis=2, tiled=True),
+        back_y,
         right_x,
         preferred_element_type=jnp.float32,
     )

time: 537 us -> 612 us (1.14)
  waiting for transfers between devices: 245 us -> 373 us
  blocking collectives: 62.4 us -> 0 us
  local copies, waits for them, and re-layouts: 69.9 us -> 81.6 us
    all_to_all x0 -> x1, waiting for transfers between devices: none -> 202 us  [shards(): back_y = lax.all_to_all(spread, ('px', 'py'), 0, 0, tiled=True)]
    all_gather x1 -> x0, waiting for transfers between devices: 74.5 us -> none  [shards(): lax.all_gather(back_y, 'px', axis=2, tiled=True)]
    all_to_all x1 -> x0, blocking collectives: 62.4 us -> none  [shards(): back_y = lax.all_to_all(back_pencil, 'py', 0, 0, tiled=True)]
    all_to_all x1, local copies, waits for them, and re-layouts: 1.79 us -> 10 us  [shards(): back_y = lax.all_to_all(spread, ('px', 'py'), 0, 0, tiled=True)]
    broadcast_in_dim x0 -> x1, local copies, waits for them, and re-layouts: none -> 6.99 us  [shards(): spread = jnp.broadcast_to(back_pencil[None], (count_x,) + back_pencil.shape)]
  transfers between devices with their start and end apart: 11 -> 11, of which waited for: 5 -> 7; matrix products, arithmetic and copies ran while one was open for 19% -> 17% of each run, Pallas kernels for 2% -> 2%
where the time goes in v7:
time: 612 us; the launch traced here: 607 us
  waiting for transfers between devices  373 us (61%)
  local copies, waits for them, and re-layouts  81.6 us (13%)
  matrix products  52.2 us (9%)
  other arithmetic  50.4 us (8%)
  starting transfers between devices  23.8 us (4%)
  between operations  14.6 us (2%)
  Pallas kernels  10.8 us (2%)
    all_to_all x1, waiting for transfers between devices, shards(): back_y = lax.all_to_all(spread, ('px', 'py'), 0, 0, tiled=True)  202 us
    ppermute x3, waiting for transfers between devices, exchange(): parts.append(lax.ppermute(block, axis, [(s, s ^ k) for s in range(count)]))  105 us
    all_to_all x1, waiting for transfers between devices, shards(): pencil = lax.all_to_all(spectral_x, 'py', 0, 0, tiled=True)  64.5 us
    dot_general x1, matrix products, shards(): jnp.einsum('jsy,szyi->zji', carried[:, :columns].reshape(-1, count_y, hei...  18.6 us
    select_n x1, other arithmetic, net(): flux_high = jnp.where(edge, 0.0, flux_high)  16.1 us
    dot_general x1, matrix products, shards(): jnp.einsum('syj,zji->szyi', lax.all_gather(right_y, 'py', axis=0, tiled=T...  15.1 us
    slice x4, local copies, waits for them, and re-layouts, net(): rest = lambda a: lax.slice_in_dim(a, 1, None, axis=dim)  13.7 us
  transfers between devices with their start and end apart: 11, of which 7 were waited for; matrix products, arithmetic and copies ran while one was open for 17% of the time, Pallas kernels for 2%

profile of v7, /device:TPU:1, one launch (start us, length us, event | category | flops | bytes accessed | tf_op | source)
XLA Modules:
  0.0 606.6 jit_solution(5431372074989228090)
XLA Ops:
  13.4 2.3 pad_maximum_fusion
  16.5 4.3 convert_element_type.37
  24.2 2.9 constant_dynamic-slice_fusion.3
  27.0 2.1 copy.224
  29.1 2.0 copy.225
  32.4 47.4 %collective-permute-done = bf16[10,256,512]{2,1,0:T(8,128)(2,1)} collective-permute-done((bf16[10,256,512]{2,1,0:T(8,128)(2,1)}, bf16[10,256,512]{2,1,0:T(8,128)(2,1)}, u32[]{:S(2)}, u32[]{:S(2)}) %collective-permute-start) | collective-permute-done | bytes 2621472 | tf_op jit(solution)/shard_map/ppermute | solution.py:13
  80.6 56.3 %collective-permute-done.2 = bf16[10,256,512]{2,1,0:T(8,128)(2,1)} collective-permute-done((bf16[10,256,512]{2,1,0:T(8,128)(2,1)}, bf16[10,256,512]{2,1,0:T(8,128)(2,1)}, u32[]{:S(2)}, u32[]{:S(2)}) %collective-permute-start.2) | collective-permute-done | bytes 2621472 | tf_op jit(solution)/shard_map/ppermute | solution.py:13
  136.9 9.8 %convert_bitcast_fusion.1 = bf16[8,10,256,64]{2,3,1,0:T(8,128)(2,1)} fusion(bf16[10,256,512]{2,1,0:T(8,128)(2,1)} %collective-permute-done.2, bf16[10,256,512]{2,1,0:T(8,128)(2,1)} %collective-permute-done.1, bf16[10,256,512]{2,1,0:T(8,128)(2,1)} %collective-permute-done, bf16[10,256,512]{2,1,0:T(8,128)(2,1)} %convert_element_type.37, ...), kind=kOutput, calls=%fused_computation.28 | convolution fusion | flops 5420351488 | bytes 15204352 | tf_op jit(solution)/shard_map/zyx,xci->czyi/dot_general | solution.py:94
  146.8 7.3 %all-to-all-start = ((bf16[8,10,256,64]{2,3,1,0:T(8,128)(2,1)}), bf16[8,10,256,64]{2,3,1,0:T(8,128)(2,1)}, u32[]{:S(2)}, u32[]{:S(2)}) async-start(bf16[8,10,256,64]{2,3,1,0:T(8,128)(2,1)} %convert_bitcast_fusion.1), calls=%async_computation | async-start | bytes 5242880 | tf_op jit(solution)/shard_map/all_to_all | solution.py:100
  155.4 8.3 %slice.204 = bf16[2048,2048]{1,0:T(8,128)(2,1)} slice(bf16[2048,2176]{1,0:T(8,128)(2,1)} %all-gather.3.cloned.1.call-done), slice={[0:2048], [0:2048]} | slice | bytes 16777216 | tf_op jit(solution)/shard_map/slice | solution.py:112
  163.7 10.4 %copy.252 = bf16[256,8,8,256]{3,2,1,0:T(8,128)(2,1)} copy(bf16[256,8,8,256]{3,1,2,0:T(8,128)(2,1)} %bitcast.103) | data formatting | bytes 16777216
  176.8 64.5 %all-to-all-done = bf16[8,10,256,64]{2,3,1,0:T(8,128)(2,1)} async-done(((bf16[8,10,256,64]{2,3,1,0:T(8,128)(2,1)}), bf16[8,10,256,64]{2,3,1,0:T(8,128)(2,1)}, u32[]{:S(2)}, u32[]{:S(2)}) %all-to-all-start) | async-done | bytes 2621472 | tf_op jit(solution)/shard_map/all_to_all | solution.py:100
  241.3 18.6 %fusion.16.rhs_ref = f32[10,2048,64]{2,1,0:T(8,128)} fusion(bf16[8,10,256,64]{2,3,1,0:T(8,128)(2,1)} %all-to-all-done, bf16[2048,8,256,1]{2,1,0,3:T(8,128)(2,1)} %bitcast.105), kind=kOutput, calls=%fused_computation.26 | convolution fusion | flops 5368709120 | bytes 16252928 | tf_op jit(solution)/shard_map/jsy,szyi->zji/dot_general | solution.py:110
  259.9 10.8 %shard_map.131 = bf16[10,2048,64]{2,1,0:T(8,128)(2,1)} custom-call(f32[9]{0:T(128)} %coupling_ref.1, f32[10]{0:T(128)} %shift_ref.1, f32[2048,1]{1,0:T(8,128)} %fusion.30.ly_ref, f32[1,64]{1,0:T(1,128)} %dynamic-slice_bitcast_fusion.lx_ref, f32[10,2048,64]{2,1,0:T(8,128)} %fusion.16.rhs_ref), custom_call_target="tpu_custom_call" | custom-call | tf_op jit(solution)/shard_map/pallas_call | solution.py:57
  270.7 15.1 %convert_bitcast_fusion = bf16[8,10,256,64]{2,3,0,1:T(8,128)(2,1)S(1)} fusion(bf16[8,256,2048,1]{2,1,0,3:T(8,128)(2,1)} %bitcast.111, bf16[10,2048,64]{2,1,0:T(8,128)(2,1)} %shard_map.131), kind=kOutput, calls=%fused_computation.27 | convolution fusion | flops 5370019840 | bytes 13631488 | tf_op jit(solution)/shard_map/syj,zji->szyi/dot_general | solution.py:120
  287.7 7.0 %broadcast_in_dim.34 = bf16[4,8,10,256,64]{3,4,2,1,0:T(8,128)(2,1)} broadcast(bf16[8,10,256,64]{2,3,1,0:T(8,128)(2,1)} %copy.231), dimensions={1,2,3,4} | broadcast | bytes 13107200 | tf_op jit(solution)/shard_map/broadcast_in_dim | solution.py:126
  294.7 4.2 all-to-all-start.1
  299.6 6.2 %select_select_fusion = f32[10,256,512]{2,1,0:T(8,128)S(1)} fusion(s32[10,256,512]{2,1,0:T(8,128)} %param.27, f32[]{:T(128)} %bitcast.25, f32[]{:T(128)} %bitcast.24, f32[]{:T(128)} %bitcast.23, f32[]{:T(128)} %bitcast.22), kind=kLoop, calls=%fused_computation.24 | loop fusion | flops 10485760 | bytes 10485776 | tf_op jit(solution)/shard_map/jit(_where)/select_n | solution.py:139
  305.8 3.9 slice.205
  309.7 3.0 slice.218
  312.7 2.8 slice_reduce_fusion
  315.6 8.3 %slice_bitcast_fusion = (s32[10,256,512]{2,1,0:T(8,128)}, s32[10,256,512]{2,1,0:T(8,128)S(1)}) fusion(s32[2,10,256,512]{3,2,1,0:T(8,128)} %param.28), kind=kLoop, calls=%fused_computation.23 | loop fusion | bytes 20971520 | tf_op jit(solution)/shard_map/squeeze | solution.py:141
  326.7 201.5 %all-to-all-done.1 = bf16[32,10,256,64]{2,3,1,0:T(8,128)(2,1)} async-done(((bf16[32,10,256,64]{2,3,1,0:T(8,128)(2,1)}), bf16[32,10,256,64]{2,3,1,0:T(8,128)(2,1)}, u32[]{:S(2)}, u32[]{:S(2)}) %all-to-all-start.1) | async-done | bytes 10485792 | tf_op jit(solution)/shard_map/all_to_all | solution.py:128
  528.2 10.0 %copy.232 = bf16[32,10,256,64]{2,3,0,1:T(8,128)(2,1)} copy(bf16[32,10,256,64]{2,3,1,0:T(8,128)(2,1)} %all-to-all-done.1) | data formatting | bytes 20971520 | tf_op jit(solution)/shard_map/all_to_all | solution.py:128
  538.2 8.7 %fusion.25 = f32[10,256,512]{2,1,0:T(8,128)S(1)} fusion(bf16[10,256,2048]{1,2,0:T(8,128)(2,1)} %bitcast.104, bf16[2048,512]{1,0:T(8,128)(2,1)S(1)} %copy-done), kind=kOutput, calls=%fused_computation.36 | convolution fusion | flops 5368709120 | bytes 17825792 | tf_op jit(solution)/shard_map/zyi,ix->zyx/dot_general | solution.py:130
  549.1 3.7 slice.209
  552.9 3.0 slice.222
  556.6 3.4 collective-permute-start.4
  573.6 2.4 collective-permute-start.5
  576.0 2.8 multiply_select_fusion
  578.9 16.1 %fusion.13 = (f32[10,256,512]{2,1,0:T(8,128)S(1)}, f32[10,256,512]{2,1,0:T(8,128)S(1)}) fusion(f32[10,1,512]{2,1,0:T(1,128)S(1)} %get-tuple-element.54, f32[10,255,512]{2,1,0:T(8,128)} %slice.218, f32[10,256,512]{2,1,0:T(8,128)S(1)} %copy-done.2, f32[10,1,512]{2,1,0:T(1,128)S(1)} %get-tuple-element.53, f32[10,255,512]{2,1,0:T(8,128)} %slice.222, ...), kind=kLoop, calls=%fused_computation.18 | loop fusion | flops 28835840 | bytes 52429584 | tf_op jit(solution)/shard_map/jit(_where)/select_n | solution.py:159
  595.0 4.5 fusion.11
  (72 shorter events, 38.1 us)
Async XLA Ops:
  7.2 531.0 %copy-start = (bf16[2048,512]{1,0:T(8,128)(2,1)S(1)}, bf16[2048,512]{1,0:T(8,128)(2,1)}, u32[]{:S(2)}) copy-start(bf16[2048,512]{1,0:T(8,128)(2,1)} %param.26) | copy-start | bytes 6291460
  7.2 148.2 %all-gather.3.cloned.1.call-start = ((), (), s32[]{:S(2)}) async-start(), calls=%async_computation.2 | async-start | bytes 10027008 | tf_op jit(solution)/shard_map/all_gather | solution.py:108
  15.8 255.0 %all-gather.5.cloned.1.call-start = ((), (), s32[]{:S(2)}) async-start(), calls=%async_computation.3 | async-start | bytes 9437184 | tf_op jit(solution)/shard_map/all_gather | solution.py:122
  20.9 58.9 %collective-permute-start = (bf16[10,256,512]{2,1,0:T(8,128)(2,1)}, bf16[10,256,512]{2,1,0:T(8,128)(2,1)}, u32[]{:S(2)}, u32[]{:S(2)}) collective-permute-start(bf16[10,256,512]{2,1,0:T(8,128)(2,1)} %convert_element_type.37), channel_id=1, source_target_pairs={{0,8},{8,0},{16,24},{24,16},{1,9},{9,1},{17,25},{25,17},{2,10},{10... | collective-permute-start | bytes 7864328 | tf_op jit(solution)/shard_map/ppermute | solution.py:13
  22.9 57.7 %collective-permute-start.1 = (bf16[10,256,512]{2,1,0:T(8,128)(2,1)}, bf16[10,256,512]{2,1,0:T(8,128)(2,1)}, u32[]{:S(2)}, u32[]{:S(2)}) collective-permute-start(bf16[10,256,512]{2,1,0:T(8,128)(2,1)} %convert_element_type.37), channel_id=1, source_target_pairs={{0,16},{8,24},{16,0},{24,8},{1,17},{9,25},{17,1},{25,9},{2,18},{10... | collective-permute-start | bytes 7864328 | tf_op jit(solution)/shard_map/ppermute | solution.py:13
  24.2 112.8 %collective-permute-start.2 = (bf16[10,256,512]{2,1,0:T(8,128)(2,1)}, bf16[10,256,512]{2,1,0:T(8,128)(2,1)}, u32[]{:S(2)}, u32[]{:S(2)}) collective-permute-start(bf16[10,256,512]{2,1,0:T(8,128)(2,1)} %convert_element_type.37), channel_id=1, source_target_pairs={{0,24},{8,16},{16,8},{24,0},{1,25},{9,17},{17,9},{25,1},{2,26},{10... | collective-permute-start | bytes 7864328 | tf_op jit(solution)/shard_map/ppermute | solution.py:13
  146.8 94.6 %all-to-all-start = ((bf16[8,10,256,64]{2,3,1,0:T(8,128)(2,1)}), bf16[8,10,256,64]{2,3,1,0:T(8,128)(2,1)}, u32[]{:S(2)}, u32[]{:S(2)}) async-start(bf16[8,10,256,64]{2,3,1,0:T(8,128)(2,1)} %convert_bitcast_fusion.1), calls=%async_computation | async-start | bytes 5242880 | tf_op jit(solution)/shard_map/all_to_all | solution.py:100
  294.7 4.2 copy-start.5
  294.7 233.5 %all-to-all-start.1 = ((bf16[32,10,256,64]{2,3,1,0:T(8,128)(2,1)}), bf16[32,10,256,64]{2,3,1,0:T(8,128)(2,1)}, u32[]{:S(2)}, u32[]{:S(2)}) async-start(bf16[32,10,256,64]{2,3,1,0:T(8,128)(2,1)} %bitcast.102), calls=%async_computation.1 | async-start | bytes 20971520 | tf_op jit(solution)/shard_map/all_to_all | solution.py:128
  305.7 3.9 copy-start.3
  546.8 6.0 copy-start.1
  556.6 10.4 %collective-permute-start.4 = (f32[3,10,256,1]{2,0,1,3:T(4,128)}, f32[3,10,256,1]{2,0,1,3:T(4,128)}, u32[]{:S(2)}, u32[]{:S(2)}) collective-permute-start(f32[3,10,256,1]{2,0,1,3:T(4,128)} %pad_maximum_fusion.2), channel_id=1, source_target_pairs={{0,8},{8,16},{16,24},{1,9},{9,17},{17,25},{2,10},{10,18},{18,26},{... | collective-permute-start | bytes 92168 | tf_op jit(solution)/shard_map/ppermute | solution.py:151
  560.0 5.0 collective-permute-start.3
  561.4 10.6 %collective-permute-start.6 = (f32[3,10,1,512]{3,2,1,0:T(1,128)S(1)}, f32[3,10,1,512]{3,2,1,0:T(1,128)S(1)}, u32[]{:S(2)}, u32[]{:S(2)}) collective-permute-start(f32[3,10,1,512]{3,2,1,0:T(1,128)S(1)} %pad_maximum_fusion.1), channel_id=1, source_target_pairs={{0,1},{1,2},{2,3},{3,4},{4,5},{5,6},{6,7},{8,9},{9,10},{10,11},{11... | collective-permute-start | bytes 184328 | tf_op jit(solution)/shard_map/ppermute | solution.py:151
  571.0 7.9 %copy-start.2 = (f32[10,256,512]{2,1,0:T(8,128)S(1)}, f32[10,256,512]{2,1,0:T(8,128)}, u32[]{:S(2)}) copy-start(f32[10,256,512]{2,1,0:T(8,128)} %copy-done.1) | copy-start | bytes 15728644
  571.0 7.9 %copy-start.4 = (f32[10,256,1]{2,1,0:T(8,128)S(1)}, f32[10,256,1]{2,1,0:T(8,128)}, u32[]{:S(2)}) copy-start(f32[10,256,1]{2,1,0:T(8,128)} %copy.235) | copy-start | bytes 30724
  573.6 5.3 collective-permute-start.5
Sparse Core Ops, SparseCore 0:
  15.9 88.8 all-gather.2
  106.4 107.5 all-gather.4

commit v8 on v5

--- a/solution.py
+++ b/solution.py
@@ -117,50 +117,76 @@
     got = carried[:, columns:columns + 3].astype(jnp.float32)
     all_y = got[:, 0] + (got[:, 1] + got[:, 2])
     solved = thomas_solve(spectral, own_x, all_y, coupling, layer_shift)
+    right_all = lax.all_gather(right_y, "py", axis=0, tiled=True)
+    rows = jnp.clip(
+        jnp.arange(count_y)[:, None] * height - 1 + jnp.arange(height + 2)[None, :], 0, right_all.shape[0] - 1
+    )
     back_pencil = jnp.einsum(
         "syj,zji->szyi",
-        lax.all_gather(right_y, "py", axis=0, tiled=True).reshape(count_y, height, -1),
+        jnp.take(right_all, rows, axis=0),
         solved,
         preferred_element_type=jnp.float32,
     ).astype(jnp.bfloat16)
     back_y = lax.all_to_all(back_pencil, "py", 0, 0, tiled=True)
-    back_y = jnp.moveaxis(back_y, 0, 2).reshape(layers, height, -1)
-    correction = jnp.einsum(
+    back_y = jnp.moveaxis(back_y, 0, 2).reshape(layers, height + 2, -1)
+
+    forward_x = [(i, i + 1) for i in range(count_x - 1)]
+    backward_x = [(i + 1, i) for i in range(count_x - 1)]
+    forward_y = [(i, i + 1) for i in range(count_y - 1)]
+    backward_y = [(i + 1, i) for i in range(count_y - 1)]
+    right_ext = jnp.concatenate(
+        [
+            lax.ppermute(right_x[:, -1:], "px", forward_x),
+            right_x,
+            lax.ppermute(right_x[:, :1], "px", backward_x),
+        ],
+        axis=1,
+    )
+    extended = jnp.einsum(
         "zyi,ix->zyx",
         lax.all_gather(back_y, "px", axis=2, tiled=True),
-        right_x,
-        preferred_element_type=jnp.float32,
-    )
+        right_ext,
+        preferred_element_type=jnp.float32,
+    )
+    correction = extended[:, 1:-1, 1:-1]
 
     mobility = jnp.zeros(regime_code.shape, jnp.float32)
     for regime in range(mobility_table.shape[0]):
         mobility = jnp.where(regime_code == regime, mobility_table[regime], mobility)
-    flag_x = upwind_flag[0]
-    flag_y = upwind_flag[1]
-
-    def net(axis, dim, flag, at, count):
-        forward = [(i, i + 1) for i in range(count - 1)]
-        backward = [(i + 1, i) for i in range(count - 1)]
-        first = lambda a: lax.slice_in_dim(a, 0, 1, axis=dim)
-        last = lambda a: lax.slice_in_dim(a, a.shape[dim] - 1, None, axis=dim)
-        rest = lambda a: lax.slice_in_dim(a, 1, None, axis=dim)
-        head = lambda a: lax.slice_in_dim(a, 0, a.shape[dim] - 1, axis=dim)
-        high = lax.ppermute(jnp.stack([first(correction), first(mobility)]), axis, backward)
-        low = lax.ppermute(
-            jnp.stack([last(correction), last(mobility), last(flag).astype(jnp.float32)]), axis, forward
-        )
-        press_next = jnp.concatenate([rest(correction), high[0]], axis=dim)
-        mobil_next = jnp.concatenate([rest(mobility), high[1]], axis=dim)
-        flux_high = jnp.where(flag == 1, mobility, mobil_next) * (correction - press_next)
-        place = lax.broadcasted_iota(jnp.int32, correction.shape, dim)
-        edge = (at == count - 1) & (place == correction.shape[dim] - 1)
-        flux_high = jnp.where(edge, 0.0, flux_high)
-        flux_edge = jnp.where(low[2] > 0.5, low[1], first(mobility)) * (low[0] - first(correction))
-        flux_edge = jnp.where(at == 0, 0.0, flux_edge)
-        flux_low = jnp.concatenate([flux_edge, head(flux_high)], axis=dim)
-        return flux_high - flux_low
-
-    balance = net("px", 2, flag_x, at_x, count_x) + net("py", 1, flag_y, at_y, count_y)
+    flag_x = upwind_flag[0].astype(jnp.float32)
+    flag_y = upwind_flag[1].astype(jnp.float32)
+
+    left = lax.ppermute(jnp.stack([mobility[:, :, -1:], flag_x[:, :, -1:]]), "px", forward_x)
+    right = lax.ppermute(mobility[:, :, :1], "px", backward_x)
+    up = lax.ppermute(jnp.stack([mobility[:, -1:, :], flag_y[:, -1:, :]]), "py", forward_y)
+    down = lax.ppermute(mobility[:, :1, :], "py", backward_y)
+
+    def net(press, mobil, flag, at, count, dim):
+        size = press.shape[dim] - 2
+        lo = lambda a: lax.slice_in_dim(a, 0, a.shape[dim] - 1, axis=dim)
+        hi = lambda a: lax.slice_in_dim(a, 1, None, axis=dim)
+        flux = jnp.where(flag == 1.0, lo(mobil), hi(mobil)) * (lo(press) - hi(press))
+        face = lax.broadcasted_iota(jnp.int32, flux.shape, dim) + at * size - 1
+        flux = jnp.where((face >= 0) & (face <= size * count - 2), flux, 0.0)
+        return hi(flux) - lo(flux)
+
+    net_x = net(
+        extended[:, 1:-1, :],
+        jnp.concatenate([left[0], mobility, right], axis=2),
+        jnp.concatenate([left[1], flag_x], axis=2),
+        at_x,
+        count_x,
+        2,
+    )
+    net_y = net(
+        extended[:, :, 1:-1],
+        jnp.concatenate([up[0], mobility, down], axis=1),
+        jnp.concatenate([up[1], flag_y], axis=1),
+        at_y,
+        count_y,
+        1,
+    )
+    balance = net_x + net_y
     return (correction, balance)
 
 

time: 537 us -> 542 us (level)
  waiting for transfers between devices: 245 us -> 191 us
  blocking collectives: 62.4 us -> 90.4 us
  local copies, waits for them, and re-layouts: 69.9 us -> 93.1 us
  matrix products: 52.1 us -> 60.5 us
    all_to_all x1, waiting for transfers between devices: 65.1 us -> 9.17 us  [shards(): pencil = lax.all_to_all(spectral_x, 'py', 0, 0, tiled=True)]
    gather x0 -> x2, local copies, waits for them, and re-layouts: none -> 33.4 us  [shards(): jnp.take(right_all, rows, axis=0)]
    all_to_all x1, blocking collectives: 62.4 us -> 90.4 us  [shards(): back_y = lax.all_to_all(back_pencil, 'py', 0, 0, tiled=True)]
    all_gather x1, waiting for transfers between devices: 0.01 us -> 18.9 us  [shards(): lax.all_gather(jnp.concatenate([left_y, pieces], axis=1), 'py', axis=0, t...]
    all_gather x1, waiting for transfers between devices: 74.5 us -> 59.4 us  [shards(): lax.all_gather(back_y, 'px', axis=2, tiled=True)]
    squeeze x8 -> x4, local copies, waits for them, and re-layouts: 14.3 us -> 3.67 us  [the longest x2 1.53 us: shards(): left[1]]
    slice x7 -> x6, local copies, waits for them, and re-layouts: 17.8 us -> 7.93 us  [the longest x1 4.26 us: shards(): correction = extended[:, 1:-1, 1:-1]]
    convert_element_type x1, other arithmetic: 0.77 us -> 8.23 us  [shards(): flag_x = upwind_flag[0].astype(jnp.float32)]
  transfers between devices with their start and end apart: 11 -> 13, of which waited for: 5 -> 6; matrix products, arithmetic and copies ran while one was open for 19% -> 26% of each run, Pallas kernels for 2% -> 0%
where the time goes in v8:
time: 542 us; the launch traced here: 535 us
  waiting for transfers between devices  191 us (35%)
  local copies, waits for them, and re-layouts  93.1 us (17%)
  blocking collectives  90.4 us (17%)
  matrix products  60.5 us (11%)
  other arithmetic  48.1 us (9%)
  starting transfers between devices  26.2 us (5%)
  between operations  14.3 us (3%)
  Pallas kernels  11.2 us (2%)
    ppermute x3, waiting for transfers between devices, exchange(): parts.append(lax.ppermute(block, axis, [(s, s ^ k) for s in range(count)]))  102 us
    all_to_all x1, blocking collectives, shards(): back_y = lax.all_to_all(back_pencil, 'py', 0, 0, tiled=True)  90.4 us
    all_gather x1, waiting for transfers between devices, shards(): lax.all_gather(back_y, 'px', axis=2, tiled=True)  59.4 us
    gather x2, local copies, waits for them, and re-layouts, shards(): jnp.take(right_all, rows, axis=0)  33.4 us
    dot_general x1, matrix products, shards(): jnp.einsum('syj,zji->szyi', jnp.take(right_all, rows, axis=0), solved, pr...  20.9 us
    all_gather x1, waiting for transfers between devices, shards(): lax.all_gather(jnp.concatenate([left_y, pieces], axis=1), 'py', axis=0, t...  18.9 us
    unnamed x16, local copies, waits for them, and re-layouts  18.1 us
    dot_general x1, matrix products, shards(): jnp.einsum('jsy,szyi->zji', carried[:, :columns].reshape(-1, count_y, hei...  17.8 us
  transfers between devices with their start and end apart: 13, of which 6 were waited for; matrix products, arithmetic and copies ran while one was open for 26% of the time, Pallas kernels for 0%

profile of v8, /device:TPU:1, one launch (start us, length us, event | category | flops | bytes accessed | tf_op | source)
XLA Modules:
  0.0 534.6 jit_solution(4820132268773098861)
XLA Ops:
  16.4 3.0 convert_element_type.43
  22.9 2.7 constant_dynamic-slice_fusion.3
  32.8 45.4 %collective-permute-done = bf16[10,256,512]{2,1,0:T(8,128)(2,1)} collective-permute-done((bf16[10,256,512]{2,1,0:T(8,128)(2,1)S(1)}, bf16[10,256,512]{2,1,0:T(8,128)(2,1)}, u32[]{:S(2)}, u32[]{:S(2)}) %collective-permute-start) | collective-permute-done | bytes 2621472 | tf_op jit(solution)/shard_map/ppermute | solution.py:13
  79.0 56.3 %collective-permute-done.2 = bf16[10,256,512]{2,1,0:T(8,128)(2,1)} collective-permute-done((bf16[10,256,512]{2,1,0:T(8,128)(2,1)S(1)}, bf16[10,256,512]{2,1,0:T(8,128)(2,1)}, u32[]{:S(2)}, u32[]{:S(2)}) %collective-permute-start.2) | collective-permute-done | bytes 2621472 | tf_op jit(solution)/shard_map/ppermute | solution.py:13
  135.3 9.6 %convert_bitcast_fusion.3 = bf16[8,10,256,64]{2,3,1,0:T(8,128)(2,1)} fusion(bf16[10,256,512]{2,1,0:T(8,128)(2,1)} %collective-permute-done.2, bf16[10,256,512]{2,1,0:T(8,128)(2,1)} %collective-permute-done.1, bf16[10,256,512]{2,1,0:T(8,128)(2,1)} %collective-permute-done, bf16[10,256,512]{2,1,0:T(8,128)(2,1)S(1)} %convert_element_type.43, ...), kind=kOutput, calls=%fused_computation.35 | convolution fusion | flops 5420351488 | bytes 15204352 | tf_op jit(solution)/shard_map/zyx,xci->czyi/dot_general | solution.py:94
  145.0 6.9 %all-to-all-start = ((bf16[8,10,256,64]{2,3,1,0:T(8,128)(2,1)}), bf16[8,10,256,64]{2,3,1,0:T(8,128)(2,1)S(1)}, u32[]{:S(2)}, u32[]{:S(2)}) async-start(bf16[8,10,256,64]{2,3,1,0:T(8,128)(2,1)} %convert_bitcast_fusion.3), calls=%async_computation | async-start | bytes 5242880 | tf_op jit(solution)/shard_map/all_to_all | solution.py:100
  152.7 22.6 %gather_fusion = bf16[2064,2048]{1,0:T(8,128)(2,1)} fusion(bf16[2048,2048]{1,0:T(8,128)(2,1)} %all-gather.6.cloned.1.call-done, s32[3072]{0:T(1024)S(1)} %pad_clamp_fusion), kind=kCustom, calls=%fused_computation | custom fusion | bytes 16916544 | tf_op jit(solution)/shard_map/jit(_take)/gather | solution.py:126
  175.3 10.8 %reshape.180 = bf16[8,258,2048]{2,1,0:T(8,128)(2,1)} reshape(bf16[2064,2048]{1,0:T(8,128)(2,1)} %gather_fusion) | data formatting | bytes 16908288 | tf_op jit(solution)/shard_map/jit(_take)/gather | solution.py:126
  186.1 18.9 %all-gather.4.cloned.1.call-done = bf16[2048,2176]{1,0:T(8,128)(2,1)} async-done(((bf16[256,2176]{1,0:T(8,128)(2,1)}), bf16[2048,2176]{1,0:T(8,128)(2,1)}) %all-gather.4.cloned.1.call-update) | async-done | bytes 8912912 | tf_op jit(solution)/shard_map/all_gather | solution.py:108
  204.9 8.3 %slice.196 = bf16[2048,2048]{1,0:T(8,128)(2,1)} slice(bf16[2048,2176]{1,0:T(8,128)(2,1)} %all-gather.4.cloned.1.call-done), slice={[0:2048], [0:2048]} | slice | bytes 16777216 | tf_op jit(solution)/shard_map/slice | solution.py:112
  213.2 10.4 %copy.132 = bf16[256,8,8,256]{3,2,1,0:T(8,128)(2,1)} copy(bf16[256,8,8,256]{3,1,2,0:T(8,128)(2,1)} %bitcast.72) | data formatting | bytes 16777216
  226.4 9.2 %all-to-all-done = bf16[8,10,256,64]{2,3,1,0:T(8,128)(2,1)S(1)} async-done(((bf16[8,10,256,64]{2,3,1,0:T(8,128)(2,1)}), bf16[8,10,256,64]{2,3,1,0:T(8,128)(2,1)S(1)}, u32[]{:S(2)}, u32[]{:S(2)}) %all-to-all-start) | async-done | bytes 2621472 | tf_op jit(solution)/shard_map/all_to_all | solution.py:100
  235.5 17.8 %fusion.19.rhs_ref = f32[10,2048,64]{2,1,0:T(8,128)} fusion(bf16[8,10,256,64]{2,3,1,0:T(8,128)(2,1)S(1)} %all-to-all-done, bf16[2048,8,256,1]{2,1,0,3:T(8,128)(2,1)} %bitcast.75), kind=kOutput, calls=%fused_computation.32 | convolution fusion | flops 5368709120 | bytes 16252928 | tf_op jit(solution)/shard_map/jsy,szyi->zji/dot_general | solution.py:110
  253.3 11.2 %shard_map.131 = bf16[10,2048,64]{2,1,0:T(8,128)(2,1)} custom-call(f32[9]{0:T(128)} %coupling_ref.1, f32[10]{0:T(128)} %shift_ref.1, f32[2048,1]{1,0:T(8,128)} %fusion.38.ly_ref, f32[1,64]{1,0:T(1,128)} %dynamic-slice_bitcast_fusion.lx_ref, f32[10,2048,64]{2,1,0:T(8,128)} %fusion.19.rhs_ref), custom_call_target="tpu_custom_call" | custom-call | tf_op jit(solution)/shard_map/pallas_call | solution.py:57
  264.6 20.9 %convert_bitcast_fusion.2 = bf16[8,10,258,64]{2,3,0,1:T(8,128)(2,1)S(1)} fusion(bf16[8,258,2048]{2,1,0:T(8,128)(2,1)} %reshape.180, pred[8,258]{1,0:T(8,128)(4,1)S(1)} %fusion.41, bf16[10,2048,64]{2,1,0:T(8,128)(2,1)} %shard_map.131), kind=kOutput, calls=%fused_computation.34 | convolution fusion | flops 5416200192 | bytes 13719568 | tf_op jit(solution)/shard_map/syj,zji->szyi/dot_general | solution.py:124
  285.9 90.4 %all_to_all.10 = bf16[8,10,258,64]{2,3,1,0:T(8,128)(2,1)S(1)} all-to-all(bf16[8,10,258,64]{2,3,1,0:T(8,128)(2,1)S(1)} %copy.113), channel_id=1, replica_groups=mesh['px'=4,'py'=8] {'py'}, dimensions={0} | all-to-all | bytes 5283840 | tf_op jit(solution)/shard_map/all_to_all | solution.py:130
  376.3 2.4 copy.114
  378.7 5.6 %copy.115 = bf16[10,258,512]{2,1,0:T(8,128)(2,1)} copy(bf16[10,258,512]{1,2,0:T(8,128)(2,1)} %bitcast.73) | data formatting | bytes 5283840 | tf_op jit(solution)/shard_map/reshape | solution.py:131
  384.3 2.9 copy.116
  387.2 3.1 collective-permute-start.3
  392.3 6.6 %select_select_fusion = f32[10,256,512]{2,1,0:T(8,128)S(1)} fusion(s32[10,256,512]{2,1,0:T(8,128)} %param.27, f32[]{:T(128)} %bitcast.22, f32[]{:T(128)} %bitcast.21, f32[]{:T(128)} %bitcast.20, f32[]{:T(128)} %bitcast.19), kind=kLoop, calls=%fused_computation.31 | loop fusion | flops 10485760 | bytes 10485776 | tf_op jit(solution)/shard_map/jit(_where)/select_n | solution.py:155
  402.1 8.2 %convert_bitcast_fusion.1 = (f32[10,256,512]{2,1,0:T(8,128)S(1)}, f32[10,256,512]{2,1,0:T(8,128)}) fusion(s32[2,10,256,512]{3,2,1,0:T(8,128)} %param.28), kind=kLoop, calls=%fused_computation.30 | loop fusion | flops 2621440 | bytes 20971520 | tf_op jit(solution)/shard_map/convert_element_type | solution.py:156
  410.3 2.4 copy-done.3
  413.5 4.0 collective-permute-start.5
  421.8 3.0 collective-permute-start.7
  424.9 3.1 collective-permute-start.8
  432.1 59.4 %all-gather.8.cloned.1.call-done = bf16[10,258,2048]{2,1,0:T(8,128)(2,1)} async-done(((bf16[10,258,512]{2,1,0:T(8,128)(2,1)}), bf16[10,258,2048]{2,1,0:T(8,128)(2,1)}) %all-gather.8.cloned.1.call-update) | async-done | bytes 10567696 | tf_op jit(solution)/shard_map/all_gather | solution.py:147
  491.5 12.3 %fusion.27 = f32[10,258,514]{2,1,0:T(8,128)S(1)} fusion(bf16[10,258,2048]{2,1,0:T(8,128)(2,1)} %all-gather.8.cloned.1.call-done, bf16[2048,1]{0,1:T(2,128)(2,1)S(1)} %collective-permute-done.4, bf16[2048,512]{0,1:T(8,128)(2,1)} %copy-done.4, bf16[2048,1]{0,1:T(2,128)(2,1)S(1)} %collective-permute-done.3), kind=kOutput, calls=%fused_computation.37 | convolution fusion | flops 5438103552 | bytes 17977504 | tf_op jit(solution)/shard_map/zyi,ix->zyx/dot_general | solution.py:145
  503.7 9.4 %fusion.14 = f32[10,256,513]{2,1,0:T(8,128)S(1)} fusion(f32[10,258,514]{2,1,0:T(8,128)S(1)} %fusion.27, f32[10,256,512]{2,1,0:T(8,128)} %copy-done.2, f32[10,256,1]{2,1,0:T(8,128)} %copy.120, f32[10,256,1]{2,1,0:T(8,128)S(1)} %copy.122, f32[10,256,512]{2,1,0:T(8,128)} %copy-done.3, f32[10,256,1]{2,1,0:T(8,128)} %copy.119, pred[513]{0:T(1024)(128)(4,1)S(1)} %fusion.44), kind=kLoop, calls=%fused_computation.17 | loop fusion | flops 10506240 | bytes 26276352 | tf_op jit(solution)/shard_map/jit(_where)/select_n | solution.py:170
  513.2 4.3 slice.199
  517.4 7.3 %fusion.16 = f32[10,257,512]{2,1,0:T(8,128)S(1)} fusion(f32[10,258,514]{2,1,0:T(8,128)S(1)} %fusion.27, f32[10,256,512]{2,1,0:T(8,128)} %copy-done.2, f32[10,1,512]{2,1,0:T(1,128)S(1)} %copy-done.5, f32[10,1,512]{2,1,0:T(1,128)} %collective-permute-done.8, f32[10,256,512]{2,1,0:T(8,128)} %get-tuple-element.39, f32[10,1,512]{2,1,0:T(1,128)S(1)} %get-tuple-element.50, ...), kind=kLoop, calls=%fused_computation.22 | loop fusion | flops 10526720 | bytes 26337536 | tf_op jit(solution)/shard_map/jit(_where)/select_n | solution.py:170
  524.7 3.1 fusion.17
  (75 shorter events, 39.2 us)
Async XLA Ops:
  7.2 144.8 %copy-start = (f32[512]{0:T(512)S(1)}, f32[512]{0:T(512)}, u32[]{:S(2)}) copy-start(f32[512]{0:T(512)} %param.19) | copy-start | bytes 6148
  7.2 145.5 %all-gather.6.cloned.1.call-start = ((), (), s32[]{:S(2)}) async-start(), calls=%async_computation.3 | async-start | bytes 9437184 | tf_op jit(solution)/shard_map/all_gather | solution.py:120
  7.9 197.0 %all-gather.4.cloned.1.call-start = ((), (), s32[]{:S(2)}) async-start(), calls=%async_computation.2 | async-start | bytes 10027008 | tf_op jit(solution)/shard_map/all_gather | solution.py:108
  19.4 58.9 %collective-permute-start = (bf16[10,256,512]{2,1,0:T(8,128)(2,1)S(1)}, bf16[10,256,512]{2,1,0:T(8,128)(2,1)}, u32[]{:S(2)}, u32[]{:S(2)}) collective-permute-start(bf16[10,256,512]{2,1,0:T(8,128)(2,1)S(1)} %convert_element_type.43), channel_id=1, source_target_pairs={{0,8},{8,0},{16,24},{24,16},{1,9},{9,1},{17,25},{25,17},{2,10},{10... | collective-permute-start | bytes 7864328 | tf_op jit(solution)/shard_map/ppermute | solution.py:13
  21.7 57.4 %collective-permute-start.1 = (bf16[10,256,512]{2,1,0:T(8,128)(2,1)S(1)}, bf16[10,256,512]{2,1,0:T(8,128)(2,1)}, u32[]{:S(2)}, u32[]{:S(2)}) collective-permute-start(bf16[10,256,512]{2,1,0:T(8,128)(2,1)S(1)} %convert_element_type.43), channel_id=1, source_target_pairs={{0,16},{8,24},{16,0},{24,8},{1,17},{9,25},{17,1},{25,9},{2,18},{10... | collective-permute-start | bytes 7864328 | tf_op jit(solution)/shard_map/ppermute | solution.py:13
  22.9 112.4 %collective-permute-start.2 = (bf16[10,256,512]{2,1,0:T(8,128)(2,1)S(1)}, bf16[10,256,512]{2,1,0:T(8,128)(2,1)}, u32[]{:S(2)}, u32[]{:S(2)}) collective-permute-start(bf16[10,256,512]{2,1,0:T(8,128)(2,1)S(1)} %convert_element_type.43), channel_id=1, source_target_pairs={{0,24},{8,16},{16,8},{24,0},{1,25},{9,17},{17,9},{25,1},{2,26},{10... | collective-permute-start | bytes 7864328 | tf_op jit(solution)/shard_map/ppermute | solution.py:13
  145.0 90.6 %all-to-all-start = ((bf16[8,10,256,64]{2,3,1,0:T(8,128)(2,1)}), bf16[8,10,256,64]{2,3,1,0:T(8,128)(2,1)S(1)}, u32[]{:S(2)}, u32[]{:S(2)}) async-start(bf16[8,10,256,64]{2,3,1,0:T(8,128)(2,1)} %convert_bitcast_fusion.3), calls=%async_computation | async-start | bytes 5242880 | tf_op jit(solution)/shard_map/all_to_all | solution.py:100
  151.8 339.6 %all-gather.8.cloned.1.call-start = ((), (), s32[]{:S(2)}) async-start(), calls=%async_computation.4 | async-start | bytes 13516800 | tf_op jit(solution)/shard_map/all_gather | solution.py:147
  378.7 13.0 %copy-start.6 = (f32[4]{0:T(128)S(1)}, f32[4]{0:T(128)}, u32[]{:S(2)}) copy-start(f32[4]{0:T(128)} %param.29) | copy-start | bytes 52
  387.2 5.0 copy-start.4
  387.2 44.8 %collective-permute-start.3 = (bf16[2048,1]{0,1:T(2,128)(2,1)S(1)}, bf16[2048,1]{0,1:T(2,128)(2,1)S(1)}, u32[]{:S(2)}, u32[]{:S(2)}) collective-permute-start(bf16[2048,1]{0,1:T(2,128)(2,1)S(1)} %get-tuple-element.44), channel_id=1, source_target_pairs={{0,8},{8,16},{16,24},{1,9},{9,17},{17,25},{2,10},{10,18},{18,26},{... | collective-permute-start | bytes 12296 | tf_op jit(solution)/shard_map/ppermute | solution.py:139
  390.3 41.8 %collective-permute-start.4 = (bf16[2048,1]{0,1:T(2,128)(2,1)S(1)}, bf16[2048,1]{0,1:T(2,128)(2,1)S(1)}, u32[]{:S(2)}, u32[]{:S(2)}) collective-permute-start(bf16[2048,1]{0,1:T(2,128)(2,1)S(1)} %get-tuple-element.45), channel_id=1, source_target_pairs={{8,0},{16,8},{24,16},{9,1},{17,9},{25,17},{10,2},{18,10},{26,18},{... | collective-permute-start | bytes 12296 | tf_op jit(solution)/shard_map/ppermute | solution.py:141
  398.8 2.4 copy-start.2
  410.3 2.4 copy-start.3
  413.5 14.9 %collective-permute-start.5 = (f32[2,10,256,1]{2,0,1,3:T(2,128)S(1)}, f32[2,10,256,1]{2,0,1,3:T(2,128)S(1)}, u32[]{:S(2)}, u32[]{:S(2)}) collective-permute-start(f32[2,10,256,1]{2,0,1,3:T(2,128)S(1)} %pad_maximum_fusion.2), channel_id=1, source_target_pairs={{0,8},{8,16},{16,24},{1,9},{9,17},{17,25},{2,10},{10,18},{18,26},{... | collective-permute-start | bytes 61448 | tf_op jit(solution)/shard_map/ppermute | solution.py:159
  417.9 7.0 %collective-permute-start.6 = (f32[10,256,1]{1,2,0:T(1,128)S(1)}, f32[10,256,1]{1,2,0:T(1,128)S(1)}, u32[]{:S(2)}, u32[]{:S(2)}) collective-permute-start(f32[10,256,1]{1,2,0:T(1,128)S(1)} %copy.121), channel_id=1, source_target_pairs={{8,0},{16,8},{24,16},{9,1},{17,9},{25,17},{10,2},{18,10},{26,18},{... | collective-permute-start | bytes 30728 | tf_op jit(solution)/shard_map/ppermute | solution.py:160
  421.8 9.7 %collective-permute-start.7 = (f32[2,10,1,512]{3,2,1,0:T(1,128)S(1)}, f32[2,10,1,512]{3,2,1,0:T(1,128)S(1)}, u32[]{:S(2)}, u32[]{:S(2)}) collective-permute-start(f32[2,10,1,512]{3,2,1,0:T(1,128)S(1)} %pad_maximum_fusion.1), channel_id=1, source_target_pairs={{0,1},{1,2},{2,3},{3,4},{4,5},{5,6},{6,7},{8,9},{9,10},{10,11},{11... | collective-permute-start | bytes 122888 | tf_op jit(solution)/shard_map/ppermute | solution.py:161
  424.9 92.6 %collective-permute-start.8 = (f32[10,1,512]{2,1,0:T(1,128)}, f32[10,1,512]{2,1,0:T(1,128)}, u32[]{:S(2)}, u32[]{:S(2)}) collective-permute-start(f32[10,1,512]{2,1,0:T(1,128)} %get-tuple-element.42), channel_id=1, source_target_pairs={{1,0},{2,1},{3,2},{4,3},{5,4},{6,5},{7,6},{9,8},{10,9},{11,10},{12... | collective-permute-start | bytes 61448 | tf_op jit(solution)/shard_map/ppermute | solution.py:162
  513.2 4.3 copy-start.5
  524.7 3.1 copy-start.1
Sparse Core Ops, SparseCore 0:
  9.6 84.5 all-gather.5
  96.4 108.4 all-gather.3
  384.4 107.0 all-gather.7

commit v9 on v8

--- a/solution.py
+++ b/solution.py
@@ -117,18 +117,14 @@
     got = carried[:, columns:columns + 3].astype(jnp.float32)
     all_y = got[:, 0] + (got[:, 1] + got[:, 2])
     solved = thomas_solve(spectral, own_x, all_y, coupling, layer_shift)
-    right_all = lax.all_gather(right_y, "py", axis=0, tiled=True)
-    rows = jnp.clip(
-        jnp.arange(count_y)[:, None] * height - 1 + jnp.arange(height + 2)[None, :], 0, right_all.shape[0] - 1
-    )
     back_pencil = jnp.einsum(
         "syj,zji->szyi",
-        jnp.take(right_all, rows, axis=0),
+        lax.all_gather(right_y, "py", axis=0, tiled=True).reshape(count_y, height, -1),
         solved,
         preferred_element_type=jnp.float32,
     ).astype(jnp.bfloat16)
     back_y = lax.all_to_all(back_pencil, "py", 0, 0, tiled=True)
-    back_y = jnp.moveaxis(back_y, 0, 2).reshape(layers, height + 2, -1)
+    back_y = jnp.moveaxis(back_y, 0, 2).reshape(layers, height, -1)
 
     forward_x = [(i, i + 1) for i in range(count_x - 1)]
     backward_x = [(i + 1, i) for i in range(count_x - 1)]
@@ -148,7 +144,7 @@
         right_ext,
         preferred_element_type=jnp.float32,
     )
-    correction = extended[:, 1:-1, 1:-1]
+    correction = extended[:, :, 1:-1]
 
     mobility = jnp.zeros(regime_code.shape, jnp.float32)
     for regime in range(mobility_table.shape[0]):
@@ -170,8 +166,10 @@
         flux = jnp.where((face >= 0) & (face <= size * count - 2), flux, 0.0)
         return hi(flux) - lo(flux)
 
+    above = lax.ppermute(correction[:, -1:, :], "py", forward_y)
+    below = lax.ppermute(correction[:, :1, :], "py", backward_y)
     net_x = net(
-        extended[:, 1:-1, :],
+        extended,
         jnp.concatenate([left[0], mobility, right], axis=2),
         jnp.concatenate([left[1], flag_x], axis=2),
         at_x,
@@ -179,7 +177,7 @@
         2,
     )
     net_y = net(
-        extended[:, :, 1:-1],
+        jnp.concatenate([above, correction, below], axis=1),
         jnp.concatenate([up[0], mobility, down], axis=1),
         jnp.concatenate([up[1], flag_y], axis=1),
         at_y,

time: 542 us -> 551 us (1.017)
  blocking collectives: 90.4 us -> 62.3 us
  other arithmetic: 48.1 us -> 63.2 us
  waiting for transfers between devices: 191 us -> 204 us
  local copies, waits for them, and re-layouts: 93.1 us -> 105 us
  matrix products: 60.5 us -> 51.6 us
    all_to_all x1, waiting for transfers between devices: 9.17 us -> 67.1 us  [shards(): pencil = lax.all_to_all(spectral_x, 'py', 0, 0, tiled=True)]
    gather x2 -> x0, local copies, waits for them, and re-layouts: 33.4 us -> none  [shards(): jnp.take(right_all, rows, axis=0)]
    all_gather x1, waiting for transfers between devices: 59.4 us -> 30.4 us  [shards(): lax.all_gather(back_y, 'px', axis=2, tiled=True)]
    all_to_all x1, blocking collectives: 90.4 us -> 62.3 us  [shards(): back_y = lax.all_to_all(back_pencil, 'py', 0, 0, tiled=True)]
    unnamed x16 -> x33, local copies, waits for them, and re-layouts: 18.1 us -> 46.2 us
    all_gather x1, waiting for transfers between devices: 18.9 us -> 0.01 us  [shards(): lax.all_gather(jnp.concatenate([left_y, pieces], axis=1), 'py', axis=0, t...]
    slice x2 -> x6, local copies, waits for them, and re-layouts: 5.03 us -> 20.7 us  [the longest x1 10.2 us: shards(): flag_x = upwind_flag[0].astype(jnp.float32)]
    select_n x2, other arithmetic: 16.7 us -> 28.8 us  [net(): flux = jnp.where((face >= 0) & (face <= size * count - 2), flux, 0.0)]
  transfers between devices with their start and end apart: 13 -> 15, of which waited for: 6 -> 6; matrix products, arithmetic and copies ran while one was open for 26% -> 28% of each run, Pallas kernels for 0% -> 2%
where the time goes in v9:
time: 551 us; the launch traced here: 542 us
  waiting for transfers between devices  204 us (37%)
  local copies, waits for them, and re-layouts  105 us (19%)
  other arithmetic  63.2 us (11%)
  blocking collectives  62.3 us (11%)
  matrix products  51.6 us (9%)
  starting transfers between devices  30.3 us (5%)
  between operations  14.6 us (3%)
  Pallas kernels  10.8 us (2%)
    ppermute x3, waiting for transfers between devices, exchange(): parts.append(lax.ppermute(block, axis, [(s, s ^ k) for s in range(count)]))  102 us
    all_to_all x1, waiting for transfers between devices, shards(): pencil = lax.all_to_all(spectral_x, 'py', 0, 0, tiled=True)  67.1 us
    all_to_all x1, blocking collectives, shards(): back_y = lax.all_to_all(back_pencil, 'py', 0, 0, tiled=True)  62.3 us
    unnamed x33, local copies, waits for them, and re-layouts  46.2 us
    all_gather x1, waiting for transfers between devices, shards(): lax.all_gather(back_y, 'px', axis=2, tiled=True)  30.4 us
    select_n x2, other arithmetic, net(): flux = jnp.where((face >= 0) & (face <= size * count - 2), flux, 0.0)  28.8 us
    dot_general x1, matrix products, shards(): jnp.einsum('jsy,szyi->zji', carried[:, :columns].reshape(-1, count_y, hei...  18 us
    dot_general x1, matrix products, shards(): jnp.einsum('syj,zji->szyi', lax.all_gather(right_y, 'py', axis=0, tiled=T...  15 us
  transfers between devices with their start and end apart: 15, of which 6 were waited for; matrix products, arithmetic and copies ran while one was open for 28% of the time, Pallas kernels for 2%

profile of v9, /device:TPU:1, one launch (start us, length us, event | category | flops | bytes accessed | tf_op | source)
XLA Modules:
  0.0 541.7 jit_solution(9614129657465669252)
XLA Ops:
  32.7 45.3 %collective-permute-done = bf16[10,256,512]{2,1,0:T(8,128)(2,1)} collective-permute-done((bf16[10,256,512]{2,1,0:T(8,128)(2,1)S(1)}, bf16[10,256,512]{2,1,0:T(8,128)(2,1)}, u32[]{:S(2)}, u32[]{:S(2)}) %collective-permute-start) | collective-permute-done | bytes 2621472 | tf_op jit(solution)/shard_map/ppermute | solution.py:13
  78.8 56.3 %collective-permute-done.2 = bf16[10,256,512]{2,1,0:T(8,128)(2,1)} collective-permute-done((bf16[10,256,512]{2,1,0:T(8,128)(2,1)S(1)}, bf16[10,256,512]{2,1,0:T(8,128)(2,1)}, u32[]{:S(2)}, u32[]{:S(2)}) %collective-permute-start.2) | collective-permute-done | bytes 2621472 | tf_op jit(solution)/shard_map/ppermute | solution.py:13
  135.1 9.8 %convert_bitcast_fusion.3 = bf16[8,10,256,64]{2,3,1,0:T(8,128)(2,1)} fusion(bf16[10,256,512]{2,1,0:T(8,128)(2,1)} %collective-permute-done.2, bf16[10,256,512]{2,1,0:T(8,128)(2,1)} %collective-permute-done.1, bf16[10,256,512]{2,1,0:T(8,128)(2,1)} %collective-permute-done, bf16[10,256,512]{2,1,0:T(8,128)(2,1)S(1)} %convert_element_type.43, ...), kind=kOutput, calls=%fused_computation.32 | convolution fusion | flops 5420351488 | bytes 15204352 | tf_op jit(solution)/shard_map/zyx,xci->czyi/dot_general | solution.py:94
  144.9 6.6 %all-to-all-start = ((bf16[8,10,256,64]{2,3,1,0:T(8,128)(2,1)}), bf16[8,10,256,64]{2,3,1,0:T(8,128)(2,1)S(1)}, u32[]{:S(2)}, u32[]{:S(2)}) async-start(bf16[8,10,256,64]{2,3,1,0:T(8,128)(2,1)} %convert_bitcast_fusion.3), calls=%async_computation | async-start | bytes 5242880 | tf_op jit(solution)/shard_map/all_to_all | solution.py:100
  152.2 8.4 %slice.194 = bf16[2048,2048]{1,0:T(8,128)(2,1)} slice(bf16[2048,2176]{1,0:T(8,128)(2,1)} %all-gather.4.cloned.1.call-done), slice={[0:2048], [0:2048]} | slice | bytes 16777216 | tf_op jit(solution)/shard_map/slice | solution.py:112
  160.6 10.5 %copy.196 = bf16[256,8,8,256]{3,2,1,0:T(8,128)(2,1)} copy(bf16[256,8,8,256]{3,1,2,0:T(8,128)(2,1)} %bitcast.72) | data formatting | bytes 16777216
  173.7 67.1 %all-to-all-done = bf16[8,10,256,64]{2,3,1,0:T(8,128)(2,1)S(1)} async-done(((bf16[8,10,256,64]{2,3,1,0:T(8,128)(2,1)}), bf16[8,10,256,64]{2,3,1,0:T(8,128)(2,1)S(1)}, u32[]{:S(2)}, u32[]{:S(2)}) %all-to-all-start) | async-done | bytes 2621472 | tf_op jit(solution)/shard_map/all_to_all | solution.py:100
  240.9 18.0 %fusion.16.rhs_ref = f32[10,2048,64]{2,1,0:T(8,128)} fusion(bf16[8,10,256,64]{2,3,1,0:T(8,128)(2,1)S(1)} %all-to-all-done, bf16[2048,8,256,1]{2,1,0,3:T(8,128)(2,1)} %bitcast.74), kind=kOutput, calls=%fused_computation.28 | convolution fusion | flops 5368709120 | bytes 16252928 | tf_op jit(solution)/shard_map/jsy,szyi->zji/dot_general | solution.py:110
  258.8 10.8 %shard_map.131 = bf16[10,2048,64]{2,1,0:T(8,128)(2,1)} custom-call(f32[9]{0:T(128)} %coupling_ref.1, f32[10]{0:T(128)} %shift_ref.1, f32[2048,1]{1,0:T(8,128)} %fusion.32.ly_ref, f32[1,64]{1,0:T(1,128)} %dynamic-slice_bitcast_fusion.lx_ref, f32[10,2048,64]{2,1,0:T(8,128)} %fusion.16.rhs_ref), custom_call_target="tpu_custom_call" | custom-call | tf_op jit(solution)/shard_map/pallas_call | solution.py:57
  269.7 15.0 %convert_bitcast_fusion.2 = bf16[8,10,256,64]{2,3,0,1:T(8,128)(2,1)S(1)} fusion(bf16[8,256,2048,1]{2,1,0,3:T(8,128)(2,1)} %bitcast.80, bf16[10,2048,64]{2,1,0:T(8,128)(2,1)} %shard_map.131), kind=kOutput, calls=%fused_computation.31 | convolution fusion | flops 5370019840 | bytes 13631488 | tf_op jit(solution)/shard_map/syj,zji->szyi/dot_general | solution.py:120
  285.0 62.3 %all_to_all.10 = bf16[8,10,256,64]{2,3,1,0:T(8,128)(2,1)S(1)} all-to-all(bf16[8,10,256,64]{2,3,1,0:T(8,128)(2,1)S(1)} %copy.163), channel_id=1, replica_groups=mesh['px'=4,'py'=8] {'py'}, dimensions={0} | all-to-all | bytes 5242880 | tf_op jit(solution)/shard_map/all_to_all | solution.py:126
  350.3 2.9 copy.166
  353.3 3.1 collective-permute-start.3
  357.7 6.5 %copy.169 = s32[10,256,512]{1,2,0:T(8,128)} copy(s32[10,256,512]{2,1,0:T(8,128)} %param.27) | data formatting | bytes 10485760 | tf_op args[9]
  364.2 10.2 %fusion.43 = (s32[1,10,256,512]{3,2,1,0:T(8,128)}, s32[1,10,256,512]{3,2,1,0:T(8,128)}) fusion(s32[2,10,256,512]{3,2,1,0:T(8,128)} %param.28), kind=kLoop, calls=%fused_computation.86 | loop fusion | bytes 20971520 | tf_op jit(solution)/shard_map/slice | solution.py:152
  374.3 5.9 %copy.194 = s32[1,10,256,512]{2,3,1,0:T(8,128)} copy(s32[1,10,256,512]{3,2,1,0:T(8,128)} %get-tuple-element.52) | data formatting | bytes 10485760
  380.9 6.7 %select_select_fusion = f32[10,256,512]{1,2,0:T(8,128)S(1)} fusion(s32[10,256,512]{1,2,0:T(8,128)} %copy.169, f32[]{:T(128)} %bitcast.23, f32[]{:T(128)} %bitcast.22, f32[]{:T(128)} %bitcast.21, f32[]{:T(128)} %bitcast.20), kind=kLoop, calls=%fused_computation.27 | loop fusion | flops 10485760 | bytes 10485776 | tf_op jit(solution)/shard_map/jit(_where)/select_n | solution.py:151
  388.1 3.8 collective-permute-start.5
  394.9 6.0 %copy.195 = s32[1,10,256,512]{2,3,1,0:T(8,128)} copy(s32[1,10,256,512]{3,2,1,0:T(8,128)} %get-tuple-element.53) | data formatting | bytes 10485760
  400.8 3.1 convert_bitcast_fusion
  407.7 3.2 collective-permute-start.7
  413.8 3.6 collective-permute-done.8
  424.3 30.4 %all-gather.8.cloned.1.call-done = bf16[10,256,2048]{2,1,0:T(8,128)(2,1)} async-done(((bf16[10,256,512]{2,1,0:T(8,128)(2,1)}), bf16[10,256,2048]{2,1,0:T(8,128)(2,1)}) %all-gather.8.cloned.1.call-update) | async-done | bytes 10485776 | tf_op jit(solution)/shard_map/all_gather | solution.py:143
  454.6 8.9 %fusion.19 = f32[10,256,514]{1,2,0:T(8,128)S(1)} fusion(bf16[10,256,2048]{2,1,0:T(8,128)(2,1)} %all-gather.8.cloned.1.call-done, bf16[2048,1]{0,1:T(2,128)(2,1)S(1)} %collective-permute-done.4, bf16[2048,512]{0,1:T(8,128)(2,1)S(1)} %copy-done.9, bf16[2048,1]{0,1:T(2,128)(2,1)S(1)} %collective-permute-done.3), kind=kOutput, calls=%fused_computation.34 | convolution fusion | flops 5395996672 | bytes 17854464 | tf_op jit(solution)/shard_map/zyi,ix->zyx/dot_general | solution.py:141
  463.6 2.9 fusion.44
  467.5 3.6 collective-permute-start.9
  475.6 12.1 %fusion.12 = f32[10,256,513]{1,2,0:T(8,128)} fusion(f32[10,256,514]{1,2,0:T(8,128)} %copy-done.3, f32[10,256,512]{1,2,0:T(8,128)} %copy-done.2, f32[10,256,1]{1,2,0:T(1,128)S(1)} %get-tuple-element.69, f32[10,256,1]{1,2,0:T(1,128)S(1)} %collective-permute-done.6, f32[10,256,512]{1,2,0:T(8,128)} %copy-done.5, f32[10,256,1]{1,2,0:T(1,128)S(1)} %get-tuple-element.68, ...), kind=kLoop, calls=%fused_computation.17 | loop fusion | flops 10506240 | bytes 26276352 | tf_op jit(solution)/shard_map/jit(_where)/select_n | solution.py:166
  487.8 2.9 slice.197
  490.7 5.9 %copy.183 = f32[10,256,512]{2,1,0:T(8,128)} copy(f32[10,256,512]{1,2,0:T(8,128)} %slice.197) | data formatting | bytes 10485760
  501.1 16.7 %fusion.10 = f32[10,257,512]{1,2,0:T(8,128)} fusion(f32[10,256,512]{1,2,0:T(8,128)} %copy-done.2, f32[10,1,512]{1,2,0:T(8,128)} %copy.176, f32[10,1,512]{1,2,0:T(8,128)S(1)} %copy-done.7, f32[10,256,512]{1,2,0:T(8,128)} %slice.197, f32[10,1,512]{1,2,0:T(8,128)} %copy.180, f32[10,1,512]{1,2,0:T(8,128)} %copy.182, f32[10,256,512]{1,2,0:T(8,128)} %copy-done.4, ...), kind=kLoop, calls=%fused_computation.13 | loop fusion | flops 13158400 | bytes 21094656 | tf_op jit(solution)/shard_map/jit(_where)/select_n | solution.py:166
  517.8 11.0 %fusion.13 = f32[10,256,512]{1,2,0:T(8,128)} fusion(f32[10,257,512]{1,2,0:T(8,128)} %fusion.10, f32[10,256,513]{1,2,0:T(8,128)} %fusion.12), kind=kLoop, calls=%fused_computation.21 | loop fusion | flops 3932160 | bytes 26214400 | tf_op jit(solution)/shard_map/add | solution.py:187
  528.8 5.9 %copy.184 = f32[10,256,512]{2,1,0:T(8,128)} copy(f32[10,256,512]{1,2,0:T(8,128)} %fusion.13) | data formatting | bytes 10485760
  (97 shorter events, 61.9 us)
Async XLA Ops:
  7.2 144.4 %copy-start = (f32[512]{0:T(512)S(1)}, f32[512]{0:T(512)}, u32[]{:S(2)}) copy-start(f32[512]{0:T(512)} %param.19) | copy-start | bytes 6148
  7.2 145.0 %all-gather.4.cloned.1.call-start = ((), (), s32[]{:S(2)}) async-start(), calls=%async_computation.2 | async-start | bytes 10027008 | tf_op jit(solution)/shard_map/all_gather | solution.py:108
  15.6 254.1 %all-gather.6.cloned.1.call-start = ((), (), s32[]{:S(2)}) async-start(), calls=%async_computation.3 | async-start | bytes 9437184 | tf_op jit(solution)/shard_map/all_gather | solution.py:122
  19.2 58.8 %collective-permute-start = (bf16[10,256,512]{2,1,0:T(8,128)(2,1)S(1)}, bf16[10,256,512]{2,1,0:T(8,128)(2,1)}, u32[]{:S(2)}, u32[]{:S(2)}) collective-permute-start(bf16[10,256,512]{2,1,0:T(8,128)(2,1)S(1)} %convert_element_type.43), channel_id=1, source_target_pairs={{0,8},{8,0},{16,24},{24,16},{1,9},{9,1},{17,25},{25,17},{2,10},{10... | collective-permute-start | bytes 7864328 | tf_op jit(solution)/shard_map/ppermute | solution.py:13
  21.3 57.5 %collective-permute-start.1 = (bf16[10,256,512]{2,1,0:T(8,128)(2,1)S(1)}, bf16[10,256,512]{2,1,0:T(8,128)(2,1)}, u32[]{:S(2)}, u32[]{:S(2)}) collective-permute-start(bf16[10,256,512]{2,1,0:T(8,128)(2,1)S(1)} %convert_element_type.43), channel_id=1, source_target_pairs={{0,16},{8,24},{16,0},{24,8},{1,17},{9,25},{17,1},{25,9},{2,18},{10... | collective-permute-start | bytes 7864328 | tf_op jit(solution)/shard_map/ppermute | solution.py:13
  22.5 112.6 %collective-permute-start.2 = (bf16[10,256,512]{2,1,0:T(8,128)(2,1)S(1)}, bf16[10,256,512]{2,1,0:T(8,128)(2,1)}, u32[]{:S(2)}, u32[]{:S(2)}) collective-permute-start(bf16[10,256,512]{2,1,0:T(8,128)(2,1)S(1)} %convert_element_type.43), channel_id=1, source_target_pairs={{0,24},{8,16},{16,8},{24,0},{1,25},{9,17},{17,9},{25,1},{2,26},{10... | collective-permute-start | bytes 7864328 | tf_op jit(solution)/shard_map/ppermute | solution.py:13
  144.9 96.0 %all-to-all-start = ((bf16[8,10,256,64]{2,3,1,0:T(8,128)(2,1)}), bf16[8,10,256,64]{2,3,1,0:T(8,128)(2,1)S(1)}, u32[]{:S(2)}, u32[]{:S(2)}) async-start(bf16[8,10,256,64]{2,3,1,0:T(8,128)(2,1)} %convert_bitcast_fusion.3), calls=%async_computation | async-start | bytes 5242880 | tf_op jit(solution)/shard_map/all_to_all | solution.py:100
  151.5 303.1 %all-gather.8.cloned.1.call-start = ((), (), s32[]{:S(2)}) async-start(), calls=%async_computation.4 | async-start | bytes 13107200 | tf_op jit(solution)/shard_map/all_gather | solution.py:143
  353.2 10.9 %copy-start.8 = (bf16[2048,512]{0,1:T(8,128)(2,1)}, bf16[2048,512]{0,1:T(8,128)(2,1)S(1)}, u32[]{:S(2)}) copy-start(bf16[2048,512]{0,1:T(8,128)(2,1)S(1)} %copy.166) | copy-start | bytes 6291460
  353.3 71.0 %collective-permute-start.3 = (bf16[2048,1]{0,1:T(2,128)(2,1)S(1)}, bf16[2048,1]{0,1:T(2,128)(2,1)S(1)}, u32[]{:S(2)}, u32[]{:S(2)}) collective-permute-start(bf16[2048,1]{0,1:T(2,128)(2,1)S(1)} %get-tuple-element.60), channel_id=1, source_target_pairs={{0,8},{8,16},{16,24},{1,9},{9,17},{17,25},{2,10},{10,18},{18,26},{... | collective-permute-start | bytes 12296 | tf_op jit(solution)/shard_map/ppermute | solution.py:135
  356.4 67.9 %collective-permute-start.4 = (bf16[2048,1]{0,1:T(2,128)(2,1)S(1)}, bf16[2048,1]{0,1:T(2,128)(2,1)S(1)}, u32[]{:S(2)}, u32[]{:S(2)}) collective-permute-start(bf16[2048,1]{0,1:T(2,128)(2,1)S(1)} %get-tuple-element.61), channel_id=1, source_target_pairs={{8,0},{16,8},{24,16},{9,1},{17,9},{25,17},{10,2},{18,10},{26,18},{... | collective-permute-start | bytes 12296 | tf_op jit(solution)/shard_map/ppermute | solution.py:137
  374.3 5.9 %copy-start.10 = (f32[4]{0:T(128)S(1)}, f32[4]{0:T(128)}, u32[]{:S(2)}) copy-start(f32[4]{0:T(128)} %param.29) | copy-start | bytes 52
  380.9 6.8 %copy-start.6 = (s32[1,10,256,512]{2,3,1,0:T(8,128)S(1)}, s32[1,10,256,512]{2,3,1,0:T(8,128)}, u32[]{:S(2)}) copy-start(s32[1,10,256,512]{2,3,1,0:T(8,128)} %copy.194) | copy-start | bytes 15728644
  387.6 5.6 %copy-start.2 = (f32[10,256,512]{1,2,0:T(8,128)}, f32[10,256,512]{1,2,0:T(8,128)S(1)}, u32[]{:S(2)}) copy-start(f32[10,256,512]{1,2,0:T(8,128)S(1)} %select_select_fusion) | copy-start | bytes 15728644
  388.1 6.8 %copy-start.5 = (f32[10,256,512]{1,2,0:T(8,128)}, f32[10,256,512]{1,2,0:T(8,128)S(1)}, u32[]{:S(2)}) copy-start(f32[10,256,512]{1,2,0:T(8,128)S(1)} %convert_bitcast_fusion.1) | copy-start | bytes 15728644
  388.1 23.6 %collective-permute-start.5 = (f32[2,10,256,1]{2,3,1,0:T(1,128)S(1)}, f32[2,10,256,1]{2,3,1,0:T(1,128)S(1)}, u32[]{:S(2)}, u32[]{:S(2)}) collective-permute-start(f32[2,10,256,1]{2,3,1,0:T(1,128)S(1)} %pad_maximum_fusion.2), channel_id=1, source_target_pairs={{0,8},{8,16},{16,24},{1,9},{9,17},{17,25},{2,10},{10,18},{18,26},{... | collective-permute-start | bytes 61448 | tf_op jit(solution)/shard_map/ppermute | solution.py:155
  392.0 83.7 %collective-permute-start.6 = (f32[10,256,1]{1,2,0:T(1,128)S(1)}, f32[10,256,1]{1,2,0:T(1,128)S(1)}, u32[]{:S(2)}, u32[]{:S(2)}) collective-permute-start(f32[10,256,1]{1,2,0:T(1,128)S(1)} %get-tuple-element.56), channel_id=1, source_target_pairs={{8,0},{16,8},{24,16},{9,1},{17,9},{25,17},{10,2},{18,10},{26,18},{... | collective-permute-start | bytes 30728 | tf_op jit(solution)/shard_map/ppermute | solution.py:156
  403.9 2.3 copy-start.4
  407.7 11.9 %collective-permute-start.7 = (f32[2,10,1,512]{3,0,1,2:T(2,128)S(1)}, f32[2,10,1,512]{3,0,1,2:T(2,128)S(1)}, u32[]{:S(2)}, u32[]{:S(2)}) collective-permute-start(f32[2,10,1,512]{3,0,1,2:T(2,128)S(1)} %pad_maximum_fusion.1), channel_id=1, source_target_pairs={{0,1},{1,2},{2,3},{3,4},{4,5},{5,6},{6,7},{8,9},{9,10},{10,11},{11... | collective-permute-start | bytes 122888 | tf_op jit(solution)/shard_map/ppermute | solution.py:157
  411.7 42.9 %copy-start.9 = (bf16[2048,512]{0,1:T(8,128)(2,1)S(1)}, bf16[2048,512]{0,1:T(8,128)(2,1)}, u32[]{:S(2)}) copy-start(bf16[2048,512]{0,1:T(8,128)(2,1)} %copy-done.8) | copy-start | bytes 6291460
  411.7 5.6 %collective-permute-start.8 = (f32[10,1,512]{2,1,0:T(1,128)S(1)}, f32[10,1,512]{2,1,0:T(1,128)S(1)}, u32[]{:S(2)}, u32[]{:S(2)}) collective-permute-start(f32[10,1,512]{2,1,0:T(1,128)S(1)} %copy.177), channel_id=1, source_target_pairs={{1,0},{2,1},{3,2},{4,3},{5,4},{6,5},{7,6},{9,8},{10,9},{11,10},{12... | collective-permute-start | bytes 61448 | tf_op jit(solution)/shard_map/ppermute | solution.py:158
  463.6 3.2 copy-start.3
  467.5 29.0 %collective-permute-start.9 = (f32[10,1,512]{2,1,0:T(1,128)S(1)}, f32[10,1,512]{2,1,0:T(1,128)S(1)}, u32[]{:S(2)}, u32[]{:S(2)}) collective-permute-start(f32[10,1,512]{2,1,0:T(1,128)S(1)} %copy.179), channel_id=1, source_target_pairs={{0,1},{1,2},{2,3},{3,4},{4,5},{5,6},{6,7},{8,9},{9,10},{10,11},{11... | collective-permute-start | bytes 61448 | tf_op jit(solution)/shard_map/ppermute | solution.py:169
  471.1 16.7 %slice-start = ((s8[5324800]{0:T(1024)(128)(4,1)}), s8[1130496]{0:T(1024)(128)(4,1)S(1)}, s32[]{:S(2)}) async-start(s8[5324800]{0:T(1024)(128)(4,1)} %bitcast.70), calls=%async_computation.5 | async-start | bytes 2260992
  473.7 25.1 %collective-permute-start.10 = (f32[10,1,512]{2,1,0:T(1,128)S(1)}, f32[10,1,512]{2,1,0:T(1,128)S(1)}, u32[]{:S(2)}, u32[]{:S(2)}) collective-permute-start(f32[10,1,512]{2,1,0:T(1,128)S(1)} %copy.181), channel_id=1, source_target_pairs={{1,0},{2,1},{3,2},{4,3},{5,4},{6,5},{7,6},{9,8},{10,9},{11,10},{12... | collective-permute-start | bytes 61448 | tf_op jit(solution)/shard_map/ppermute | solution.py:170
  475.6 12.1 %slice-start.1 = ((s8[5324800]{0:T(1024)(128)(4,1)}), s8[4194304]{0:T(1024)(128)(4,1)S(1)}, s32[]{:S(2)}) async-start(s8[5324800]{0:T(1024)(128)(4,1)} %bitcast.70), calls=%async_computation.6 | async-start | bytes 8388608
  496.5 4.6 copy-start.7
  517.8 16.9 %copy-start.1 = (f32[512]{0:T(512)S(1)}, f32[512]{0:T(512)}, u32[]{:S(2)}) copy-start(f32[512]{0:T(512)} %param.19) | copy-start | bytes 6148
Sparse Core Ops, SparseCore 0:
  15.7 88.8 all-gather.3
  106.2 124.0 all-gather.5
  350.4 104.1 all-gather.7

commit v10 on v5

--- a/solution.py
+++ b/solution.py
@@ -51,8 +51,8 @@
 
 
 def thomas_solve(rhs, lambda_x, lambda_y, coupling, layer_shift):
-    layers, rows, modes = rhs.shape
-    tile = min(rows, 256)
+    layers, modes, rows = rhs.shape
+    tile = min(rows, 512)
     smem = pl.BlockSpec(memory_space=pltpu.SMEM)
     return pl.pallas_call(
         thomas_kernel,
@@ -60,13 +60,13 @@
         in_specs=[
             smem,
             smem,
-            pl.BlockSpec((tile, 1), lambda j: (j, 0)),
-            pl.BlockSpec((1, modes), lambda j: (0, 0)),
-            pl.BlockSpec((layers, tile, modes), lambda j: (0, j, 0)),
+            pl.BlockSpec((1, tile), lambda j: (0, j)),
+            pl.BlockSpec((modes, 1), lambda j: (0, 0)),
+            pl.BlockSpec((layers, modes, tile), lambda j: (0, 0, j)),
         ],
-        out_specs=pl.BlockSpec((layers, tile, modes), lambda j: (0, j, 0)),
+        out_specs=pl.BlockSpec((layers, modes, tile), lambda j: (0, 0, j)),
         out_shape=jax.ShapeDtypeStruct(rhs.shape, jnp.bfloat16),
-    )(coupling, layer_shift, lambda_y.reshape(rows, 1), lambda_x.reshape(1, modes), rhs)
+    )(coupling, layer_shift, lambda_y.reshape(1, rows), lambda_x.reshape(modes, 1), rhs)
 
 
 def shards(
@@ -107,22 +107,24 @@
     pieces = pieces.at[:, 0].set(high).at[:, 1].set(middle).at[:, 2].set(low)
     carried = lax.all_gather(jnp.concatenate([left_y, pieces], axis=1), "py", axis=0, tiled=True)
     columns = left_y.shape[1]
+    flat = jnp.transpose(pencil, (1, 3, 0, 2)).reshape(layers * modes, -1)
     spectral = jnp.einsum(
-        "jsy,szyi->zji",
-        carried[:, :columns].reshape(-1, count_y, height),
-        pencil,
+        "ny,jy->nj",
+        flat,
+        carried[:, :columns],
         preferred_element_type=jnp.float32,
-    )
+    ).reshape(layers, modes, -1)
     own_x = lax.dynamic_slice_in_dim(lambda_x, at_y * modes, modes)
     got = carried[:, columns:columns + 3].astype(jnp.float32)
     all_y = got[:, 0] + (got[:, 1] + got[:, 2])
     solved = thomas_solve(spectral, own_x, all_y, coupling, layer_shift)
-    back_pencil = jnp.einsum(
-        "syj,zji->szyi",
-        lax.all_gather(right_y, "py", axis=0, tiled=True).reshape(count_y, height, -1),
-        solved,
+    back_flat = jnp.einsum(
+        "nj,yj->ny",
+        solved.reshape(layers * modes, -1),
+        lax.all_gather(right_y, "py", axis=0, tiled=True),
         preferred_element_type=jnp.float32,
     ).astype(jnp.bfloat16)
+    back_pencil = jnp.transpose(back_flat.reshape(layers, modes, count_y, height), (2, 0, 3, 1))
     back_y = lax.all_to_all(back_pencil, "py", 0, 0, tiled=True)
     back_y = jnp.moveaxis(back_y, 0, 2).reshape(layers, height, -1)
     correction = jnp.einsum(

time: 537 us -> 518 us (0.965); the launches traced: 528 us -> 516 us
  waiting for transfers between devices: 245 us -> 266 us
  local copies, waits for them, and re-layouts: 69.9 us -> 56.1 us
  matrix products: 52.1 us -> 39.2 us
    all_to_all x1, waiting for transfers between devices: 65.1 us -> 86.3 us  [shards(): pencil = lax.all_to_all(spectral_x, 'py', 0, 0, tiled=True)]
    dot_general x2, matrix products: 33.7 us -> 20.8 us  [the longest x1 11.1 us: shards(): jnp.einsum('ny,jy->nj', flat, carried[:, :columns], preferred_element_typ...]
    slice x1 -> x0, local copies, waits for them, and re-layouts: 8.29 us -> none  [shards(): carried[:, :columns].reshape(-1, count_y, height)]
    unnamed x13 -> x17, local copies, waits for them, and re-layouts: 11.1 us -> 6.89 us
  transfers between devices with their start and end apart: 11 -> 11, of which waited for: 5 -> 5; matrix products, arithmetic and copies ran while one was open for 19% -> 16% of each run, Pallas kernels for 2% -> 1%
where the time goes in v10:
time: 518 us; the launch traced here: 516 us
  waiting for transfers between devices  266 us (51%)
  blocking collectives  62.2 us (12%)
  local copies, waits for them, and re-layouts  56.1 us (11%)
  other arithmetic  50.7 us (10%)
  matrix products  39.2 us (8%)
  starting transfers between devices  22.2 us (4%)
  between operations  14.1 us (3%)
  Pallas kernels  5.82 us (1%)
    ppermute x3, waiting for transfers between devices, exchange(): parts.append(lax.ppermute(block, axis, [(s, s ^ k) for s in range(count)]))  105 us
    all_to_all x1, waiting for transfers between devices, shards(): pencil = lax.all_to_all(spectral_x, 'py', 0, 0, tiled=True)  86.3 us
    all_gather x1, waiting for transfers between devices, shards(): lax.all_gather(back_y, 'px', axis=2, tiled=True)  74.6 us
    all_to_all x1, blocking collectives, shards(): back_y = lax.all_to_all(back_pencil, 'py', 0, 0, tiled=True)  62.2 us
    select_n x1, other arithmetic, net(): flux_high = jnp.where(edge, 0.0, flux_high)  16.4 us
    slice x4, local copies, waits for them, and re-layouts, net(): rest = lambda a: lax.slice_in_dim(a, 1, None, axis=dim)  13.8 us
    dot_general x1, matrix products, shards(): jnp.einsum('ny,jy->nj', flat, carried[:, :columns], preferred_element_typ...  11.1 us
  transfers between devices with their start and end apart: 11, of which 5 were waited for; matrix products, arithmetic and copies ran while one was open for 16% of the time, Pallas kernels for 1%

profile of v10, /device:TPU:1, one launch (start us, length us, event | category | flops | bytes accessed | tf_op | source)
XLA Modules:
  0.0 516.5 jit_solution(11679086646156760020)
XLA Ops:
  13.2 2.4 pad_maximum_fusion
  16.4 4.3 convert_element_type.34
  20.7 2.0 collective-permute-start
  24.0 2.9 constant_dynamic-slice_fusion.3
  26.9 2.1 copy.250
  29.0 2.0 copy.251
  32.3 47.4 %collective-permute-done = bf16[10,256,512]{2,1,0:T(8,128)(2,1)} collective-permute-done((bf16[10,256,512]{2,1,0:T(8,128)(2,1)}, bf16[10,256,512]{2,1,0:T(8,128)(2,1)}, u32[]{:S(2)}, u32[]{:S(2)}) %collective-permute-start) | collective-permute-done | bytes 2621472 | tf_op jit(solution)/shard_map/ppermute | solution.py:13
  80.5 56.3 %collective-permute-done.2 = bf16[10,256,512]{2,1,0:T(8,128)(2,1)} collective-permute-done((bf16[10,256,512]{2,1,0:T(8,128)(2,1)}, bf16[10,256,512]{2,1,0:T(8,128)(2,1)}, u32[]{:S(2)}, u32[]{:S(2)}) %collective-permute-start.2) | collective-permute-done | bytes 2621472 | tf_op jit(solution)/shard_map/ppermute | solution.py:13
  136.8 9.8 %convert_bitcast_fusion = bf16[8,10,256,64]{2,3,1,0:T(8,128)(2,1)} fusion(bf16[10,256,512]{2,1,0:T(8,128)(2,1)} %collective-permute-done.2, bf16[10,256,512]{2,1,0:T(8,128)(2,1)} %collective-permute-done.1, bf16[10,256,512]{2,1,0:T(8,128)(2,1)} %collective-permute-done, bf16[10,256,512]{2,1,0:T(8,128)(2,1)} %convert_element_type.34, ...), kind=kOutput, calls=%fused_computation.26 | convolution fusion | flops 5420351488 | bytes 15204352 | tf_op jit(solution)/shard_map/zyx,xci->czyi/dot_general | solution.py:94
  146.6 6.7 %all-to-all-start = ((bf16[8,10,256,64]{2,3,1,0:T(8,128)(2,1)}), bf16[8,10,256,64]{2,3,1,0:T(8,128)(2,1)}, u32[]{:S(2)}, u32[]{:S(2)}) async-start(bf16[8,10,256,64]{2,3,1,0:T(8,128)(2,1)} %convert_bitcast_fusion), calls=%async_computation | async-start | bytes 5242880 | tf_op jit(solution)/shard_map/all_to_all | solution.py:100
  154.8 86.3 %all-to-all-done = bf16[8,10,256,64]{2,3,1,0:T(8,128)(2,1)} async-done(((bf16[8,10,256,64]{2,3,1,0:T(8,128)(2,1)}), bf16[8,10,256,64]{2,3,1,0:T(8,128)(2,1)}, u32[]{:S(2)}, u32[]{:S(2)}) %all-to-all-start) | async-done | bytes 2621472 | tf_op jit(solution)/shard_map/all_to_all | solution.py:100
  241.1 3.6 copy.255
  247.3 11.1 %fusion.7.rhs_ref = f32[10,64,2048]{2,1,0:T(8,128)} fusion(bf16[10,64,2048]{2,1,0:T(8,128)(2,1)} %bitcast.100, bf16[2048,2176]{1,0:T(8,128)(2,1)} %all-gather.4.cloned.1.call-done), kind=kOutput, calls=%fused_computation.9 | convolution fusion | flops 5368709120 | bytes 16252928 | tf_op jit(solution)/shard_map/ny,jy->nj/dot_general | solution.py:111
  258.5 5.8 %shard_map.131 = bf16[10,64,2048]{2,1,0:T(8,128)(2,1)} custom-call(f32[9]{0:T(128)} %coupling_ref.1, f32[10]{0:T(128)} %shift_ref.1, f32[1,2048]{1,0:T(1,128)} %bitcast.107, f32[64,1]{1,0:T(8,128)} %copy.238.lx_ref, f32[10,64,2048]{2,1,0:T(8,128)} %fusion.7.rhs_ref), custom_call_target="tpu_custom_call" | custom-call | tf_op jit(solution)/shard_map/pallas_call | solution.py:57
  264.3 9.6 %convolution_convert_fusion = bf16[640,2048]{1,0:T(8,128)(2,1)S(1)} fusion(bf16[640,2048]{1,0:T(8,128)(2,1)} %bitcast.99, bf16[2048,2048]{1,0:T(8,128)(2,1)} %all-gather.6.cloned.1.call-done), kind=kOutput, calls=%fused_computation.24 | convolution fusion | flops 5370019840 | bytes 13631488 | tf_op jit(solution)/shard_map/nj,yj->ny/dot_general | solution.py:121
  275.4 62.2 %all_to_all.10 = bf16[8,10,256,64]{2,3,1,0:T(8,128)(2,1)S(1)} all-to-all(bf16[8,10,256,64]{2,3,1,0:T(8,128)(2,1)S(1)} %bitcast.97), channel_id=1, replica_groups=mesh['px'=4,'py'=8] {'py'}, dimensions={0} | all-to-all | bytes 5242880 | tf_op jit(solution)/shard_map/all_to_all | solution.py:128
  339.4 4.4 copy.241
  344.5 6.4 %select_select_fusion = f32[10,256,512]{2,1,0:T(8,128)S(1)} fusion(s32[10,256,512]{2,1,0:T(8,128)} %param.27, f32[]{:T(128)} %bitcast.21, f32[]{:T(128)} %bitcast.20, f32[]{:T(128)} %bitcast.19, f32[]{:T(128)} %bitcast.18), kind=kLoop, calls=%fused_computation.22 | loop fusion | flops 10485760 | bytes 10485776 | tf_op jit(solution)/shard_map/jit(_where)/select_n | solution.py:139
  350.9 4.0 slice.205
  355.5 3.0 slice.218
  358.6 3.0 slice_reduce_fusion
  361.6 8.3 %slice_bitcast_fusion.2 = (s32[10,256,512]{2,1,0:T(8,128)}, s32[10,256,512]{2,1,0:T(8,128)S(1)}) fusion(s32[2,10,256,512]{3,2,1,0:T(8,128)} %param.28), kind=kLoop, calls=%fused_computation.21 | loop fusion | bytes 20971520 | tf_op jit(solution)/shard_map/squeeze | solution.py:141
  373.6 74.6 %all-gather.8.cloned.1.call-done = bf16[10,256,2048]{2,1,0:T(8,128)(2,1)} async-done(((bf16[10,256,512]{2,1,0:T(8,128)(2,1)}), bf16[10,256,2048]{2,1,0:T(8,128)(2,1)}) %all-gather.8.cloned.1.call-update) | async-done | bytes 10485776 | tf_op jit(solution)/shard_map/all_gather | solution.py:132
  448.1 8.6 %fusion.19 = f32[10,256,512]{2,1,0:T(8,128)S(1)} fusion(bf16[10,256,2048]{2,1,0:T(8,128)(2,1)} %all-gather.8.cloned.1.call-done, bf16[2048,512]{1,0:T(8,128)(2,1)S(1)} %copy-done), kind=kOutput, calls=%fused_computation.34 | convolution fusion | flops 5368709120 | bytes 17825792 | tf_op jit(solution)/shard_map/zyi,ix->zyx/dot_general | solution.py:130
  457.9 3.7 slice.209
  461.6 3.0 slice.222
  465.3 3.7 collective-permute-start.4
  470.4 4.0 collective-permute-start.6
  483.0 3.2 collective-permute-start.5
  486.2 2.8 multiply_select_fusion
  489.0 16.4 %fusion.12 = (f32[10,256,512]{2,1,0:T(8,128)S(1)}, f32[10,256,512]{2,1,0:T(8,128)S(1)}) fusion(f32[10,1,512]{2,1,0:T(1,128)S(1)} %get-tuple-element.54, f32[10,255,512]{2,1,0:T(8,128)} %slice.218, f32[10,256,512]{2,1,0:T(8,128)S(1)} %copy-done.2, f32[10,1,512]{2,1,0:T(1,128)S(1)} %get-tuple-element.53, f32[10,255,512]{2,1,0:T(8,128)} %slice.222, ...), kind=kLoop, calls=%fused_computation.18 | loop fusion | flops 28835840 | bytes 52429584 | tf_op jit(solution)/shard_map/jit(_where)/select_n | solution.py:159
  505.4 4.5 fusion.10
  (76 shorter events, 34.2 us)
Async XLA Ops:
  7.2 441.0 %copy-start = (bf16[2048,512]{1,0:T(8,128)(2,1)S(1)}, bf16[2048,512]{1,0:T(8,128)(2,1)}, u32[]{:S(2)}) copy-start(bf16[2048,512]{1,0:T(8,128)(2,1)} %param.26) | copy-start | bytes 6291460
  7.2 237.6 %all-gather.4.cloned.1.call-start = ((), (), s32[]{:S(2)}) async-start(), calls=%async_computation.2 | async-start | bytes 10027008 | tf_op jit(solution)/shard_map/all_gather | solution.py:108
  15.6 248.6 %all-gather.6.cloned.1.call-start = ((), (), s32[]{:S(2)}) async-start(), calls=%async_computation.3 | async-start | bytes 9437184 | tf_op jit(solution)/shard_map/all_gather | solution.py:124
  20.7 58.9 %collective-permute-start = (bf16[10,256,512]{2,1,0:T(8,128)(2,1)}, bf16[10,256,512]{2,1,0:T(8,128)(2,1)}, u32[]{:S(2)}, u32[]{:S(2)}) collective-permute-start(bf16[10,256,512]{2,1,0:T(8,128)(2,1)} %convert_element_type.34), channel_id=1, source_target_pairs={{0,8},{8,0},{16,24},{24,16},{1,9},{9,1},{17,25},{25,17},{2,10},{10... | collective-permute-start | bytes 7864328 | tf_op jit(solution)/shard_map/ppermute | solution.py:13
  22.8 57.7 %collective-permute-start.1 = (bf16[10,256,512]{2,1,0:T(8,128)(2,1)}, bf16[10,256,512]{2,1,0:T(8,128)(2,1)}, u32[]{:S(2)}, u32[]{:S(2)}) collective-permute-start(bf16[10,256,512]{2,1,0:T(8,128)(2,1)} %convert_element_type.34), channel_id=1, source_target_pairs={{0,16},{8,24},{16,0},{24,8},{1,17},{9,25},{17,1},{25,9},{2,18},{10... | collective-permute-start | bytes 7864328 | tf_op jit(solution)/shard_map/ppermute | solution.py:13
  24.0 112.8 %collective-permute-start.2 = (bf16[10,256,512]{2,1,0:T(8,128)(2,1)}, bf16[10,256,512]{2,1,0:T(8,128)(2,1)}, u32[]{:S(2)}, u32[]{:S(2)}) collective-permute-start(bf16[10,256,512]{2,1,0:T(8,128)(2,1)} %convert_element_type.34), channel_id=1, source_target_pairs={{0,24},{8,16},{16,8},{24,0},{1,25},{9,17},{17,9},{25,1},{2,26},{10... | collective-permute-start | bytes 7864328 | tf_op jit(solution)/shard_map/ppermute | solution.py:13
  146.6 94.5 %all-to-all-start = ((bf16[8,10,256,64]{2,3,1,0:T(8,128)(2,1)}), bf16[8,10,256,64]{2,3,1,0:T(8,128)(2,1)}, u32[]{:S(2)}, u32[]{:S(2)}) async-start(bf16[8,10,256,64]{2,3,1,0:T(8,128)(2,1)} %convert_bitcast_fusion), calls=%async_computation | async-start | bytes 5242880 | tf_op jit(solution)/shard_map/all_to_all | solution.py:100
  153.3 294.8 %all-gather.8.cloned.1.call-start = ((), (), s32[]{:S(2)}) async-start(), calls=%async_computation.4 | async-start | bytes 13107200 | tf_op jit(solution)/shard_map/all_gather | solution.py:132
  339.4 4.4 copy-start.5
  350.9 4.6 copy-start.3
  456.7 4.9 copy-start.1
  465.3 11.1 %collective-permute-start.4 = (f32[3,10,256,1]{2,0,1,3:T(4,128)}, f32[3,10,256,1]{2,0,1,3:T(4,128)}, u32[]{:S(2)}, u32[]{:S(2)}) collective-permute-start(f32[3,10,256,1]{2,0,1,3:T(4,128)} %pad_maximum_fusion.2), channel_id=1, source_target_pairs={{0,8},{8,16},{16,24},{1,9},{9,17},{17,25},{2,10},{10,18},{18,26},{... | collective-permute-start | bytes 92168 | tf_op jit(solution)/shard_map/ppermute | solution.py:151
  469.0 5.3 %collective-permute-start.3 = (f32[2,10,256,1]{2,0,1,3:T(2,128)S(1)}, f32[2,10,256,1]{2,0,1,3:T(2,128)S(1)}, u32[]{:S(2)}, u32[]{:S(2)}) collective-permute-start(f32[2,10,256,1]{2,0,1,3:T(2,128)S(1)} %pad_maximum_fusion.4), channel_id=1, source_target_pairs={{8,0},{16,8},{24,16},{9,1},{17,9},{25,17},{10,2},{18,10},{26,18},{... | collective-permute-start | bytes 61448 | tf_op jit(solution)/shard_map/ppermute | solution.py:150
  470.4 11.0 %collective-permute-start.6 = (f32[3,10,1,512]{3,2,1,0:T(1,128)S(1)}, f32[3,10,1,512]{3,2,1,0:T(1,128)S(1)}, u32[]{:S(2)}, u32[]{:S(2)}) collective-permute-start(f32[3,10,1,512]{3,2,1,0:T(1,128)S(1)} %pad_maximum_fusion.1), channel_id=1, source_target_pairs={{0,1},{1,2},{2,3},{3,4},{4,5},{5,6},{6,7},{8,9},{9,10},{10,11},{11... | collective-permute-start | bytes 184328 | tf_op jit(solution)/shard_map/ppermute | solution.py:151
  480.3 8.7 %copy-start.2 = (f32[10,256,512]{2,1,0:T(8,128)S(1)}, f32[10,256,512]{2,1,0:T(8,128)}, u32[]{:S(2)}) copy-start(f32[10,256,512]{2,1,0:T(8,128)} %copy-done.1) | copy-start | bytes 15728644
  480.3 8.7 %copy-start.4 = (f32[10,256,1]{2,1,0:T(8,128)S(1)}, f32[10,256,1]{2,1,0:T(8,128)}, u32[]{:S(2)}) copy-start(f32[10,256,1]{2,1,0:T(8,128)} %copy.243) | copy-start | bytes 30724
  483.0 6.0 %collective-permute-start.5 = (f32[2,10,1,512]{3,2,1,0:T(1,128)S(1)}, f32[2,10,1,512]{3,2,1,0:T(1,128)S(1)}, u32[]{:S(2)}, u32[]{:S(2)}) collective-permute-start(f32[2,10,1,512]{3,2,1,0:T(1,128)S(1)} %pad_maximum_fusion.3), channel_id=1, source_target_pairs={{1,0},{2,1},{3,2},{4,3},{5,4},{6,5},{7,6},{9,8},{10,9},{11,10},{12... | collective-permute-start | bytes 122888 | tf_op jit(solution)/shard_map/ppermute | solution.py:150
Sparse Core Ops, SparseCore 0:
  15.8 88.8 all-gather.3
  106.3 107.9 all-gather.5
  343.9 104.1 all-gather.7

commit v11 on v10

--- a/solution.py
+++ b/solution.py
@@ -147,17 +147,19 @@
         last = lambda a: lax.slice_in_dim(a, a.shape[dim] - 1, None, axis=dim)
         rest = lambda a: lax.slice_in_dim(a, 1, None, axis=dim)
         head = lambda a: lax.slice_in_dim(a, 0, a.shape[dim] - 1, axis=dim)
-        high = lax.ppermute(jnp.stack([first(correction), first(mobility)]), axis, backward)
-        low = lax.ppermute(
-            jnp.stack([last(correction), last(mobility), last(flag).astype(jnp.float32)]), axis, forward
+        mobil_high = lax.ppermute(first(mobility), axis, backward)
+        mobil_low, flag_low = lax.ppermute(
+            (last(mobility), last(flag).astype(jnp.float32)), axis, forward
         )
-        press_next = jnp.concatenate([rest(correction), high[0]], axis=dim)
-        mobil_next = jnp.concatenate([rest(mobility), high[1]], axis=dim)
+        press_high = lax.ppermute(first(correction), axis, backward)
+        press_low = lax.ppermute(last(correction), axis, forward)
+        press_next = jnp.concatenate([rest(correction), press_high], axis=dim)
+        mobil_next = jnp.concatenate([rest(mobility), mobil_high], axis=dim)
         flux_high = jnp.where(flag == 1, mobility, mobil_next) * (correction - press_next)
         place = lax.broadcasted_iota(jnp.int32, correction.shape, dim)
         edge = (at == count - 1) & (place == correction.shape[dim] - 1)
         flux_high = jnp.where(edge, 0.0, flux_high)
-        flux_edge = jnp.where(low[2] > 0.5, low[1], first(mobility)) * (low[0] - first(correction))
+        flux_edge = jnp.where(flag_low > 0.5, mobil_low, first(mobility)) * (press_low - first(correction))
         flux_edge = jnp.where(at == 0, 0.0, flux_edge)
         flux_low = jnp.concatenate([flux_edge, head(flux_high)], axis=dim)
         return flux_high - flux_low

time: 518 us -> 580 us (1.12); the launches traced: 516 us -> 572 us
  local copies, waits for them, and re-layouts: 56.1 us -> 111 us
  waiting for transfers between devices: 266 us -> 233 us
  other arithmetic: 50.7 us -> 71.3 us
  starting transfers between devices: 22.2 us -> 35.3 us
    all_gather x1, waiting for transfers between devices: 74.6 us -> 41.1 us  [shards(): lax.all_gather(back_y, 'px', axis=2, tiled=True)]
    unnamed x17 -> x21, local copies, waits for them, and re-layouts: 6.89 us -> 34.7 us
    slice x1 -> x3, local copies, waits for them, and re-layouts: 0.01 us -> 14.9 us  [the longest x1 9.9 us: shards(): flag_y = upwind_flag[1]]
    squeeze x8 -> x0, local copies, waits for them, and re-layouts: 14.3 us -> none  [the longest x1 8.29 us: shards(): flag_y = upwind_flag[1]]
    ppermute x4 -> x10, starting transfers between devices: 12.1 us -> 25.1 us  [the longest x4 11.4 us: net(): lax.ppermute((last(mobility), last(flag).astype(jnp.float32)), axis, forw...]
    ppermute x0 -> x4, local copies, waits for them, and re-layouts: none -> 9.12 us  [the longest x1 2.31 us: net(): mobil_high = lax.ppermute(first(mobility), axis, backward)]
    select_n x1, other arithmetic: 16.4 us -> 24.9 us  [net(): flux_high = jnp.where(edge, 0.0, flux_high)]
    add x1, other arithmetic: 4.52 us -> 11.3 us  [shards(): net('px', 2, flag_x, at_x, count_x) + net('py', 1, flag_y, at_y, count_y)]
  transfers between devices with their start and end apart: 11 -> 17, of which waited for: 5 -> 5; matrix products, arithmetic and copies ran while one was open for 16% -> 26% of each run, Pallas kernels for 1% -> 1%
where the time goes in v11:
time: 580 us; the launch traced here: 572 us
  waiting for transfers between devices  233 us (40%)
  local copies, waits for them, and re-layouts  111 us (19%)
  other arithmetic  71.3 us (12%)
  blocking collectives  62.2 us (11%)
  matrix products  38.9 us (7%)
  starting transfers between devices  35.3 us (6%)
  between operations  14.5 us (2%)
  Pallas kernels  5.82 us (1%)
    ppermute x3, waiting for transfers between devices, exchange(): parts.append(lax.ppermute(block, axis, [(s, s ^ k) for s in range(count)]))  105 us
    all_to_all x1, waiting for transfers between devices, shards(): pencil = lax.all_to_all(spectral_x, 'py', 0, 0, tiled=True)  86.2 us
    all_to_all x1, blocking collectives, shards(): back_y = lax.all_to_all(back_pencil, 'py', 0, 0, tiled=True)  62.2 us
    all_gather x1, waiting for transfers between devices, shards(): lax.all_gather(back_y, 'px', axis=2, tiled=True)  41.1 us
    unnamed x21, local copies, waits for them, and re-layouts  34.7 us
    select_n x1, other arithmetic, net(): flux_high = jnp.where(edge, 0.0, flux_high)  24.9 us
    slice x4, local copies, waits for them, and re-layouts, net(): rest = lambda a: lax.slice_in_dim(a, 1, None, axis=dim)  18.4 us
  transfers between devices with their start and end apart: 17, of which 5 were waited for; matrix products, arithmetic and copies ran while one was open for 26% of the time, Pallas kernels for 1%

profile of v11, /device:TPU:1, one launch (start us, length us, event | category | flops | bytes accessed | tf_op | source)
XLA Modules:
  0.0 571.6 jit_solution(2654372778011971734)
XLA Ops:
  16.6 4.3 convert_element_type.34
  32.5 47.4 %collective-permute-done = bf16[10,256,512]{2,1,0:T(8,128)(2,1)} collective-permute-done((bf16[10,256,512]{2,1,0:T(8,128)(2,1)}, bf16[10,256,512]{2,1,0:T(8,128)(2,1)}, u32[]{:S(2)}, u32[]{:S(2)}) %collective-permute-start) | collective-permute-done | bytes 2621472 | tf_op jit(solution)/shard_map/ppermute | solution.py:13
  80.7 56.3 %collective-permute-done.2 = bf16[10,256,512]{2,1,0:T(8,128)(2,1)} collective-permute-done((bf16[10,256,512]{2,1,0:T(8,128)(2,1)}, bf16[10,256,512]{2,1,0:T(8,128)(2,1)}, u32[]{:S(2)}, u32[]{:S(2)}) %collective-permute-start.2) | collective-permute-done | bytes 2621472 | tf_op jit(solution)/shard_map/ppermute | solution.py:13
  137.0 9.8 %convert_bitcast_fusion = bf16[8,10,256,64]{2,3,1,0:T(8,128)(2,1)} fusion(bf16[10,256,512]{2,1,0:T(8,128)(2,1)} %collective-permute-done.2, bf16[10,256,512]{2,1,0:T(8,128)(2,1)} %collective-permute-done.1, bf16[10,256,512]{2,1,0:T(8,128)(2,1)} %collective-permute-done, bf16[10,256,512]{2,1,0:T(8,128)(2,1)} %convert_element_type.34, ...), kind=kOutput, calls=%fused_computation.26 | convolution fusion | flops 5420351488 | bytes 15204352 | tf_op jit(solution)/shard_map/zyx,xci->czyi/dot_general | solution.py:94
  146.8 6.7 %all-to-all-start = ((bf16[8,10,256,64]{2,3,1,0:T(8,128)(2,1)}), bf16[8,10,256,64]{2,3,1,0:T(8,128)(2,1)}, u32[]{:S(2)}, u32[]{:S(2)}) async-start(bf16[8,10,256,64]{2,3,1,0:T(8,128)(2,1)} %convert_bitcast_fusion), calls=%async_computation | async-start | bytes 5242880 | tf_op jit(solution)/shard_map/all_to_all | solution.py:100
  155.2 86.2 %all-to-all-done = bf16[8,10,256,64]{2,3,1,0:T(8,128)(2,1)} async-done(((bf16[8,10,256,64]{2,3,1,0:T(8,128)(2,1)}), bf16[8,10,256,64]{2,3,1,0:T(8,128)(2,1)}, u32[]{:S(2)}, u32[]{:S(2)}) %all-to-all-start) | async-done | bytes 2621472 | tf_op jit(solution)/shard_map/all_to_all | solution.py:100
  241.3 3.6 copy.124
  247.5 11.1 %fusion.7.rhs_ref = f32[10,64,2048]{2,1,0:T(8,128)} fusion(bf16[10,64,2048]{2,1,0:T(8,128)(2,1)} %bitcast.65, bf16[2048,2176]{1,0:T(8,128)(2,1)} %all-gather.4.cloned.1.call-done), kind=kOutput, calls=%fused_computation.9 | convolution fusion | flops 5368709120 | bytes 16252928 | tf_op jit(solution)/shard_map/ny,jy->nj/dot_general | solution.py:111
  258.6 5.8 %shard_map.131 = bf16[10,64,2048]{2,1,0:T(8,128)(2,1)} custom-call(f32[9]{0:T(128)} %coupling_ref.1, f32[10]{0:T(128)} %shift_ref.1, f32[1,2048]{1,0:T(1,128)} %bitcast.72, f32[64,1]{1,0:T(8,128)} %copy.89.lx_ref, f32[10,64,2048]{2,1,0:T(8,128)} %fusion.7.rhs_ref), custom_call_target="tpu_custom_call" | custom-call | tf_op jit(solution)/shard_map/pallas_call | solution.py:57
  264.5 9.6 %convolution_convert_fusion = bf16[640,2048]{1,0:T(8,128)(2,1)S(1)} fusion(bf16[640,2048]{1,0:T(8,128)(2,1)} %bitcast.64, bf16[2048,2048]{1,0:T(8,128)(2,1)} %all-gather.6.cloned.1.call-done), kind=kOutput, calls=%fused_computation.22 | convolution fusion | flops 5370019840 | bytes 13631488 | tf_op jit(solution)/shard_map/nj,yj->ny/dot_general | solution.py:121
  275.6 62.2 %all_to_all.10 = bf16[8,10,256,64]{2,3,1,0:T(8,128)(2,1)S(1)} all-to-all(bf16[8,10,256,64]{2,3,1,0:T(8,128)(2,1)S(1)} %bitcast.62), channel_id=1, replica_groups=mesh['px'=4,'py'=8] {'py'}, dimensions={0} | all-to-all | bytes 5242880 | tf_op jit(solution)/shard_map/all_to_all | solution.py:128
  339.6 4.3 copy.92
  344.0 5.9 %copy.94 = s32[10,256,512]{1,2,0:T(8,128)} copy(s32[10,256,512]{2,1,0:T(8,128)} %param.27) | data formatting | bytes 10485760 | tf_op args[9]
  350.6 6.8 %select_select_fusion = f32[10,256,512]{1,2,0:T(8,128)S(1)} fusion(s32[10,256,512]{1,2,0:T(8,128)} %copy.94, f32[]{:T(128)} %bitcast.21, f32[]{:T(128)} %bitcast.20, f32[]{:T(128)} %bitcast.19, f32[]{:T(128)} %bitcast.18), kind=kLoop, calls=%fused_computation.21 | loop fusion | flops 10485760 | bytes 10485776 | tf_op jit(solution)/shard_map/jit(_where)/select_n | solution.py:139
  359.8 3.4 collective-permute-start.6
  363.2 9.9 %fusion.28 = (s32[1,10,256,512]{3,2,1,0:T(8,128)}, s32[1,10,256,512]{3,2,1,0:T(8,128)}) fusion(s32[2,10,256,512]{3,2,1,0:T(8,128)} %param.28), kind=kLoop, calls=%fused_computation.68 | loop fusion | bytes 20971520 | tf_op jit(solution)/shard_map/slice | solution.py:141
  373.1 5.9 %copy.122 = s32[1,10,256,512]{2,3,1,0:T(8,128)} copy(s32[1,10,256,512]{3,2,1,0:T(8,128)} %get-tuple-element.45) | data formatting | bytes 10485760
  379.8 3.1 collective-permute-start.5
  382.9 4.0 slice.178
  392.5 6.0 %copy.123 = s32[1,10,256,512]{2,3,1,0:T(8,128)} copy(s32[1,10,256,512]{3,2,1,0:T(8,128)} %get-tuple-element.44) | data formatting | bytes 10485760
  398.5 4.1 slice_convert_fusion
  407.1 41.1 %all-gather.8.cloned.1.call-done = bf16[10,256,2048]{2,1,0:T(8,128)(2,1)} async-done(((bf16[10,256,512]{2,1,0:T(8,128)(2,1)}), bf16[10,256,2048]{2,1,0:T(8,128)(2,1)}) %all-gather.8.cloned.1.call-update) | async-done | bytes 10485776 | tf_op jit(solution)/shard_map/all_gather | solution.py:132
  448.3 8.3 %fusion.19 = f32[10,256,512]{2,1,0:T(8,128)S(1)} fusion(bf16[10,256,2048]{2,1,0:T(8,128)(2,1)} %all-gather.8.cloned.1.call-done, bf16[2048,512]{1,0:T(8,128)(2,1)S(1)} %copy-done), kind=kOutput, calls=%fused_computation.34 | convolution fusion | flops 5368709120 | bytes 17825792 | tf_op jit(solution)/shard_map/zyi,ix->zyx/dot_general | solution.py:130
  466.2 5.9 %copy.100 = f32[10,256,512]{1,2,0:T(8,128)} copy(f32[10,256,512]{2,1,0:T(8,128)} %copy-done.2) | data formatting | bytes 10485760 | tf_op jit(solution)/shard_map/zyi,ix->zyx/dot_general | solution.py:130
  473.0 3.9 collective-permute-start.12
  482.8 7.6 %multiply_select_fusion = (f32[10,1,512]{1,2,0:T(8,128)}, f32[10,1,512]{1,2,0:T(8,128)}, f32[10,1,512]{1,2,0:T(8,128)}) fusion(f32[10,1,512]{1,2,0:T(8,128)} %copy.115, pred[10,1,512]{1,2,0:T(8,128)(4,1)S(1)} %copy.113, f32[10,1,512]{1,2,0:T(8,128)} %copy.114, pred[]{:T(512)S(6)} %eq.69, f32[10,256,512]{1,2,0:T(8,128)} %copy.100, f32[10,256,512]{1,2,0:T(8,128)} %copy-done.1), kind=kLoop, calls=%fused_computation.25 | loop fusion | flops 20480 | bytes 148481 | tf_op jit(solution)/shard_map/jit(_where)/select_n | solution.py:163
  499.5 5.6 slice.165
  505.1 6.3 %slice.173 = f32[10,255,512]{1,2,0:T(8,128)} slice(f32[10,256,512]{1,2,0:T(8,128)} %copy-done.1), slice={[0:10], [1:256], [0:512]} | slice | bytes 10444800 | tf_op jit(solution)/shard_map/slice | solution.py:148
  514.1 3.8 slice.175
  522.6 24.9 %fusion.12 = (f32[10,256,512]{1,2,0:T(8,128)}, f32[10,256,512]{1,2,0:T(8,128)}) fusion(f32[10,1,512]{1,2,0:T(8,128)} %copy.104, f32[10,255,512]{1,2,0:T(8,128)} %slice.173, f32[10,256,512]{1,2,0:T(8,128)} %copy.100, f32[10,1,512]{1,2,0:T(8,128)} %copy.108, f32[10,255,512]{1,2,0:T(8,128)} %slice.175, pred[256]{0:T(512)(128)(4,1)S(1)} %compare_and_fusion, ...), kind=kLoop, calls=%fused_computation.18 | loop fusion | flops 28835840 | bytes 52429584 | tf_op jit(solution)/shard_map/jit(_where)/select_n | solution.py:161
  547.5 11.3 %fusion.10 = f32[10,256,512]{1,2,0:T(8,128)} fusion(f32[10,256,512]{1,2,0:T(8,128)} %get-tuple-element.43, f32[10,256,511]{1,2,0:T(8,128)} %bitcast.58, f32[10,256,1]{1,2,0:T(1,128)S(1)} %get-tuple-element.49, f32[10,256,512]{1,2,0:T(8,128)} %get-tuple-element.42, f32[10,255,512]{1,2,0:T(8,128)} %bitcast.57, f32[10,1,512]{1,2,0:T(8,128)} %get-tuple-element.46), kind=kLoop, calls=%fused_computation.15 | loop fusion | flops 6553600 | bytes 26214400 | tf_op jit(solution)/shard_map/add | solution.py:167
  558.7 5.9 %copy.116 = f32[10,256,512]{2,1,0:T(8,128)} copy(f32[10,256,512]{1,2,0:T(8,128)} %fusion.10) | data formatting | bytes 10485760
  (86 shorter events, 76.0 us)
Async XLA Ops:
  7.2 441.1 %copy-start = (bf16[2048,512]{1,0:T(8,128)(2,1)S(1)}, bf16[2048,512]{1,0:T(8,128)(2,1)}, u32[]{:S(2)}) copy-start(bf16[2048,512]{1,0:T(8,128)(2,1)} %param.26) | copy-start | bytes 6291460
  7.2 237.7 %all-gather.4.cloned.1.call-start = ((), (), s32[]{:S(2)}) async-start(), calls=%async_computation.2 | async-start | bytes 10027008 | tf_op jit(solution)/shard_map/all_gather | solution.py:108
  15.8 248.6 %all-gather.6.cloned.1.call-start = ((), (), s32[]{:S(2)}) async-start(), calls=%async_computation.3 | async-start | bytes 9437184 | tf_op jit(solution)/shard_map/all_gather | solution.py:124
  20.9 58.9 %collective-permute-start = (bf16[10,256,512]{2,1,0:T(8,128)(2,1)}, bf16[10,256,512]{2,1,0:T(8,128)(2,1)}, u32[]{:S(2)}, u32[]{:S(2)}) collective-permute-start(bf16[10,256,512]{2,1,0:T(8,128)(2,1)} %convert_element_type.34), channel_id=1, source_target_pairs={{0,8},{8,0},{16,24},{24,16},{1,9},{9,1},{17,25},{25,17},{2,10},{10... | collective-permute-start | bytes 7864328 | tf_op jit(solution)/shard_map/ppermute | solution.py:13
  23.0 57.7 %collective-permute-start.1 = (bf16[10,256,512]{2,1,0:T(8,128)(2,1)}, bf16[10,256,512]{2,1,0:T(8,128)(2,1)}, u32[]{:S(2)}, u32[]{:S(2)}) collective-permute-start(bf16[10,256,512]{2,1,0:T(8,128)(2,1)} %convert_element_type.34), channel_id=1, source_target_pairs={{0,16},{8,24},{16,0},{24,8},{1,17},{9,25},{17,1},{25,9},{2,18},{10... | collective-permute-start | bytes 7864328 | tf_op jit(solution)/shard_map/ppermute | solution.py:13
  24.2 112.8 %collective-permute-start.2 = (bf16[10,256,512]{2,1,0:T(8,128)(2,1)}, bf16[10,256,512]{2,1,0:T(8,128)(2,1)}, u32[]{:S(2)}, u32[]{:S(2)}) collective-permute-start(bf16[10,256,512]{2,1,0:T(8,128)(2,1)} %convert_element_type.34), channel_id=1, source_target_pairs={{0,24},{8,16},{16,8},{24,0},{1,25},{9,17},{17,9},{25,1},{2,26},{10... | collective-permute-start | bytes 7864328 | tf_op jit(solution)/shard_map/ppermute | solution.py:13
  146.8 94.5 %all-to-all-start = ((bf16[8,10,256,64]{2,3,1,0:T(8,128)(2,1)}), bf16[8,10,256,64]{2,3,1,0:T(8,128)(2,1)}, u32[]{:S(2)}, u32[]{:S(2)}) async-start(bf16[8,10,256,64]{2,3,1,0:T(8,128)(2,1)} %convert_bitcast_fusion), calls=%async_computation | async-start | bytes 5242880 | tf_op jit(solution)/shard_map/all_to_all | solution.py:100
  153.5 294.7 %all-gather.8.cloned.1.call-start = ((), (), s32[]{:S(2)}) async-start(), calls=%async_computation.4 | async-start | bytes 13107200 | tf_op jit(solution)/shard_map/all_gather | solution.py:132
  344.0 5.9 %copy-start.3 = (f32[4]{0:T(128)S(1)}, f32[4]{0:T(128)}, u32[]{:S(2)}) copy-start(f32[4]{0:T(128)} %param.29) | copy-start | bytes 52
  357.4 2.4 copy-start.1
  359.8 117.1 %collective-permute-start.6 = (f32[10,256,1]{1,2,0:T(1,128)S(1)}, f32[10,256,1]{1,2,0:T(1,128)S(1)}, u32[]{:S(2)}, u32[]{:S(2)}) collective-permute-start(f32[10,256,1]{1,2,0:T(1,128)S(1)} %slice.170), channel_id=1, source_target_pairs={{0,8},{8,16},{16,24},{1,9},{9,17},{17,25},{2,10},{10,18},{18,26},{... | collective-permute-start | bytes 30728 | tf_op jit(solution)/shard_map/ppermute | solution.py:151
  379.8 97.1 %collective-permute-start.5 = (f32[10,256,1]{1,2,0:T(1,128)S(1)}, f32[10,256,1]{1,2,0:T(1,128)S(1)}, u32[]{:S(2)}, u32[]{:S(2)}) collective-permute-start(f32[10,256,1]{1,2,0:T(1,128)S(1)} %slice_convert_fusion.2), channel_id=1, source_target_pairs={{0,8},{8,16},{16,24},{1,9},{9,17},{17,25},{2,10},{10,18},{18,26},{... | collective-permute-start | bytes 30728 | tf_op jit(solution)/shard_map/ppermute | solution.py:151
  389.4 74.5 %collective-permute-start.11 = (f32[10,1,512]{2,1,0:T(1,128)S(1)}, f32[10,1,512]{2,1,0:T(1,128)S(1)}, u32[]{:S(2)}, u32[]{:S(2)}) collective-permute-start(f32[10,1,512]{2,1,0:T(1,128)S(1)} %copy.112), channel_id=1, source_target_pairs={{0,1},{1,2},{2,3},{3,4},{4,5},{5,6},{6,7},{8,9},{9,10},{10,11},{11... | collective-permute-start | bytes 61448 | tf_op jit(solution)/shard_map/ppermute | solution.py:151
  405.2 57.6 %collective-permute-start.10 = (f32[10,1,512]{2,1,0:T(1,128)S(1)}, f32[10,1,512]{2,1,0:T(1,128)S(1)}, u32[]{:S(2)}, u32[]{:S(2)}) collective-permute-start(f32[10,1,512]{2,1,0:T(1,128)S(1)} %copy.110), channel_id=1, source_target_pairs={{0,1},{1,2},{2,3},{3,4},{4,5},{5,6},{6,7},{8,9},{9,10},{10,11},{11... | collective-permute-start | bytes 61448 | tf_op jit(solution)/shard_map/ppermute | solution.py:151
  456.6 2.4 copy-start.2
  459.8 17.2 %collective-permute-start.7 = (f32[10,256,1]{1,2,0:T(1,128)S(1)}, f32[10,256,1]{1,2,0:T(1,128)S(1)}, u32[]{:S(2)}, u32[]{:S(2)}) collective-permute-start(f32[10,256,1]{1,2,0:T(1,128)S(1)} %copy.101), channel_id=1, source_target_pairs={{0,8},{8,16},{16,24},{1,9},{9,17},{17,25},{2,10},{10,18},{18,26},{... | collective-permute-start | bytes 30728 | tf_op jit(solution)/shard_map/ppermute | solution.py:155
  473.0 7.6 %collective-permute-start.12 = (f32[10,1,512]{2,1,0:T(1,128)S(1)}, f32[10,1,512]{2,1,0:T(1,128)S(1)}, u32[]{:S(2)}, u32[]{:S(2)}) collective-permute-start(f32[10,1,512]{2,1,0:T(1,128)S(1)} %slice.179), channel_id=1, source_target_pairs={{0,1},{1,2},{2,3},{3,4},{4,5},{5,6},{6,7},{8,9},{9,10},{10,11},{11... | collective-permute-start | bytes 61448 | tf_op jit(solution)/shard_map/ppermute | solution.py:155
  477.9 44.6 %collective-permute-start.3 = (f32[10,256,1]{1,2,0:T(1,128)S(1)}, f32[10,256,1]{1,2,0:T(1,128)S(1)}, u32[]{:S(2)}, u32[]{:S(2)}) collective-permute-start(f32[10,256,1]{1,2,0:T(1,128)S(1)} %get-tuple-element.50), channel_id=1, source_target_pairs={{8,0},{16,8},{24,16},{9,1},{17,9},{25,17},{10,2},{18,10},{26,18},{... | collective-permute-start | bytes 30728 | tf_op jit(solution)/shard_map/ppermute | solution.py:150
  479.2 43.3 %collective-permute-start.4 = (f32[10,256,1]{1,2,0:T(1,128)S(1)}, f32[10,256,1]{1,2,0:T(1,128)S(1)}, u32[]{:S(2)}, u32[]{:S(2)}) collective-permute-start(f32[10,256,1]{1,2,0:T(1,128)S(1)} %get-tuple-element.51), channel_id=1, source_target_pairs={{8,0},{16,8},{24,16},{9,1},{17,9},{25,17},{10,2},{18,10},{26,18},{... | collective-permute-start | bytes 30728 | tf_op jit(solution)/shard_map/ppermute | solution.py:154
  492.9 25.0 %collective-permute-start.8 = (f32[10,1,512]{2,1,0:T(1,128)S(1)}, f32[10,1,512]{2,1,0:T(1,128)S(1)}, u32[]{:S(2)}, u32[]{:S(2)}) collective-permute-start(f32[10,1,512]{2,1,0:T(1,128)S(1)} %copy.103), channel_id=1, source_target_pairs={{1,0},{2,1},{3,2},{4,3},{5,4},{6,5},{7,6},{9,8},{10,9},{11,10},{12... | collective-permute-start | bytes 61448 | tf_op jit(solution)/shard_map/ppermute | solution.py:150
  497.3 22.9 %collective-permute-start.9 = (f32[10,1,512]{2,1,0:T(1,128)S(1)}, f32[10,1,512]{2,1,0:T(1,128)S(1)}, u32[]{:S(2)}, u32[]{:S(2)}) collective-permute-start(f32[10,1,512]{2,1,0:T(1,128)S(1)} %copy.107), channel_id=1, source_target_pairs={{1,0},{2,1},{3,2},{4,3},{5,4},{6,5},{7,6},{9,8},{10,9},{11,10},{12... | collective-permute-start | bytes 61448 | tf_op jit(solution)/shard_map/ppermute | solution.py:154
  499.5 11.9 %slice-start = ((s8[5242880]{0:T(1024)(128)(4,1)}), s8[4194304]{0:T(1024)(128)(4,1)S(1)}, s32[]{:S(2)}) async-start(s8[5242880]{0:T(1024)(128)(4,1)} %bitcast.55), calls=%async_computation.5 | async-start | bytes 8388608
  505.1 6.3 %slice-start.1 = ((s8[5242880]{0:T(1024)(128)(4,1)}), s8[1048576]{0:T(1024)(128)(4,1)S(1)}, s32[]{:S(2)}) async-start(s8[5242880]{0:T(1024)(128)(4,1)} %bitcast.55), calls=%async_computation.6 | async-start | bytes 2097152
Sparse Core Ops, SparseCore 0:
  15.9 88.8 all-gather.3
  106.5 107.9 all-gather.5
  344.1 104.1 all-gather.7

commit v12 on v10

--- a/solution.py
+++ b/solution.py
@@ -21,6 +21,16 @@
     return jnp.concatenate(
         [lax.dynamic_index_in_dim(blocks, own ^ k, 0, keepdims=False) for k in range(count)]
     )
+
+
+def chip_gather(block, count, at):
+    groups = [list(range(core, count, 2)) for core in range(2)]
+    mine = lax.all_gather(block, "py", axis=0, axis_index_groups=groups)
+    other = lax.ppermute(mine, "py", [(s, s ^ 1) for s in range(count)])
+    even = jnp.stack([mine, other], axis=1)
+    odd = jnp.stack([other, mine], axis=1)
+    whole = jnp.where(at % 2 == 0, even, odd)
+    return whole.reshape((-1,) + block.shape[1:])
 
 
 def thomas_kernel(coupling_ref, shift_ref, ly_ref, lx_ref, rhs_ref, out_ref):
@@ -105,7 +115,7 @@
     high, middle, low = (p.astype(jnp.bfloat16) for p in (high, middle, low))
     pieces = jnp.zeros((lambda_y.shape[0], 128), jnp.bfloat16)
     pieces = pieces.at[:, 0].set(high).at[:, 1].set(middle).at[:, 2].set(low)
-    carried = lax.all_gather(jnp.concatenate([left_y, pieces], axis=1), "py", axis=0, tiled=True)
+    carried = chip_gather(jnp.concatenate([left_y, pieces], axis=1), count_y, at_y)
     columns = left_y.shape[1]
     flat = jnp.transpose(pencil, (1, 3, 0, 2)).reshape(layers * modes, -1)
     spectral = jnp.einsum(
@@ -121,7 +131,7 @@
     back_flat = jnp.einsum(
         "nj,yj->ny",
         solved.reshape(layers * modes, -1),
-        lax.all_gather(right_y, "py", axis=0, tiled=True),
+        chip_gather(right_y, count_y, at_y),
         preferred_element_type=jnp.float32,
     ).astype(jnp.bfloat16)
     back_pencil = jnp.transpose(back_flat.reshape(layers, modes, count_y, height), (2, 0, 3, 1))

time: 518 us -> 518 us (level)
  other arithmetic: 50.7 us -> 63.1 us
  waiting for transfers between devices: 266 us -> 257 us
    all_to_all x1, waiting for transfers between devices: 86.3 us -> 31.1 us  [shards(): pencil = lax.all_to_all(spectral_x, 'py', 0, 0, tiled=True)]
    all_gather x2, waiting for transfers between devices: 0.01 us -> 46.4 us  [chip_gather(): mine = lax.all_gather(block, 'py', axis=0, axis_index_groups=groups)]
    select_n x0 -> x2, other arithmetic: none -> 13.5 us  [chip_gather(): whole = jnp.where(at % 2 == 0, even, odd)]
  transfers between devices with their start and end apart: 11 -> 13, of which waited for: 5 -> 6; matrix products, arithmetic and copies ran while one was open for 16% -> 16% of each run, Pallas kernels for 1% -> 0%
where the time goes in v12:
time: 518 us; the launch traced here: 517 us
  waiting for transfers between devices  257 us (50%)
  other arithmetic  63.1 us (12%)
  blocking collectives  62.2 us (12%)
  local copies, waits for them, and re-layouts  54.8 us (11%)
  matrix products  35.4 us (7%)
  starting transfers between devices  24.3 us (5%)
  between operations  14.1 us (3%)
  Pallas kernels  5.82 us (1%)
    ppermute x3, waiting for transfers between devices, exchange(): parts.append(lax.ppermute(block, axis, [(s, s ^ k) for s in range(count)]))  105 us
    all_gather x1, waiting for transfers between devices, shards(): lax.all_gather(back_y, 'px', axis=2, tiled=True)  74.5 us
    all_to_all x1, blocking collectives, shards(): back_y = lax.all_to_all(back_pencil, 'py', 0, 0, tiled=True)  62.2 us
    all_gather x2, waiting for transfers between devices, chip_gather(): mine = lax.all_gather(block, 'py', axis=0, axis_index_groups=groups)  46.4 us
    all_to_all x1, waiting for transfers between devices, shards(): pencil = lax.all_to_all(spectral_x, 'py', 0, 0, tiled=True)  31.1 us
    select_n x1, other arithmetic, net(): flux_high = jnp.where(edge, 0.0, flux_high)  16.2 us
    slice x4, local copies, waits for them, and re-layouts, net(): rest = lambda a: lax.slice_in_dim(a, 1, None, axis=dim)  13.8 us
    select_n x2, other arithmetic, chip_gather(): whole = jnp.where(at % 2 == 0, even, odd)  13.5 us
  transfers between devices with their start and end apart: 13, of which 6 were waited for; matrix products, arithmetic and copies ran while one was open for 16% of the time, Pallas kernels for 0%

profile of v12, /device:TPU:1, one launch (start us, length us, event | category | flops | bytes accessed | tf_op | source)
XLA Modules:
  0.0 517.0 jit_solution(7216200308047337504)
XLA Ops:
  13.4 2.3 pad_maximum_fusion
  15.8 4.3 convert_element_type.34
  23.5 2.7 constant_dynamic-slice_fusion.3
  31.6 47.5 %collective-permute-done.1 = bf16[10,256,512]{2,1,0:T(8,128)(2,1)} collective-permute-done((bf16[10,256,512]{2,1,0:T(8,128)(2,1)}, bf16[10,256,512]{2,1,0:T(8,128)(2,1)}, u32[]{:S(2)}, u32[]{:S(2)}) %collective-permute-start.1) | collective-permute-done | bytes 2621472 | tf_op jit(solution)/shard_map/ppermute | solution.py:13
  79.9 56.3 %collective-permute-done.3 = bf16[10,256,512]{2,1,0:T(8,128)(2,1)} collective-permute-done((bf16[10,256,512]{2,1,0:T(8,128)(2,1)}, bf16[10,256,512]{2,1,0:T(8,128)(2,1)}, u32[]{:S(2)}, u32[]{:S(2)}) %collective-permute-start.3) | collective-permute-done | bytes 2621472 | tf_op jit(solution)/shard_map/ppermute | solution.py:13
  136.2 9.9 %convert_bitcast_fusion = bf16[8,10,256,64]{2,3,1,0:T(8,128)(2,1)} fusion(bf16[10,256,512]{2,1,0:T(8,128)(2,1)} %collective-permute-done.3, bf16[10,256,512]{2,1,0:T(8,128)(2,1)} %collective-permute-done.2, bf16[10,256,512]{2,1,0:T(8,128)(2,1)} %collective-permute-done.1, bf16[10,256,512]{2,1,0:T(8,128)(2,1)} %convert_element_type.34, ...), kind=kOutput, calls=%fused_computation.28 | convolution fusion | flops 5420351488 | bytes 15204352 | tf_op jit(solution)/shard_map/zyx,xci->czyi/dot_general | solution.py:104
  146.0 6.8 %all-to-all-start = ((bf16[8,10,256,64]{2,3,1,0:T(8,128)(2,1)}), bf16[8,10,256,64]{2,3,1,0:T(8,128)(2,1)}, u32[]{:S(2)}, u32[]{:S(2)}) async-start(bf16[8,10,256,64]{2,3,1,0:T(8,128)(2,1)} %convert_bitcast_fusion), calls=%async_computation | async-start | bytes 5242880 | tf_op jit(solution)/shard_map/all_to_all | solution.py:110
  153.2 46.4 %all-gather.8.cloned.1.call-done = bf16[1024,2176]{1,0:T(8,128)(2,1)} async-done(((bf16[256,2176]{1,0:T(8,128)(2,1)}), bf16[1024,2176]{1,0:T(8,128)(2,1)}) %all-gather.8.cloned.1.call-update) | async-done | bytes 4456464 | tf_op jit(solution)/shard_map/all_gather | solution.py:28
  202.6 31.1 %all-to-all-done = bf16[8,10,256,64]{2,3,1,0:T(8,128)(2,1)} async-done(((bf16[8,10,256,64]{2,3,1,0:T(8,128)(2,1)}), bf16[8,10,256,64]{2,3,1,0:T(8,128)(2,1)}, u32[]{:S(2)}, u32[]{:S(2)}) %all-to-all-start) | async-done | bytes 2621472 | tf_op jit(solution)/shard_map/all_to_all | solution.py:110
  233.7 2.2 copy.257
  236.7 7.9 %maximum_select_fusion.1 = bf16[4,2,256,2048]{3,2,1,0:T(8,128)(2,1)} fusion(bf16[4,1,256,2048]{3,2,1,0:T(8,128)(2,1)} %bitcast.21, bf16[4,1,256,2048]{3,2,1,0:T(8,128)(2,1)S(1)} %bitcast.118, pred[]{:T(512)S(6)} %eq.60), kind=kLoop, calls=%fused_computation.11 | loop fusion | flops 12582912 | bytes 16777216 | tf_op jit(solution)/shard_map/jit(_where)/select_n | solution.py:32
  244.6 5.6 %maximum_select_fusion = bf16[4,2,256,2176]{3,2,1,0:T(8,128)(2,1)S(1)} fusion(bf16[4,1,256,2176]{3,2,1,0:T(8,128)(2,1)} %bitcast.3, bf16[4,1,256,2176]{3,2,1,0:T(8,128)(2,1)S(1)} %bitcast.116, pred[]{:T(512)S(6)} %eq.60), kind=kLoop, calls=%fused_computation.8 | loop fusion | flops 13369344 | bytes 17825792 | tf_op jit(solution)/shard_map/jit(_where)/select_n | solution.py:32
  250.3 7.3 %fusion.7.rhs_ref = f32[10,64,2048]{2,1,0:T(8,128)} fusion(bf16[10,64,2048]{2,1,0:T(8,128)(2,1)S(1)} %bitcast.120, bf16[2048,2176]{1,0:T(8,128)(2,1)S(1)} %bitcast.111), kind=kOutput, calls=%fused_computation.10 | convolution fusion | flops 5368709120 | bytes 16252928 | tf_op jit(solution)/shard_map/ny,jy->nj/dot_general | solution.py:121
  259.2 5.8 %shard_map.131 = bf16[10,64,2048]{2,1,0:T(8,128)(2,1)} custom-call(f32[9]{0:T(128)} %coupling_ref.1, f32[10]{0:T(128)} %shift_ref.1, f32[1,2048]{1,0:T(1,128)} %bitcast.127, f32[64,1]{1,0:T(8,128)} %copy.240.lx_ref, f32[10,64,2048]{2,1,0:T(8,128)} %fusion.7.rhs_ref), custom_call_target="tpu_custom_call" | custom-call | tf_op jit(solution)/shard_map/pallas_call | solution.py:67
  265.0 9.6 %convolution_convert_fusion = bf16[640,2048]{1,0:T(8,128)(2,1)S(1)} fusion(bf16[640,2048]{1,0:T(8,128)(2,1)} %bitcast.119, bf16[2048,2048]{1,0:T(8,128)(2,1)} %bitcast.112), kind=kOutput, calls=%fused_computation.26 | convolution fusion | flops 5370019840 | bytes 13631488 | tf_op jit(solution)/shard_map/nj,yj->ny/dot_general | solution.py:131
  276.1 62.2 %all_to_all.10 = bf16[8,10,256,64]{2,3,1,0:T(8,128)(2,1)S(1)} all-to-all(bf16[8,10,256,64]{2,3,1,0:T(8,128)(2,1)S(1)} %bitcast.108), channel_id=1, replica_groups=mesh['px'=4,'py'=8] {'py'}, dimensions={0} | all-to-all | bytes 5242880 | tf_op jit(solution)/shard_map/all_to_all | solution.py:138
  340.1 4.4 copy.243
  345.2 6.3 %select_select_fusion = f32[10,256,512]{2,1,0:T(8,128)S(1)} fusion(s32[10,256,512]{2,1,0:T(8,128)} %param.27, f32[]{:T(128)} %bitcast.31, f32[]{:T(128)} %bitcast.30, f32[]{:T(128)} %bitcast.29, f32[]{:T(128)} %bitcast.28), kind=kLoop, calls=%fused_computation.24 | loop fusion | flops 10485760 | bytes 10485776 | tf_op jit(solution)/shard_map/jit(_where)/select_n | solution.py:149
  351.6 4.0 slice.205
  356.2 3.0 slice.218
  359.2 3.0 slice_reduce_fusion
  362.2 8.3 %slice_bitcast_fusion.2 = (s32[10,256,512]{2,1,0:T(8,128)}, s32[10,256,512]{2,1,0:T(8,128)S(1)}) fusion(s32[2,10,256,512]{3,2,1,0:T(8,128)} %param.28), kind=kLoop, calls=%fused_computation.23 | loop fusion | bytes 20971520 | tf_op jit(solution)/shard_map/squeeze | solution.py:151
  374.3 74.5 %all-gather.6.cloned.1.call-done = bf16[10,256,2048]{2,1,0:T(8,128)(2,1)} async-done(((bf16[10,256,512]{2,1,0:T(8,128)(2,1)}), bf16[10,256,2048]{2,1,0:T(8,128)(2,1)}) %all-gather.6.cloned.1.call-update) | async-done | bytes 10485776 | tf_op jit(solution)/shard_map/all_gather | solution.py:142
  448.8 8.6 %fusion.19 = f32[10,256,512]{2,1,0:T(8,128)S(1)} fusion(bf16[10,256,2048]{2,1,0:T(8,128)(2,1)} %all-gather.6.cloned.1.call-done, bf16[2048,512]{1,0:T(8,128)(2,1)S(1)} %copy-done), kind=kOutput, calls=%fused_computation.36 | convolution fusion | flops 5368709120 | bytes 17825792 | tf_op jit(solution)/shard_map/zyi,ix->zyx/dot_general | solution.py:140
  458.5 3.7 slice.209
  462.3 3.0 slice.222
  466.0 3.7 collective-permute-start.6
  471.0 3.9 collective-permute-start.8
  483.6 3.2 collective-permute-start.7
  486.8 2.8 multiply_select_fusion
  489.7 16.2 %fusion.12 = (f32[10,256,512]{2,1,0:T(8,128)S(1)}, f32[10,256,512]{2,1,0:T(8,128)S(1)}) fusion(f32[10,1,512]{2,1,0:T(1,128)S(1)} %get-tuple-element.54, f32[10,255,512]{2,1,0:T(8,128)} %slice.218, f32[10,256,512]{2,1,0:T(8,128)S(1)} %copy-done.2, f32[10,1,512]{2,1,0:T(1,128)S(1)} %get-tuple-element.53, f32[10,255,512]{2,1,0:T(8,128)} %slice.222, ...), kind=kLoop, calls=%fused_computation.20 | loop fusion | flops 28835840 | bytes 52429584 | tf_op jit(solution)/shard_map/jit(_where)/select_n | solution.py:169
  505.9 4.5 fusion.10
  (90 shorter events, 41.6 us)
Async XLA Ops:
  7.2 441.6 %copy-start = (bf16[2048,512]{1,0:T(8,128)(2,1)S(1)}, bf16[2048,512]{1,0:T(8,128)(2,1)}, u32[]{:S(2)}) copy-start(bf16[2048,512]{1,0:T(8,128)(2,1)} %param.26) | copy-start | bytes 6291460
  7.2 145.7 %all-gather.10.cloned.1.call-start = ((), (), s32[]{:S(2)}) async-start(), calls=%async_computation.4 | async-start | bytes 5242880 | tf_op jit(solution)/shard_map/all_gather | solution.py:28
  7.9 191.7 %all-gather.8.cloned.1.call-start = ((), (), s32[]{:S(2)}) async-start(), calls=%async_computation.3 | async-start | bytes 5570560 | tf_op jit(solution)/shard_map/all_gather | solution.py:28
  20.1 58.9 %collective-permute-start.1 = (bf16[10,256,512]{2,1,0:T(8,128)(2,1)}, bf16[10,256,512]{2,1,0:T(8,128)(2,1)}, u32[]{:S(2)}, u32[]{:S(2)}) collective-permute-start(bf16[10,256,512]{2,1,0:T(8,128)(2,1)} %convert_element_type.34), channel_id=1, source_target_pairs={{0,8},{8,0},{16,24},{24,16},{1,9},{9,1},{17,25},{25,17},{2,10},{10... | collective-permute-start | bytes 7864328 | tf_op jit(solution)/shard_map/ppermute | solution.py:13
  22.3 57.6 %collective-permute-start.2 = (bf16[10,256,512]{2,1,0:T(8,128)(2,1)}, bf16[10,256,512]{2,1,0:T(8,128)(2,1)}, u32[]{:S(2)}, u32[]{:S(2)}) collective-permute-start(bf16[10,256,512]{2,1,0:T(8,128)(2,1)} %convert_element_type.34), channel_id=1, source_target_pairs={{0,16},{8,24},{16,0},{24,8},{1,17},{9,25},{17,1},{25,9},{2,18},{10... | collective-permute-start | bytes 7864328 | tf_op jit(solution)/shard_map/ppermute | solution.py:13
  23.5 112.6 %collective-permute-start.3 = (bf16[10,256,512]{2,1,0:T(8,128)(2,1)}, bf16[10,256,512]{2,1,0:T(8,128)(2,1)}, u32[]{:S(2)}, u32[]{:S(2)}) collective-permute-start(bf16[10,256,512]{2,1,0:T(8,128)(2,1)} %convert_element_type.34), channel_id=1, source_target_pairs={{0,24},{8,16},{16,8},{24,0},{1,25},{9,17},{17,9},{25,1},{2,26},{10... | collective-permute-start | bytes 7864328 | tf_op jit(solution)/shard_map/ppermute | solution.py:13
  146.0 87.7 %all-to-all-start = ((bf16[8,10,256,64]{2,3,1,0:T(8,128)(2,1)}), bf16[8,10,256,64]{2,3,1,0:T(8,128)(2,1)}, u32[]{:S(2)}, u32[]{:S(2)}) async-start(bf16[8,10,256,64]{2,3,1,0:T(8,128)(2,1)} %convert_bitcast_fusion), calls=%async_computation | async-start | bytes 5242880 | tf_op jit(solution)/shard_map/all_to_all | solution.py:110
  152.9 295.9 %all-gather.6.cloned.1.call-start = ((), (), s32[]{:S(2)}) async-start(), calls=%async_computation.2 | async-start | bytes 13107200 | tf_op jit(solution)/shard_map/all_gather | solution.py:142
  152.9 83.1 %collective-permute-start.4 = (bf16[4,256,2048]{2,1,0:T(8,128)(2,1)}, bf16[4,256,2048]{2,1,0:T(8,128)(2,1)}, u32[]{:S(2)}, u32[]{:S(2)}) collective-permute-start(bf16[4,256,2048]{2,1,0:T(8,128)(2,1)} %bitcast.117), channel_id=1, source_target_pairs={{0,1},{1,0},{2,3},{3,2},{4,5},{5,4},{6,7},{7,6},{8,9},{9,8},{10,11... | collective-permute-start | bytes 12582920 | tf_op jit(solution)/shard_map/ppermute | solution.py:29
  199.6 44.9 %collective-permute-start = (bf16[4,256,2176]{2,1,0:T(8,128)(2,1)}, bf16[4,256,2176]{2,1,0:T(8,128)(2,1)}, u32[]{:S(2)}, u32[]{:S(2)}) collective-permute-start(bf16[4,256,2176]{2,1,0:T(8,128)(2,1)} %bitcast.113), channel_id=1, source_target_pairs={{0,1},{1,0},{2,3},{3,2},{4,5},{5,4},{6,7},{7,6},{8,9},{9,8},{10,11... | collective-permute-start | bytes 13369352 | tf_op jit(solution)/shard_map/ppermute | solution.py:29
  233.7 3.0 copy-start.5
  233.7 10.9 %slice-start = ((s8[4456448]{0:T(1024)(128)(4,1)}), s8[4194304]{0:T(1024)(128)(4,1)S(1)}, s32[]{:S(2)}) async-start(s8[4456448]{0:T(1024)(128)(4,1)} %bitcast.114), calls=%async_computation.5 | async-start | bytes 8388608
  236.7 7.9 %slice-start.1 = ((s8[4456448]{0:T(1024)(128)(4,1)}), s8[262144]{0:T(1024)(128)(4,1)S(1)}, s32[]{:S(2)}) async-start(s8[4456448]{0:T(1024)(128)(4,1)} %bitcast.114), calls=%async_computation.6 | async-start | bytes 524288
  340.1 4.4 copy-start.6
  351.5 4.6 copy-start.3
  457.4 4.9 copy-start.1
  466.0 11.1 %collective-permute-start.6 = (f32[3,10,256,1]{2,0,1,3:T(4,128)}, f32[3,10,256,1]{2,0,1,3:T(4,128)}, u32[]{:S(2)}, u32[]{:S(2)}) collective-permute-start(f32[3,10,256,1]{2,0,1,3:T(4,128)} %pad_maximum_fusion.2), channel_id=1, source_target_pairs={{0,8},{8,16},{16,24},{1,9},{9,17},{17,25},{2,10},{10,18},{18,26},{... | collective-permute-start | bytes 92168 | tf_op jit(solution)/shard_map/ppermute | solution.py:161
  469.7 5.3 %collective-permute-start.5 = (f32[2,10,256,1]{2,0,1,3:T(2,128)S(1)}, f32[2,10,256,1]{2,0,1,3:T(2,128)S(1)}, u32[]{:S(2)}, u32[]{:S(2)}) collective-permute-start(f32[2,10,256,1]{2,0,1,3:T(2,128)S(1)} %pad_maximum_fusion.4), channel_id=1, source_target_pairs={{8,0},{16,8},{24,16},{9,1},{17,9},{25,17},{10,2},{18,10},{26,18},{... | collective-permute-start | bytes 61448 | tf_op jit(solution)/shard_map/ppermute | solution.py:160
  471.0 10.9 %collective-permute-start.8 = (f32[3,10,1,512]{3,2,1,0:T(1,128)S(1)}, f32[3,10,1,512]{3,2,1,0:T(1,128)S(1)}, u32[]{:S(2)}, u32[]{:S(2)}) collective-permute-start(f32[3,10,1,512]{3,2,1,0:T(1,128)S(1)} %pad_maximum_fusion.1), channel_id=1, source_target_pairs={{0,1},{1,2},{2,3},{3,4},{4,5},{5,6},{6,7},{8,9},{9,10},{10,11},{11... | collective-permute-start | bytes 184328 | tf_op jit(solution)/shard_map/ppermute | solution.py:161
  481.0 8.7 %copy-start.2 = (f32[10,256,512]{2,1,0:T(8,128)S(1)}, f32[10,256,512]{2,1,0:T(8,128)}, u32[]{:S(2)}) copy-start(f32[10,256,512]{2,1,0:T(8,128)} %copy-done.1) | copy-start | bytes 15728644
  481.0 8.7 %copy-start.4 = (f32[10,256,1]{2,1,0:T(8,128)S(1)}, f32[10,256,1]{2,1,0:T(8,128)}, u32[]{:S(2)}) copy-start(f32[10,256,1]{2,1,0:T(8,128)} %copy.245) | copy-start | bytes 30724
  483.6 6.0 %collective-permute-start.7 = (f32[2,10,1,512]{3,2,1,0:T(1,128)S(1)}, f32[2,10,1,512]{3,2,1,0:T(1,128)S(1)}, u32[]{:S(2)}, u32[]{:S(2)}) collective-permute-start(f32[2,10,1,512]{3,2,1,0:T(1,128)S(1)} %pad_maximum_fusion.3), channel_id=1, source_target_pairs={{1,0},{2,1},{3,2},{4,3},{5,4},{6,5},{7,6},{9,8},{10,9},{11,10},{12... | collective-permute-start | bytes 122888 | tf_op jit(solution)/shard_map/ppermute | solution.py:160
Sparse Core Ops, SparseCore 0:
  9.6 82.8 all-gather.9
  94.0 105.5 all-gather.7
  344.6 104.1 all-gather.5

commit v13 on v10

--- a/solution.py
+++ b/solution.py
@@ -105,8 +105,9 @@
     high, middle, low = (p.astype(jnp.bfloat16) for p in (high, middle, low))
     pieces = jnp.zeros((lambda_y.shape[0], 128), jnp.bfloat16)
     pieces = pieces.at[:, 0].set(high).at[:, 1].set(middle).at[:, 2].set(low)
-    carried = lax.all_gather(jnp.concatenate([left_y, pieces], axis=1), "py", axis=0, tiled=True)
+    carried = lax.all_gather(jnp.concatenate([left_y, pieces, right_y], axis=1), "py", axis=0, tiled=True)
     columns = left_y.shape[1]
+    right_all = carried[:, columns + pieces.shape[1]:]
     flat = jnp.transpose(pencil, (1, 3, 0, 2)).reshape(layers * modes, -1)
     spectral = jnp.einsum(
         "ny,jy->nj",
@@ -121,7 +122,7 @@
     back_flat = jnp.einsum(
         "nj,yj->ny",
         solved.reshape(layers * modes, -1),
-        lax.all_gather(right_y, "py", axis=0, tiled=True),
+        right_all,
         preferred_element_type=jnp.float32,
     ).astype(jnp.bfloat16)
     back_pencil = jnp.transpose(back_flat.reshape(layers, modes, count_y, height), (2, 0, 3, 1))

time: 518 us -> 505 us (0.975)
  waiting for transfers between devices: 266 us -> 253 us
    all_to_all x1, waiting for transfers between devices: 86.3 us -> 73.8 us  [shards(): pencil = lax.all_to_all(spectral_x, 'py', 0, 0, tiled=True)]
  transfers between devices with their start and end apart: 11 -> 10, of which waited for: 5 -> 5; matrix products, arithmetic and copies ran while one was open for 16% -> 13% of each run, Pallas kernels for 1% -> 0%
where the time goes in v13:
time: 505 us; the launch traced here: 504 us
  waiting for transfers between devices  253 us (50%)
  blocking collectives  62.3 us (12%)
  local copies, waits for them, and re-layouts  56.2 us (11%)
  other arithmetic  51.6 us (10%)
  matrix products  39.2 us (8%)
  starting transfers between devices  22 us (4%)
  between operations  14.4 us (3%)
  Pallas kernels  5.82 us (1%)
    ppermute x3, waiting for transfers between devices, exchange(): parts.append(lax.ppermute(block, axis, [(s, s ^ k) for s in range(count)]))  105 us
    all_gather x1, waiting for transfers between devices, shards(): lax.all_gather(back_y, 'px', axis=2, tiled=True)  74.5 us
    all_to_all x1, waiting for transfers between devices, shards(): pencil = lax.all_to_all(spectral_x, 'py', 0, 0, tiled=True)  73.8 us
    all_to_all x1, blocking collectives, shards(): back_y = lax.all_to_all(back_pencil, 'py', 0, 0, tiled=True)  62.3 us
    select_n x1, other arithmetic, net(): flux_high = jnp.where(edge, 0.0, flux_high)  16.3 us
    slice x4, local copies, waits for them, and re-layouts, net(): rest = lambda a: lax.slice_in_dim(a, 1, None, axis=dim)  13.8 us
    dot_general x1, matrix products, shards(): jnp.einsum('ny,jy->nj', flat, carried[:, :columns], preferred_element_typ...  11.1 us
  transfers between devices with their start and end apart: 10, of which 5 were waited for; matrix products, arithmetic and copies ran while one was open for 13% of the time, Pallas kernels for 0%

profile of v13, /device:TPU:1, one launch (start us, length us, event | category | flops | bytes accessed | tf_op | source)
XLA Modules:
  0.0 504.4 jit_solution(8221836508894925356)
XLA Ops:
  13.4 3.1 pad_maximum_fusion
  16.5 4.3 convert_element_type.34
  20.8 2.0 collective-permute-start
  24.1 2.7 constant_dynamic-slice_fusion.3
  26.9 2.1 copy.250
  29.0 2.2 copy.251
  32.4 47.4 %collective-permute-done = bf16[10,256,512]{2,1,0:T(8,128)(2,1)} collective-permute-done((bf16[10,256,512]{2,1,0:T(8,128)(2,1)}, bf16[10,256,512]{2,1,0:T(8,128)(2,1)}, u32[]{:S(2)}, u32[]{:S(2)}) %collective-permute-start) | collective-permute-done | bytes 2621472 | tf_op jit(solution)/shard_map/ppermute | solution.py:13
  80.6 56.3 %collective-permute-done.2 = bf16[10,256,512]{2,1,0:T(8,128)(2,1)} collective-permute-done((bf16[10,256,512]{2,1,0:T(8,128)(2,1)}, bf16[10,256,512]{2,1,0:T(8,128)(2,1)}, u32[]{:S(2)}, u32[]{:S(2)}) %collective-permute-start.2) | collective-permute-done | bytes 2621472 | tf_op jit(solution)/shard_map/ppermute | solution.py:13
  136.9 9.9 %convert_bitcast_fusion = bf16[8,10,256,64]{2,3,1,0:T(8,128)(2,1)} fusion(bf16[10,256,512]{2,1,0:T(8,128)(2,1)} %collective-permute-done.2, bf16[10,256,512]{2,1,0:T(8,128)(2,1)} %collective-permute-done.1, bf16[10,256,512]{2,1,0:T(8,128)(2,1)} %collective-permute-done, bf16[10,256,512]{2,1,0:T(8,128)(2,1)} %convert_element_type.34, ...), kind=kOutput, calls=%fused_computation.28 | convolution fusion | flops 5420351488 | bytes 15204352 | tf_op jit(solution)/shard_map/zyx,xci->czyi/dot_general | solution.py:94
  146.8 6.6 %all-to-all-start = ((bf16[8,10,256,64]{2,3,1,0:T(8,128)(2,1)}), bf16[8,10,256,64]{2,3,1,0:T(8,128)(2,1)}, u32[]{:S(2)}, u32[]{:S(2)}) async-start(bf16[8,10,256,64]{2,3,1,0:T(8,128)(2,1)} %convert_bitcast_fusion), calls=%async_computation | async-start | bytes 5242880 | tf_op jit(solution)/shard_map/all_to_all | solution.py:100
  154.9 73.8 %all-to-all-done = bf16[8,10,256,64]{2,3,1,0:T(8,128)(2,1)} async-done(((bf16[8,10,256,64]{2,3,1,0:T(8,128)(2,1)}), bf16[8,10,256,64]{2,3,1,0:T(8,128)(2,1)}, u32[]{:S(2)}, u32[]{:S(2)}) %all-to-all-start) | async-done | bytes 2621472 | tf_op jit(solution)/shard_map/all_to_all | solution.py:100
  228.7 3.6 copy.255
  234.9 11.1 %fusion.9.rhs_ref = f32[10,64,2048]{2,1,0:T(8,128)} fusion(bf16[10,64,2048]{2,1,0:T(8,128)(2,1)} %bitcast.99, bf16[2048,4224]{1,0:T(8,128)(2,1)} %all-gather.3.cloned.1.call-done), kind=kOutput, calls=%fused_computation.11 | convolution fusion | flops 5368709120 | bytes 16252928 | tf_op jit(solution)/shard_map/ny,jy->nj/dot_general | solution.py:112
  246.0 5.8 %shard_map.131 = bf16[10,64,2048]{2,1,0:T(8,128)(2,1)} custom-call(f32[9]{0:T(128)} %coupling_ref.1, f32[10]{0:T(128)} %shift_ref.1, f32[1,2048]{1,0:T(1,128)} %bitcast.106, f32[64,1]{1,0:T(8,128)} %copy.238.lx_ref, f32[10,64,2048]{2,1,0:T(8,128)} %fusion.9.rhs_ref), custom_call_target="tpu_custom_call" | custom-call | tf_op jit(solution)/shard_map/pallas_call | solution.py:57
  251.8 9.6 %fusion.15 = bf16[640,2048]{1,0:T(8,128)(2,1)S(1)} fusion(bf16[640,2048]{1,0:T(8,128)(2,1)} %bitcast.98, bf16[2048,4224]{1,0:T(8,128)(2,1)} %all-gather.3.cloned.1.call-done), kind=kOutput, calls=%fused_computation.26 | convolution fusion | flops 5370019840 | bytes 13631488 | tf_op jit(solution)/shard_map/nj,yj->ny/dot_general | solution.py:122
  263.0 62.3 %all_to_all.10 = bf16[8,10,256,64]{2,3,1,0:T(8,128)(2,1)S(1)} all-to-all(bf16[8,10,256,64]{2,3,1,0:T(8,128)(2,1)S(1)} %bitcast.96), channel_id=1, replica_groups=mesh['px'=4,'py'=8] {'py'}, dimensions={0} | all-to-all | bytes 5242880 | tf_op jit(solution)/shard_map/all_to_all | solution.py:129
  327.1 4.4 copy.241
  332.2 6.4 %select_select_fusion = f32[10,256,512]{2,1,0:T(8,128)S(1)} fusion(s32[10,256,512]{2,1,0:T(8,128)} %param.27, f32[]{:T(128)} %bitcast.21, f32[]{:T(128)} %bitcast.20, f32[]{:T(128)} %bitcast.19, f32[]{:T(128)} %bitcast.18), kind=kLoop, calls=%fused_computation.24 | loop fusion | flops 10485760 | bytes 10485776 | tf_op jit(solution)/shard_map/jit(_where)/select_n | solution.py:140
  338.6 4.0 slice.210
  343.2 3.1 slice.223
  346.3 3.0 slice_reduce_fusion
  349.2 8.3 %slice_bitcast_fusion.2 = (s32[10,256,512]{2,1,0:T(8,128)}, s32[10,256,512]{2,1,0:T(8,128)S(1)}) fusion(s32[2,10,256,512]{3,2,1,0:T(8,128)} %param.28), kind=kLoop, calls=%fused_computation.23 | loop fusion | bytes 20971520 | tf_op jit(solution)/shard_map/squeeze | solution.py:142
  361.3 74.5 %all-gather.5.cloned.1.call-done = bf16[10,256,2048]{2,1,0:T(8,128)(2,1)} async-done(((bf16[10,256,512]{2,1,0:T(8,128)(2,1)}), bf16[10,256,2048]{2,1,0:T(8,128)(2,1)}) %all-gather.5.cloned.1.call-update) | async-done | bytes 10485776 | tf_op jit(solution)/shard_map/all_gather | solution.py:133
  435.8 8.6 %fusion.24 = f32[10,256,512]{2,1,0:T(8,128)S(1)} fusion(bf16[10,256,2048]{2,1,0:T(8,128)(2,1)} %all-gather.5.cloned.1.call-done, bf16[2048,512]{1,0:T(8,128)(2,1)S(1)} %copy-done), kind=kOutput, calls=%fused_computation.37 | convolution fusion | flops 5368709120 | bytes 17825792 | tf_op jit(solution)/shard_map/zyi,ix->zyx/dot_general | solution.py:131
  445.5 3.7 slice.214
  449.2 3.0 slice.227
  452.9 3.7 collective-permute-start.4
  458.0 3.9 collective-permute-start.6
  470.6 3.2 collective-permute-start.5
  473.9 2.8 multiply_select_fusion
  476.7 16.3 %fusion.14 = (f32[10,256,512]{2,1,0:T(8,128)S(1)}, f32[10,256,512]{2,1,0:T(8,128)S(1)}) fusion(f32[10,1,512]{2,1,0:T(1,128)S(1)} %get-tuple-element.54, f32[10,255,512]{2,1,0:T(8,128)} %slice.223, f32[10,256,512]{2,1,0:T(8,128)S(1)} %copy-done.2, f32[10,1,512]{2,1,0:T(1,128)S(1)} %get-tuple-element.53, f32[10,255,512]{2,1,0:T(8,128)} %slice.227, ...), kind=kLoop, calls=%fused_computation.20 | loop fusion | flops 28835840 | bytes 52429584 | tf_op jit(solution)/shard_map/jit(_where)/select_n | solution.py:160
  493.0 4.5 fusion.12
  (73 shorter events, 33.7 us)
Async XLA Ops:
  7.2 428.6 %copy-start = (bf16[2048,512]{1,0:T(8,128)(2,1)S(1)}, bf16[2048,512]{1,0:T(8,128)(2,1)}, u32[]{:S(2)}) copy-start(bf16[2048,512]{1,0:T(8,128)(2,1)} %param.26) | copy-start | bytes 6291460
  7.2 225.1 %all-gather.3.cloned.1.call-start = ((), (), s32[]{:S(2)}) async-start(), calls=%async_computation.2 | async-start | bytes 19464192 | tf_op jit(solution)/shard_map/all_gather | solution.py:108
  20.8 58.9 %collective-permute-start = (bf16[10,256,512]{2,1,0:T(8,128)(2,1)}, bf16[10,256,512]{2,1,0:T(8,128)(2,1)}, u32[]{:S(2)}, u32[]{:S(2)}) collective-permute-start(bf16[10,256,512]{2,1,0:T(8,128)(2,1)} %convert_element_type.34), channel_id=1, source_target_pairs={{0,8},{8,0},{16,24},{24,16},{1,9},{9,1},{17,25},{25,17},{2,10},{10... | collective-permute-start | bytes 7864328 | tf_op jit(solution)/shard_map/ppermute | solution.py:13
  22.9 57.7 %collective-permute-start.1 = (bf16[10,256,512]{2,1,0:T(8,128)(2,1)}, bf16[10,256,512]{2,1,0:T(8,128)(2,1)}, u32[]{:S(2)}, u32[]{:S(2)}) collective-permute-start(bf16[10,256,512]{2,1,0:T(8,128)(2,1)} %convert_element_type.34), channel_id=1, source_target_pairs={{0,16},{8,24},{16,0},{24,8},{1,17},{9,25},{17,1},{25,9},{2,18},{10... | collective-permute-start | bytes 7864328 | tf_op jit(solution)/shard_map/ppermute | solution.py:13
  24.1 112.8 %collective-permute-start.2 = (bf16[10,256,512]{2,1,0:T(8,128)(2,1)}, bf16[10,256,512]{2,1,0:T(8,128)(2,1)}, u32[]{:S(2)}, u32[]{:S(2)}) collective-permute-start(bf16[10,256,512]{2,1,0:T(8,128)(2,1)} %convert_element_type.34), channel_id=1, source_target_pairs={{0,24},{8,16},{16,8},{24,0},{1,25},{9,17},{17,9},{25,1},{2,26},{10... | collective-permute-start | bytes 7864328 | tf_op jit(solution)/shard_map/ppermute | solution.py:13
  146.8 81.9 %all-to-all-start = ((bf16[8,10,256,64]{2,3,1,0:T(8,128)(2,1)}), bf16[8,10,256,64]{2,3,1,0:T(8,128)(2,1)}, u32[]{:S(2)}, u32[]{:S(2)}) async-start(bf16[8,10,256,64]{2,3,1,0:T(8,128)(2,1)} %convert_bitcast_fusion), calls=%async_computation | async-start | bytes 5242880 | tf_op jit(solution)/shard_map/all_to_all | solution.py:100
  153.4 282.4 %all-gather.5.cloned.1.call-start = ((), (), s32[]{:S(2)}) async-start(), calls=%async_computation.3 | async-start | bytes 13107200 | tf_op jit(solution)/shard_map/all_gather | solution.py:133
  327.1 4.4 copy-start.5
  338.6 4.6 copy-start.3
  444.4 4.9 copy-start.1
  452.9 11.1 %collective-permute-start.4 = (f32[3,10,256,1]{2,0,1,3:T(4,128)}, f32[3,10,256,1]{2,0,1,3:T(4,128)}, u32[]{:S(2)}, u32[]{:S(2)}) collective-permute-start(f32[3,10,256,1]{2,0,1,3:T(4,128)} %pad_maximum_fusion.2), channel_id=1, source_target_pairs={{0,8},{8,16},{16,24},{1,9},{9,17},{17,25},{2,10},{10,18},{18,26},{... | collective-permute-start | bytes 92168 | tf_op jit(solution)/shard_map/ppermute | solution.py:152
  456.7 5.3 %collective-permute-start.3 = (f32[2,10,256,1]{2,0,1,3:T(2,128)S(1)}, f32[2,10,256,1]{2,0,1,3:T(2,128)S(1)}, u32[]{:S(2)}, u32[]{:S(2)}) collective-permute-start(f32[2,10,256,1]{2,0,1,3:T(2,128)S(1)} %pad_maximum_fusion.4), channel_id=1, source_target_pairs={{8,0},{16,8},{24,16},{9,1},{17,9},{25,17},{10,2},{18,10},{26,18},{... | collective-permute-start | bytes 61448 | tf_op jit(solution)/shard_map/ppermute | solution.py:151
  458.0 11.0 %collective-permute-start.6 = (f32[3,10,1,512]{3,2,1,0:T(1,128)S(1)}, f32[3,10,1,512]{3,2,1,0:T(1,128)S(1)}, u32[]{:S(2)}, u32[]{:S(2)}) collective-permute-start(f32[3,10,1,512]{3,2,1,0:T(1,128)S(1)} %pad_maximum_fusion.1), channel_id=1, source_target_pairs={{0,1},{1,2},{2,3},{3,4},{4,5},{5,6},{6,7},{8,9},{9,10},{10,11},{11... | collective-permute-start | bytes 184328 | tf_op jit(solution)/shard_map/ppermute | solution.py:152
  468.0 8.7 %copy-start.2 = (f32[10,256,512]{2,1,0:T(8,128)S(1)}, f32[10,256,512]{2,1,0:T(8,128)}, u32[]{:S(2)}) copy-start(f32[10,256,512]{2,1,0:T(8,128)} %copy-done.1) | copy-start | bytes 15728644
  468.0 8.7 %copy-start.4 = (f32[10,256,1]{2,1,0:T(8,128)S(1)}, f32[10,256,1]{2,1,0:T(8,128)}, u32[]{:S(2)}) copy-start(f32[10,256,1]{2,1,0:T(8,128)} %copy.243) | copy-start | bytes 30724
  470.6 6.1 %collective-permute-start.5 = (f32[2,10,1,512]{3,2,1,0:T(1,128)S(1)}, f32[2,10,1,512]{3,2,1,0:T(1,128)S(1)}, u32[]{:S(2)}, u32[]{:S(2)}) collective-permute-start(f32[2,10,1,512]{3,2,1,0:T(1,128)S(1)} %pad_maximum_fusion.3), channel_id=1, source_target_pairs={{1,0},{2,1},{3,2},{4,3},{5,4},{6,5},{7,6},{9,8},{10,9},{11,10},{12... | collective-permute-start | bytes 122888 | tf_op jit(solution)/shard_map/ppermute | solution.py:151
Sparse Core Ops, SparseCore 0:
  16.6 177.1 all-gather.2
  331.6 104.1 all-gather.4

commit v14 on v13

--- a/solution.py
+++ b/solution.py
@@ -91,12 +91,14 @@
     modes = left_x.shape[1] // count_y
 
     rounded = residual.astype(jnp.bfloat16)
-    spectral_x = jnp.einsum(
-        "zyx,xci->czyi",
-        jnp.concatenate(exchange(rounded, "px"), axis=2),
-        in_exchange_order(left_x, "px").reshape(-1, count_y, modes),
-        preferred_element_type=jnp.float32,
-    ).astype(jnp.bfloat16)
+    weights_x = in_exchange_order(left_x, "px").reshape(count_x, width, count_y, modes)
+    blocks = exchange(rounded, "px")
+    spectral_x = jnp.einsum("zyx,xci->czyi", blocks[0], weights_x[0], preferred_element_type=jnp.float32)
+    for k in range(1, count_x):
+        spectral_x = spectral_x + jnp.einsum(
+            "zyx,xci->czyi", blocks[k], weights_x[k], preferred_element_type=jnp.float32
+        )
+    spectral_x = spectral_x.astype(jnp.bfloat16)
     pencil = lax.all_to_all(spectral_x, "py", 0, 0, tiled=True)
     high = lax.reduce_precision(lambda_y, exponent_bits=8, mantissa_bits=7)
     rest = lambda_y - high

time: 505 us -> 505 us (level)
  waiting for transfers between devices: 253 us -> 247 us
  matrix products: 39.2 us -> 44.7 us
    ppermute x3, waiting for transfers between devices: 105 us -> 93.7 us  [exchange(): parts.append(lax.ppermute(block, axis, [(s, s ^ k) for s in range(count)]))]
    dot_general x1 -> x4, matrix products: 9.91 us -> 15.3 us  [the longest x3 11.9 us: shards(): jnp.einsum('zyx,xci->czyi', blocks[k], weights_x[k], preferred_element_ty...]
  transfers between devices with their start and end apart: 10 -> 10, of which waited for: 5 -> 4; matrix products, arithmetic and copies ran while one was open for 13% -> 14% of each run, Pallas kernels for 0% -> 0%
where the time goes in v14:
time: 505 us; the launch traced here: 504 us
  waiting for transfers between devices  247 us (49%)
  blocking collectives  62.1 us (12%)
  local copies, waits for them, and re-layouts  56.6 us (11%)
  other arithmetic  51.5 us (10%)
  matrix products  44.7 us (9%)
  starting transfers between devices  22.1 us (4%)
  between operations  14.4 us (3%)
  Pallas kernels  5.82 us (1%)
    ppermute x3, waiting for transfers between devices, exchange(): parts.append(lax.ppermute(block, axis, [(s, s ^ k) for s in range(count)]))  93.7 us
    all_to_all x1, waiting for transfers between devices, shards(): pencil = lax.all_to_all(spectral_x, 'py', 0, 0, tiled=True)  78.9 us
    all_gather x1, waiting for transfers between devices, shards(): lax.all_gather(back_y, 'px', axis=2, tiled=True)  74.4 us
    all_to_all x1, blocking collectives, shards(): back_y = lax.all_to_all(back_pencil, 'py', 0, 0, tiled=True)  62.1 us
    select_n x1, other arithmetic, net(): flux_high = jnp.where(edge, 0.0, flux_high)  16.2 us
    slice x4, local copies, waits for them, and re-layouts, net(): rest = lambda a: lax.slice_in_dim(a, 1, None, axis=dim)  13.8 us
    dot_general x3, matrix products, shards(): jnp.einsum('zyx,xci->czyi', blocks[k], weights_x[k], preferred_element_ty...  11.9 us
    dot_general x1, matrix products, shards(): jnp.einsum('ny,jy->nj', flat, carried[:, :columns], preferred_element_typ...  11.1 us
  transfers between devices with their start and end apart: 10, of which 4 were waited for; matrix products, arithmetic and copies ran while one was open for 14% of the time, Pallas kernels for 0%

profile of v14, /device:TPU:1, one launch (start us, length us, event | category | flops | bytes accessed | tf_op | source)
XLA Modules:
  0.0 504.2 jit_solution(4645907751242153468)
XLA Ops:
  13.3 3.1 pad_maximum_fusion
  16.4 4.3 convert_element_type.34
  24.1 2.8 constant_dynamic-slice_fusion
  32.7 3.5 fusion.18
  36.2 43.5 %collective-permute-done.1 = bf16[10,256,512]{2,1,0:T(8,128)(2,1)} collective-permute-done((bf16[10,256,512]{2,1,0:T(8,128)(2,1)}, bf16[10,256,512]{2,1,0:T(8,128)(2,1)}, u32[]{:S(2)}, u32[]{:S(2)}) %collective-permute-start.1) | collective-permute-done | bytes 2621472 | tf_op jit(solution)/shard_map/ppermute | solution.py:13
  79.7 3.4 fusion.14
  83.2 3.5 fusion.16
  86.6 50.2 %collective-permute-done.2 = bf16[10,256,512]{2,1,0:T(8,128)(2,1)} collective-permute-done((bf16[10,256,512]{2,1,0:T(8,128)(2,1)}, bf16[10,256,512]{2,1,0:T(8,128)(2,1)}, u32[]{:S(2)}, u32[]{:S(2)}) %collective-permute-start.2) | collective-permute-done | bytes 2621472 | tf_op jit(solution)/shard_map/ppermute | solution.py:13
  136.8 5.0 fusion.11
  141.8 6.6 %all-to-all-start = ((bf16[8,10,256,64]{2,3,1,0:T(8,128)(2,1)}), bf16[8,10,256,64]{2,3,1,0:T(8,128)(2,1)}, u32[]{:S(2)}, u32[]{:S(2)}) async-start(bf16[8,10,256,64]{2,3,1,0:T(8,128)(2,1)} %fusion.11), calls=%async_computation | async-start | bytes 5242880 | tf_op jit(solution)/shard_map/all_to_all | solution.py:102
  149.9 78.9 %all-to-all-done = bf16[8,10,256,64]{2,3,1,0:T(8,128)(2,1)} async-done(((bf16[8,10,256,64]{2,3,1,0:T(8,128)(2,1)}), bf16[8,10,256,64]{2,3,1,0:T(8,128)(2,1)}, u32[]{:S(2)}, u32[]{:S(2)}) %all-to-all-start) | async-done | bytes 2621472 | tf_op jit(solution)/shard_map/all_to_all | solution.py:102
  228.8 3.6 copy.258
  235.0 11.1 %fusion.2.rhs_ref = f32[10,64,2048]{2,1,0:T(8,128)} fusion(bf16[10,64,2048]{2,1,0:T(8,128)(2,1)} %bitcast.124, bf16[2048,4224]{1,0:T(8,128)(2,1)} %all-gather.3.cloned.1.call-done), kind=kOutput, calls=%fused_computation.3 | convolution fusion | flops 5368709120 | bytes 16252928 | tf_op jit(solution)/shard_map/ny,jy->nj/dot_general | solution.py:114
  246.1 5.8 %shard_map.131 = bf16[10,64,2048]{2,1,0:T(8,128)(2,1)} custom-call(f32[9]{0:T(128)} %coupling_ref.1, f32[10]{0:T(128)} %shift_ref.1, f32[1,2048]{1,0:T(1,128)} %bitcast.128, f32[64,1]{1,0:T(8,128)} %copy.238.lx_ref, f32[10,64,2048]{2,1,0:T(8,128)} %fusion.2.rhs_ref), custom_call_target="tpu_custom_call" | custom-call | tf_op jit(solution)/shard_map/pallas_call | solution.py:57
  251.9 9.6 %fusion.8 = bf16[640,2048]{1,0:T(8,128)(2,1)S(1)} fusion(bf16[640,2048]{1,0:T(8,128)(2,1)} %bitcast.123, bf16[2048,4224]{1,0:T(8,128)(2,1)} %all-gather.3.cloned.1.call-done), kind=kOutput, calls=%fused_computation.19 | convolution fusion | flops 5370019840 | bytes 13631488 | tf_op jit(solution)/shard_map/nj,yj->ny/dot_general | solution.py:124
  263.1 62.1 %all_to_all.10 = bf16[8,10,256,64]{2,3,1,0:T(8,128)(2,1)S(1)} all-to-all(bf16[8,10,256,64]{2,3,1,0:T(8,128)(2,1)S(1)} %bitcast.118), channel_id=1, replica_groups=mesh['px'=4,'py'=8] {'py'}, dimensions={0} | all-to-all | bytes 5242880 | tf_op jit(solution)/shard_map/all_to_all | solution.py:131
  327.0 4.4 copy.241
  332.1 6.3 %select_select_fusion = f32[10,256,512]{2,1,0:T(8,128)S(1)} fusion(s32[10,256,512]{2,1,0:T(8,128)} %param.27, f32[]{:T(128)} %bitcast.30, f32[]{:T(128)} %bitcast.29, f32[]{:T(128)} %bitcast.28, f32[]{:T(128)} %bitcast.27), kind=kLoop, calls=%fused_computation.16 | loop fusion | flops 10485760 | bytes 10485776 | tf_op jit(solution)/shard_map/jit(_where)/select_n | solution.py:142
  338.4 4.0 slice.218
  343.0 3.1 slice.231
  346.1 3.0 slice_reduce_fusion
  349.1 8.3 %slice_bitcast_fusion.2 = (s32[10,256,512]{2,1,0:T(8,128)}, s32[10,256,512]{2,1,0:T(8,128)S(1)}) fusion(s32[2,10,256,512]{3,2,1,0:T(8,128)} %param.28), kind=kLoop, calls=%fused_computation.15 | loop fusion | bytes 20971520 | tf_op jit(solution)/shard_map/squeeze | solution.py:144
  361.2 74.4 %all-gather.5.cloned.1.call-done = bf16[10,256,2048]{2,1,0:T(8,128)(2,1)} async-done(((bf16[10,256,512]{2,1,0:T(8,128)(2,1)}), bf16[10,256,2048]{2,1,0:T(8,128)(2,1)}) %all-gather.5.cloned.1.call-update) | async-done | bytes 10485776 | tf_op jit(solution)/shard_map/all_gather | solution.py:135
  435.7 8.6 %fusion.20 = f32[10,256,512]{2,1,0:T(8,128)S(1)} fusion(bf16[10,256,2048]{2,1,0:T(8,128)(2,1)} %all-gather.5.cloned.1.call-done, bf16[2048,512]{1,0:T(8,128)(2,1)S(1)} %copy-done), kind=kOutput, calls=%fused_computation.31 | convolution fusion | flops 5368709120 | bytes 17825792 | tf_op jit(solution)/shard_map/zyi,ix->zyx/dot_general | solution.py:133
  445.4 3.7 slice.222
  449.1 3.0 slice.235
  452.8 3.6 collective-permute-start.4
  457.9 4.0 collective-permute-start.6
  470.5 3.2 collective-permute-start.5
  473.7 2.8 multiply_select_fusion
  476.6 16.2 %fusion.7 = (f32[10,256,512]{2,1,0:T(8,128)S(1)}, f32[10,256,512]{2,1,0:T(8,128)S(1)}) fusion(f32[10,1,512]{2,1,0:T(1,128)S(1)} %get-tuple-element.54, f32[10,255,512]{2,1,0:T(8,128)} %slice.231, f32[10,256,512]{2,1,0:T(8,128)S(1)} %copy-done.2, f32[10,1,512]{2,1,0:T(1,128)S(1)} %get-tuple-element.53, f32[10,255,512]{2,1,0:T(8,128)} %slice.235, ...), kind=kLoop, calls=%fused_computation.12 | loop fusion | flops 28835840 | bytes 52429584 | tf_op jit(solution)/shard_map/jit(_where)/select_n | solution.py:162
  492.8 4.5 fusion.5
  (78 shorter events, 39.6 us)
Async XLA Ops:
  7.2 428.5 %copy-start = (bf16[2048,512]{1,0:T(8,128)(2,1)S(1)}, bf16[2048,512]{1,0:T(8,128)(2,1)}, u32[]{:S(2)}) copy-start(bf16[2048,512]{1,0:T(8,128)(2,1)} %param.26) | copy-start | bytes 6291460
  7.2 225.2 %all-gather.3.cloned.1.call-start = ((), (), s32[]{:S(2)}) async-start(), calls=%async_computation.2 | async-start | bytes 19464192 | tf_op jit(solution)/shard_map/all_gather | solution.py:110
  20.8 59.0 %collective-permute-start.1 = (bf16[10,256,512]{2,1,0:T(8,128)(2,1)}, bf16[10,256,512]{2,1,0:T(8,128)(2,1)}, u32[]{:S(2)}, u32[]{:S(2)}) collective-permute-start(bf16[10,256,512]{2,1,0:T(8,128)(2,1)} %convert_element_type.34), channel_id=1, source_target_pairs={{0,16},{8,24},{16,0},{24,8},{1,17},{9,25},{17,1},{25,9},{2,18},{10... | collective-permute-start | bytes 7864328 | tf_op jit(solution)/shard_map/ppermute | solution.py:13
  22.8 60.3 %collective-permute-start = (bf16[10,256,512]{2,1,0:T(8,128)(2,1)}, bf16[10,256,512]{2,1,0:T(8,128)(2,1)}, u32[]{:S(2)}, u32[]{:S(2)}) collective-permute-start(bf16[10,256,512]{2,1,0:T(8,128)(2,1)} %convert_element_type.34), channel_id=1, source_target_pairs={{0,8},{8,0},{16,24},{24,16},{1,9},{9,1},{17,25},{25,17},{2,10},{10... | collective-permute-start | bytes 7864328 | tf_op jit(solution)/shard_map/ppermute | solution.py:13
  24.0 112.7 %collective-permute-start.2 = (bf16[10,256,512]{2,1,0:T(8,128)(2,1)}, bf16[10,256,512]{2,1,0:T(8,128)(2,1)}, u32[]{:S(2)}, u32[]{:S(2)}) collective-permute-start(bf16[10,256,512]{2,1,0:T(8,128)(2,1)} %convert_element_type.34), channel_id=1, source_target_pairs={{0,24},{8,16},{16,8},{24,0},{1,25},{9,17},{17,9},{25,1},{2,26},{10... | collective-permute-start | bytes 7864328 | tf_op jit(solution)/shard_map/ppermute | solution.py:13
  83.2 53.6 %copy-start.5 = (bf16[1,512,512]{1,2,0:T(8,128)(2,1)S(1)}, bf16[1,512,512]{1,2,0:T(8,128)(2,1)}, u32[]{:S(2)}) copy-start(bf16[1,512,512]{1,2,0:T(8,128)(2,1)} %copy.256) | copy-start | bytes 1572868
  141.8 87.0 %all-to-all-start = ((bf16[8,10,256,64]{2,3,1,0:T(8,128)(2,1)}), bf16[8,10,256,64]{2,3,1,0:T(8,128)(2,1)}, u32[]{:S(2)}, u32[]{:S(2)}) async-start(bf16[8,10,256,64]{2,3,1,0:T(8,128)(2,1)} %fusion.11), calls=%async_computation | async-start | bytes 5242880 | tf_op jit(solution)/shard_map/all_to_all | solution.py:102
  148.4 287.2 %all-gather.5.cloned.1.call-start = ((), (), s32[]{:S(2)}) async-start(), calls=%async_computation.3 | async-start | bytes 13107200 | tf_op jit(solution)/shard_map/all_gather | solution.py:135
  327.0 4.4 copy-start.6
  338.4 4.6 copy-start.3
  444.3 4.9 copy-start.1
  452.8 11.1 %collective-permute-start.4 = (f32[3,10,256,1]{2,0,1,3:T(4,128)}, f32[3,10,256,1]{2,0,1,3:T(4,128)}, u32[]{:S(2)}, u32[]{:S(2)}) collective-permute-start(f32[3,10,256,1]{2,0,1,3:T(4,128)} %pad_maximum_fusion.2), channel_id=1, source_target_pairs={{0,8},{8,16},{16,24},{1,9},{9,17},{17,25},{2,10},{10,18},{18,26},{... | collective-permute-start | bytes 92168 | tf_op jit(solution)/shard_map/ppermute | solution.py:154
  456.5 5.3 %collective-permute-start.3 = (f32[2,10,256,1]{2,0,1,3:T(2,128)S(1)}, f32[2,10,256,1]{2,0,1,3:T(2,128)S(1)}, u32[]{:S(2)}, u32[]{:S(2)}) collective-permute-start(f32[2,10,256,1]{2,0,1,3:T(2,128)S(1)} %pad_maximum_fusion.4), channel_id=1, source_target_pairs={{8,0},{16,8},{24,16},{9,1},{17,9},{25,17},{10,2},{18,10},{26,18},{... | collective-permute-start | bytes 61448 | tf_op jit(solution)/shard_map/ppermute | solution.py:153
  457.9 11.0 %collective-permute-start.6 = (f32[3,10,1,512]{3,2,1,0:T(1,128)S(1)}, f32[3,10,1,512]{3,2,1,0:T(1,128)S(1)}, u32[]{:S(2)}, u32[]{:S(2)}) collective-permute-start(f32[3,10,1,512]{3,2,1,0:T(1,128)S(1)} %pad_maximum_fusion.1), channel_id=1, source_target_pairs={{0,1},{1,2},{2,3},{3,4},{4,5},{5,6},{6,7},{8,9},{9,10},{10,11},{11... | collective-permute-start | bytes 184328 | tf_op jit(solution)/shard_map/ppermute | solution.py:154
  467.9 8.7 %copy-start.2 = (f32[10,256,512]{2,1,0:T(8,128)S(1)}, f32[10,256,512]{2,1,0:T(8,128)}, u32[]{:S(2)}) copy-start(f32[10,256,512]{2,1,0:T(8,128)} %copy-done.1) | copy-start | bytes 15728644
  467.9 8.7 %copy-start.4 = (f32[10,256,1]{2,1,0:T(8,128)S(1)}, f32[10,256,1]{2,1,0:T(8,128)}, u32[]{:S(2)}) copy-start(f32[10,256,1]{2,1,0:T(8,128)} %copy.243) | copy-start | bytes 30724
  470.5 6.0 %collective-permute-start.5 = (f32[2,10,1,512]{3,2,1,0:T(1,128)S(1)}, f32[2,10,1,512]{3,2,1,0:T(1,128)S(1)}, u32[]{:S(2)}, u32[]{:S(2)}) collective-permute-start(f32[2,10,1,512]{3,2,1,0:T(1,128)S(1)} %pad_maximum_fusion.3), channel_id=1, source_target_pairs={{1,0},{2,1},{3,2},{4,3},{5,4},{6,5},{7,6},{9,8},{10,9},{11,10},{12... | collective-permute-start | bytes 122888 | tf_op jit(solution)/shard_map/ppermute | solution.py:153
Sparse Core Ops, SparseCore 0:
  16.5 180.6 all-gather.2
  331.5 104.1 all-gather.4

commit v15 on v13

--- a/solution.py
+++ b/solution.py
@@ -126,11 +126,15 @@
         preferred_element_type=jnp.float32,
     ).astype(jnp.bfloat16)
     back_pencil = jnp.transpose(back_flat.reshape(layers, modes, count_y, height), (2, 0, 3, 1))
-    back_y = lax.all_to_all(back_pencil, "py", 0, 0, tiled=True)
-    back_y = jnp.moveaxis(back_y, 0, 2).reshape(layers, height, -1)
+    split = layers // 2
+    gathered = []
+    for lo, hi in ((0, split), (split, layers)):
+        part = lax.all_to_all(back_pencil[:, lo:hi], "py", 0, 0, tiled=True)
+        part = jnp.moveaxis(part, 0, 2).reshape(hi - lo, height, -1)
+        gathered.append(lax.all_gather(part, "px", axis=2, tiled=True))
     correction = jnp.einsum(
         "zyi,ix->zyx",
-        lax.all_gather(back_y, "px", axis=2, tiled=True),
+        jnp.concatenate(gathered),
         right_x,
         preferred_element_type=jnp.float32,
     )

time: 505 us -> 495 us (0.980)
  waiting for transfers between devices: 253 us -> 237 us
  blocking collectives: 62.3 us -> 68.9 us
    all_gather x1 -> x2, waiting for transfers between devices: 74.5 us -> 59 us  [shards(): gathered.append(lax.all_gather(part, 'px', axis=2, tiled=True))]
    all_to_all x1 -> x2, blocking collectives: 62.3 us -> 68.9 us  [shards(): part = lax.all_to_all(back_pencil[:, lo:hi], 'py', 0, 0, tiled=True)]
  transfers between devices with their start and end apart: 10 -> 11, of which waited for: 5 -> 5; matrix products, arithmetic and copies ran while one was open for 13% -> 14% of each run, Pallas kernels for 0% -> 0%
where the time goes in v15:
time: 495 us; the launch traced here: 494 us
  waiting for transfers between devices  237 us (48%)
  blocking collectives  68.9 us (14%)
  local copies, waits for them, and re-layouts  54.9 us (11%)
  other arithmetic  51.6 us (10%)
  matrix products  39.3 us (8%)
  starting transfers between devices  22.1 us (4%)
  between operations  14.1 us (3%)
  Pallas kernels  5.82 us (1%)
    ppermute x3, waiting for transfers between devices, exchange(): parts.append(lax.ppermute(block, axis, [(s, s ^ k) for s in range(count)]))  105 us
    all_to_all x1, waiting for transfers between devices, shards(): pencil = lax.all_to_all(spectral_x, 'py', 0, 0, tiled=True)  73.8 us
    all_to_all x2, blocking collectives, shards(): part = lax.all_to_all(back_pencil[:, lo:hi], 'py', 0, 0, tiled=True)  68.9 us
    all_gather x2, waiting for transfers between devices, shards(): gathered.append(lax.all_gather(part, 'px', axis=2, tiled=True))  59 us
    select_n x1, other arithmetic, net(): flux_high = jnp.where(edge, 0.0, flux_high)  16.3 us
    slice x4, local copies, waits for them, and re-layouts, net(): rest = lambda a: lax.slice_in_dim(a, 1, None, axis=dim)  14.1 us
    dot_general x1, matrix products, shards(): jnp.einsum('ny,jy->nj', flat, carried[:, :columns], preferred_element_typ...  11.1 us
    dot_general x1, matrix products, shards(): jnp.einsum('zyx,xci->czyi', jnp.concatenate(exchange(rounded, 'px'), axis...  9.92 us
  transfers between devices with their start and end apart: 11, of which 5 were waited for; matrix products, arithmetic and copies ran while one was open for 14% of the time, Pallas kernels for 0%

profile of v15, /device:TPU:1, one launch (start us, length us, event | category | flops | bytes accessed | tf_op | source)
XLA Modules:
  0.0 494.1 jit_solution(10059270699946807408)
XLA Ops:
  13.5 3.1 pad_maximum_fusion
  16.6 4.3 convert_element_type.34
  24.2 2.7 constant_dynamic-slice_fusion.3
  26.9 2.1 copy.262
  29.0 2.2 copy.263
  32.4 47.4 %collective-permute-done = bf16[10,256,512]{2,1,0:T(8,128)(2,1)} collective-permute-done((bf16[10,256,512]{2,1,0:T(8,128)(2,1)}, bf16[10,256,512]{2,1,0:T(8,128)(2,1)}, u32[]{:S(2)}, u32[]{:S(2)}) %collective-permute-start) | collective-permute-done | bytes 2621472 | tf_op jit(solution)/shard_map/ppermute | solution.py:13
  80.7 56.3 %collective-permute-done.2 = bf16[10,256,512]{2,1,0:T(8,128)(2,1)} collective-permute-done((bf16[10,256,512]{2,1,0:T(8,128)(2,1)}, bf16[10,256,512]{2,1,0:T(8,128)(2,1)}, u32[]{:S(2)}, u32[]{:S(2)}) %collective-permute-start.2) | collective-permute-done | bytes 2621472 | tf_op jit(solution)/shard_map/ppermute | solution.py:13
  137.0 9.9 %convert_bitcast_fusion = bf16[8,10,256,64]{2,3,1,0:T(8,128)(2,1)} fusion(bf16[10,256,512]{2,1,0:T(8,128)(2,1)} %collective-permute-done.2, bf16[10,256,512]{2,1,0:T(8,128)(2,1)} %collective-permute-done.1, bf16[10,256,512]{2,1,0:T(8,128)(2,1)} %collective-permute-done, bf16[10,256,512]{2,1,0:T(8,128)(2,1)} %convert_element_type.34, ...), kind=kOutput, calls=%fused_computation.32 | convolution fusion | flops 5420351488 | bytes 15204352 | tf_op jit(solution)/shard_map/zyx,xci->czyi/dot_general | solution.py:94
  146.9 6.6 %all-to-all-start = ((bf16[8,10,256,64]{2,3,1,0:T(8,128)(2,1)}), bf16[8,10,256,64]{2,3,1,0:T(8,128)(2,1)}, u32[]{:S(2)}, u32[]{:S(2)}) async-start(bf16[8,10,256,64]{2,3,1,0:T(8,128)(2,1)} %convert_bitcast_fusion), calls=%async_computation | async-start | bytes 5242880 | tf_op jit(solution)/shard_map/all_to_all | solution.py:100
  154.9 73.8 %all-to-all-done = bf16[8,10,256,64]{2,3,1,0:T(8,128)(2,1)} async-done(((bf16[8,10,256,64]{2,3,1,0:T(8,128)(2,1)}), bf16[8,10,256,64]{2,3,1,0:T(8,128)(2,1)}, u32[]{:S(2)}, u32[]{:S(2)}) %all-to-all-start) | async-done | bytes 2621472 | tf_op jit(solution)/shard_map/all_to_all | solution.py:100
  228.8 3.6 copy.267
  235.0 11.1 %fusion.13.rhs_ref = f32[10,64,2048]{2,1,0:T(8,128)} fusion(bf16[10,64,2048]{2,1,0:T(8,128)(2,1)} %bitcast.102, bf16[2048,4224]{1,0:T(8,128)(2,1)} %all-gather.4.cloned.1.call-done), kind=kOutput, calls=%fused_computation.15 | convolution fusion | flops 5368709120 | bytes 16252928 | tf_op jit(solution)/shard_map/ny,jy->nj/dot_general | solution.py:112
  246.1 5.8 %shard_map.131 = bf16[10,64,2048]{2,1,0:T(8,128)(2,1)} custom-call(f32[9]{0:T(128)} %coupling_ref.1, f32[10]{0:T(128)} %shift_ref.1, f32[1,2048]{1,0:T(1,128)} %bitcast.109, f32[64,1]{1,0:T(8,128)} %copy.248.lx_ref, f32[10,64,2048]{2,1,0:T(8,128)} %fusion.13.rhs_ref), custom_call_target="tpu_custom_call" | custom-call | tf_op jit(solution)/shard_map/pallas_call | solution.py:57
  251.9 9.6 %fusion.19 = bf16[640,2048]{1,0:T(8,128)(2,1)S(1)} fusion(bf16[640,2048]{1,0:T(8,128)(2,1)} %bitcast.101, bf16[2048,4224]{1,0:T(8,128)(2,1)} %all-gather.4.cloned.1.call-done), kind=kOutput, calls=%fused_computation.30 | convolution fusion | flops 5370019840 | bytes 13631488 | tf_op jit(solution)/shard_map/nj,yj->ny/dot_general | solution.py:122
  263.2 34.2 %all_to_all.15 = bf16[8,5,256,64]{2,3,1,0:T(8,128)(2,1)S(1)} all-to-all(bf16[8,5,256,64]{2,3,1,0:T(8,128)(2,1)S(1)} %get-tuple-element.49), channel_id=1, replica_groups=mesh['px'=4,'py'=8] {'py'}, dimensions={0} | all-to-all | bytes 2621440 | tf_op jit(solution)/shard_map/all_to_all | solution.py:132
  298.6 2.5 copy.251
  301.2 34.7 %all_to_all.16 = bf16[8,5,256,64]{2,3,1,0:T(8,128)(2,1)S(1)} all-to-all(bf16[8,5,256,64]{2,3,1,0:T(8,128)(2,1)S(1)} %get-tuple-element.50), channel_id=1, replica_groups=mesh['px'=4,'py'=8] {'py'}, dimensions={0} | all-to-all | bytes 2621440 | tf_op jit(solution)/shard_map/all_to_all | solution.py:132
  338.2 6.4 %select_select_fusion = f32[10,256,512]{2,1,0:T(8,128)S(1)} fusion(s32[10,256,512]{2,1,0:T(8,128)} %param.27, f32[]{:T(128)} %bitcast.23, f32[]{:T(128)} %bitcast.22, f32[]{:T(128)} %bitcast.21, f32[]{:T(128)} %bitcast.20), kind=kLoop, calls=%fused_computation.28 | loop fusion | flops 10485760 | bytes 10485776 | tf_op jit(solution)/shard_map/jit(_where)/select_n | solution.py:144
  344.6 3.9 slice.220
  348.5 3.0 slice.233
  351.5 2.8 slice_reduce_fusion
  354.4 8.3 %slice_bitcast_fusion.2 = (s32[10,256,512]{2,1,0:T(8,128)}, s32[10,256,512]{2,1,0:T(8,128)S(1)}) fusion(s32[2,10,256,512]{3,2,1,0:T(8,128)} %param.28), kind=kLoop, calls=%fused_computation.27 | loop fusion | bytes 20971520 | tf_op jit(solution)/shard_map/squeeze | solution.py:146
  366.5 59.0 %all-gather.8.cloned.1.call-done = bf16[5,256,2048]{2,1,0:T(8,128)(2,1)} async-done(((bf16[5,256,512]{2,1,0:T(8,128)(2,1)}), bf16[5,256,2048]{2,1,0:T(8,128)(2,1)}) %all-gather.8.cloned.1.call-update) | async-done | bytes 5242896 | tf_op jit(solution)/shard_map/all_gather | solution.py:134
  425.5 8.6 %fusion.7 = f32[10,256,512]{2,1,0:T(8,128)S(1)} fusion(bf16[5,256,2048]{2,1,0:T(8,128)(2,1)} %all-gather.8.cloned.1.call-done, bf16[5,256,2048]{2,1,0:T(8,128)(2,1)} %all-gather.6.cloned.1.call-done, bf16[2048,512]{1,0:T(8,128)(2,1)S(1)} %copy-done), kind=kOutput, calls=%fused_computation.8 | convolution fusion | flops 5373952000 | bytes 17825792 | tf_op jit(solution)/shard_map/zyi,ix->zyx/dot_general | solution.py:135
  435.3 3.8 slice.224
  439.0 3.4 slice.237
  443.1 3.7 collective-permute-start.4
  448.2 4.0 collective-permute-start.6
  460.7 3.2 collective-permute-start.5
  463.9 2.8 multiply_select_fusion
  466.8 16.3 %fusion.18 = (f32[10,256,512]{2,1,0:T(8,128)S(1)}, f32[10,256,512]{2,1,0:T(8,128)S(1)}) fusion(f32[10,1,512]{2,1,0:T(1,128)S(1)} %get-tuple-element.56, f32[10,255,512]{2,1,0:T(8,128)} %slice.233, f32[10,256,512]{2,1,0:T(8,128)S(1)} %copy-done.2, f32[10,1,512]{2,1,0:T(1,128)S(1)} %get-tuple-element.55, f32[10,255,512]{2,1,0:T(8,128)} %slice.237, ...), kind=kLoop, calls=%fused_computation.24 | loop fusion | flops 28835840 | bytes 52429584 | tf_op jit(solution)/shard_map/jit(_where)/select_n | solution.py:164
  483.1 4.5 fusion.16
  (80 shorter events, 36.4 us)
Async XLA Ops:
  7.2 418.3 %copy-start = (bf16[2048,512]{1,0:T(8,128)(2,1)S(1)}, bf16[2048,512]{1,0:T(8,128)(2,1)}, u32[]{:S(2)}) copy-start(bf16[2048,512]{1,0:T(8,128)(2,1)} %param.26) | copy-start | bytes 6291460
  7.2 225.2 %all-gather.4.cloned.1.call-start = ((), (), s32[]{:S(2)}) async-start(), calls=%async_computation.3 | async-start | bytes 19464192 | tf_op jit(solution)/shard_map/all_gather | solution.py:108
  20.9 58.9 %collective-permute-start = (bf16[10,256,512]{2,1,0:T(8,128)(2,1)}, bf16[10,256,512]{2,1,0:T(8,128)(2,1)}, u32[]{:S(2)}, u32[]{:S(2)}) collective-permute-start(bf16[10,256,512]{2,1,0:T(8,128)(2,1)} %convert_element_type.34), channel_id=1, source_target_pairs={{0,8},{8,0},{16,24},{24,16},{1,9},{9,1},{17,25},{25,17},{2,10},{10... | collective-permute-start | bytes 7864328 | tf_op jit(solution)/shard_map/ppermute | solution.py:13
  22.9 57.7 %collective-permute-start.1 = (bf16[10,256,512]{2,1,0:T(8,128)(2,1)}, bf16[10,256,512]{2,1,0:T(8,128)(2,1)}, u32[]{:S(2)}, u32[]{:S(2)}) collective-permute-start(bf16[10,256,512]{2,1,0:T(8,128)(2,1)} %convert_element_type.34), channel_id=1, source_target_pairs={{0,16},{8,24},{16,0},{24,8},{1,17},{9,25},{17,1},{25,9},{2,18},{10... | collective-permute-start | bytes 7864328 | tf_op jit(solution)/shard_map/ppermute | solution.py:13
  24.2 112.8 %collective-permute-start.2 = (bf16[10,256,512]{2,1,0:T(8,128)(2,1)}, bf16[10,256,512]{2,1,0:T(8,128)(2,1)}, u32[]{:S(2)}, u32[]{:S(2)}) collective-permute-start(bf16[10,256,512]{2,1,0:T(8,128)(2,1)} %convert_element_type.34), channel_id=1, source_target_pairs={{0,24},{8,16},{16,8},{24,0},{1,25},{9,17},{17,9},{25,1},{2,26},{10... | collective-permute-start | bytes 7864328 | tf_op jit(solution)/shard_map/ppermute | solution.py:13
  146.9 81.9 %all-to-all-start = ((bf16[8,10,256,64]{2,3,1,0:T(8,128)(2,1)}), bf16[8,10,256,64]{2,3,1,0:T(8,128)(2,1)}, u32[]{:S(2)}, u32[]{:S(2)}) async-start(bf16[8,10,256,64]{2,3,1,0:T(8,128)(2,1)} %convert_bitcast_fusion), calls=%async_computation | async-start | bytes 5242880 | tf_op jit(solution)/shard_map/all_to_all | solution.py:100
  153.5 213.0 %all-gather.6.cloned.1.call-start = ((), (), s32[]{:S(2)}) async-start(), calls=%async_computation.4 | async-start | bytes 6553600 | tf_op jit(solution)/shard_map/all_gather | solution.py:134
  301.1 36.5 %copy-start.5 = (f32[4]{0:T(128)S(1)}, f32[4]{0:T(128)}, u32[]{:S(2)}) copy-start(f32[4]{0:T(128)} %param.29) | copy-start | bytes 52
  301.1 124.4 %all-gather.8.cloned.1.call-start = ((), (), s32[]{:S(2)}) async-start(), calls=%async_computation.5 | async-start | bytes 6553600 | tf_op jit(solution)/shard_map/all_gather | solution.py:134
  344.6 3.9 copy-start.3
  434.1 4.9 copy-start.1
  443.1 11.0 %collective-permute-start.4 = (f32[3,10,256,1]{2,0,1,3:T(4,128)}, f32[3,10,256,1]{2,0,1,3:T(4,128)}, u32[]{:S(2)}, u32[]{:S(2)}) collective-permute-start(f32[3,10,256,1]{2,0,1,3:T(4,128)} %pad_maximum_fusion.2), channel_id=1, source_target_pairs={{0,8},{8,16},{16,24},{1,9},{9,17},{17,25},{2,10},{10,18},{18,26},{... | collective-permute-start | bytes 92168 | tf_op jit(solution)/shard_map/ppermute | solution.py:156
  446.8 5.3 %collective-permute-start.3 = (f32[2,10,256,1]{2,0,1,3:T(2,128)S(1)}, f32[2,10,256,1]{2,0,1,3:T(2,128)S(1)}, u32[]{:S(2)}, u32[]{:S(2)}) collective-permute-start(f32[2,10,256,1]{2,0,1,3:T(2,128)S(1)} %pad_maximum_fusion.4), channel_id=1, source_target_pairs={{8,0},{16,8},{24,16},{9,1},{17,9},{25,17},{10,2},{18,10},{26,18},{... | collective-permute-start | bytes 61448 | tf_op jit(solution)/shard_map/ppermute | solution.py:155
  448.2 10.9 %collective-permute-start.6 = (f32[3,10,1,512]{3,2,1,0:T(1,128)S(1)}, f32[3,10,1,512]{3,2,1,0:T(1,128)S(1)}, u32[]{:S(2)}, u32[]{:S(2)}) collective-permute-start(f32[3,10,1,512]{3,2,1,0:T(1,128)S(1)} %pad_maximum_fusion.1), channel_id=1, source_target_pairs={{0,1},{1,2},{2,3},{3,4},{4,5},{5,6},{6,7},{8,9},{9,10},{10,11},{11... | collective-permute-start | bytes 184328 | tf_op jit(solution)/shard_map/ppermute | solution.py:156
  458.1 8.7 %copy-start.2 = (f32[10,256,512]{2,1,0:T(8,128)S(1)}, f32[10,256,512]{2,1,0:T(8,128)}, u32[]{:S(2)}) copy-start(f32[10,256,512]{2,1,0:T(8,128)} %copy-done.1) | copy-start | bytes 15728644
  458.1 8.7 %copy-start.4 = (f32[10,256,1]{2,1,0:T(8,128)S(1)}, f32[10,256,1]{2,1,0:T(8,128)}, u32[]{:S(2)}) copy-start(f32[10,256,1]{2,1,0:T(8,128)} %copy.255) | copy-start | bytes 30724
  460.7 6.0 %collective-permute-start.5 = (f32[2,10,1,512]{3,2,1,0:T(1,128)S(1)}, f32[2,10,1,512]{3,2,1,0:T(1,128)S(1)}, u32[]{:S(2)}, u32[]{:S(2)}) collective-permute-start(f32[2,10,1,512]{3,2,1,0:T(1,128)S(1)} %pad_maximum_fusion.3), channel_id=1, source_target_pairs={{1,0},{2,1},{3,2},{4,3},{5,4},{6,5},{7,6},{9,8},{10,9},{11,10},{12... | collective-permute-start | bytes 122888 | tf_op jit(solution)/shard_map/ppermute | solution.py:155
Sparse Core Ops, SparseCore 0:
  16.7 177.1 all-gather.3
  301.2 60.4 all-gather.5
  364.2 61.2 all-gather.7

commit v16 on v15

--- a/solution.py
+++ b/solution.py
@@ -128,7 +128,7 @@
     back_pencil = jnp.transpose(back_flat.reshape(layers, modes, count_y, height), (2, 0, 3, 1))
     split = layers // 2
     gathered = []
-    for lo, hi in ((0, split), (split, layers)):
+    for lo, hi in ((0, layers // 3), (layers // 3, 2 * layers // 3), (2 * layers // 3, layers)):
         part = lax.all_to_all(back_pencil[:, lo:hi], "py", 0, 0, tiled=True)
         part = jnp.moveaxis(part, 0, 2).reshape(hi - lo, height, -1)
         gathered.append(lax.all_gather(part, "px", axis=2, tiled=True))

time: 495 us -> 503 us (1.016)
  blocking collectives: 68.9 us -> 76.4 us
    all_to_all x2 -> x3, blocking collectives: 68.9 us -> 76.4 us  [shards(): part = lax.all_to_all(back_pencil[:, lo:hi], 'py', 0, 0, tiled=True)]
    all_gather x2 -> x3, waiting for transfers between devices: 59 us -> 57 us  [shards(): gathered.append(lax.all_gather(part, 'px', axis=2, tiled=True))]
  transfers between devices with their start and end apart: 11 -> 12, of which waited for: 5 -> 6; matrix products, arithmetic and copies ran while one was open for 14% -> 14% of each run, Pallas kernels for 0% -> 0%
where the time goes in v16:
time: 503 us; the launch traced here: 502 us
  waiting for transfers between devices  235 us (47%)
  blocking collectives  76.4 us (15%)
  local copies, waits for them, and re-layouts  56.9 us (11%)
  other arithmetic  51.7 us (10%)
  matrix products  39.3 us (8%)
  starting transfers between devices  22.2 us (4%)
  between operations  14.1 us (3%)
  Pallas kernels  5.82 us (1%)
    ppermute x3, waiting for transfers between devices, exchange(): parts.append(lax.ppermute(block, axis, [(s, s ^ k) for s in range(count)]))  105 us
    all_to_all x3, blocking collectives, shards(): part = lax.all_to_all(back_pencil[:, lo:hi], 'py', 0, 0, tiled=True)  76.4 us
    all_to_all x1, waiting for transfers between devices, shards(): pencil = lax.all_to_all(spectral_x, 'py', 0, 0, tiled=True)  73.7 us
    all_gather x3, waiting for transfers between devices, shards(): gathered.append(lax.all_gather(part, 'px', axis=2, tiled=True))  57 us
    select_n x1, other arithmetic, net(): flux_high = jnp.where(edge, 0.0, flux_high)  16.3 us
    slice x4, local copies, waits for them, and re-layouts, net(): rest = lambda a: lax.slice_in_dim(a, 1, None, axis=dim)  13.7 us
    dot_general x1, matrix products, shards(): jnp.einsum('ny,jy->nj', flat, carried[:, :columns], preferred_element_typ...  11.1 us
  transfers between devices with their start and end apart: 12, of which 6 were waited for; matrix products, arithmetic and copies ran while one was open for 14% of the time, Pallas kernels for 0%

profile of v16, /device:TPU:1, one launch (start us, length us, event | category | flops | bytes accessed | tf_op | source)
XLA Modules:
  0.0 501.7 jit_solution(15990885637840198702)
XLA Ops:
  13.3 3.1 pad_maximum_fusion
  16.5 4.3 convert_element_type.34
  24.1 2.8 constant_dynamic-slice_fusion.3
  26.8 2.1 copy.274
  29.0 2.2 copy.275
  32.3 47.4 %collective-permute-done = bf16[10,256,512]{2,1,0:T(8,128)(2,1)} collective-permute-done((bf16[10,256,512]{2,1,0:T(8,128)(2,1)}, bf16[10,256,512]{2,1,0:T(8,128)(2,1)}, u32[]{:S(2)}, u32[]{:S(2)}) %collective-permute-start) | collective-permute-done | bytes 2621472 | tf_op jit(solution)/shard_map/ppermute | solution.py:13
  80.6 56.3 %collective-permute-done.2 = bf16[10,256,512]{2,1,0:T(8,128)(2,1)} collective-permute-done((bf16[10,256,512]{2,1,0:T(8,128)(2,1)}, bf16[10,256,512]{2,1,0:T(8,128)(2,1)}, u32[]{:S(2)}, u32[]{:S(2)}) %collective-permute-start.2) | collective-permute-done | bytes 2621472 | tf_op jit(solution)/shard_map/ppermute | solution.py:13
  136.9 9.9 %convert_bitcast_fusion = bf16[8,10,256,64]{2,3,1,0:T(8,128)(2,1)} fusion(bf16[10,256,512]{2,1,0:T(8,128)(2,1)} %collective-permute-done.2, bf16[10,256,512]{2,1,0:T(8,128)(2,1)} %collective-permute-done.1, bf16[10,256,512]{2,1,0:T(8,128)(2,1)} %collective-permute-done, bf16[10,256,512]{2,1,0:T(8,128)(2,1)} %convert_element_type.34, ...), kind=kOutput, calls=%fused_computation.34 | convolution fusion | flops 5420351488 | bytes 15204352 | tf_op jit(solution)/shard_map/zyx,xci->czyi/dot_general | solution.py:94
  146.8 6.6 %all-to-all-start = ((bf16[8,10,256,64]{2,3,1,0:T(8,128)(2,1)}), bf16[8,10,256,64]{2,3,1,0:T(8,128)(2,1)}, u32[]{:S(2)}, u32[]{:S(2)}) async-start(bf16[8,10,256,64]{2,3,1,0:T(8,128)(2,1)} %convert_bitcast_fusion), calls=%async_computation | async-start | bytes 5242880 | tf_op jit(solution)/shard_map/all_to_all | solution.py:100
  154.9 73.7 %all-to-all-done = bf16[8,10,256,64]{2,3,1,0:T(8,128)(2,1)} async-done(((bf16[8,10,256,64]{2,3,1,0:T(8,128)(2,1)}), bf16[8,10,256,64]{2,3,1,0:T(8,128)(2,1)}, u32[]{:S(2)}, u32[]{:S(2)}) %all-to-all-start) | async-done | bytes 2621472 | tf_op jit(solution)/shard_map/all_to_all | solution.py:100
  228.7 3.6 copy.279
  234.9 11.1 %fusion.15.rhs_ref = f32[10,64,2048]{2,1,0:T(8,128)} fusion(bf16[10,64,2048]{2,1,0:T(8,128)(2,1)} %bitcast.107, bf16[2048,4224]{1,0:T(8,128)(2,1)} %all-gather.5.cloned.1.call-done), kind=kOutput, calls=%fused_computation.17 | convolution fusion | flops 5368709120 | bytes 16252928 | tf_op jit(solution)/shard_map/ny,jy->nj/dot_general | solution.py:112
  246.0 5.8 %shard_map.131 = bf16[10,64,2048]{2,1,0:T(8,128)(2,1)} custom-call(f32[9]{0:T(128)} %coupling_ref.1, f32[10]{0:T(128)} %shift_ref.1, f32[1,2048]{1,0:T(1,128)} %bitcast.114, f32[64,1]{1,0:T(8,128)} %copy.258.lx_ref, f32[10,64,2048]{2,1,0:T(8,128)} %fusion.15.rhs_ref), custom_call_target="tpu_custom_call" | custom-call | tf_op jit(solution)/shard_map/pallas_call | solution.py:57
  251.8 9.6 %fusion.21 = bf16[640,2048]{1,0:T(8,128)(2,1)S(1)} fusion(bf16[640,2048]{1,0:T(8,128)(2,1)} %bitcast.106, bf16[2048,4224]{1,0:T(8,128)(2,1)} %all-gather.5.cloned.1.call-done), kind=kOutput, calls=%fused_computation.32 | convolution fusion | flops 5370019840 | bytes 13631488 | tf_op jit(solution)/shard_map/nj,yj->ny/dot_general | solution.py:122
  265.5 22.9 %all_to_all.20 = bf16[8,3,256,64]{2,3,1,0:T(8,128)(2,1)S(1)} all-to-all(bf16[8,3,256,64]{2,3,1,0:T(8,128)(2,1)S(1)} %get-tuple-element.49), channel_id=1, replica_groups=mesh['px'=4,'py'=8] {'py'}, dimensions={0} | all-to-all | bytes 1572864 | tf_op jit(solution)/shard_map/all_to_all | solution.py:132
  289.7 24.4 %all_to_all.21 = bf16[8,3,256,64]{2,3,1,0:T(8,128)(2,1)S(1)} all-to-all(bf16[8,3,256,64]{2,3,1,0:T(8,128)(2,1)} %get-tuple-element.50), channel_id=1, replica_groups=mesh['px'=4,'py'=8] {'py'}, dimensions={0} | all-to-all | bytes 1572864 | tf_op jit(solution)/shard_map/all_to_all | solution.py:132
  316.8 29.0 %all_to_all.22 = bf16[8,4,256,64]{2,3,1,0:T(8,128)(2,1)S(1)} all-to-all(bf16[8,4,256,64]{2,3,1,0:T(8,128)(2,1)S(1)} %slice.224), channel_id=1, replica_groups=mesh['px'=4,'py'=8] {'py'}, dimensions={0} | all-to-all | bytes 2097152 | tf_op jit(solution)/shard_map/all_to_all | solution.py:132
  347.9 6.5 %select_select_fusion = f32[10,256,512]{2,1,0:T(8,128)S(1)} fusion(s32[10,256,512]{2,1,0:T(8,128)} %param.27, f32[]{:T(128)} %bitcast.25, f32[]{:T(128)} %bitcast.24, f32[]{:T(128)} %bitcast.23, f32[]{:T(128)} %bitcast.22), kind=kLoop, calls=%fused_computation.30 | loop fusion | flops 10485760 | bytes 10485776 | tf_op jit(solution)/shard_map/jit(_where)/select_n | solution.py:144
  354.4 3.9 slice.225
  358.4 3.0 slice.238
  361.3 3.0 slice_reduce_fusion
  364.3 8.3 %slice_bitcast_fusion.2 = (s32[10,256,512]{2,1,0:T(8,128)}, s32[10,256,512]{2,1,0:T(8,128)S(1)}) fusion(s32[2,10,256,512]{3,2,1,0:T(8,128)} %param.28), kind=kLoop, calls=%fused_computation.29 | loop fusion | bytes 20971520 | tf_op jit(solution)/shard_map/squeeze | solution.py:146
  378.5 54.9 %all-gather.11.cloned.1.call-done = bf16[4,256,2048]{2,1,0:T(8,128)(2,1)} async-done(((bf16[4,256,512]{2,1,0:T(8,128)(2,1)}), bf16[4,256,2048]{2,1,0:T(8,128)(2,1)}) %all-gather.11.cloned.1.call-update) | async-done | bytes 4194320 | tf_op jit(solution)/shard_map/all_gather | solution.py:134
  433.4 8.6 %fusion.7 = f32[10,256,512]{2,1,0:T(8,128)S(1)} fusion(bf16[4,256,2048]{2,1,0:T(8,128)(2,1)} %all-gather.11.cloned.1.call-done, bf16[3,256,2048]{2,1,0:T(8,128)(2,1)} %all-gather.9.cloned.1.call-done, bf16[3,256,2048]{2,1,0:T(8,128)(2,1)} %all-gather.7.cloned.1.call-done, bf16[2048,512]{1,0:T(8,128)(2,1)S(1)} %copy-done), kind=kOutput, calls=%fused_computation.8 | convolution fusion | flops 5379194880 | bytes 17825792 | tf_op jit(solution)/shard_map/zyi,ix->zyx/dot_general | solution.py:135
  443.2 3.8 slice.229
  447.0 3.0 slice.242
  450.7 3.7 collective-permute-start.4
  455.7 4.0 collective-permute-start.6
  468.3 3.2 collective-permute-start.5
  471.5 2.8 multiply_select_fusion
  474.3 16.3 %fusion.20 = (f32[10,256,512]{2,1,0:T(8,128)S(1)}, f32[10,256,512]{2,1,0:T(8,128)S(1)}) fusion(f32[10,1,512]{2,1,0:T(1,128)S(1)} %get-tuple-element.56, f32[10,255,512]{2,1,0:T(8,128)} %slice.238, f32[10,256,512]{2,1,0:T(8,128)S(1)} %copy-done.2, f32[10,1,512]{2,1,0:T(1,128)S(1)} %get-tuple-element.55, f32[10,255,512]{2,1,0:T(8,128)} %slice.242, ...), kind=kLoop, calls=%fused_computation.26 | loop fusion | flops 28835840 | bytes 52429584 | tf_op jit(solution)/shard_map/jit(_where)/select_n | solution.py:164
  490.7 4.5 fusion.18
  (89 shorter events, 43.1 us)
Async XLA Ops:
  7.2 426.2 %copy-start = (bf16[2048,512]{1,0:T(8,128)(2,1)S(1)}, bf16[2048,512]{1,0:T(8,128)(2,1)}, u32[]{:S(2)}) copy-start(bf16[2048,512]{1,0:T(8,128)(2,1)} %param.26) | copy-start | bytes 6291460
  7.2 225.1 %all-gather.5.cloned.1.call-start = ((), (), s32[]{:S(2)}) async-start(), calls=%async_computation.4 | async-start | bytes 19464192 | tf_op jit(solution)/shard_map/all_gather | solution.py:108
  20.8 58.9 %collective-permute-start = (bf16[10,256,512]{2,1,0:T(8,128)(2,1)}, bf16[10,256,512]{2,1,0:T(8,128)(2,1)}, u32[]{:S(2)}, u32[]{:S(2)}) collective-permute-start(bf16[10,256,512]{2,1,0:T(8,128)(2,1)} %convert_element_type.34), channel_id=1, source_target_pairs={{0,8},{8,0},{16,24},{24,16},{1,9},{9,1},{17,25},{25,17},{2,10},{10... | collective-permute-start | bytes 7864328 | tf_op jit(solution)/shard_map/ppermute | solution.py:13
  22.8 57.7 %collective-permute-start.1 = (bf16[10,256,512]{2,1,0:T(8,128)(2,1)}, bf16[10,256,512]{2,1,0:T(8,128)(2,1)}, u32[]{:S(2)}, u32[]{:S(2)}) collective-permute-start(bf16[10,256,512]{2,1,0:T(8,128)(2,1)} %convert_element_type.34), channel_id=1, source_target_pairs={{0,16},{8,24},{16,0},{24,8},{1,17},{9,25},{17,1},{25,9},{2,18},{10... | collective-permute-start | bytes 7864328 | tf_op jit(solution)/shard_map/ppermute | solution.py:13
  24.1 112.8 %collective-permute-start.2 = (bf16[10,256,512]{2,1,0:T(8,128)(2,1)}, bf16[10,256,512]{2,1,0:T(8,128)(2,1)}, u32[]{:S(2)}, u32[]{:S(2)}) collective-permute-start(bf16[10,256,512]{2,1,0:T(8,128)(2,1)} %convert_element_type.34), channel_id=1, source_target_pairs={{0,24},{8,16},{16,8},{24,0},{1,25},{9,17},{17,9},{25,1},{2,26},{10... | collective-permute-start | bytes 7864328 | tf_op jit(solution)/shard_map/ppermute | solution.py:13
  146.8 81.9 %all-to-all-start = ((bf16[8,10,256,64]{2,3,1,0:T(8,128)(2,1)}), bf16[8,10,256,64]{2,3,1,0:T(8,128)(2,1)}, u32[]{:S(2)}, u32[]{:S(2)}) async-start(bf16[8,10,256,64]{2,3,1,0:T(8,128)(2,1)} %convert_bitcast_fusion), calls=%async_computation | async-start | bytes 5242880 | tf_op jit(solution)/shard_map/all_to_all | solution.py:100
  153.4 223.0 %all-gather.7.cloned.1.call-start = ((), (), s32[]{:S(2)}) async-start(), calls=%async_computation.5 | async-start | bytes 3932160 | tf_op jit(solution)/shard_map/all_gather | solution.py:134
  263.0 1.5 copy-start.4
  289.6 88.9 %all-gather.9.cloned.1.call-start = ((), (), s32[]{:S(2)}) async-start(), calls=%async_computation.6 | async-start | bytes 3932160 | tf_op jit(solution)/shard_map/all_gather | solution.py:134
  315.4 31.9 %copy-start.6 = (f32[4]{0:T(128)S(1)}, f32[4]{0:T(128)}, u32[]{:S(2)}) copy-start(f32[4]{0:T(128)} %param.29) | copy-start | bytes 52
  315.4 118.0 %all-gather.11.cloned.1.call-start = ((), (), s32[]{:S(2)}) async-start(), calls=%async_computation.7 | async-start | bytes 5242880 | tf_op jit(solution)/shard_map/all_gather | solution.py:134
  354.4 3.9 copy-start.3
  442.0 4.9 copy-start.1
  450.7 11.0 %collective-permute-start.4 = (f32[3,10,256,1]{2,0,1,3:T(4,128)}, f32[3,10,256,1]{2,0,1,3:T(4,128)}, u32[]{:S(2)}, u32[]{:S(2)}) collective-permute-start(f32[3,10,256,1]{2,0,1,3:T(4,128)} %pad_maximum_fusion.2), channel_id=1, source_target_pairs={{0,8},{8,16},{16,24},{1,9},{9,17},{17,25},{2,10},{10,18},{18,26},{... | collective-permute-start | bytes 92168 | tf_op jit(solution)/shard_map/ppermute | solution.py:156
  454.4 5.3 %collective-permute-start.3 = (f32[2,10,256,1]{2,0,1,3:T(2,128)S(1)}, f32[2,10,256,1]{2,0,1,3:T(2,128)S(1)}, u32[]{:S(2)}, u32[]{:S(2)}) collective-permute-start(f32[2,10,256,1]{2,0,1,3:T(2,128)S(1)} %pad_maximum_fusion.4), channel_id=1, source_target_pairs={{8,0},{16,8},{24,16},{9,1},{17,9},{25,17},{10,2},{18,10},{26,18},{... | collective-permute-start | bytes 61448 | tf_op jit(solution)/shard_map/ppermute | solution.py:155
  455.7 10.9 %collective-permute-start.6 = (f32[3,10,1,512]{3,2,1,0:T(1,128)S(1)}, f32[3,10,1,512]{3,2,1,0:T(1,128)S(1)}, u32[]{:S(2)}, u32[]{:S(2)}) collective-permute-start(f32[3,10,1,512]{3,2,1,0:T(1,128)S(1)} %pad_maximum_fusion.1), channel_id=1, source_target_pairs={{0,1},{1,2},{2,3},{3,4},{4,5},{5,6},{6,7},{8,9},{9,10},{10,11},{11... | collective-permute-start | bytes 184328 | tf_op jit(solution)/shard_map/ppermute | solution.py:156
  465.6 8.7 %copy-start.2 = (f32[10,256,512]{2,1,0:T(8,128)S(1)}, f32[10,256,512]{2,1,0:T(8,128)}, u32[]{:S(2)}) copy-start(f32[10,256,512]{2,1,0:T(8,128)} %copy-done.1) | copy-start | bytes 15728644
  465.6 8.7 %copy-start.5 = (f32[10,256,1]{2,1,0:T(8,128)S(1)}, f32[10,256,1]{2,1,0:T(8,128)}, u32[]{:S(2)}) copy-start(f32[10,256,1]{2,1,0:T(8,128)} %copy.267) | copy-start | bytes 30724
  468.3 6.0 %collective-permute-start.5 = (f32[2,10,1,512]{3,2,1,0:T(1,128)S(1)}, f32[2,10,1,512]{3,2,1,0:T(1,128)S(1)}, u32[]{:S(2)}, u32[]{:S(2)}) collective-permute-start(f32[2,10,1,512]{3,2,1,0:T(1,128)S(1)} %pad_maximum_fusion.3), channel_id=1, source_target_pairs={{1,0},{2,1},{3,2},{4,3},{5,4},{6,5},{7,6},{9,8},{10,9},{11,10},{12... | collective-permute-start | bytes 122888 | tf_op jit(solution)/shard_map/ppermute | solution.py:155
Sparse Core Ops, SparseCore 0:
  16.6 176.9 all-gather.4
  289.8 43.0 all-gather.6
  334.6 43.8 all-gather.8
  380.8 52.5 all-gather.10
